TPU v7x, 256 devices: a whole 4x4x8 slice. The times are simulated.
256 devices in a mesh: spot: 16 (over x, y_hi, core), gene: 16 (over y_lo, z).
Axes of the slice: x: 4, y: 4 (y_hi: 2, y_lo: 2; y = y_hi * 2 + y_lo), z: 8, core: 2. Of those that a mesh axis runs over, the one named last changes fastest.
Arguments:
- counts: int32 [64, 512, 4096], P('spot', None, 'gene'), may hold values from 0 to 56, as said below
- tissue: int32 [64, 512], P('spot'), may hold values from 0 to 1
- tile_ids: int32 [64, 512], P('spot'), may hold values from 0 to 32767, as said below
Outputs:
- statistic: float32 [4096, 4096], P('gene', 'spot')
Inputs may be any that keep to these rules, and one draw needn't show every extreme that they name: `counts`: whole numbers of molecules. `tile_ids`: bins of one tile form a rectangle of the grid; tiles are bands of rows crossed with bands of columns.
All inputs are finite; a program needn't handle non-finite values.
Results may differ from a plain program's by a relative error of at most 0.003.
Values may be sent and summed in bfloat16 or wider, within the bound.
No kernel may reach another device: no remote copies, remote signals or barrier semaphores. Data moves between devices by JAX's collectives and lax.ppermute only.
A program may use at most 64 MiB of HBM per device.

v0:
```python
import jax
import jax.numpy as jnp
from jax import lax
from jax.sharding import PartitionSpec as P

stencil_taps = [
    (row_off, col_off, 1.0 / (row_off * row_off + col_off * col_off))
    for row_off in range(-2, 3)
    for col_off in range(-2, 3)
    if row_off != 0 or col_off != 0
]
contract_bins = (((0,), (0,)), ((), ()))


def padded(cells, sides, width):
    for axis, dim in sides:
        count = lax.axis_size(axis)
        ends = count - 1
        head = lax.slice_in_dim(cells, 0, width, axis=dim)
        tail = lax.slice_in_dim(cells, cells.shape[dim] - width, cells.shape[dim], axis=dim)
        cells = jnp.concatenate(
            [
                lax.ppermute(tail, axis, [(i, (i + 1) % count) for i in range(ends)]),
                cells,
                lax.ppermute(head, axis, [((i + 1) % count, i) for i in range(ends)]),
            ],
            axis=dim,
        )
    return cells


def cross_panel(left, right):
    return lax.dot_general(left, right, contract_bins, preferred_element_type=jnp.float32)


def shards(counts, tissue, tile_ids):
    row_count, col_count, panel_width = counts.shape
    tile_code = tile_ids * 2 + tissue
    code_rims = padded(tile_code, (("spot", 0),), 2)
    code_wide = jnp.pad(code_rims, ((0, 0), (2, 2)))
    tissue_wide = (code_wide % 2).astype(jnp.float32)
    ids_wide = code_wide // 2
    in_tissue = tissue.astype(jnp.float32)
    weight_sq = jnp.zeros((row_count, col_count), jnp.float32)
    same_list = []
    for row_off, col_off, weight in stencil_taps:
        near_ids = ids_wide[
            2 + row_off : 2 + row_off + row_count, 2 + col_off : 2 + col_off + col_count
        ]
        near_tissue = tissue_wide[
            2 + row_off : 2 + row_off + row_count, 2 + col_off : 2 + col_off + col_count
        ]
        same_tile = (near_ids == tile_ids).astype(jnp.float32)
        weight_sq = weight_sq + weight * weight * same_tile * near_tissue
        same_list.append(same_tile)
    pair_local = jnp.sum(in_tissue * weight_sq)
    count_local = jnp.sum(in_tissue)
    values = counts.astype(jnp.float32)
    masked = values * in_tissue[:, :, None]
    first_sums = jnp.sum(masked, axis=(0, 1))
    total_first, tissue_count, pair_norm = lax.psum((first_sums, count_local, pair_local), "spot")
    gene_mean = total_first / tissue_count
    centred = (values - gene_mean) * in_tissue[:, :, None]
    variance = lax.psum(jnp.sum(centred * centred, axis=(0, 1)), "spot") / tissue_count
    zscores = (centred / jnp.sqrt(variance + 1e-05)).astype(jnp.bfloat16)
    zscore_rims = padded(zscores, (("spot", 0),), 2)
    zscore_wide = jnp.pad(zscore_rims, ((0, 0), (2, 2), (0, 0)))
    lagged_sum = jnp.zeros(values.shape, jnp.float32)
    for (row_off, col_off, weight), same_tile in zip(stencil_taps, same_list):
        near_z = zscore_wide[
            2 + row_off : 2 + row_off + row_count, 2 + col_off : 2 + col_off + col_count, :
        ]
        lagged_sum = lagged_sum + weight * same_tile[:, :, None] * near_z.astype(jnp.float32)
    lagged = lagged_sum.astype(jnp.bfloat16)
    bin_count = row_count * col_count
    flat_z = zscores.reshape(bin_count, panel_width)
    flat_lag = lagged.reshape(bin_count, panel_width)
    totals = cross_panel(flat_z, lax.all_gather(flat_lag, "gene", axis=1, tiled=True))
    share = lax.psum_scatter(totals, "spot", scatter_dimension=1, tiled=True)
    return share / jnp.sqrt(pair_norm)


def solution(mesh):
    placed = (P("spot", None, "gene"), P("spot", None), P("spot", None))
    return jax.shard_map(
        shards, mesh=mesh, in_specs=placed, out_specs=P("gene", "spot"), check_vma=False
    )
```

profile of v0, /device:TPU:6, one launch (start us, length us, event | category | flops | bytes accessed | tf_op | source)
XLA Modules:
  0.0 425.2 jit_solution(14319070710412826453)
XLA Ops:
  6.5 0.0 copy-start
  6.5 0.0 all-gather.2.cloned.1.call-start
  6.5 0.9 multiply_add_fusion
  7.4 1.9 collective-permute-start
  9.4 6.0 %collective-permute-start.1 = (s32[2,512]{1,0:T(2,128)S(1)}, s32[2,512]{1,0:T(2,128)S(1)}, u32[]{:S(2)}, u32[]{:S(2)}) collective-permute-start(s32[2,512]{1,0:T(2,128)S(1)} %get-tuple-element.104), channel_id=1, source_target_pairs={{16,0},{32,16},{48,32},{64,48},{80,64},{96,80},{112,96},{128,112},... | collective-permute-start | bytes 12296 | tf_op jit(solution)/shard_map/ppermute | solution.py:25
  15.4 1.3 convert_reduce_fusion
  16.7 0.0 copy-start.1
  16.7 0.0 copy-start.2
  16.7 2.0 multiply_reduce_fusion.1
  18.7 29.0 %all-reduce.3 = (f32[256]{0:T(256)S(1)}, f32[]{:T(128)}) all-reduce(f32[256]{0:T(256)S(1)} %multiply_reduce_fusion.1, f32[]{:T(128)} %convert_reduce_fusion), channel_id=1, replica_groups=mesh['spot'=16,'gene'=16] {'spot'}, use_global_device_ids=true, to_apply=%region_1.2 | all-reduce | flops 257 | bytes 2056 | tf_op jit(solution)/shard_map/psum | solution.py:61
  47.7 0.6 broadcast_divide_fusion.1
  48.3 0.0 copy-done
  48.3 0.4 multiply_reduce_fusion
  48.7 0.0 collective-permute-done
  48.7 0.0 collective-permute-done.1
  48.7 0.1 add_select_fusion.1
  48.8 0.0 copy-done.1
  48.9 0.1 broadcast_select_fusion.8
  48.9 0.1 fusion.37
  49.0 0.2 broadcast_select_fusion.19
  49.2 0.0 copy-done.2
  49.2 0.7 fusion.14
  49.9 31.2 %all-reduce.2 = (f32[256]{0:T(256)S(1)}, f32[]{:T(128)}) all-reduce(f32[256]{0:T(256)S(1)} %multiply_reduce_fusion, f32[]{:T(128)} %fusion.14), channel_id=1, replica_groups=mesh['spot'=16,'gene'=16] {'spot'}, use_global_device_ids=true, to_apply=%region_5.6 | all-reduce | flops 257 | bytes 2056 | tf_op jit(solution)/shard_map/psum | solution.py:64
  81.1 0.7 add_sqrt_fusion
  81.8 0.4 divide_convert_fusion
  82.2 0.1 fusion.41
  82.2 2.5 collective-permute-start.2
  84.7 5.5 %collective-permute-start.3 = (bf16[2,512,256]{2,1,0:T(8,128)(2,1)S(1)}, bf16[2,512,256]{2,1,0:T(8,128)(2,1)S(1)}, u32[]{:S(2)}, u32[]{:S(2)}) collective-permute-start(bf16[2,512,256]{2,1,0:T(8,128)(2,1)S(1)} %get-tuple-element.58), channel_id=1, source_target_pairs={{16,0},{32,16},{48,32},{64,48},{80,64},{96,80},{112,96},{128,112},... | collective-permute-start | bytes 1572872 | tf_op jit(solution)/shard_map/ppermute | solution.py:25
  90.2 4.9 %collective-permute-done.2 = bf16[2,512,256]{2,1,0:T(8,128)(2,1)S(1)} collective-permute-done((bf16[2,512,256]{2,1,0:T(8,128)(2,1)S(1)}, bf16[2,512,256]{2,1,0:T(8,128)(2,1)S(1)}, u32[]{:S(2)}, u32[]{:S(2)}) %collective-permute-start.2) | collective-permute-done | bytes 524320 | tf_op jit(solution)/shard_map/ppermute | solution.py:23
  95.1 1.8 collective-permute-done.3
  96.9 0.7 fusion.5
  97.6 12.2 %add_convert_fusion = bf16[4,512,256]{2,1,0:T(8,128)(2,1)} fusion(bf16[4,512,256]{2,1,0:T(8,128)(2,1)S(1)} %divide_convert_fusion, bf16[2,512,256]{2,1,0:T(8,128)(2,1)S(1)} %collective-permute-done.3, bf16[2,512,256]{2,1,0:T(8,128)(2,1)S(1)} %collective-permute-done.2, bf16[8,516,256]{2,1,0:T(8,128)(2,1)S(1)} %fusion.5, f32[4,512]{1,0:T(4,128)S(1)} %get-tuple-element.93, ...), kind=kLoop, calls=%fused_computation.8 | loop fusion | flops 39845888 | bytes 24313856 | tf_op jit(solution)/shard_map/convert_element_type | solution.py:74
  109.9 0.0 all-gather.2.cloned.1.call-update
  109.9 0.0 reduce-scatter.2.cloned.1.call-start
  110.0 208.4 %all-gather.2.cloned.1.call-done = bf16[2048,4096]{1,0:T(8,128)(2,1)} async-done(((bf16[2048,256]{1,0:T(8,128)(2,1)}), bf16[2048,4096]{1,0:T(8,128)(2,1)}) %all-gather.2.cloned.1.call-update) | async-done | bytes 16777232 | tf_op jit(solution)/shard_map/all_gather | solution.py:78
  318.3 10.1 %fusion.43 = f32[256,4096]{1,0:T(8,128)} fusion(bf16[2048,256]{1,0:T(8,128)(2,1)S(1)} %bitcast.4, bf16[2048,4096]{1,0:T(8,128)(2,1)} %all-gather.2.cloned.1.call-done), kind=kOutput, calls=%fused_computation.137 | convolution fusion | flops 4294967296 | bytes 22020096 | tf_op jit(solution)/shard_map/dot_general | solution.py:33
  328.4 0.0 reduce-scatter.2.cloned.1.call-update
  329.1 87.6 %reduce-scatter.2.cloned.1.call-done = f32[256,256]{1,0:T(8,128)} async-done(((f32[256,4096]{1,0:T(8,128)}), f32[256,256]{1,0:T(8,128)}) %reduce-scatter.2.cloned.1.call-update) | async-done | bytes 262160 | tf_op jit(solution)/shard_map/reduce_scatter | solution.py:79
  416.7 1.7 broadcast_divide_fusion
  (2 shorter events, 0.0 us)
Async XLA Ops:
  6.5 41.8 %copy-start = (s32[4,512,256]{2,1,0:T(8,128)S(1)}, s32[4,512,256]{2,1,0:T(8,128)}, u32[]{:S(2)}) copy-start(s32[4,512,256]{2,1,0:T(8,128)} %param.3) | copy-start | bytes 6291460
  6.5 311.8 %all-gather.2.cloned.1.call-start = ((), (), s32[]{:S(2)}) async-start(), calls=%async_computation.1 | async-start | bytes 17825792 | tf_op jit(solution)/shard_map/all_gather | solution.py:78
  7.4 41.3 %collective-permute-start = (s32[2,512]{1,0:T(2,128)S(1)}, s32[2,512]{1,0:T(2,128)S(1)}, u32[]{:S(2)}, u32[]{:S(2)}) collective-permute-start(s32[2,512]{1,0:T(2,128)S(1)} %get-tuple-element.103), channel_id=1, source_target_pairs={{0,16},{16,32},{32,48},{48,64},{64,80},{80,96},{96,112},{112,128},... | collective-permute-start | bytes 12296 | tf_op jit(solution)/shard_map/ppermute | solution.py:23
  9.4 39.4 %collective-permute-start.1 = (s32[2,512]{1,0:T(2,128)S(1)}, s32[2,512]{1,0:T(2,128)S(1)}, u32[]{:S(2)}, u32[]{:S(2)}) collective-permute-start(s32[2,512]{1,0:T(2,128)S(1)} %get-tuple-element.104), channel_id=1, source_target_pairs={{16,0},{32,16},{48,32},{64,48},{80,64},{96,80},{112,96},{128,112},... | collective-permute-start | bytes 12296 | tf_op jit(solution)/shard_map/ppermute | solution.py:25
  16.7 32.1 %copy-start.1 = (s32[4,512]{1,0:T(4,128)S(1)}, s32[4,512]{1,0:T(4,128)}, u32[]{:S(2)}) copy-start(s32[4,512]{1,0:T(4,128)} %param.5) | copy-start | bytes 24580
  16.7 32.5 %copy-start.2 = (s32[4,512]{1,0:T(4,128)S(1)}, s32[4,512]{1,0:T(4,128)}, u32[]{:S(2)}) copy-start(s32[4,512]{1,0:T(4,128)} %param.4) | copy-start | bytes 24580
  82.2 12.9 %collective-permute-start.2 = (bf16[2,512,256]{2,1,0:T(8,128)(2,1)S(1)}, bf16[2,512,256]{2,1,0:T(8,128)(2,1)S(1)}, u32[]{:S(2)}, u32[]{:S(2)}) collective-permute-start(bf16[2,512,256]{2,1,0:T(8,128)(2,1)S(1)} %get-tuple-element.57), channel_id=1, source_target_pairs={{0,16},{16,32},{32,48},{48,64},{64,80},{80,96},{96,112},{112,128},... | collective-permute-start | bytes 1572872 | tf_op jit(solution)/shard_map/ppermute | solution.py:23
  84.7 12.2 %collective-permute-start.3 = (bf16[2,512,256]{2,1,0:T(8,128)(2,1)S(1)}, bf16[2,512,256]{2,1,0:T(8,128)(2,1)S(1)}, u32[]{:S(2)}, u32[]{:S(2)}) collective-permute-start(bf16[2,512,256]{2,1,0:T(8,128)(2,1)S(1)} %get-tuple-element.58), channel_id=1, source_target_pairs={{16,0},{32,16},{48,32},{64,48},{80,64},{96,80},{112,96},{128,112},... | collective-permute-start | bytes 1572872 | tf_op jit(solution)/shard_map/ppermute | solution.py:25
  109.9 306.8 %reduce-scatter.2.cloned.1.call-start = ((), (), s32[]{:S(2)}) async-start(), calls=%async_computation.2 | async-start | bytes 4456448 | tf_op jit(solution)/shard_map/reduce_scatter | solution.py:79
Sparse Core Ops, SparseCore 0:
  110.0 208.2 all-gather.1
  328.6 88.0 reduce-scatter.1
where the time goes:
time: 426 us; the launch traced here: 425 us
  waiting for transfers between devices  303 us (71%)
  blocking collectives  60.1 us (14%)
  other arithmetic  22 us (5%)
  starting transfers between devices  16 us (4%)
  between operations  14.1 us (3%)
  matrix products  10.1 us (2%)
    all_gather x1, waiting for transfers between devices, shards(): lax.all_gather(flat_lag, 'gene', axis=1, tiled=True)  208 us
    reduce_scatter x1, waiting for transfers between devices, shards(): share = lax.psum_scatter(totals, 'spot', scatter_dimension=1, tiled=True)  87.6 us
    psum x1, blocking collectives, shards(): lax.psum(jnp.sum(centred * centred, axis=(0, 1)), 'spot') / tissue_count  31.2 us
    psum x1, blocking collectives, shards(): lax.psum((first_sums, count_local, pair_local), 'spot')  29 us
    convert_element_type x1, other arithmetic, shards(): lagged = lagged_sum.astype(jnp.bfloat16)  12.2 us
    ppermute x2, starting transfers between devices, padded(): lax.ppermute(head, axis, [((i + 1) % count, i) for i in range(ends)])  11.5 us
    dot_general x1, matrix products, cross_panel(): lax.dot_general(left, right, contract_bins, preferred_element_type=jnp.fl...  10.1 us
  transfers between devices with their start and end apart: 6, of which 4 were waited for; matrix products, arithmetic and copies ran while one was open for 1% of the time, Pallas kernels for 0%

commit v1 on v0

--- a/solution.py
+++ b/solution.py
@@ -1,3 +1,5 @@
+import math
+
 import jax
 import jax.numpy as jnp
 from jax import lax
@@ -29,12 +31,47 @@
     return cells
 
 
-def cross_panel(left, right):
-    return lax.dot_general(left, right, contract_bins, preferred_element_type=jnp.float32)
+def merge_moments(left, right):
+    n_a, s_a, m_a, q_a = left
+    n_b, s_b, m_b, q_b = right
+    n = n_a + n_b
+    gap = s_a / jnp.maximum(n_a, 1.0) - s_b / jnp.maximum(n_b, 1.0)
+    m = m_a + m_b + gap * gap * (n_a * n_b / jnp.maximum(n, 1.0))
+    return n, s_a + s_b, m, q_a + q_b
+
+
+def allreduce_moments(moments, axis):
+    count = lax.axis_size(axis)
+    width = moments[1].shape[0]
+    step = 1
+    while step < count:
+        perm = [(i, i ^ step) for i in range(count)]
+        n, s, m, q = moments
+        packed = jnp.concatenate([s, m, jnp.stack([n, q])])
+        packed = lax.ppermute(packed, axis, perm)
+        other = (packed[2 * width], packed[:width], packed[width : 2 * width], packed[2 * width + 1])
+        moments = merge_moments(moments, other)
+        step *= 2
+    return moments
+
+
+def gather_group(block, axis, members, shift):
+    parts = [block]
+    for t in range(1, shift):
+        perm = []
+        for group in members:
+            size = len(group)
+            for k, src in enumerate(group):
+                perm.append((src, group[(k + t) % size]))
+        parts.append(lax.ppermute(block, axis, perm))
+    return jnp.concatenate(parts, axis=1)
 
 
 def shards(counts, tissue, tile_ids):
     row_count, col_count, panel_width = counts.shape
+    spot_n = lax.axis_size("spot")
+    gene_n = lax.axis_size("gene")
+    side = math.isqrt(gene_n)
     tile_code = tile_ids * 2 + tissue
     code_rims = padded(tile_code, (("spot", 0),), 2)
     code_wide = jnp.pad(code_rims, ((0, 0), (2, 2)))
@@ -56,12 +93,17 @@
     pair_local = jnp.sum(in_tissue * weight_sq)
     count_local = jnp.sum(in_tissue)
     values = counts.astype(jnp.float32)
-    masked = values * in_tissue[:, :, None]
-    first_sums = jnp.sum(masked, axis=(0, 1))
-    total_first, tissue_count, pair_norm = lax.psum((first_sums, count_local, pair_local), "spot")
+    mask = in_tissue[:, :, None]
+    sum_local = jnp.sum(values * mask, axis=(0, 1))
+    mean_local = sum_local / jnp.maximum(count_local, 1.0)
+    dev_local = (values - mean_local) * mask
+    sq_local = jnp.sum(dev_local * dev_local, axis=(0, 1))
+    tissue_count, total_first, sq_total, pair_norm = allreduce_moments(
+        (count_local, sum_local, sq_local, pair_local), "spot"
+    )
     gene_mean = total_first / tissue_count
-    centred = (values - gene_mean) * in_tissue[:, :, None]
-    variance = lax.psum(jnp.sum(centred * centred, axis=(0, 1)), "spot") / tissue_count
+    variance = sq_total / tissue_count
+    centred = (values - gene_mean) * mask
     zscores = (centred / jnp.sqrt(variance + 1e-05)).astype(jnp.bfloat16)
     zscore_rims = padded(zscores, (("spot", 0),), 2)
     zscore_wide = jnp.pad(zscore_rims, ((0, 0), (2, 2), (0, 0)))
@@ -75,8 +117,23 @@
     bin_count = row_count * col_count
     flat_z = zscores.reshape(bin_count, panel_width)
     flat_lag = lagged.reshape(bin_count, panel_width)
-    totals = cross_panel(flat_z, lax.all_gather(flat_lag, "gene", axis=1, tiled=True))
-    share = lax.psum_scatter(totals, "spot", scatter_dimension=1, tiled=True)
+    rows = [[side * i + k for k in range(side)] for i in range(side)]
+    cols = [[side * k + j for k in range(side)] for j in range(side)]
+    z_cat = gather_group(flat_z, "gene", rows, side)
+    lag_cat = gather_group(flat_lag, "gene", cols, side)
+    block = lax.dot_general(z_cat, lag_cat, contract_bins, preferred_element_type=jnp.float32)
+    block = block.reshape(side, panel_width, side, panel_width).transpose(0, 2, 1, 3)
+    block = block.reshape(side * side * panel_width, panel_width)
+    share = lax.psum_scatter(block, "spot", scatter_dimension=0, tiled=True)
+    perm = []
+    for sigma in range(spot_n):
+        for c in range(gene_n):
+            i, j = divmod(c, side)
+            t1, t2 = divmod(sigma, side)
+            g = side * i + (j - t1) % side
+            s = side * ((i - t2) % side) + j
+            perm.append((sigma * gene_n + c, s * gene_n + g))
+    share = lax.ppermute(share, ("spot", "gene"), perm)
     return share / jnp.sqrt(pair_norm)
 
 

time: 426 us -> 377 us (0.88)
  the two profiles are of different devices: /device:TPU:6 before, /device:TPU:16 now
where the time goes in v1:
time: 377 us; the launch traced here: 376 us
  waiting for transfers between devices  270 us (72%)
  starting transfers between devices  39.5 us (10%)
  between operations  26.4 us (7%)
  other arithmetic  20.4 us (5%)
  local copies, waits for them, and re-layouts  13.2 us (4%)
  matrix products  6.63 us (2%)
    ppermute x6, waiting for transfers between devices, gather_group(): parts.append(lax.ppermute(block, axis, perm))  139 us
    reduce_scatter x1, waiting for transfers between devices, shards(): share = lax.psum_scatter(block, 'spot', scatter_dimension=0, tiled=True)  100 us
    ppermute x6, starting transfers between devices, gather_group(): parts.append(lax.ppermute(block, axis, perm))  15.7 us
    ppermute x1, waiting for transfers between devices, shards(): share = lax.ppermute(share, ('spot', 'gene'), perm)  14.8 us
    convert_element_type x1, other arithmetic, shards(): lagged = lagged_sum.astype(jnp.bfloat16)  11.2 us
    ppermute x2, starting transfers between devices, padded(): lax.ppermute(head, axis, [((i + 1) % count, i) for i in range(ends)])  10.3 us
    ppermute x4, waiting for transfers between devices, allreduce_moments(): packed = lax.ppermute(packed, axis, perm)  10.3 us
  transfers between devices with their start and end apart: 16, of which 8 were waited for; matrix products, arithmetic and copies ran while one was open for 4% of the time, Pallas kernels for 0%

profile of v1, /device:TPU:16, one launch (start us, length us, event | category | flops | bytes accessed | tf_op | source)
XLA Modules:
  0.0 376.0 jit_solution(4726001863523787226)
XLA Ops:
  6.5 0.0 copy-start
  6.5 0.0 reduce-scatter.2.cloned.1.call-start
  6.5 0.9 multiply_add_fusion
  7.4 1.9 collective-permute-start
  9.4 5.1 %collective-permute-start.1 = (s32[2,512]{1,0:T(2,128)S(1)}, s32[2,512]{1,0:T(2,128)S(1)}, u32[]{:S(2)}, u32[]{:S(2)}) collective-permute-start(s32[2,512]{1,0:T(2,128)S(1)} %get-tuple-element.100), channel_id=1, source_target_pairs={{16,0},{32,16},{48,32},{64,48},{80,64},{96,80},{112,96},{128,112},... | collective-permute-start | bytes 12296 | tf_op jit(solution)/shard_map/ppermute | solution.py:27
  14.5 1.3 convert_reduce_fusion
  16.5 0.0 copy-start.1
  16.5 0.0 copy-start.2
  16.5 1.9 multiply_reduce_fusion.1
  18.5 0.0 copy-done
  18.5 0.4 multiply_reduce_fusion
  18.9 0.0 collective-permute-done
  18.9 0.0 collective-permute-done.1
  18.9 0.1 add_select_fusion.1
  19.0 0.0 copy-done.1
  19.0 0.1 broadcast_select_fusion.4
  19.1 0.1 fusion.57
  19.2 0.2 broadcast_select_fusion.15
  19.4 0.0 copy-done.2
  19.4 0.8 fusion.29
  20.1 1.3 pad_maximum_fusion.2
  21.5 0.0 collective-permute-start.2
  21.5 1.2 collective-permute-done.2
  22.7 0.6 fusion.66
  27.8 0.1 pad_maximum_fusion.3
  27.9 0.2 collective-permute-start.3
  28.1 4.9 %collective-permute-done.3 = f32[514]{0:T(1024)S(1)} collective-permute-done((f32[514]{0:T(1024)S(1)}, f32[514]{0:T(1024)S(1)}, u32[]{:S(2)}, u32[]{:S(2)}) %collective-permute-start.3) | collective-permute-done | bytes 2088 | tf_op jit(solution)/shard_map/ppermute | solution.py:51
  33.0 0.6 fusion.65
  36.2 0.1 pad_maximum_fusion.4
  36.3 1.5 collective-permute-start.4
  37.8 2.1 collective-permute-done.4
  39.9 0.6 fusion.64
  43.1 0.1 pad_maximum_fusion.5
  43.2 3.1 collective-permute-start.5
  46.2 2.1 collective-permute-done.5
  48.3 0.6 fusion.63
  50.9 0.4 divide_convert_fusion
  51.3 0.1 fusion.61
  51.4 1.9 collective-permute-start.9
  53.3 5.1 %collective-permute-start.10 = (bf16[2,512,256]{2,1,0:T(8,128)(2,1)S(1)}, bf16[2,512,256]{2,1,0:T(8,128)(2,1)S(1)}, u32[]{:S(2)}, u32[]{:S(2)}) collective-permute-start(bf16[2,512,256]{2,1,0:T(8,128)(2,1)S(1)} %get-tuple-element.54), channel_id=1, source_target_pairs={{16,0},{32,16},{48,32},{64,48},{80,64},{96,80},{112,96},{128,112},... | collective-permute-start | bytes 1572872 | tf_op jit(solution)/shard_map/ppermute | solution.py:27
  58.5 4.7 %collective-permute-start.8 = (bf16[2048,256]{1,0:T(8,128)(2,1)S(1)}, bf16[2048,256]{1,0:T(8,128)(2,1)S(1)}, u32[]{:S(2)}, u32[]{:S(2)}) collective-permute-start(bf16[2048,256]{1,0:T(8,128)(2,1)S(1)} %bitcast.22), channel_id=1, source_target_pairs={{0,3},{1,0},{2,1},{3,2},{4,7},{5,4},{6,5},{7,6},{8,11},{9,8},{10,9... | collective-permute-start | bytes 3145736 | tf_op jit(solution)/shard_map/ppermute | solution.py:66
  63.2 0.0 collective-permute-start.7
  63.2 0.7 collective-permute-start.6
  63.9 5.2 %collective-permute-done.9 = bf16[2,512,256]{2,1,0:T(8,128)(2,1)S(1)} collective-permute-done((bf16[2,512,256]{2,1,0:T(8,128)(2,1)S(1)}, bf16[2,512,256]{2,1,0:T(8,128)(2,1)S(1)}, u32[]{:S(2)}, u32[]{:S(2)}) %collective-permute-start.9) | collective-permute-done | bytes 524320 | tf_op jit(solution)/shard_map/ppermute | solution.py:25
  69.0 0.0 collective-permute-done.10
  69.0 0.7 fusion.20
  69.8 11.2 %add_convert_fusion = bf16[4,512,256]{2,1,0:T(8,128)(2,1)S(1)} fusion(bf16[4,512,256]{2,1,0:T(8,128)(2,1)S(1)} %divide_convert_fusion, bf16[2,512,256]{2,1,0:T(8,128)(2,1)S(1)} %collective-permute-done.10, bf16[2,512,256]{2,1,0:T(8,128)(2,1)S(1)} %collective-permute-done.9, bf16[8,516,256]{2,1,0:T(8,128)(2,1)S(1)} %fusion.20, ...), kind=kLoop, calls=%fused_computation.23 | loop fusion | flops 39845888 | bytes 24313856 | tf_op jit(solution)/shard_map/convert_element_type | solution.py:116
  81.0 4.1 %collective-permute-start.13 = (bf16[2048,256]{1,0:T(8,128)(2,1)S(1)}, bf16[2048,256]{1,0:T(8,128)(2,1)S(1)}, u32[]{:S(2)}, u32[]{:S(2)}) collective-permute-start(bf16[2048,256]{1,0:T(8,128)(2,1)S(1)} %bitcast.26), channel_id=1, source_target_pairs={{0,12},{4,0},{8,4},{12,8},{1,13},{5,1},{9,5},{13,9},{2,14},{6,2},{... | collective-permute-start | bytes 3145736 | tf_op jit(solution)/shard_map/ppermute | solution.py:66
  85.1 4.6 %collective-permute-start.12 = (bf16[2048,256]{1,0:T(8,128)(2,1)S(1)}, bf16[2048,256]{1,0:T(8,128)(2,1)S(1)}, u32[]{:S(2)}, u32[]{:S(2)}) collective-permute-start(bf16[2048,256]{1,0:T(8,128)(2,1)S(1)} %bitcast.27), channel_id=1, source_target_pairs={{0,8},{4,12},{8,0},{12,4},{1,9},{5,13},{9,1},{13,5},{2,10},{6,14},... | collective-permute-start | bytes 3145736 | tf_op jit(solution)/shard_map/ppermute | solution.py:66
  89.7 0.0 collective-permute-done.8
  89.7 1.6 collective-permute-start.11
  91.3 139.1 %collective-permute-done.7 = bf16[2048,256]{1,0:T(8,128)(2,1)S(1)} collective-permute-done((bf16[2048,256]{1,0:T(8,128)(2,1)S(1)}, bf16[2048,256]{1,0:T(8,128)(2,1)S(1)}, u32[]{:S(2)}, u32[]{:S(2)}) %collective-permute-start.7) | collective-permute-done | bytes 1048608 | tf_op jit(solution)/shard_map/ppermute | solution.py:66
  230.4 0.0 collective-permute-done.6
  230.4 0.0 collective-permute-done.13
  230.4 0.0 collective-permute-done.12
  230.4 0.0 collective-permute-done.11
  230.4 6.6 %fusion.1 = f32[1024,1024]{1,0:T(8,128)} fusion(bf16[2048,256]{1,0:T(8,128)(2,1)S(1)} %collective-permute-done.8, bf16[2048,256]{1,0:T(8,128)(2,1)S(1)} %collective-permute-done.7, bf16[2048,256]{1,0:T(8,128)(2,1)S(1)} %collective-permute-done.6, bf16[2048,256]{1,0:T(8,128)(2,1)S(1)} %bitcast.25, bf16[2048,256]{1,0:T(8,128)(2,1)S(1)} %collective-permute-done.13, ...), kind=kOutput, calls=%fused_computation.3 | convolution fusion | flops 4328521728 | bytes 12582912 | tf_op jit(solution)/shard_map/dot_general | solution.py:124
  237.1 5.6 %reshape.64 = f32[4,256,4,256]{3,2,1,0:T(4,128)} reshape(f32[1024,1024]{1,0:T(8,128)} %fusion.1) | data formatting | bytes 8388608 | tf_op jit(solution)/shard_map/reshape | solution.py:125
  242.7 4.9 %copy.4 = f32[4,4,256,256]{3,2,1,0:T(8,128)} copy(f32[4,4,256,256]{3,1,2,0:T(4,128)} %bitcast.21) | data formatting | bytes 8388608 | tf_op jit(solution)/shard_map/transpose | solution.py:125
  247.6 0.0 reduce-scatter.2.cloned.1.call-update
  247.6 100.5 %reduce-scatter.2.cloned.1.call-done = f32[256,256]{1,0:T(8,128)} async-done(((f32[4096,256]{1,0:T(8,128)}), f32[256,256]{1,0:T(8,128)}) %reduce-scatter.2.cloned.1.call-update) | async-done | bytes 262160 | tf_op jit(solution)/shard_map/reduce_scatter | solution.py:127
  348.1 4.8 %collective-permute-start.14 = (f32[256,256]{1,0:T(8,128)}, f32[256,256]{1,0:T(8,128)S(1)}, u32[]{:S(2)}, u32[]{:S(2)}) collective-permute-start(f32[256,256]{1,0:T(8,128)} %reduce-scatter.2.cloned.1.call-done), channel_id=1, source_target_pairs={{0,0},{1,17},{2,34},{3,51},{4,68},{5,85},{6,102},{7,119},{8,136},{... | collective-permute-start | bytes 786440 | tf_op jit(solution)/shard_map/ppermute | solution.py:136
  353.6 14.8 %collective-permute-done.14 = f32[256,256]{1,0:T(8,128)S(1)} collective-permute-done((f32[256,256]{1,0:T(8,128)}, f32[256,256]{1,0:T(8,128)S(1)}, u32[]{:S(2)}, u32[]{:S(2)}) %collective-permute-start.14) | collective-permute-done | bytes 262176 | tf_op jit(solution)/shard_map/ppermute | solution.py:136
  368.4 0.7 broadcast_divide_fusion
  (7 shorter events, 0.1 us)
Async XLA Ops:
  6.5 11.9 %copy-start = (s32[4,512,256]{2,1,0:T(8,128)S(1)}, s32[4,512,256]{2,1,0:T(8,128)}, u32[]{:S(2)}) copy-start(s32[4,512,256]{2,1,0:T(8,128)} %param.3) | copy-start | bytes 6291460
  6.5 341.6 %reduce-scatter.2.cloned.1.call-start = ((), (), s32[]{:S(2)}) async-start(), calls=%async_computation.1 | async-start | bytes 4456448 | tf_op jit(solution)/shard_map/reduce_scatter | solution.py:127
  7.4 11.4 %collective-permute-start = (s32[2,512]{1,0:T(2,128)S(1)}, s32[2,512]{1,0:T(2,128)S(1)}, u32[]{:S(2)}, u32[]{:S(2)}) collective-permute-start(s32[2,512]{1,0:T(2,128)S(1)} %get-tuple-element.99), channel_id=1, source_target_pairs={{0,16},{16,32},{32,48},{48,64},{64,80},{80,96},{96,112},{112,128},... | collective-permute-start | bytes 12296 | tf_op jit(solution)/shard_map/ppermute | solution.py:25
  9.4 9.5 %collective-permute-start.1 = (s32[2,512]{1,0:T(2,128)S(1)}, s32[2,512]{1,0:T(2,128)S(1)}, u32[]{:S(2)}, u32[]{:S(2)}) collective-permute-start(s32[2,512]{1,0:T(2,128)S(1)} %get-tuple-element.100), channel_id=1, source_target_pairs={{16,0},{32,16},{48,32},{64,48},{80,64},{96,80},{112,96},{128,112},... | collective-permute-start | bytes 12296 | tf_op jit(solution)/shard_map/ppermute | solution.py:27
  16.5 2.5 copy-start.1
  16.5 2.9 copy-start.2
  21.5 1.2 collective-permute-start.2
  27.9 5.1 %collective-permute-start.3 = (f32[514]{0:T(1024)S(1)}, f32[514]{0:T(1024)S(1)}, u32[]{:S(2)}, u32[]{:S(2)}) collective-permute-start(f32[514]{0:T(1024)S(1)} %pad_maximum_fusion.3), channel_id=1, source_target_pairs={{0,32},{16,48},{32,0},{48,16},{64,96},{80,112},{96,64},{112,80},{1... | collective-permute-start | bytes 6176 | tf_op jit(solution)/shard_map/ppermute | solution.py:51
  36.3 3.6 collective-permute-start.4
  43.2 5.1 %collective-permute-start.5 = (f32[514]{0:T(1024)S(1)}, f32[514]{0:T(1024)S(1)}, u32[]{:S(2)}, u32[]{:S(2)}) collective-permute-start(f32[514]{0:T(1024)S(1)} %pad_maximum_fusion.5), channel_id=1, source_target_pairs={{0,128},{16,144},{32,160},{48,176},{64,192},{80,208},{96,224},{112... | collective-permute-start | bytes 6176 | tf_op jit(solution)/shard_map/ppermute | solution.py:51
  51.4 17.6 %collective-permute-start.9 = (bf16[2,512,256]{2,1,0:T(8,128)(2,1)S(1)}, bf16[2,512,256]{2,1,0:T(8,128)(2,1)S(1)}, u32[]{:S(2)}, u32[]{:S(2)}) collective-permute-start(bf16[2,512,256]{2,1,0:T(8,128)(2,1)S(1)} %get-tuple-element.53), channel_id=1, source_target_pairs={{0,16},{16,32},{32,48},{48,64},{64,80},{80,96},{96,112},{112,128},... | collective-permute-start | bytes 1572872 | tf_op jit(solution)/shard_map/ppermute | solution.py:25
  53.3 15.7 %collective-permute-start.10 = (bf16[2,512,256]{2,1,0:T(8,128)(2,1)S(1)}, bf16[2,512,256]{2,1,0:T(8,128)(2,1)S(1)}, u32[]{:S(2)}, u32[]{:S(2)}) collective-permute-start(bf16[2,512,256]{2,1,0:T(8,128)(2,1)S(1)} %get-tuple-element.54), channel_id=1, source_target_pairs={{16,0},{32,16},{48,32},{64,48},{80,64},{96,80},{112,96},{128,112},... | collective-permute-start | bytes 1572872 | tf_op jit(solution)/shard_map/ppermute | solution.py:27
  58.5 31.2 %collective-permute-start.8 = (bf16[2048,256]{1,0:T(8,128)(2,1)S(1)}, bf16[2048,256]{1,0:T(8,128)(2,1)S(1)}, u32[]{:S(2)}, u32[]{:S(2)}) collective-permute-start(bf16[2048,256]{1,0:T(8,128)(2,1)S(1)} %bitcast.22), channel_id=1, source_target_pairs={{0,3},{1,0},{2,1},{3,2},{4,7},{5,4},{6,5},{7,6},{8,11},{9,8},{10,9... | collective-permute-start | bytes 3145736 | tf_op jit(solution)/shard_map/ppermute | solution.py:66
  63.2 167.2 %collective-permute-start.7 = (bf16[2048,256]{1,0:T(8,128)(2,1)S(1)}, bf16[2048,256]{1,0:T(8,128)(2,1)S(1)}, u32[]{:S(2)}, u32[]{:S(2)}) collective-permute-start(bf16[2048,256]{1,0:T(8,128)(2,1)S(1)} %bitcast.23), channel_id=1, source_target_pairs={{0,2},{1,3},{2,0},{3,1},{4,6},{5,7},{6,4},{7,5},{8,10},{9,11},{10,... | collective-permute-start | bytes 3145736 | tf_op jit(solution)/shard_map/ppermute | solution.py:66
  63.2 167.2 %collective-permute-start.6 = (bf16[2048,256]{1,0:T(8,128)(2,1)S(1)}, bf16[2048,256]{1,0:T(8,128)(2,1)S(1)}, u32[]{:S(2)}, u32[]{:S(2)}) collective-permute-start(bf16[2048,256]{1,0:T(8,128)(2,1)S(1)} %bitcast.24), channel_id=1, source_target_pairs={{0,1},{1,2},{2,3},{3,0},{4,5},{5,6},{6,7},{7,4},{8,9},{9,10},{10,1... | collective-permute-start | bytes 3145736 | tf_op jit(solution)/shard_map/ppermute | solution.py:66
  81.0 149.5 %collective-permute-start.13 = (bf16[2048,256]{1,0:T(8,128)(2,1)S(1)}, bf16[2048,256]{1,0:T(8,128)(2,1)S(1)}, u32[]{:S(2)}, u32[]{:S(2)}) collective-permute-start(bf16[2048,256]{1,0:T(8,128)(2,1)S(1)} %bitcast.26), channel_id=1, source_target_pairs={{0,12},{4,0},{8,4},{12,8},{1,13},{5,1},{9,5},{13,9},{2,14},{6,2},{... | collective-permute-start | bytes 3145736 | tf_op jit(solution)/shard_map/ppermute | solution.py:66
  85.1 145.3 %collective-permute-start.12 = (bf16[2048,256]{1,0:T(8,128)(2,1)S(1)}, bf16[2048,256]{1,0:T(8,128)(2,1)S(1)}, u32[]{:S(2)}, u32[]{:S(2)}) collective-permute-start(bf16[2048,256]{1,0:T(8,128)(2,1)S(1)} %bitcast.27), channel_id=1, source_target_pairs={{0,8},{4,12},{8,0},{12,4},{1,9},{5,13},{9,1},{13,5},{2,10},{6,14},... | collective-permute-start | bytes 3145736 | tf_op jit(solution)/shard_map/ppermute | solution.py:66
  89.7 140.7 %collective-permute-start.11 = (bf16[2048,256]{1,0:T(8,128)(2,1)S(1)}, bf16[2048,256]{1,0:T(8,128)(2,1)S(1)}, u32[]{:S(2)}, u32[]{:S(2)}) collective-permute-start(bf16[2048,256]{1,0:T(8,128)(2,1)S(1)} %bitcast.28), channel_id=1, source_target_pairs={{0,4},{4,8},{8,12},{12,0},{1,5},{5,9},{9,13},{13,1},{2,6},{6,10},{... | collective-permute-start | bytes 3145736 | tf_op jit(solution)/shard_map/ppermute | solution.py:66
  348.1 20.3 %collective-permute-start.14 = (f32[256,256]{1,0:T(8,128)}, f32[256,256]{1,0:T(8,128)S(1)}, u32[]{:S(2)}, u32[]{:S(2)}) collective-permute-start(f32[256,256]{1,0:T(8,128)} %reduce-scatter.2.cloned.1.call-done), channel_id=1, source_target_pairs={{0,0},{1,17},{2,34},{3,51},{4,68},{5,85},{6,102},{7,119},{8,136},{... | collective-permute-start | bytes 786440 | tf_op jit(solution)/shard_map/ppermute | solution.py:136
Sparse Core Ops, SparseCore 0:
  247.7 100.3 reduce-scatter.1

commit v2 on v1

--- a/solution.py
+++ b/solution.py
@@ -12,6 +12,12 @@
     if row_off != 0 or col_off != 0
 ]
 contract_bins = (((0,), (0,)), ((), ()))
+GENE_AXES = ("ylo", "za", "zv")
+ROW_AXES = ("ylo", "zv")
+COL_AXES = ("za",)
+SPOT_AXES = ("sx", "syh", "sc")
+ROW_RING = [0, 1, 3, 2]
+COL_RING = [0, 1, 2, 3]
 
 
 def padded(cells, sides, width):
@@ -55,25 +61,40 @@
     return moments
 
 
-def gather_group(block, axis, members, shift):
-    parts = [block]
-    for t in range(1, shift):
-        perm = []
-        for group in members:
-            size = len(group)
-            for k, src in enumerate(group):
-                perm.append((src, group[(k + t) % size]))
-        parts.append(lax.ppermute(block, axis, perm))
-    return jnp.concatenate(parts, axis=1)
+def ring_gather(block, axes, ring):
+    size = len(ring)
+    fwd = [(ring[k], ring[(k + 1) % size]) for k in range(size)]
+    bwd = [(ring[(k + 1) % size], ring[k]) for k in range(size)]
+    prev = lax.ppermute(block, axes, fwd)
+    nxt = lax.ppermute(block, axes, bwd)
+    half = block.shape[0] // 2
+    far_lo = lax.ppermute(prev[:half], axes, fwd)
+    far_hi = lax.ppermute(nxt[half:], axes, bwd)
+    return [block, prev, jnp.concatenate([far_lo, far_hi], axis=0), nxt]
+
+
+def unravel(index, sizes):
+    out = []
+    for size in reversed(sizes):
+        index, rest = divmod(index, size)
+        out.append(rest)
+    return out[::-1]
+
+
+def ravel(coords, sizes):
+    index = 0
+    for coord, size in zip(coords, sizes):
+        index = index * size + coord
+    return index
 
 
 def shards(counts, tissue, tile_ids):
     row_count, col_count, panel_width = counts.shape
-    spot_n = lax.axis_size("spot")
-    gene_n = lax.axis_size("gene")
+    spot_n = math.prod(lax.axis_size(a) for a in SPOT_AXES)
+    gene_n = math.prod(lax.axis_size(a) for a in GENE_AXES)
     side = math.isqrt(gene_n)
     tile_code = tile_ids * 2 + tissue
-    code_rims = padded(tile_code, (("spot", 0),), 2)
+    code_rims = padded(tile_code, ((SPOT_AXES, 0),), 2)
     code_wide = jnp.pad(code_rims, ((0, 0), (2, 2)))
     tissue_wide = (code_wide % 2).astype(jnp.float32)
     ids_wide = code_wide // 2
@@ -99,13 +120,13 @@
     dev_local = (values - mean_local) * mask
     sq_local = jnp.sum(dev_local * dev_local, axis=(0, 1))
     tissue_count, total_first, sq_total, pair_norm = allreduce_moments(
-        (count_local, sum_local, sq_local, pair_local), "spot"
+        (count_local, sum_local, sq_local, pair_local), SPOT_AXES
     )
     gene_mean = total_first / tissue_count
     variance = sq_total / tissue_count
     centred = (values - gene_mean) * mask
     zscores = (centred / jnp.sqrt(variance + 1e-05)).astype(jnp.bfloat16)
-    zscore_rims = padded(zscores, (("spot", 0),), 2)
+    zscore_rims = padded(zscores, ((SPOT_AXES, 0),), 2)
     zscore_wide = jnp.pad(zscore_rims, ((0, 0), (2, 2), (0, 0)))
     lagged_sum = jnp.zeros(values.shape, jnp.float32)
     for (row_off, col_off, weight), same_tile in zip(stencil_taps, same_list):
@@ -117,28 +138,51 @@
     bin_count = row_count * col_count
     flat_z = zscores.reshape(bin_count, panel_width)
     flat_lag = lagged.reshape(bin_count, panel_width)
-    rows = [[side * i + k for k in range(side)] for i in range(side)]
-    cols = [[side * k + j for k in range(side)] for j in range(side)]
-    z_cat = gather_group(flat_z, "gene", rows, side)
-    lag_cat = gather_group(flat_lag, "gene", cols, side)
-    block = lax.dot_general(z_cat, lag_cat, contract_bins, preferred_element_type=jnp.float32)
-    block = block.reshape(side, panel_width, side, panel_width).transpose(0, 2, 1, 3)
-    block = block.reshape(side * side * panel_width, panel_width)
-    share = lax.psum_scatter(block, "spot", scatter_dimension=0, tiled=True)
+    z_parts = ring_gather(flat_z, ROW_AXES, ROW_RING)
+    lag_parts = ring_gather(flat_lag, COL_AXES, COL_RING)
+    z_cat = jnp.concatenate(z_parts, axis=1)
+    block = jnp.concatenate(
+        [lax.dot_general(z_cat, part, contract_bins, preferred_element_type=jnp.float32) for part in lag_parts],
+        axis=0,
+    )
+    half = side * side // 2
+    core = lax.axis_index("sc")
+    mine = lax.dynamic_slice_in_dim(block, core * half * panel_width, half * panel_width, 0)
+    other = lax.dynamic_slice_in_dim(block, (1 - core) * half * panel_width, half * panel_width, 0)
+    mine = mine + lax.ppermute(other, "sc", [(0, 1), (1, 0)])
+    share = lax.psum_scatter(mine, ("sx", "syh"), scatter_dimension=0, tiled=True)
+    sizes = {a: lax.axis_size(a) for a in GENE_AXES}
+    rings = {ROW_AXES: ROW_RING, COL_AXES: COL_RING}
+
+    def member(coord, axes, back):
+        ring = rings[axes]
+        pos = ring.index(ravel([coord[a] for a in axes], [sizes[a] for a in axes]))
+        out = dict(coord)
+        out.update(zip(axes, unravel(ring[(pos - back) % len(ring)], [sizes[a] for a in axes])))
+        return ravel([out[a] for a in GENE_AXES], [sizes[a] for a in GENE_AXES])
+
     perm = []
     for sigma in range(spot_n):
+        q = half * (sigma % 2) + sigma // 2
+        t2, t1 = divmod(q, side)
         for c in range(gene_n):
-            i, j = divmod(c, side)
-            t1, t2 = divmod(sigma, side)
-            g = side * i + (j - t1) % side
-            s = side * ((i - t2) % side) + j
+            coord = dict(zip(GENE_AXES, unravel(c, [sizes[a] for a in GENE_AXES])))
+            g = member(coord, ROW_AXES, t1)
+            s = member(coord, COL_AXES, t2)
             perm.append((sigma * gene_n + c, s * gene_n + g))
-    share = lax.ppermute(share, ("spot", "gene"), perm)
+    share = lax.ppermute(share, SPOT_AXES + GENE_AXES, perm)
     return share / jnp.sqrt(pair_norm)
 
 
 def solution(mesh):
-    placed = (P("spot", None, "gene"), P("spot", None), P("spot", None))
+    spot_n, gene_n = mesh.devices.shape
+    y_lo = 2 if gene_n >= 16 else 1
+    z_a = gene_n // (y_lo * 2)
+    split = jax.sharding.Mesh(
+        mesh.devices.reshape(spot_n // 4, 2, 2, y_lo, z_a, 2), SPOT_AXES + GENE_AXES
+    )
+    gene = GENE_AXES
+    placed = (P(SPOT_AXES, None, gene), P(SPOT_AXES, None), P(SPOT_AXES, None))
     return jax.shard_map(
-        shards, mesh=mesh, in_specs=placed, out_specs=P("gene", "spot"), check_vma=False
+        shards, mesh=split, in_specs=placed, out_specs=P(gene, SPOT_AXES), check_vma=False
     )

time: 377 us -> 301 us (0.80)
  the two profiles are of different devices: /device:TPU:16 before, /device:TPU:6 now
where the time goes in v2:
time: 301 us; the launch traced here: 299 us
  waiting for transfers between devices  164 us (54%)
  starting transfers between devices  62.7 us (21%)
  other arithmetic  28 us (9%)
  between operations  26.8 us (9%)
  local copies, waits for them, and re-layouts  9.07 us (3%)
  matrix products  8.82 us (3%)
    reduce_scatter x1, waiting for transfers between devices, shards(): lax.psum_scatter(mine, ('sx', 'syh'), scatter_dimension=0, tiled=True)  86 us
    ppermute x2, waiting for transfers between devices, ring_gather(): prev = lax.ppermute(block, axes, fwd)  27.7 us
    ppermute x2, waiting for transfers between devices, ring_gather(): far_lo = lax.ppermute(prev[:half], axes, fwd)  16.2 us
    convert_element_type x1, other arithmetic, shards(): lagged = lagged_sum.astype(jnp.bfloat16)  12.3 us
    ppermute x2, starting transfers between devices, padded(): lax.ppermute(head, axis, [((i + 1) % count, i) for i in range(ends)])  12.1 us
    ppermute x4, waiting for transfers between devices, allreduce_moments(): packed = lax.ppermute(packed, axis, perm)  10.5 us
    ppermute x1, starting transfers between devices, shards(): mine = mine + lax.ppermute(other, 'sc', [(0, 1), (1, 0)])  10.3 us
    ppermute x2, starting transfers between devices, ring_gather(): far_lo = lax.ppermute(prev[:half], axes, fwd)  9.88 us
  transfers between devices with their start and end apart: 19, of which 13 were waited for; matrix products, arithmetic and copies ran while one was open for 10% of the time, Pallas kernels for 0%

profile of v2, /device:TPU:6, one launch (start us, length us, event | category | flops | bytes accessed | tf_op | source)
XLA Modules:
  0.0 299.3 jit_solution(8218397278560452514)
XLA Ops:
  6.5 0.9 multiply_add_fusion
  7.4 1.9 collective-permute-start
  9.4 6.0 %collective-permute-start.1 = (s32[2,512]{1,0:T(2,128)S(1)}, s32[2,512]{1,0:T(2,128)S(1)}, u32[]{:S(2)}, u32[]{:S(2)}) collective-permute-start(s32[2,512]{1,0:T(2,128)S(1)} %get-tuple-element.100), channel_id=1, source_target_pairs={{16,0},{32,16},{48,32},{64,48},{80,64},{96,80},{112,96},{128,112},... | collective-permute-start | bytes 12296 | tf_op jit(solution)/shard_map/ppermute | solution.py:33
  15.4 1.3 convert_reduce_fusion
  16.7 2.0 multiply_reduce_fusion.1
  19.3 0.4 multiply_reduce_fusion
  19.7 0.1 add_select_fusion.1
  19.8 0.2 broadcast_select_fusion.15
  20.0 0.1 fusion.46
  20.1 0.1 broadcast_select_fusion.4
  20.2 0.8 fusion.18
  20.9 1.3 pad_maximum_fusion.4
  22.3 1.2 collective-permute-done.2
  23.4 0.6 fusion.55
  28.7 0.1 pad_maximum_fusion.5
  28.7 2.3 collective-permute-start.3
  31.1 2.8 collective-permute-done.3
  33.9 0.6 fusion.54
  37.3 0.1 pad_maximum_fusion.6
  37.4 0.9 collective-permute-start.4
  38.3 2.8 collective-permute-done.4
  41.0 0.6 fusion.53
  44.5 0.1 pad_maximum_fusion.7
  44.6 1.4 collective-permute-start.5
  46.0 3.7 %collective-permute-done.5 = f32[514]{0:T(1024)S(1)} collective-permute-done((f32[514]{0:T(1024)S(1)}, f32[514]{0:T(1024)S(1)}, u32[]{:S(2)}, u32[]{:S(2)}) %collective-permute-start.5) | collective-permute-done | bytes 2088 | tf_op jit(solution)/shard_map/ppermute | solution.py:57
  49.7 0.6 fusion.52
  52.1 0.4 divide_convert_fusion
  52.6 1.9 collective-permute-start.10
  54.5 6.0 %collective-permute-start.11 = (bf16[2,512,256]{2,1,0:T(8,128)(2,1)S(1)}, bf16[2,512,256]{2,1,0:T(8,128)(2,1)S(1)}, u32[]{:S(2)}, u32[]{:S(2)}) collective-permute-start(bf16[2,512,256]{2,1,0:T(8,128)(2,1)S(1)} %get-tuple-element.54), channel_id=1, source_target_pairs={{16,0},{32,16},{48,32},{64,48},{80,64},{96,80},{112,96},{128,112},... | collective-permute-start | bytes 1572872 | tf_op jit(solution)/shard_map/ppermute | solution.py:33
  60.6 2.0 collective-permute-start.6
  62.5 0.1 collective-permute-start.8
  62.7 2.9 collective-permute-done.10
  65.6 1.7 collective-permute-done.11
  67.3 0.7 fusion.5
  68.0 12.3 %add_convert_fusion = bf16[4,512,256]{2,1,0:T(8,128)(2,1)} fusion(bf16[4,512,256]{2,1,0:T(8,128)(2,1)S(1)} %divide_convert_fusion, bf16[2,512,256]{2,1,0:T(8,128)(2,1)S(1)} %collective-permute-done.11, bf16[2,512,256]{2,1,0:T(8,128)(2,1)S(1)} %collective-permute-done.10, bf16[8,516,256]{2,1,0:T(8,128)(2,1)S(1)} %fusion.5, ...), kind=kLoop, calls=%fused_computation.11 | loop fusion | flops 39845888 | bytes 24313856 | tf_op jit(solution)/shard_map/convert_element_type | solution.py:137
  80.3 3.3 %collective-permute-start.12 = (bf16[2048,256]{1,0:T(8,128)(2,1)}, bf16[2048,256]{1,0:T(8,128)(2,1)}, u32[]{:S(2)}, u32[]{:S(2)}) collective-permute-start(bf16[2048,256]{1,0:T(8,128)(2,1)} %bitcast.16), channel_id=1, source_target_pairs={{0,2},{2,4},{4,6},{6,0},{1,3},{3,5},{5,7},{7,1},{8,10},{10,12},{12... | collective-permute-start | bytes 3145736 | tf_op jit(solution)/shard_map/ppermute | solution.py:68
  83.6 2.9 collective-permute-done.6
  86.5 0.8 slice.442
  87.3 0.8 collective-permute-start.7
  88.1 0.8 slice.443
  88.9 1.2 collective-permute-start.9
  90.2 6.3 %collective-permute-start.14 = (bf16[2048,256]{1,0:T(8,128)(2,1)}, bf16[2048,256]{1,0:T(8,128)(2,1)}, u32[]{:S(2)}, u32[]{:S(2)}) collective-permute-start(bf16[2048,256]{1,0:T(8,128)(2,1)} %bitcast.16), channel_id=1, source_target_pairs={{2,0},{4,2},{6,4},{0,6},{3,1},{5,3},{7,5},{1,7},{10,8},{12,10},{14... | collective-permute-start | bytes 3145736 | tf_op jit(solution)/shard_map/ppermute | solution.py:69
  96.5 24.8 %collective-permute-done.12 = bf16[2048,256]{1,0:T(8,128)(2,1)} collective-permute-done((bf16[2048,256]{1,0:T(8,128)(2,1)}, bf16[2048,256]{1,0:T(8,128)(2,1)}, u32[]{:S(2)}, u32[]{:S(2)}) %collective-permute-start.12) | collective-permute-done | bytes 1048608 | tf_op jit(solution)/shard_map/ppermute | solution.py:68
  121.3 1.1 slice.470
  122.4 9.1 %collective-permute-start.13 = (bf16[1024,256]{1,0:T(8,128)(2,1)S(1)}, bf16[1024,256]{1,0:T(8,128)(2,1)S(1)}, u32[]{:S(2)}, u32[]{:S(2)}) collective-permute-start(bf16[1024,256]{1,0:T(8,128)(2,1)S(1)} %slice.470), channel_id=1, source_target_pairs={{0,2},{2,4},{4,6},{6,0},{1,3},{3,5},{5,7},{7,1},{8,10},{10,12},{12... | collective-permute-start | bytes 1572872 | tf_op jit(solution)/shard_map/ppermute | solution.py:71
  131.5 16.2 %collective-permute-done.7 = bf16[1024,256]{1,0:T(8,128)(2,1)} collective-permute-done((bf16[1024,256]{1,0:T(8,128)(2,1)}, bf16[1024,256]{1,0:T(8,128)(2,1)}, u32[]{:S(2)}, u32[]{:S(2)}) %collective-permute-start.7) | collective-permute-done | bytes 524320 | tf_op jit(solution)/shard_map/ppermute | solution.py:71
  147.7 3.0 %pad_maximum_fusion = bf16[2048,1024]{1,0:T(8,128)(2,1)S(1)} fusion(bf16[2048,256]{1,0:T(8,128)(2,1)S(1)} %collective-permute-done.8, bf16[1024,256]{1,0:T(8,128)(2,1)} %collective-permute-done.9, bf16[1024,256]{1,0:T(8,128)(2,1)} %collective-permute-done.7, bf16[2048,256]{1,0:T(8,128)(2,1)S(1)} %collective-permute-done.6, bf16[2048,256]{1,0:T(8,128)(2,1)S(1)} %bitcast.27), kind=kLoop, calls=%fused_computation.3 | loop fusion | flops 20971520 | bytes 8388608 | tf_op jit(solution)/shard_map/concatenate | solution.py:143
  150.7 2.5 fusion.56
  153.2 1.1 slice.471
  154.3 3.9 %collective-permute-start.15 = (bf16[1024,256]{1,0:T(8,128)(2,1)S(1)}, bf16[1024,256]{1,0:T(8,128)(2,1)S(1)}, u32[]{:S(2)}, u32[]{:S(2)}) collective-permute-start(bf16[1024,256]{1,0:T(8,128)(2,1)S(1)} %slice.471), channel_id=1, source_target_pairs={{2,0},{4,2},{6,4},{0,6},{3,1},{5,3},{7,5},{1,7},{10,8},{12,10},{14... | collective-permute-start | bytes 1572872 | tf_op jit(solution)/shard_map/ppermute | solution.py:72
  158.2 2.5 fusion.57
  160.8 2.5 fusion.58
  163.3 6.9 %collective-permute-done.15 = bf16[1024,256]{1,0:T(8,128)(2,1)S(1)} collective-permute-done((bf16[1024,256]{1,0:T(8,128)(2,1)S(1)}, bf16[1024,256]{1,0:T(8,128)(2,1)S(1)}, u32[]{:S(2)}, u32[]{:S(2)}) %collective-permute-start.15) | collective-permute-done | bytes 524320 | tf_op jit(solution)/shard_map/ppermute | solution.py:72
  170.2 1.3 fusion.8
  171.5 0.3 pad_maximum_fusion.1
  171.8 1.6 constant_dynamic-slice_fusion
  173.4 1.0 copy-done.1
  174.4 10.3 %collective-permute-start.16 = (f32[2048,256]{1,0:T(8,128)}, f32[2048,256]{1,0:T(8,128)S(1)}, u32[]{:S(2)}, u32[]{:S(2)}) collective-permute-start(f32[2048,256]{1,0:T(8,128)} %constant_dynamic-slice_fusion), channel_id=1, source_target_pairs={{0,16},{16,0},{1,17},{17,1},{2,18},{18,2},{3,19},{19,3},{4,20},{20... | collective-permute-start | bytes 6291464 | tf_op jit(solution)/shard_map/ppermute | solution.py:152
  184.7 4.0 %collective-permute-done.16 = f32[2048,256]{1,0:T(8,128)S(1)} collective-permute-done((f32[2048,256]{1,0:T(8,128)}, f32[2048,256]{1,0:T(8,128)S(1)}, u32[]{:S(2)}, u32[]{:S(2)}) %collective-permute-start.16) | collective-permute-done | bytes 2097184 | tf_op jit(solution)/shard_map/ppermute | solution.py:152
  188.7 3.2 %dynamic-slice_add_fusion = f32[2048,256]{1,0:T(8,128)} fusion(f32[2048,256]{1,0:T(8,128)S(1)} %collective-permute-done.16, f32[4096,256]{1,0:T(8,128)} %copy-done.1, s32[]{:T(128)S(6)} %select_n.20), kind=kLoop, calls=%fused_computation.10 | loop fusion | flops 524288 | bytes 6291460 | tf_op jit(solution)/shard_map/add | solution.py:152
  191.9 86.0 %reduce-scatter.2.cloned.1.call-done = f32[256,256]{1,0:T(8,128)} async-done(((f32[2048,256]{1,0:T(8,128)}), f32[256,256]{1,0:T(8,128)}) %reduce-scatter.2.cloned.1.call-update) | async-done | bytes 262160 | tf_op jit(solution)/shard_map/reduce_scatter | solution.py:153
  277.9 5.0 %collective-permute-start.17 = (f32[256,256]{1,0:T(8,128)}, f32[256,256]{1,0:T(8,128)S(1)}, u32[]{:S(2)}, u32[]{:S(2)}) collective-permute-start(f32[256,256]{1,0:T(8,128)} %reduce-scatter.2.cloned.1.call-done), channel_id=1, source_target_pairs={{0,0},{1,17},{2,34},{3,51},{4,68},{5,85},{6,102},{7,119},{8,136},{... | collective-permute-start | bytes 786440 | tf_op jit(solution)/shard_map/ppermute | solution.py:173
  283.6 8.1 %collective-permute-done.17 = f32[256,256]{1,0:T(8,128)S(1)} collective-permute-done((f32[256,256]{1,0:T(8,128)}, f32[256,256]{1,0:T(8,128)S(1)}, u32[]{:S(2)}, u32[]{:S(2)}) %collective-permute-start.17) | collective-permute-done | bytes 262176 | tf_op jit(solution)/shard_map/ppermute | solution.py:173
  291.7 0.7 broadcast_divide_fusion
  (24 shorter events, 0.2 us)
Async XLA Ops:
  6.5 12.8 %copy-start = (s32[4,512,256]{2,1,0:T(8,128)S(1)}, s32[4,512,256]{2,1,0:T(8,128)}, u32[]{:S(2)}) copy-start(s32[4,512,256]{2,1,0:T(8,128)} %param.3) | copy-start | bytes 6291460
  6.5 271.3 %reduce-scatter.2.cloned.1.call-start = ((), (), s32[]{:S(2)}) async-start(), calls=%async_computation.1 | async-start | bytes 2359296 | tf_op jit(solution)/shard_map/reduce_scatter | solution.py:153
  7.4 12.3 %collective-permute-start = (s32[2,512]{1,0:T(2,128)S(1)}, s32[2,512]{1,0:T(2,128)S(1)}, u32[]{:S(2)}, u32[]{:S(2)}) collective-permute-start(s32[2,512]{1,0:T(2,128)S(1)} %get-tuple-element.99), channel_id=1, source_target_pairs={{0,16},{16,32},{32,48},{48,64},{64,80},{80,96},{96,112},{112,128},... | collective-permute-start | bytes 12296 | tf_op jit(solution)/shard_map/ppermute | solution.py:31
  9.4 10.3 %collective-permute-start.1 = (s32[2,512]{1,0:T(2,128)S(1)}, s32[2,512]{1,0:T(2,128)S(1)}, u32[]{:S(2)}, u32[]{:S(2)}) collective-permute-start(s32[2,512]{1,0:T(2,128)S(1)} %get-tuple-element.100), channel_id=1, source_target_pairs={{16,0},{32,16},{48,32},{64,48},{80,64},{96,80},{112,96},{128,112},... | collective-permute-start | bytes 12296 | tf_op jit(solution)/shard_map/ppermute | solution.py:33
  16.7 3.1 %copy-start.2 = (s32[4,512]{1,0:T(4,128)S(1)}, s32[4,512]{1,0:T(4,128)}, u32[]{:S(2)}) copy-start(s32[4,512]{1,0:T(4,128)} %param.5) | copy-start | bytes 24580
  16.7 3.4 %copy-start.3 = (s32[4,512]{1,0:T(4,128)S(1)}, s32[4,512]{1,0:T(4,128)}, u32[]{:S(2)}) copy-start(s32[4,512]{1,0:T(4,128)} %param.4) | copy-start | bytes 24580
  22.2 1.2 collective-permute-start.2
  28.7 5.1 %collective-permute-start.3 = (f32[514]{0:T(1024)S(1)}, f32[514]{0:T(1024)S(1)}, u32[]{:S(2)}, u32[]{:S(2)}) collective-permute-start(f32[514]{0:T(1024)S(1)} %pad_maximum_fusion.5), channel_id=1, source_target_pairs={{0,32},{16,48},{32,0},{48,16},{64,96},{80,112},{96,64},{112,80},{1... | collective-permute-start | bytes 6176 | tf_op jit(solution)/shard_map/ppermute | solution.py:57
  37.4 3.6 %collective-permute-start.4 = (f32[514]{0:T(1024)S(1)}, f32[514]{0:T(1024)S(1)}, u32[]{:S(2)}, u32[]{:S(2)}) collective-permute-start(f32[514]{0:T(1024)S(1)} %pad_maximum_fusion.6), channel_id=1, source_target_pairs={{0,64},{16,80},{32,96},{48,112},{64,0},{80,16},{96,32},{112,48},{1... | collective-permute-start | bytes 6176 | tf_op jit(solution)/shard_map/ppermute | solution.py:57
  44.6 5.1 %collective-permute-start.5 = (f32[514]{0:T(1024)S(1)}, f32[514]{0:T(1024)S(1)}, u32[]{:S(2)}, u32[]{:S(2)}) collective-permute-start(f32[514]{0:T(1024)S(1)} %pad_maximum_fusion.7), channel_id=1, source_target_pairs={{0,128},{16,144},{32,160},{48,176},{64,192},{80,208},{96,224},{112... | collective-permute-start | bytes 6176 | tf_op jit(solution)/shard_map/ppermute | solution.py:57
  52.6 13.0 %collective-permute-start.10 = (bf16[2,512,256]{2,1,0:T(8,128)(2,1)S(1)}, bf16[2,512,256]{2,1,0:T(8,128)(2,1)S(1)}, u32[]{:S(2)}, u32[]{:S(2)}) collective-permute-start(bf16[2,512,256]{2,1,0:T(8,128)(2,1)S(1)} %get-tuple-element.53), channel_id=1, source_target_pairs={{0,16},{16,32},{32,48},{48,64},{64,80},{80,96},{96,112},{112,128},... | collective-permute-start | bytes 1572872 | tf_op jit(solution)/shard_map/ppermute | solution.py:31
  54.5 12.8 %collective-permute-start.11 = (bf16[2,512,256]{2,1,0:T(8,128)(2,1)S(1)}, bf16[2,512,256]{2,1,0:T(8,128)(2,1)S(1)}, u32[]{:S(2)}, u32[]{:S(2)}) collective-permute-start(bf16[2,512,256]{2,1,0:T(8,128)(2,1)S(1)} %get-tuple-element.54), channel_id=1, source_target_pairs={{16,0},{32,16},{48,32},{64,48},{80,64},{96,80},{112,96},{128,112},... | collective-permute-start | bytes 1572872 | tf_op jit(solution)/shard_map/ppermute | solution.py:33
  60.6 25.9 %collective-permute-start.6 = (bf16[2048,256]{1,0:T(8,128)(2,1)S(1)}, bf16[2048,256]{1,0:T(8,128)(2,1)S(1)}, u32[]{:S(2)}, u32[]{:S(2)}) collective-permute-start(bf16[2048,256]{1,0:T(8,128)(2,1)S(1)} %bitcast.25), channel_id=1, source_target_pairs={{0,1},{1,9},{9,8},{8,0},{2,3},{3,11},{11,10},{10,2},{4,5},{5,13},{... | collective-permute-start | bytes 3145736 | tf_op jit(solution)/shard_map/ppermute | solution.py:68
  62.5 25.6 %collective-permute-start.8 = (bf16[2048,256]{1,0:T(8,128)(2,1)S(1)}, bf16[2048,256]{1,0:T(8,128)(2,1)S(1)}, u32[]{:S(2)}, u32[]{:S(2)}) collective-permute-start(bf16[2048,256]{1,0:T(8,128)(2,1)S(1)} %bitcast.26), channel_id=1, source_target_pairs={{1,0},{9,1},{8,9},{0,8},{3,2},{11,3},{10,11},{2,10},{5,4},{13,5},{... | collective-permute-start | bytes 3145736 | tf_op jit(solution)/shard_map/ppermute | solution.py:69
  80.3 41.0 %collective-permute-start.12 = (bf16[2048,256]{1,0:T(8,128)(2,1)}, bf16[2048,256]{1,0:T(8,128)(2,1)}, u32[]{:S(2)}, u32[]{:S(2)}) collective-permute-start(bf16[2048,256]{1,0:T(8,128)(2,1)} %bitcast.16), channel_id=1, source_target_pairs={{0,2},{2,4},{4,6},{6,0},{1,3},{3,5},{5,7},{7,1},{8,10},{10,12},{12... | collective-permute-start | bytes 3145736 | tf_op jit(solution)/shard_map/ppermute | solution.py:68
  87.3 60.3 %collective-permute-start.7 = (bf16[1024,256]{1,0:T(8,128)(2,1)}, bf16[1024,256]{1,0:T(8,128)(2,1)}, u32[]{:S(2)}, u32[]{:S(2)}) collective-permute-start(bf16[1024,256]{1,0:T(8,128)(2,1)} %slice.442), channel_id=1, source_target_pairs={{0,1},{1,9},{9,8},{8,0},{2,3},{3,11},{11,10},{10,2},{4,5},{5,13},{... | collective-permute-start | bytes 1572872 | tf_op jit(solution)/shard_map/ppermute | solution.py:71
  88.9 58.7 %collective-permute-start.9 = (bf16[1024,256]{1,0:T(8,128)(2,1)}, bf16[1024,256]{1,0:T(8,128)(2,1)}, u32[]{:S(2)}, u32[]{:S(2)}) collective-permute-start(bf16[1024,256]{1,0:T(8,128)(2,1)} %slice.443), channel_id=1, source_target_pairs={{1,0},{9,1},{8,9},{0,8},{3,2},{11,3},{10,11},{2,10},{5,4},{13,5},{... | collective-permute-start | bytes 1572872 | tf_op jit(solution)/shard_map/ppermute | solution.py:72
  90.2 63.0 %collective-permute-start.14 = (bf16[2048,256]{1,0:T(8,128)(2,1)}, bf16[2048,256]{1,0:T(8,128)(2,1)}, u32[]{:S(2)}, u32[]{:S(2)}) collective-permute-start(bf16[2048,256]{1,0:T(8,128)(2,1)} %bitcast.16), channel_id=1, source_target_pairs={{2,0},{4,2},{6,4},{0,6},{3,1},{5,3},{7,5},{1,7},{10,8},{12,10},{14... | collective-permute-start | bytes 3145736 | tf_op jit(solution)/shard_map/ppermute | solution.py:69
  122.4 40.9 %collective-permute-start.13 = (bf16[1024,256]{1,0:T(8,128)(2,1)S(1)}, bf16[1024,256]{1,0:T(8,128)(2,1)S(1)}, u32[]{:S(2)}, u32[]{:S(2)}) collective-permute-start(bf16[1024,256]{1,0:T(8,128)(2,1)S(1)} %slice.470), channel_id=1, source_target_pairs={{0,2},{2,4},{4,6},{6,0},{1,3},{3,5},{5,7},{7,1},{8,10},{10,12},{12... | collective-permute-start | bytes 1572872 | tf_op jit(solution)/shard_map/ppermute | solution.py:71
  154.3 15.9 %collective-permute-start.15 = (bf16[1024,256]{1,0:T(8,128)(2,1)S(1)}, bf16[1024,256]{1,0:T(8,128)(2,1)S(1)}, u32[]{:S(2)}, u32[]{:S(2)}) collective-permute-start(bf16[1024,256]{1,0:T(8,128)(2,1)S(1)} %slice.471), channel_id=1, source_target_pairs={{2,0},{4,2},{6,4},{0,6},{3,1},{5,3},{7,5},{1,7},{10,8},{12,10},{14... | collective-permute-start | bytes 1572872 | tf_op jit(solution)/shard_map/ppermute | solution.py:72
  171.8 2.6 copy-start.1
  174.4 14.3 %collective-permute-start.16 = (f32[2048,256]{1,0:T(8,128)}, f32[2048,256]{1,0:T(8,128)S(1)}, u32[]{:S(2)}, u32[]{:S(2)}) collective-permute-start(f32[2048,256]{1,0:T(8,128)} %constant_dynamic-slice_fusion), channel_id=1, source_target_pairs={{0,16},{16,0},{1,17},{17,1},{2,18},{18,2},{3,19},{19,3},{4,20},{20... | collective-permute-start | bytes 6291464 | tf_op jit(solution)/shard_map/ppermute | solution.py:152
  277.9 13.8 %collective-permute-start.17 = (f32[256,256]{1,0:T(8,128)}, f32[256,256]{1,0:T(8,128)S(1)}, u32[]{:S(2)}, u32[]{:S(2)}) collective-permute-start(f32[256,256]{1,0:T(8,128)} %reduce-scatter.2.cloned.1.call-done), channel_id=1, source_target_pairs={{0,0},{1,17},{2,34},{3,51},{4,68},{5,85},{6,102},{7,119},{8,136},{... | collective-permute-start | bytes 786440 | tf_op jit(solution)/shard_map/ppermute | solution.py:173
Sparse Core Ops, SparseCore 0:
  192.0 85.8 reduce-scatter.1

commit v3 on v2

--- a/solution.py
+++ b/solution.py
@@ -150,7 +150,17 @@
     mine = lax.dynamic_slice_in_dim(block, core * half * panel_width, half * panel_width, 0)
     other = lax.dynamic_slice_in_dim(block, (1 - core) * half * panel_width, half * panel_width, 0)
     mine = mine + lax.ppermute(other, "sc", [(0, 1), (1, 0)])
-    share = lax.psum_scatter(mine, ("sx", "syh"), scatter_dimension=0, tiled=True)
+    ring_x = lax.axis_size("sx")
+    pos_x = lax.axis_index("sx")
+    pair = 2 * panel_width
+    total = lax.dynamic_slice_in_dim(mine, pos_x * pair, pair, 0)
+    for d in range(1, ring_x):
+        sent = lax.dynamic_slice_in_dim(mine, ((pos_x + d) % ring_x) * pair, pair, 0)
+        total = total + lax.ppermute(sent, "sx", [(k, (k + d) % ring_x) for k in range(ring_x)])
+    high = lax.axis_index("syh")
+    keep = lax.dynamic_slice_in_dim(total, high * panel_width, panel_width, 0)
+    give = lax.dynamic_slice_in_dim(total, (1 - high) * panel_width, panel_width, 0)
+    share = keep + lax.ppermute(give, "syh", [(0, 1), (1, 0)])
     sizes = {a: lax.axis_size(a) for a in GENE_AXES}
     rings = {ROW_AXES: ROW_RING, COL_AXES: COL_RING}
 

time: 301 us -> 242 us (0.80)
  waiting for transfers between devices: 164 us -> 108 us
  between operations: 26.8 us -> 13.4 us
  starting transfers between devices: 62.7 us -> 73.6 us
    reduce_scatter x1 -> x0, waiting for transfers between devices: 86 us -> none  [shards(): lax.psum_scatter(mine, ('sx', 'syh'), scatter_dimension=0, tiled=True)]
    ppermute x0 -> x4, waiting for transfers between devices: none -> 30 us  [the longest x3 23.5 us: shards(): lax.ppermute(sent, 'sx', [(k, (k + d) % ring_x) for k in range(ring_x)])]
    ppermute x0 -> x4, starting transfers between devices: none -> 10.8 us  [the longest x3 6.7 us: shards(): lax.ppermute(sent, 'sx', [(k, (k + d) % ring_x) for k in range(ring_x)])]
  transfers between devices with their start and end apart: 19 -> 22, of which waited for: 13 -> 16; matrix products, arithmetic and copies ran while one was open for 10% -> 13% of each run, Pallas kernels for 0% -> 0%
where the time goes in v3:
time: 242 us
  waiting for transfers between devices  108 us (45%)
  starting transfers between devices  73.6 us (30%)
  other arithmetic  28.8 us (12%)
  between operations  13.4 us (6%)
  local copies, waits for them, and re-layouts  9.2 us (4%)
  matrix products  8.83 us (4%)
    ppermute x2, waiting for transfers between devices, ring_gather(): prev = lax.ppermute(block, axes, fwd)  27.7 us
    ppermute x3, waiting for transfers between devices, shards(): lax.ppermute(sent, 'sx', [(k, (k + d) % ring_x) for k in range(ring_x)])  23.5 us
    ppermute x2, waiting for transfers between devices, ring_gather(): far_lo = lax.ppermute(prev[:half], axes, fwd)  16.2 us
    convert_element_type x1, other arithmetic, shards(): lagged = lagged_sum.astype(jnp.bfloat16)  12.2 us
    ppermute x2, starting transfers between devices, padded(): lax.ppermute(head, axis, [((i + 1) % count, i) for i in range(ends)])  12.1 us
    ppermute x4, waiting for transfers between devices, allreduce_moments(): packed = lax.ppermute(packed, axis, perm)  10.5 us
    ppermute x1, starting transfers between devices, shards(): mine = mine + lax.ppermute(other, 'sc', [(0, 1), (1, 0)])  10.2 us
    ppermute x2, starting transfers between devices, ring_gather(): far_lo = lax.ppermute(prev[:half], axes, fwd)  9.83 us
  transfers between devices with their start and end apart: 22, of which 16 were waited for; matrix products, arithmetic and copies ran while one was open for 13% of the time, Pallas kernels for 0%

profile of v3, /device:TPU:6, one launch (start us, length us, event | category | flops | bytes accessed | tf_op | source)
XLA Modules:
  0.0 241.7 jit_solution(941700481010526589)
XLA Ops:
  0.0 0.9 multiply_add_fusion
  0.9 1.9 collective-permute-start
  2.8 6.0 %collective-permute-start.1 = (s32[2,512]{1,0:T(2,128)S(1)}, s32[2,512]{1,0:T(2,128)S(1)}, u32[]{:S(2)}, u32[]{:S(2)}) collective-permute-start(s32[2,512]{1,0:T(2,128)S(1)} %get-tuple-element.103), channel_id=1, source_target_pairs={{16,0},{32,16},{48,32},{64,48},{80,64},{96,80},{112,96},{128,112},... | collective-permute-start | bytes 12296 | tf_op jit(solution)/shard_map/ppermute | solution.py:33
  8.9 1.4 convert_reduce_fusion
  10.3 2.0 multiply_reduce_fusion.1
  13.0 0.4 multiply_reduce_fusion
  13.5 0.2 broadcast_select_fusion.15
  13.8 0.8 fusion.18
  14.6 1.4 pad_maximum_fusion.4
  16.1 1.2 collective-permute-done.2
  17.2 0.6 fusion.55
  22.4 2.3 collective-permute-start.3
  24.8 2.8 %collective-permute-done.3 = f32[514]{0:T(1024)S(1)} collective-permute-done((f32[514]{0:T(1024)S(1)}, f32[514]{0:T(1024)S(1)}, u32[]{:S(2)}, u32[]{:S(2)}) %collective-permute-start.3) | collective-permute-done | bytes 2088 | tf_op jit(solution)/shard_map/ppermute | solution.py:57
  27.6 0.6 fusion.54
  30.8 0.9 collective-permute-start.4
  31.6 2.8 %collective-permute-done.4 = f32[514]{0:T(1024)S(1)} collective-permute-done((f32[514]{0:T(1024)S(1)}, f32[514]{0:T(1024)S(1)}, u32[]{:S(2)}, u32[]{:S(2)}) %collective-permute-start.4) | collective-permute-done | bytes 2088 | tf_op jit(solution)/shard_map/ppermute | solution.py:57
  34.4 0.6 fusion.53
  37.6 1.4 collective-permute-start.5
  39.0 3.7 %collective-permute-done.5 = f32[514]{0:T(1024)S(1)} collective-permute-done((f32[514]{0:T(1024)S(1)}, f32[514]{0:T(1024)S(1)}, u32[]{:S(2)}, u32[]{:S(2)}) %collective-permute-start.5) | collective-permute-done | bytes 2088 | tf_op jit(solution)/shard_map/ppermute | solution.py:57
  42.7 0.6 fusion.52
  45.5 0.4 divide_convert_fusion
  45.9 1.9 collective-permute-start.10
  47.9 6.0 %collective-permute-start.11 = (bf16[2,512,256]{2,1,0:T(8,128)(2,1)S(1)}, bf16[2,512,256]{2,1,0:T(8,128)(2,1)S(1)}, u32[]{:S(2)}, u32[]{:S(2)}) collective-permute-start(bf16[2,512,256]{2,1,0:T(8,128)(2,1)S(1)} %get-tuple-element.57), channel_id=1, source_target_pairs={{16,0},{32,16},{48,32},{64,48},{80,64},{96,80},{112,96},{128,112},... | collective-permute-start | bytes 1572872 | tf_op jit(solution)/shard_map/ppermute | solution.py:33
  53.9 2.0 collective-permute-start.6
  56.0 2.9 %collective-permute-done.10 = bf16[2,512,256]{2,1,0:T(8,128)(2,1)S(1)} collective-permute-done((bf16[2,512,256]{2,1,0:T(8,128)(2,1)S(1)}, bf16[2,512,256]{2,1,0:T(8,128)(2,1)S(1)}, u32[]{:S(2)}, u32[]{:S(2)}) %collective-permute-start.10) | collective-permute-done | bytes 524320 | tf_op jit(solution)/shard_map/ppermute | solution.py:31
  58.9 1.7 collective-permute-done.11
  60.6 0.7 fusion.5
  61.4 12.2 %add_convert_fusion = bf16[4,512,256]{2,1,0:T(8,128)(2,1)} fusion(bf16[4,512,256]{2,1,0:T(8,128)(2,1)S(1)} %divide_convert_fusion, bf16[2,512,256]{2,1,0:T(8,128)(2,1)S(1)} %collective-permute-done.11, bf16[2,512,256]{2,1,0:T(8,128)(2,1)S(1)} %collective-permute-done.10, bf16[8,516,256]{2,1,0:T(8,128)(2,1)S(1)} %fusion.5, ...), kind=kLoop, calls=%fused_computation.11 | loop fusion | flops 39845888 | bytes 24313856 | tf_op jit(solution)/shard_map/convert_element_type | solution.py:137
  73.6 3.3 %collective-permute-start.12 = (bf16[2048,256]{1,0:T(8,128)(2,1)}, bf16[2048,256]{1,0:T(8,128)(2,1)}, u32[]{:S(2)}, u32[]{:S(2)}) collective-permute-start(bf16[2048,256]{1,0:T(8,128)(2,1)} %bitcast.16), channel_id=1, source_target_pairs={{0,2},{2,4},{4,6},{6,0},{1,3},{3,5},{5,7},{7,1},{8,10},{10,12},{12... | collective-permute-start | bytes 3145736 | tf_op jit(solution)/shard_map/ppermute | solution.py:68
  76.9 3.0 %collective-permute-done.6 = bf16[2048,256]{1,0:T(8,128)(2,1)S(1)} collective-permute-done((bf16[2048,256]{1,0:T(8,128)(2,1)S(1)}, bf16[2048,256]{1,0:T(8,128)(2,1)S(1)}, u32[]{:S(2)}, u32[]{:S(2)}) %collective-permute-start.6) | collective-permute-done | bytes 1048608 | tf_op jit(solution)/shard_map/ppermute | solution.py:68
  79.9 0.9 slice.442
  80.7 0.8 collective-permute-start.7
  81.5 0.9 slice.443
  82.4 1.2 collective-permute-start.9
  83.6 6.3 %collective-permute-start.14 = (bf16[2048,256]{1,0:T(8,128)(2,1)}, bf16[2048,256]{1,0:T(8,128)(2,1)}, u32[]{:S(2)}, u32[]{:S(2)}) collective-permute-start(bf16[2048,256]{1,0:T(8,128)(2,1)} %bitcast.16), channel_id=1, source_target_pairs={{2,0},{4,2},{6,4},{0,6},{3,1},{5,3},{7,5},{1,7},{10,8},{12,10},{14... | collective-permute-start | bytes 3145736 | tf_op jit(solution)/shard_map/ppermute | solution.py:69
  89.9 24.7 %collective-permute-done.12 = bf16[2048,256]{1,0:T(8,128)(2,1)} collective-permute-done((bf16[2048,256]{1,0:T(8,128)(2,1)}, bf16[2048,256]{1,0:T(8,128)(2,1)}, u32[]{:S(2)}, u32[]{:S(2)}) %collective-permute-start.12) | collective-permute-done | bytes 1048608 | tf_op jit(solution)/shard_map/ppermute | solution.py:68
  114.6 1.1 slice.470
  115.7 9.1 %collective-permute-start.13 = (bf16[1024,256]{1,0:T(8,128)(2,1)S(1)}, bf16[1024,256]{1,0:T(8,128)(2,1)S(1)}, u32[]{:S(2)}, u32[]{:S(2)}) collective-permute-start(bf16[1024,256]{1,0:T(8,128)(2,1)S(1)} %slice.470), channel_id=1, source_target_pairs={{0,2},{2,4},{4,6},{6,0},{1,3},{3,5},{5,7},{7,1},{8,10},{10,12},{12... | collective-permute-start | bytes 1572872 | tf_op jit(solution)/shard_map/ppermute | solution.py:71
  124.8 16.2 %collective-permute-done.7 = bf16[1024,256]{1,0:T(8,128)(2,1)} collective-permute-done((bf16[1024,256]{1,0:T(8,128)(2,1)}, bf16[1024,256]{1,0:T(8,128)(2,1)}, u32[]{:S(2)}, u32[]{:S(2)}) %collective-permute-start.7) | collective-permute-done | bytes 524320 | tf_op jit(solution)/shard_map/ppermute | solution.py:71
  140.9 2.9 %pad_maximum_fusion = bf16[2048,1024]{1,0:T(8,128)(2,1)S(1)} fusion(bf16[2048,256]{1,0:T(8,128)(2,1)S(1)} %collective-permute-done.8, bf16[1024,256]{1,0:T(8,128)(2,1)} %collective-permute-done.9, bf16[1024,256]{1,0:T(8,128)(2,1)} %collective-permute-done.7, bf16[2048,256]{1,0:T(8,128)(2,1)S(1)} %collective-permute-done.6, bf16[2048,256]{1,0:T(8,128)(2,1)S(1)} %bitcast.27), kind=kLoop, calls=%fused_computation.3 | loop fusion | flops 20971520 | bytes 8388608 | tf_op jit(solution)/shard_map/concatenate | solution.py:143
  143.9 2.5 %fusion.56 = f32[1024,256]{1,0:T(8,128)S(1)} fusion(bf16[2048,1024]{1,0:T(8,128)(2,1)S(1)} %pad_maximum_fusion, bf16[2048,256]{1,0:T(8,128)(2,1)} %bitcast.16), kind=kOutput, calls=%fused_computation.174 | convolution fusion | flops 1073741824 | bytes 6291456 | tf_op jit(solution)/shard_map/dot_general | solution.py:145
  146.4 1.1 slice.471
  147.5 4.0 %collective-permute-start.15 = (bf16[1024,256]{1,0:T(8,128)(2,1)S(1)}, bf16[1024,256]{1,0:T(8,128)(2,1)S(1)}, u32[]{:S(2)}, u32[]{:S(2)}) collective-permute-start(bf16[1024,256]{1,0:T(8,128)(2,1)S(1)} %slice.471), channel_id=1, source_target_pairs={{2,0},{4,2},{6,4},{0,6},{3,1},{5,3},{7,5},{1,7},{10,8},{12,10},{14... | collective-permute-start | bytes 1572872 | tf_op jit(solution)/shard_map/ppermute | solution.py:72
  151.5 2.5 %fusion.57 = f32[1024,256]{1,0:T(8,128)S(1)} fusion(bf16[2048,1024]{1,0:T(8,128)(2,1)S(1)} %pad_maximum_fusion, bf16[2048,256]{1,0:T(8,128)(2,1)} %collective-permute-done.12), kind=kOutput, calls=%fused_computation.175 | convolution fusion | flops 1073741824 | bytes 6291456 | tf_op jit(solution)/shard_map/dot_general | solution.py:145
  154.0 2.5 %fusion.58 = f32[1024,256]{1,0:T(8,128)S(1)} fusion(bf16[2048,1024]{1,0:T(8,128)(2,1)S(1)} %pad_maximum_fusion, bf16[2048,256]{1,0:T(8,128)(2,1)} %collective-permute-done.14), kind=kOutput, calls=%fused_computation.176 | convolution fusion | flops 1073741824 | bytes 6291456 | tf_op jit(solution)/shard_map/dot_general | solution.py:145
  156.5 6.9 %collective-permute-done.15 = bf16[1024,256]{1,0:T(8,128)(2,1)S(1)} collective-permute-done((bf16[1024,256]{1,0:T(8,128)(2,1)S(1)}, bf16[1024,256]{1,0:T(8,128)(2,1)S(1)}, u32[]{:S(2)}, u32[]{:S(2)}) %collective-permute-start.15) | collective-permute-done | bytes 524320 | tf_op jit(solution)/shard_map/ppermute | solution.py:72
  163.4 1.3 fusion.8
  164.7 0.3 pad_maximum_fusion.1
  165.0 0.1 constant_dynamic-slice_fusion.4
  165.1 1.8 copy-done.1
  166.9 10.2 %collective-permute-start.16 = (f32[2048,256]{1,0:T(8,128)S(1)}, f32[2048,256]{1,0:T(8,128)}, u32[]{:S(2)}, u32[]{:S(2)}) collective-permute-start(f32[2048,256]{1,0:T(8,128)S(1)} %constant_dynamic-slice_fusion.4), channel_id=1, source_target_pairs={{0,16},{16,0},{1,17},{17,1},{2,18},{18,2},{3,19},{19,3},{4,20},{20... | collective-permute-start | bytes 6291464 | tf_op jit(solution)/shard_map/ppermute | solution.py:152
  177.1 3.9 %collective-permute-done.16 = f32[2048,256]{1,0:T(8,128)} collective-permute-done((f32[2048,256]{1,0:T(8,128)S(1)}, f32[2048,256]{1,0:T(8,128)}, u32[]{:S(2)}, u32[]{:S(2)}) %collective-permute-start.16) | collective-permute-done | bytes 2097184 | tf_op jit(solution)/shard_map/ppermute | solution.py:152
  181.0 2.5 %dynamic-slice_add_fusion = f32[2048,256]{1,0:T(8,128)S(1)} fusion(f32[2048,256]{1,0:T(8,128)} %collective-permute-done.16, f32[4096,256]{1,0:T(8,128)} %copy-done.1, s32[]{:T(128)S(6)} %select_n.52), kind=kLoop, calls=%fused_computation.10 | loop fusion | flops 524288 | bytes 6291460 | tf_op jit(solution)/shard_map/add | solution.py:152
  183.5 0.9 constant_dynamic-slice_fusion.3
  184.5 6.7 %collective-permute-start.18 = (f32[512,256]{1,0:T(8,128)S(1)}, f32[512,256]{1,0:T(8,128)}, u32[]{:S(2)}, u32[]{:S(2)}) collective-permute-start(f32[512,256]{1,0:T(8,128)S(1)} %get-tuple-element.55), channel_id=1, source_target_pairs={{0,128},{64,192},{128,0},{192,64},{1,129},{65,193},{129,1},{193,65... | collective-permute-start | bytes 1572872 | tf_op jit(solution)/shard_map/ppermute | solution.py:159
  191.2 11.0 %collective-permute-done.17 = f32[512,256]{1,0:T(8,128)} collective-permute-done((f32[512,256]{1,0:T(8,128)}, f32[512,256]{1,0:T(8,128)}, u32[]{:S(2)}, u32[]{:S(2)}) %collective-permute-start.17) | collective-permute-done | bytes 524320 | tf_op jit(solution)/shard_map/ppermute | solution.py:159
  202.2 1.9 collective-permute-done.18
  204.1 10.6 %collective-permute-done.19 = f32[512,256]{1,0:T(8,128)} collective-permute-done((f32[512,256]{1,0:T(8,128)S(1)}, f32[512,256]{1,0:T(8,128)}, u32[]{:S(2)}, u32[]{:S(2)}) %collective-permute-start.19) | collective-permute-done | bytes 524320 | tf_op jit(solution)/shard_map/ppermute | solution.py:159
  214.7 1.5 add_add_fusion
  216.2 4.1 %collective-permute-start.20 = (f32[256,256]{1,0:T(8,128)S(1)}, f32[256,256]{1,0:T(8,128)S(1)}, u32[]{:S(2)}, u32[]{:S(2)}) collective-permute-start(f32[256,256]{1,0:T(8,128)S(1)} %constant_dynamic-slice_fusion), channel_id=1, source_target_pairs={{0,32},{32,0},{1,33},{33,1},{2,34},{34,2},{3,35},{35,3},{4,36},{36... | collective-permute-start | bytes 786440 | tf_op jit(solution)/shard_map/ppermute | solution.py:163
  220.3 6.5 %collective-permute-done.20 = f32[256,256]{1,0:T(8,128)S(1)} collective-permute-done((f32[256,256]{1,0:T(8,128)S(1)}, f32[256,256]{1,0:T(8,128)S(1)}, u32[]{:S(2)}, u32[]{:S(2)}) %collective-permute-start.20) | collective-permute-done | bytes 262176 | tf_op jit(solution)/shard_map/ppermute | solution.py:163
  226.9 5.2 %collective-permute-start.21 = (f32[256,256]{1,0:T(8,128)S(1)}, f32[256,256]{1,0:T(8,128)S(1)}, u32[]{:S(2)}, u32[]{:S(2)}) collective-permute-start(f32[256,256]{1,0:T(8,128)S(1)} %dynamic-slice_add_fusion.1), channel_id=1, source_target_pairs={{0,0},{1,17},{2,34},{3,51},{4,68},{5,85},{6,102},{7,119},{8,136},{... | collective-permute-start | bytes 786440 | tf_op jit(solution)/shard_map/ppermute | solution.py:183
  232.8 8.2 %collective-permute-done.21 = f32[256,256]{1,0:T(8,128)S(1)} collective-permute-done((f32[256,256]{1,0:T(8,128)S(1)}, f32[256,256]{1,0:T(8,128)S(1)}, u32[]{:S(2)}, u32[]{:S(2)}) %collective-permute-start.21) | collective-permute-done | bytes 262176 | tf_op jit(solution)/shard_map/ppermute | solution.py:183
  241.0 0.7 broadcast_divide_fusion
  (33 shorter events, 0.9 us)
Async XLA Ops:
  0.0 13.0 %copy-start = (s32[4,512,256]{2,1,0:T(8,128)S(1)}, s32[4,512,256]{2,1,0:T(8,128)}, u32[]{:S(2)}) copy-start(s32[4,512,256]{2,1,0:T(8,128)} %param.3) | copy-start | bytes 6291460
  0.9 12.5 %collective-permute-start = (s32[2,512]{1,0:T(2,128)S(1)}, s32[2,512]{1,0:T(2,128)S(1)}, u32[]{:S(2)}, u32[]{:S(2)}) collective-permute-start(s32[2,512]{1,0:T(2,128)S(1)} %get-tuple-element.102), channel_id=1, source_target_pairs={{0,16},{16,32},{32,48},{48,64},{64,80},{80,96},{96,112},{112,128},... | collective-permute-start | bytes 12296 | tf_op jit(solution)/shard_map/ppermute | solution.py:31
  2.8 10.5 %collective-permute-start.1 = (s32[2,512]{1,0:T(2,128)S(1)}, s32[2,512]{1,0:T(2,128)S(1)}, u32[]{:S(2)}, u32[]{:S(2)}) collective-permute-start(s32[2,512]{1,0:T(2,128)S(1)} %get-tuple-element.103), channel_id=1, source_target_pairs={{16,0},{32,16},{48,32},{64,48},{80,64},{96,80},{112,96},{128,112},... | collective-permute-start | bytes 12296 | tf_op jit(solution)/shard_map/ppermute | solution.py:33
  10.3 3.2 %copy-start.2 = (s32[4,512]{1,0:T(4,128)S(1)}, s32[4,512]{1,0:T(4,128)}, u32[]{:S(2)}) copy-start(s32[4,512]{1,0:T(4,128)} %param.5) | copy-start | bytes 24580
  10.3 3.6 %copy-start.3 = (s32[4,512]{1,0:T(4,128)S(1)}, s32[4,512]{1,0:T(4,128)}, u32[]{:S(2)}) copy-start(s32[4,512]{1,0:T(4,128)} %param.4) | copy-start | bytes 24580
  16.0 1.2 collective-permute-start.2
  22.4 5.1 %collective-permute-start.3 = (f32[514]{0:T(1024)S(1)}, f32[514]{0:T(1024)S(1)}, u32[]{:S(2)}, u32[]{:S(2)}) collective-permute-start(f32[514]{0:T(1024)S(1)} %pad_maximum_fusion.5), channel_id=1, source_target_pairs={{0,32},{16,48},{32,0},{48,16},{64,96},{80,112},{96,64},{112,80},{1... | collective-permute-start | bytes 6176 | tf_op jit(solution)/shard_map/ppermute | solution.py:57
  30.8 3.6 %collective-permute-start.4 = (f32[514]{0:T(1024)S(1)}, f32[514]{0:T(1024)S(1)}, u32[]{:S(2)}, u32[]{:S(2)}) collective-permute-start(f32[514]{0:T(1024)S(1)} %pad_maximum_fusion.6), channel_id=1, source_target_pairs={{0,64},{16,80},{32,96},{48,112},{64,0},{80,16},{96,32},{112,48},{1... | collective-permute-start | bytes 6176 | tf_op jit(solution)/shard_map/ppermute | solution.py:57
  37.6 5.1 %collective-permute-start.5 = (f32[514]{0:T(1024)S(1)}, f32[514]{0:T(1024)S(1)}, u32[]{:S(2)}, u32[]{:S(2)}) collective-permute-start(f32[514]{0:T(1024)S(1)} %pad_maximum_fusion.7), channel_id=1, source_target_pairs={{0,128},{16,144},{32,160},{48,176},{64,192},{80,208},{96,224},{112... | collective-permute-start | bytes 6176 | tf_op jit(solution)/shard_map/ppermute | solution.py:57
  45.9 13.0 %collective-permute-start.10 = (bf16[2,512,256]{2,1,0:T(8,128)(2,1)S(1)}, bf16[2,512,256]{2,1,0:T(8,128)(2,1)S(1)}, u32[]{:S(2)}, u32[]{:S(2)}) collective-permute-start(bf16[2,512,256]{2,1,0:T(8,128)(2,1)S(1)} %get-tuple-element.56), channel_id=1, source_target_pairs={{0,16},{16,32},{32,48},{48,64},{64,80},{80,96},{96,112},{112,128},... | collective-permute-start | bytes 1572872 | tf_op jit(solution)/shard_map/ppermute | solution.py:31
  47.9 12.8 %collective-permute-start.11 = (bf16[2,512,256]{2,1,0:T(8,128)(2,1)S(1)}, bf16[2,512,256]{2,1,0:T(8,128)(2,1)S(1)}, u32[]{:S(2)}, u32[]{:S(2)}) collective-permute-start(bf16[2,512,256]{2,1,0:T(8,128)(2,1)S(1)} %get-tuple-element.57), channel_id=1, source_target_pairs={{16,0},{32,16},{48,32},{64,48},{80,64},{96,80},{112,96},{128,112},... | collective-permute-start | bytes 1572872 | tf_op jit(solution)/shard_map/ppermute | solution.py:33
  53.9 25.9 %collective-permute-start.6 = (bf16[2048,256]{1,0:T(8,128)(2,1)S(1)}, bf16[2048,256]{1,0:T(8,128)(2,1)S(1)}, u32[]{:S(2)}, u32[]{:S(2)}) collective-permute-start(bf16[2048,256]{1,0:T(8,128)(2,1)S(1)} %bitcast.25), channel_id=1, source_target_pairs={{0,1},{1,9},{9,8},{8,0},{2,3},{3,11},{11,10},{10,2},{4,5},{5,13},{... | collective-permute-start | bytes 3145736 | tf_op jit(solution)/shard_map/ppermute | solution.py:68
  55.9 25.6 %collective-permute-start.8 = (bf16[2048,256]{1,0:T(8,128)(2,1)S(1)}, bf16[2048,256]{1,0:T(8,128)(2,1)S(1)}, u32[]{:S(2)}, u32[]{:S(2)}) collective-permute-start(bf16[2048,256]{1,0:T(8,128)(2,1)S(1)} %bitcast.26), channel_id=1, source_target_pairs={{1,0},{9,1},{8,9},{0,8},{3,2},{11,3},{10,11},{2,10},{5,4},{13,5},{... | collective-permute-start | bytes 3145736 | tf_op jit(solution)/shard_map/ppermute | solution.py:69
  73.6 41.0 %collective-permute-start.12 = (bf16[2048,256]{1,0:T(8,128)(2,1)}, bf16[2048,256]{1,0:T(8,128)(2,1)}, u32[]{:S(2)}, u32[]{:S(2)}) collective-permute-start(bf16[2048,256]{1,0:T(8,128)(2,1)} %bitcast.16), channel_id=1, source_target_pairs={{0,2},{2,4},{4,6},{6,0},{1,3},{3,5},{5,7},{7,1},{8,10},{10,12},{12... | collective-permute-start | bytes 3145736 | tf_op jit(solution)/shard_map/ppermute | solution.py:68
  80.7 60.2 %collective-permute-start.7 = (bf16[1024,256]{1,0:T(8,128)(2,1)}, bf16[1024,256]{1,0:T(8,128)(2,1)}, u32[]{:S(2)}, u32[]{:S(2)}) collective-permute-start(bf16[1024,256]{1,0:T(8,128)(2,1)} %slice.442), channel_id=1, source_target_pairs={{0,1},{1,9},{9,8},{8,0},{2,3},{3,11},{11,10},{10,2},{4,5},{5,13},{... | collective-permute-start | bytes 1572872 | tf_op jit(solution)/shard_map/ppermute | solution.py:71
  82.4 58.6 %collective-permute-start.9 = (bf16[1024,256]{1,0:T(8,128)(2,1)}, bf16[1024,256]{1,0:T(8,128)(2,1)}, u32[]{:S(2)}, u32[]{:S(2)}) collective-permute-start(bf16[1024,256]{1,0:T(8,128)(2,1)} %slice.443), channel_id=1, source_target_pairs={{1,0},{9,1},{8,9},{0,8},{3,2},{11,3},{10,11},{2,10},{5,4},{13,5},{... | collective-permute-start | bytes 1572872 | tf_op jit(solution)/shard_map/ppermute | solution.py:72
  83.6 62.8 %collective-permute-start.14 = (bf16[2048,256]{1,0:T(8,128)(2,1)}, bf16[2048,256]{1,0:T(8,128)(2,1)}, u32[]{:S(2)}, u32[]{:S(2)}) collective-permute-start(bf16[2048,256]{1,0:T(8,128)(2,1)} %bitcast.16), channel_id=1, source_target_pairs={{2,0},{4,2},{6,4},{0,6},{3,1},{5,3},{7,5},{1,7},{10,8},{12,10},{14... | collective-permute-start | bytes 3145736 | tf_op jit(solution)/shard_map/ppermute | solution.py:69
  115.7 40.8 %collective-permute-start.13 = (bf16[1024,256]{1,0:T(8,128)(2,1)S(1)}, bf16[1024,256]{1,0:T(8,128)(2,1)S(1)}, u32[]{:S(2)}, u32[]{:S(2)}) collective-permute-start(bf16[1024,256]{1,0:T(8,128)(2,1)S(1)} %slice.470), channel_id=1, source_target_pairs={{0,2},{2,4},{4,6},{6,0},{1,3},{3,5},{5,7},{7,1},{8,10},{10,12},{12... | collective-permute-start | bytes 1572872 | tf_op jit(solution)/shard_map/ppermute | solution.py:71
  147.5 15.9 %collective-permute-start.15 = (bf16[1024,256]{1,0:T(8,128)(2,1)S(1)}, bf16[1024,256]{1,0:T(8,128)(2,1)S(1)}, u32[]{:S(2)}, u32[]{:S(2)}) collective-permute-start(bf16[1024,256]{1,0:T(8,128)(2,1)S(1)} %slice.471), channel_id=1, source_target_pairs={{2,0},{4,2},{6,4},{0,6},{3,1},{5,3},{7,5},{1,7},{10,8},{12,10},{14... | collective-permute-start | bytes 1572872 | tf_op jit(solution)/shard_map/ppermute | solution.py:72
  165.0 2.0 copy-start.1
  166.9 14.1 %collective-permute-start.16 = (f32[2048,256]{1,0:T(8,128)S(1)}, f32[2048,256]{1,0:T(8,128)}, u32[]{:S(2)}, u32[]{:S(2)}) collective-permute-start(f32[2048,256]{1,0:T(8,128)S(1)} %constant_dynamic-slice_fusion.4), channel_id=1, source_target_pairs={{0,16},{16,0},{1,17},{17,1},{2,18},{18,2},{3,19},{19,3},{4,20},{20... | collective-permute-start | bytes 6291464 | tf_op jit(solution)/shard_map/ppermute | solution.py:152
  184.5 17.7 %collective-permute-start.17 = (f32[512,256]{1,0:T(8,128)}, f32[512,256]{1,0:T(8,128)}, u32[]{:S(2)}, u32[]{:S(2)}) collective-permute-start(f32[512,256]{1,0:T(8,128)} %get-tuple-element.53), channel_id=1, source_target_pairs={{0,64},{64,128},{128,192},{192,0},{1,65},{65,129},{129,193},{193,1... | collective-permute-start | bytes 1572872 | tf_op jit(solution)/shard_map/ppermute | solution.py:159
  184.5 19.6 %collective-permute-start.18 = (f32[512,256]{1,0:T(8,128)S(1)}, f32[512,256]{1,0:T(8,128)}, u32[]{:S(2)}, u32[]{:S(2)}) collective-permute-start(f32[512,256]{1,0:T(8,128)S(1)} %get-tuple-element.55), channel_id=1, source_target_pairs={{0,128},{64,192},{128,0},{192,64},{1,129},{65,193},{129,1},{193,65... | collective-permute-start | bytes 1572872 | tf_op jit(solution)/shard_map/ppermute | solution.py:159
  191.2 23.5 %collective-permute-start.19 = (f32[512,256]{1,0:T(8,128)S(1)}, f32[512,256]{1,0:T(8,128)}, u32[]{:S(2)}, u32[]{:S(2)}) collective-permute-start(f32[512,256]{1,0:T(8,128)S(1)} %get-tuple-element.54), channel_id=1, source_target_pairs={{0,192},{64,0},{128,64},{192,128},{1,193},{65,1},{129,65},{193,129... | collective-permute-start | bytes 1572872 | tf_op jit(solution)/shard_map/ppermute | solution.py:159
  216.2 10.6 %collective-permute-start.20 = (f32[256,256]{1,0:T(8,128)S(1)}, f32[256,256]{1,0:T(8,128)S(1)}, u32[]{:S(2)}, u32[]{:S(2)}) collective-permute-start(f32[256,256]{1,0:T(8,128)S(1)} %constant_dynamic-slice_fusion), channel_id=1, source_target_pairs={{0,32},{32,0},{1,33},{33,1},{2,34},{34,2},{3,35},{35,3},{4,36},{36... | collective-permute-start | bytes 786440 | tf_op jit(solution)/shard_map/ppermute | solution.py:163
  226.9 14.1 %collective-permute-start.21 = (f32[256,256]{1,0:T(8,128)S(1)}, f32[256,256]{1,0:T(8,128)S(1)}, u32[]{:S(2)}, u32[]{:S(2)}) collective-permute-start(f32[256,256]{1,0:T(8,128)S(1)} %dynamic-slice_add_fusion.1), channel_id=1, source_target_pairs={{0,0},{1,17},{2,34},{3,51},{4,68},{5,85},{6,102},{7,119},{8,136},{... | collective-permute-start | bytes 786440 | tf_op jit(solution)/shard_map/ppermute | solution.py:183

commit v4 on v3

--- a/solution.py
+++ b/solution.py
@@ -160,7 +160,6 @@
     high = lax.axis_index("syh")
     keep = lax.dynamic_slice_in_dim(total, high * panel_width, panel_width, 0)
     give = lax.dynamic_slice_in_dim(total, (1 - high) * panel_width, panel_width, 0)
-    share = keep + lax.ppermute(give, "syh", [(0, 1), (1, 0)])
     sizes = {a: lax.axis_size(a) for a in GENE_AXES}
     rings = {ROW_AXES: ROW_RING, COL_AXES: COL_RING}
 
@@ -171,16 +170,21 @@
         out.update(zip(axes, unravel(ring[(pos - back) % len(ring)], [sizes[a] for a in axes])))
         return ravel([out[a] for a in GENE_AXES], [sizes[a] for a in GENE_AXES])
 
-    perm = []
-    for sigma in range(spot_n):
+    def home(sigma, c):
         q = half * (sigma % 2) + sigma // 2
         t2, t1 = divmod(q, side)
+        coord = dict(zip(GENE_AXES, unravel(c, [sizes[a] for a in GENE_AXES])))
+        g = member(coord, ROW_AXES, t1)
+        s = member(coord, COL_AXES, t2)
+        return s * gene_n + g
+
+    keep_perm, give_perm = [], []
+    for sigma in range(spot_n):
         for c in range(gene_n):
-            coord = dict(zip(GENE_AXES, unravel(c, [sizes[a] for a in GENE_AXES])))
-            g = member(coord, ROW_AXES, t1)
-            s = member(coord, COL_AXES, t2)
-            perm.append((sigma * gene_n + c, s * gene_n + g))
-    share = lax.ppermute(share, SPOT_AXES + GENE_AXES, perm)
+            keep_perm.append((sigma * gene_n + c, home(sigma, c)))
+            give_perm.append((sigma * gene_n + c, home(sigma ^ 2, c)))
+    every = SPOT_AXES + GENE_AXES
+    share = lax.ppermute(keep, every, keep_perm) + lax.ppermute(give, every, give_perm)
     return share / jnp.sqrt(pair_norm)
 
 

time: 242 us -> 238 us (0.983)
  waiting for transfers between devices: 108 us -> 104 us
    ppermute x2, waiting for transfers between devices: 14.7 us -> 10.5 us  [the longest x1 5.75 us: shards(): lax.ppermute(give, every, give_perm)]
where the time goes in v4:
time: 238 us; the launch traced here: 236 us
  waiting for transfers between devices  104 us (44%)
  starting transfers between devices  72.9 us (31%)
  other arithmetic  28.6 us (12%)
  between operations  12.6 us (5%)
  local copies, waits for them, and re-layouts  9.48 us (4%)
  matrix products  8.83 us (4%)
    ppermute x2, waiting for transfers between devices, ring_gather(): prev = lax.ppermute(block, axes, fwd)  27.8 us
    ppermute x3, waiting for transfers between devices, shards(): lax.ppermute(sent, 'sx', [(k, (k + d) % ring_x) for k in range(ring_x)])  23.5 us
    ppermute x2, waiting for transfers between devices, ring_gather(): far_lo = lax.ppermute(prev[:half], axes, fwd)  16.2 us
    convert_element_type x1, other arithmetic, shards(): lagged = lagged_sum.astype(jnp.bfloat16)  12.2 us
    ppermute x2, starting transfers between devices, padded(): lax.ppermute(head, axis, [((i + 1) % count, i) for i in range(ends)])  12.1 us
    ppermute x4, waiting for transfers between devices, allreduce_moments(): packed = lax.ppermute(packed, axis, perm)  10.5 us
    ppermute x1, starting transfers between devices, shards(): mine = mine + lax.ppermute(other, 'sc', [(0, 1), (1, 0)])  10.2 us
    ppermute x2, starting transfers between devices, ring_gather(): far_lo = lax.ppermute(prev[:half], axes, fwd)  9.78 us
  transfers between devices with their start and end apart: 22, of which 16 were waited for; matrix products, arithmetic and copies ran while one was open for 13% of the time, Pallas kernels for 0%

profile of v4, /device:TPU:6, one launch (start us, length us, event | category | flops | bytes accessed | tf_op | source)
XLA Modules:
  0.0 236.1 jit_solution(3182748347045570774)
XLA Ops:
  0.0 0.9 multiply_add_fusion
  0.9 1.9 collective-permute-start
  2.8 6.0 %collective-permute-start.1 = (s32[2,512]{1,0:T(2,128)S(1)}, s32[2,512]{1,0:T(2,128)S(1)}, u32[]{:S(2)}, u32[]{:S(2)}) collective-permute-start(s32[2,512]{1,0:T(2,128)S(1)} %get-tuple-element.105), channel_id=1, source_target_pairs={{16,0},{32,16},{48,32},{64,48},{80,64},{96,80},{112,96},{128,112},... | collective-permute-start | bytes 12296 | tf_op jit(solution)/shard_map/ppermute | solution.py:33
  8.9 1.3 convert_reduce_fusion
  10.2 2.0 multiply_reduce_fusion.1
  12.7 0.4 multiply_reduce_fusion
  13.3 0.2 broadcast_select_fusion.15
  13.6 0.8 fusion.18
  14.4 1.3 pad_maximum_fusion.4
  15.7 1.2 collective-permute-done.2
  16.9 0.7 fusion.55
  21.9 2.3 collective-permute-start.3
  24.2 2.8 %collective-permute-done.3 = f32[514]{0:T(1024)S(1)} collective-permute-done((f32[514]{0:T(1024)S(1)}, f32[514]{0:T(1024)S(1)}, u32[]{:S(2)}, u32[]{:S(2)}) %collective-permute-start.3) | collective-permute-done | bytes 2088 | tf_op jit(solution)/shard_map/ppermute | solution.py:57
  27.0 0.7 fusion.54
  30.3 0.9 collective-permute-start.4
  31.1 2.8 %collective-permute-done.4 = f32[514]{0:T(1024)S(1)} collective-permute-done((f32[514]{0:T(1024)S(1)}, f32[514]{0:T(1024)S(1)}, u32[]{:S(2)}, u32[]{:S(2)}) %collective-permute-start.4) | collective-permute-done | bytes 2088 | tf_op jit(solution)/shard_map/ppermute | solution.py:57
  33.9 0.7 fusion.53
  37.2 1.4 collective-permute-start.5
  38.6 3.7 %collective-permute-done.5 = f32[514]{0:T(1024)S(1)} collective-permute-done((f32[514]{0:T(1024)S(1)}, f32[514]{0:T(1024)S(1)}, u32[]{:S(2)}, u32[]{:S(2)}) %collective-permute-start.5) | collective-permute-done | bytes 2088 | tf_op jit(solution)/shard_map/ppermute | solution.py:57
  42.3 0.7 fusion.52
  44.8 0.4 divide_convert_fusion
  45.2 1.9 collective-permute-start.10
  47.1 6.0 %collective-permute-start.11 = (bf16[2,512,256]{2,1,0:T(8,128)(2,1)S(1)}, bf16[2,512,256]{2,1,0:T(8,128)(2,1)S(1)}, u32[]{:S(2)}, u32[]{:S(2)}) collective-permute-start(bf16[2,512,256]{2,1,0:T(8,128)(2,1)S(1)} %get-tuple-element.57), channel_id=1, source_target_pairs={{16,0},{32,16},{48,32},{64,48},{80,64},{96,80},{112,96},{128,112},... | collective-permute-start | bytes 1572872 | tf_op jit(solution)/shard_map/ppermute | solution.py:33
  53.2 2.0 collective-permute-start.6
  55.3 2.9 %collective-permute-done.10 = bf16[2,512,256]{2,1,0:T(8,128)(2,1)S(1)} collective-permute-done((bf16[2,512,256]{2,1,0:T(8,128)(2,1)S(1)}, bf16[2,512,256]{2,1,0:T(8,128)(2,1)S(1)}, u32[]{:S(2)}, u32[]{:S(2)}) %collective-permute-start.10) | collective-permute-done | bytes 524320 | tf_op jit(solution)/shard_map/ppermute | solution.py:31
  58.2 1.7 collective-permute-done.11
  59.9 0.7 fusion.5
  60.7 12.2 %add_convert_fusion = bf16[4,512,256]{2,1,0:T(8,128)(2,1)} fusion(bf16[4,512,256]{2,1,0:T(8,128)(2,1)S(1)} %divide_convert_fusion, bf16[2,512,256]{2,1,0:T(8,128)(2,1)S(1)} %collective-permute-done.11, bf16[2,512,256]{2,1,0:T(8,128)(2,1)S(1)} %collective-permute-done.10, bf16[8,516,256]{2,1,0:T(8,128)(2,1)S(1)} %fusion.5, ...), kind=kLoop, calls=%fused_computation.11 | loop fusion | flops 39845888 | bytes 24313856 | tf_op jit(solution)/shard_map/convert_element_type | solution.py:137
  72.9 3.3 %collective-permute-start.12 = (bf16[2048,256]{1,0:T(8,128)(2,1)}, bf16[2048,256]{1,0:T(8,128)(2,1)}, u32[]{:S(2)}, u32[]{:S(2)}) collective-permute-start(bf16[2048,256]{1,0:T(8,128)(2,1)} %bitcast.16), channel_id=1, source_target_pairs={{0,2},{2,4},{4,6},{6,0},{1,3},{3,5},{5,7},{7,1},{8,10},{10,12},{12... | collective-permute-start | bytes 3145736 | tf_op jit(solution)/shard_map/ppermute | solution.py:68
  76.2 3.0 %collective-permute-done.6 = bf16[2048,256]{1,0:T(8,128)(2,1)S(1)} collective-permute-done((bf16[2048,256]{1,0:T(8,128)(2,1)S(1)}, bf16[2048,256]{1,0:T(8,128)(2,1)S(1)}, u32[]{:S(2)}, u32[]{:S(2)}) %collective-permute-start.6) | collective-permute-done | bytes 1048608 | tf_op jit(solution)/shard_map/ppermute | solution.py:68
  79.1 0.9 slice.442
  80.0 0.8 collective-permute-start.7
  80.8 0.8 slice.443
  81.6 1.2 collective-permute-start.9
  82.9 6.3 %collective-permute-start.14 = (bf16[2048,256]{1,0:T(8,128)(2,1)}, bf16[2048,256]{1,0:T(8,128)(2,1)}, u32[]{:S(2)}, u32[]{:S(2)}) collective-permute-start(bf16[2048,256]{1,0:T(8,128)(2,1)} %bitcast.16), channel_id=1, source_target_pairs={{2,0},{4,2},{6,4},{0,6},{3,1},{5,3},{7,5},{1,7},{10,8},{12,10},{14... | collective-permute-start | bytes 3145736 | tf_op jit(solution)/shard_map/ppermute | solution.py:69
  89.2 24.8 %collective-permute-done.12 = bf16[2048,256]{1,0:T(8,128)(2,1)} collective-permute-done((bf16[2048,256]{1,0:T(8,128)(2,1)}, bf16[2048,256]{1,0:T(8,128)(2,1)}, u32[]{:S(2)}, u32[]{:S(2)}) %collective-permute-start.12) | collective-permute-done | bytes 1048608 | tf_op jit(solution)/shard_map/ppermute | solution.py:68
  114.0 1.1 slice.470
  115.0 9.0 %collective-permute-start.13 = (bf16[1024,256]{1,0:T(8,128)(2,1)S(1)}, bf16[1024,256]{1,0:T(8,128)(2,1)S(1)}, u32[]{:S(2)}, u32[]{:S(2)}) collective-permute-start(bf16[1024,256]{1,0:T(8,128)(2,1)S(1)} %slice.470), channel_id=1, source_target_pairs={{0,2},{2,4},{4,6},{6,0},{1,3},{3,5},{5,7},{7,1},{8,10},{10,12},{12... | collective-permute-start | bytes 1572872 | tf_op jit(solution)/shard_map/ppermute | solution.py:71
  124.0 16.2 %collective-permute-done.7 = bf16[1024,256]{1,0:T(8,128)(2,1)} collective-permute-done((bf16[1024,256]{1,0:T(8,128)(2,1)}, bf16[1024,256]{1,0:T(8,128)(2,1)}, u32[]{:S(2)}, u32[]{:S(2)}) %collective-permute-start.7) | collective-permute-done | bytes 524320 | tf_op jit(solution)/shard_map/ppermute | solution.py:71
  140.2 2.9 %pad_maximum_fusion = bf16[2048,1024]{1,0:T(8,128)(2,1)S(1)} fusion(bf16[2048,256]{1,0:T(8,128)(2,1)S(1)} %collective-permute-done.8, bf16[1024,256]{1,0:T(8,128)(2,1)} %collective-permute-done.9, bf16[1024,256]{1,0:T(8,128)(2,1)} %collective-permute-done.7, bf16[2048,256]{1,0:T(8,128)(2,1)S(1)} %collective-permute-done.6, bf16[2048,256]{1,0:T(8,128)(2,1)S(1)} %bitcast.27), kind=kLoop, calls=%fused_computation.3 | loop fusion | flops 20971520 | bytes 8388608 | tf_op jit(solution)/shard_map/concatenate | solution.py:143
  143.1 2.5 %fusion.56 = f32[1024,256]{1,0:T(8,128)S(1)} fusion(bf16[2048,1024]{1,0:T(8,128)(2,1)S(1)} %pad_maximum_fusion, bf16[2048,256]{1,0:T(8,128)(2,1)} %bitcast.16), kind=kOutput, calls=%fused_computation.174 | convolution fusion | flops 1073741824 | bytes 6291456 | tf_op jit(solution)/shard_map/dot_general | solution.py:145
  145.7 1.1 slice.471
  146.7 4.0 %collective-permute-start.15 = (bf16[1024,256]{1,0:T(8,128)(2,1)S(1)}, bf16[1024,256]{1,0:T(8,128)(2,1)S(1)}, u32[]{:S(2)}, u32[]{:S(2)}) collective-permute-start(bf16[1024,256]{1,0:T(8,128)(2,1)S(1)} %slice.471), channel_id=1, source_target_pairs={{2,0},{4,2},{6,4},{0,6},{3,1},{5,3},{7,5},{1,7},{10,8},{12,10},{14... | collective-permute-start | bytes 1572872 | tf_op jit(solution)/shard_map/ppermute | solution.py:72
  150.8 2.5 %fusion.57 = f32[1024,256]{1,0:T(8,128)S(1)} fusion(bf16[2048,1024]{1,0:T(8,128)(2,1)S(1)} %pad_maximum_fusion, bf16[2048,256]{1,0:T(8,128)(2,1)} %collective-permute-done.12), kind=kOutput, calls=%fused_computation.175 | convolution fusion | flops 1073741824 | bytes 6291456 | tf_op jit(solution)/shard_map/dot_general | solution.py:145
  153.3 2.5 %fusion.58 = f32[1024,256]{1,0:T(8,128)S(1)} fusion(bf16[2048,1024]{1,0:T(8,128)(2,1)S(1)} %pad_maximum_fusion, bf16[2048,256]{1,0:T(8,128)(2,1)} %collective-permute-done.14), kind=kOutput, calls=%fused_computation.176 | convolution fusion | flops 1073741824 | bytes 6291456 | tf_op jit(solution)/shard_map/dot_general | solution.py:145
  155.8 6.8 %collective-permute-done.15 = bf16[1024,256]{1,0:T(8,128)(2,1)S(1)} collective-permute-done((bf16[1024,256]{1,0:T(8,128)(2,1)S(1)}, bf16[1024,256]{1,0:T(8,128)(2,1)S(1)}, u32[]{:S(2)}, u32[]{:S(2)}) %collective-permute-start.15) | collective-permute-done | bytes 524320 | tf_op jit(solution)/shard_map/ppermute | solution.py:72
  162.7 1.3 fusion.8
  164.0 0.3 pad_maximum_fusion.1
  164.2 0.1 constant_dynamic-slice_fusion.5
  164.4 1.8 copy-done.1
  166.2 10.2 %collective-permute-start.16 = (f32[2048,256]{1,0:T(8,128)S(1)}, f32[2048,256]{1,0:T(8,128)}, u32[]{:S(2)}, u32[]{:S(2)}) collective-permute-start(f32[2048,256]{1,0:T(8,128)S(1)} %constant_dynamic-slice_fusion.5), channel_id=1, source_target_pairs={{0,16},{16,0},{1,17},{17,1},{2,18},{18,2},{3,19},{19,3},{4,20},{20... | collective-permute-start | bytes 6291464 | tf_op jit(solution)/shard_map/ppermute | solution.py:152
  176.4 3.9 %collective-permute-done.16 = f32[2048,256]{1,0:T(8,128)} collective-permute-done((f32[2048,256]{1,0:T(8,128)S(1)}, f32[2048,256]{1,0:T(8,128)}, u32[]{:S(2)}, u32[]{:S(2)}) %collective-permute-start.16) | collective-permute-done | bytes 2097184 | tf_op jit(solution)/shard_map/ppermute | solution.py:152
  180.3 2.5 %dynamic-slice_add_fusion = f32[2048,256]{1,0:T(8,128)S(1)} fusion(f32[2048,256]{1,0:T(8,128)} %collective-permute-done.16, f32[4096,256]{1,0:T(8,128)} %copy-done.1, s32[]{:T(128)S(6)} %select_n.52), kind=kLoop, calls=%fused_computation.10 | loop fusion | flops 524288 | bytes 6291460 | tf_op jit(solution)/shard_map/add | solution.py:152
  182.8 0.9 constant_dynamic-slice_fusion.4
  183.7 6.7 %collective-permute-start.18 = (f32[512,256]{1,0:T(8,128)S(1)}, f32[512,256]{1,0:T(8,128)}, u32[]{:S(2)}, u32[]{:S(2)}) collective-permute-start(f32[512,256]{1,0:T(8,128)S(1)} %get-tuple-element.55), channel_id=1, source_target_pairs={{0,128},{64,192},{128,0},{192,64},{1,129},{65,193},{129,1},{193,65... | collective-permute-start | bytes 1572872 | tf_op jit(solution)/shard_map/ppermute | solution.py:159
  190.4 11.0 %collective-permute-done.17 = f32[512,256]{1,0:T(8,128)} collective-permute-done((f32[512,256]{1,0:T(8,128)}, f32[512,256]{1,0:T(8,128)}, u32[]{:S(2)}, u32[]{:S(2)}) %collective-permute-start.17) | collective-permute-done | bytes 524320 | tf_op jit(solution)/shard_map/ppermute | solution.py:159
  201.4 1.9 collective-permute-done.18
  203.3 10.6 %collective-permute-done.19 = f32[512,256]{1,0:T(8,128)} collective-permute-done((f32[512,256]{1,0:T(8,128)S(1)}, f32[512,256]{1,0:T(8,128)}, u32[]{:S(2)}, u32[]{:S(2)}) %collective-permute-start.19) | collective-permute-done | bytes 524320 | tf_op jit(solution)/shard_map/ppermute | solution.py:159
  213.9 1.5 add_add_fusion
  215.5 6.8 %collective-permute-start.20 = (f32[256,256]{1,0:T(8,128)S(1)}, f32[256,256]{1,0:T(8,128)S(1)}, u32[]{:S(2)}, u32[]{:S(2)}) collective-permute-start(f32[256,256]{1,0:T(8,128)S(1)} %get-tuple-element.59), channel_id=1, source_target_pairs={{0,0},{1,17},{2,34},{3,51},{4,68},{5,85},{6,102},{7,119},{8,136},{... | collective-permute-start | bytes 786440 | tf_op jit(solution)/shard_map/ppermute | solution.py:187
  222.3 1.9 collective-permute-start.21
  224.9 4.7 %collective-permute-done.20 = f32[256,256]{1,0:T(8,128)S(1)} collective-permute-done((f32[256,256]{1,0:T(8,128)S(1)}, f32[256,256]{1,0:T(8,128)S(1)}, u32[]{:S(2)}, u32[]{:S(2)}) %collective-permute-start.20) | collective-permute-done | bytes 262176 | tf_op jit(solution)/shard_map/ppermute | solution.py:187
  229.7 5.8 %collective-permute-done.21 = f32[256,256]{1,0:T(8,128)S(1)} collective-permute-done((f32[256,256]{1,0:T(8,128)S(1)}, f32[256,256]{1,0:T(8,128)S(1)}, u32[]{:S(2)}, u32[]{:S(2)}) %collective-permute-start.21) | collective-permute-done | bytes 262176 | tf_op jit(solution)/shard_map/ppermute | solution.py:187
  235.4 0.7 add_divide_fusion
  (32 shorter events, 0.9 us)
Async XLA Ops:
  0.0 12.7 %copy-start = (s32[4,512,256]{2,1,0:T(8,128)S(1)}, s32[4,512,256]{2,1,0:T(8,128)}, u32[]{:S(2)}) copy-start(s32[4,512,256]{2,1,0:T(8,128)} %param.3) | copy-start | bytes 6291460
  0.9 12.2 %collective-permute-start = (s32[2,512]{1,0:T(2,128)S(1)}, s32[2,512]{1,0:T(2,128)S(1)}, u32[]{:S(2)}, u32[]{:S(2)}) collective-permute-start(s32[2,512]{1,0:T(2,128)S(1)} %get-tuple-element.104), channel_id=1, source_target_pairs={{0,16},{16,32},{32,48},{48,64},{64,80},{80,96},{96,112},{112,128},... | collective-permute-start | bytes 12296 | tf_op jit(solution)/shard_map/ppermute | solution.py:31
  2.8 10.3 %collective-permute-start.1 = (s32[2,512]{1,0:T(2,128)S(1)}, s32[2,512]{1,0:T(2,128)S(1)}, u32[]{:S(2)}, u32[]{:S(2)}) collective-permute-start(s32[2,512]{1,0:T(2,128)S(1)} %get-tuple-element.105), channel_id=1, source_target_pairs={{16,0},{32,16},{48,32},{64,48},{80,64},{96,80},{112,96},{128,112},... | collective-permute-start | bytes 12296 | tf_op jit(solution)/shard_map/ppermute | solution.py:33
  10.2 3.1 %copy-start.2 = (s32[4,512]{1,0:T(4,128)S(1)}, s32[4,512]{1,0:T(4,128)}, u32[]{:S(2)}) copy-start(s32[4,512]{1,0:T(4,128)} %param.5) | copy-start | bytes 24580
  10.2 3.4 %copy-start.3 = (s32[4,512]{1,0:T(4,128)S(1)}, s32[4,512]{1,0:T(4,128)}, u32[]{:S(2)}) copy-start(s32[4,512]{1,0:T(4,128)} %param.4) | copy-start | bytes 24580
  15.7 1.2 collective-permute-start.2
  21.9 5.1 %collective-permute-start.3 = (f32[514]{0:T(1024)S(1)}, f32[514]{0:T(1024)S(1)}, u32[]{:S(2)}, u32[]{:S(2)}) collective-permute-start(f32[514]{0:T(1024)S(1)} %pad_maximum_fusion.5), channel_id=1, source_target_pairs={{0,32},{16,48},{32,0},{48,16},{64,96},{80,112},{96,64},{112,80},{1... | collective-permute-start | bytes 6176 | tf_op jit(solution)/shard_map/ppermute | solution.py:57
  30.3 3.6 %collective-permute-start.4 = (f32[514]{0:T(1024)S(1)}, f32[514]{0:T(1024)S(1)}, u32[]{:S(2)}, u32[]{:S(2)}) collective-permute-start(f32[514]{0:T(1024)S(1)} %pad_maximum_fusion.6), channel_id=1, source_target_pairs={{0,64},{16,80},{32,96},{48,112},{64,0},{80,16},{96,32},{112,48},{1... | collective-permute-start | bytes 6176 | tf_op jit(solution)/shard_map/ppermute | solution.py:57
  37.2 5.1 %collective-permute-start.5 = (f32[514]{0:T(1024)S(1)}, f32[514]{0:T(1024)S(1)}, u32[]{:S(2)}, u32[]{:S(2)}) collective-permute-start(f32[514]{0:T(1024)S(1)} %pad_maximum_fusion.7), channel_id=1, source_target_pairs={{0,128},{16,144},{32,160},{48,176},{64,192},{80,208},{96,224},{112... | collective-permute-start | bytes 6176 | tf_op jit(solution)/shard_map/ppermute | solution.py:57
  45.2 13.0 %collective-permute-start.10 = (bf16[2,512,256]{2,1,0:T(8,128)(2,1)S(1)}, bf16[2,512,256]{2,1,0:T(8,128)(2,1)S(1)}, u32[]{:S(2)}, u32[]{:S(2)}) collective-permute-start(bf16[2,512,256]{2,1,0:T(8,128)(2,1)S(1)} %get-tuple-element.56), channel_id=1, source_target_pairs={{0,16},{16,32},{32,48},{48,64},{64,80},{80,96},{96,112},{112,128},... | collective-permute-start | bytes 1572872 | tf_op jit(solution)/shard_map/ppermute | solution.py:31
  47.1 12.8 %collective-permute-start.11 = (bf16[2,512,256]{2,1,0:T(8,128)(2,1)S(1)}, bf16[2,512,256]{2,1,0:T(8,128)(2,1)S(1)}, u32[]{:S(2)}, u32[]{:S(2)}) collective-permute-start(bf16[2,512,256]{2,1,0:T(8,128)(2,1)S(1)} %get-tuple-element.57), channel_id=1, source_target_pairs={{16,0},{32,16},{48,32},{64,48},{80,64},{96,80},{112,96},{128,112},... | collective-permute-start | bytes 1572872 | tf_op jit(solution)/shard_map/ppermute | solution.py:33
  53.2 25.9 %collective-permute-start.6 = (bf16[2048,256]{1,0:T(8,128)(2,1)S(1)}, bf16[2048,256]{1,0:T(8,128)(2,1)S(1)}, u32[]{:S(2)}, u32[]{:S(2)}) collective-permute-start(bf16[2048,256]{1,0:T(8,128)(2,1)S(1)} %bitcast.25), channel_id=1, source_target_pairs={{0,1},{1,9},{9,8},{8,0},{2,3},{3,11},{11,10},{10,2},{4,5},{5,13},{... | collective-permute-start | bytes 3145736 | tf_op jit(solution)/shard_map/ppermute | solution.py:68
  55.2 25.6 %collective-permute-start.8 = (bf16[2048,256]{1,0:T(8,128)(2,1)S(1)}, bf16[2048,256]{1,0:T(8,128)(2,1)S(1)}, u32[]{:S(2)}, u32[]{:S(2)}) collective-permute-start(bf16[2048,256]{1,0:T(8,128)(2,1)S(1)} %bitcast.26), channel_id=1, source_target_pairs={{1,0},{9,1},{8,9},{0,8},{3,2},{11,3},{10,11},{2,10},{5,4},{13,5},{... | collective-permute-start | bytes 3145736 | tf_op jit(solution)/shard_map/ppermute | solution.py:69
  72.9 41.1 %collective-permute-start.12 = (bf16[2048,256]{1,0:T(8,128)(2,1)}, bf16[2048,256]{1,0:T(8,128)(2,1)}, u32[]{:S(2)}, u32[]{:S(2)}) collective-permute-start(bf16[2048,256]{1,0:T(8,128)(2,1)} %bitcast.16), channel_id=1, source_target_pairs={{0,2},{2,4},{4,6},{6,0},{1,3},{3,5},{5,7},{7,1},{8,10},{10,12},{12... | collective-permute-start | bytes 3145736 | tf_op jit(solution)/shard_map/ppermute | solution.py:68
  80.0 60.2 %collective-permute-start.7 = (bf16[1024,256]{1,0:T(8,128)(2,1)}, bf16[1024,256]{1,0:T(8,128)(2,1)}, u32[]{:S(2)}, u32[]{:S(2)}) collective-permute-start(bf16[1024,256]{1,0:T(8,128)(2,1)} %slice.442), channel_id=1, source_target_pairs={{0,1},{1,9},{9,8},{8,0},{2,3},{3,11},{11,10},{10,2},{4,5},{5,13},{... | collective-permute-start | bytes 1572872 | tf_op jit(solution)/shard_map/ppermute | solution.py:71
  81.6 58.6 %collective-permute-start.9 = (bf16[1024,256]{1,0:T(8,128)(2,1)}, bf16[1024,256]{1,0:T(8,128)(2,1)}, u32[]{:S(2)}, u32[]{:S(2)}) collective-permute-start(bf16[1024,256]{1,0:T(8,128)(2,1)} %slice.443), channel_id=1, source_target_pairs={{1,0},{9,1},{8,9},{0,8},{3,2},{11,3},{10,11},{2,10},{5,4},{13,5},{... | collective-permute-start | bytes 1572872 | tf_op jit(solution)/shard_map/ppermute | solution.py:72
  82.9 62.8 %collective-permute-start.14 = (bf16[2048,256]{1,0:T(8,128)(2,1)}, bf16[2048,256]{1,0:T(8,128)(2,1)}, u32[]{:S(2)}, u32[]{:S(2)}) collective-permute-start(bf16[2048,256]{1,0:T(8,128)(2,1)} %bitcast.16), channel_id=1, source_target_pairs={{2,0},{4,2},{6,4},{0,6},{3,1},{5,3},{7,5},{1,7},{10,8},{12,10},{14... | collective-permute-start | bytes 3145736 | tf_op jit(solution)/shard_map/ppermute | solution.py:69
  115.0 40.8 %collective-permute-start.13 = (bf16[1024,256]{1,0:T(8,128)(2,1)S(1)}, bf16[1024,256]{1,0:T(8,128)(2,1)S(1)}, u32[]{:S(2)}, u32[]{:S(2)}) collective-permute-start(bf16[1024,256]{1,0:T(8,128)(2,1)S(1)} %slice.470), channel_id=1, source_target_pairs={{0,2},{2,4},{4,6},{6,0},{1,3},{3,5},{5,7},{7,1},{8,10},{10,12},{12... | collective-permute-start | bytes 1572872 | tf_op jit(solution)/shard_map/ppermute | solution.py:71
  146.7 15.9 %collective-permute-start.15 = (bf16[1024,256]{1,0:T(8,128)(2,1)S(1)}, bf16[1024,256]{1,0:T(8,128)(2,1)S(1)}, u32[]{:S(2)}, u32[]{:S(2)}) collective-permute-start(bf16[1024,256]{1,0:T(8,128)(2,1)S(1)} %slice.471), channel_id=1, source_target_pairs={{2,0},{4,2},{6,4},{0,6},{3,1},{5,3},{7,5},{1,7},{10,8},{12,10},{14... | collective-permute-start | bytes 1572872 | tf_op jit(solution)/shard_map/ppermute | solution.py:72
  164.2 2.0 copy-start.1
  166.2 14.1 %collective-permute-start.16 = (f32[2048,256]{1,0:T(8,128)S(1)}, f32[2048,256]{1,0:T(8,128)}, u32[]{:S(2)}, u32[]{:S(2)}) collective-permute-start(f32[2048,256]{1,0:T(8,128)S(1)} %constant_dynamic-slice_fusion.5), channel_id=1, source_target_pairs={{0,16},{16,0},{1,17},{17,1},{2,18},{18,2},{3,19},{19,3},{4,20},{20... | collective-permute-start | bytes 6291464 | tf_op jit(solution)/shard_map/ppermute | solution.py:152
  183.7 17.7 %collective-permute-start.17 = (f32[512,256]{1,0:T(8,128)}, f32[512,256]{1,0:T(8,128)}, u32[]{:S(2)}, u32[]{:S(2)}) collective-permute-start(f32[512,256]{1,0:T(8,128)} %get-tuple-element.53), channel_id=1, source_target_pairs={{0,64},{64,128},{128,192},{192,0},{1,65},{65,129},{129,193},{193,1... | collective-permute-start | bytes 1572872 | tf_op jit(solution)/shard_map/ppermute | solution.py:159
  183.7 19.6 %collective-permute-start.18 = (f32[512,256]{1,0:T(8,128)S(1)}, f32[512,256]{1,0:T(8,128)}, u32[]{:S(2)}, u32[]{:S(2)}) collective-permute-start(f32[512,256]{1,0:T(8,128)S(1)} %get-tuple-element.55), channel_id=1, source_target_pairs={{0,128},{64,192},{128,0},{192,64},{1,129},{65,193},{129,1},{193,65... | collective-permute-start | bytes 1572872 | tf_op jit(solution)/shard_map/ppermute | solution.py:159
  190.4 23.5 %collective-permute-start.19 = (f32[512,256]{1,0:T(8,128)S(1)}, f32[512,256]{1,0:T(8,128)}, u32[]{:S(2)}, u32[]{:S(2)}) collective-permute-start(f32[512,256]{1,0:T(8,128)S(1)} %get-tuple-element.54), channel_id=1, source_target_pairs={{0,192},{64,0},{128,64},{192,128},{1,193},{65,1},{129,65},{193,129... | collective-permute-start | bytes 1572872 | tf_op jit(solution)/shard_map/ppermute | solution.py:159
  215.5 14.2 %collective-permute-start.20 = (f32[256,256]{1,0:T(8,128)S(1)}, f32[256,256]{1,0:T(8,128)S(1)}, u32[]{:S(2)}, u32[]{:S(2)}) collective-permute-start(f32[256,256]{1,0:T(8,128)S(1)} %get-tuple-element.59), channel_id=1, source_target_pairs={{0,0},{1,17},{2,34},{3,51},{4,68},{5,85},{6,102},{7,119},{8,136},{... | collective-permute-start | bytes 786440 | tf_op jit(solution)/shard_map/ppermute | solution.py:187
  222.3 13.1 %collective-permute-start.21 = (f32[256,256]{1,0:T(8,128)S(1)}, f32[256,256]{1,0:T(8,128)S(1)}, u32[]{:S(2)}, u32[]{:S(2)}) collective-permute-start(f32[256,256]{1,0:T(8,128)S(1)} %get-tuple-element.58), channel_id=1, source_target_pairs={{0,8},{1,16},{2,42},{3,50},{4,76},{5,84},{6,110},{7,118},{8,137},{... | collective-permute-start | bytes 786440 | tf_op jit(solution)/shard_map/ppermute | solution.py:187

commit v5 on v4

--- a/solution.py
+++ b/solution.py
@@ -138,8 +138,8 @@
     bin_count = row_count * col_count
     flat_z = zscores.reshape(bin_count, panel_width)
     flat_lag = lagged.reshape(bin_count, panel_width)
-    z_parts = ring_gather(flat_z, ROW_AXES, ROW_RING)
-    lag_parts = ring_gather(flat_lag, COL_AXES, COL_RING)
+    z_parts = ring_gather(flat_z, COL_AXES, COL_RING)
+    lag_parts = ring_gather(flat_lag, ROW_AXES, ROW_RING)
     z_cat = jnp.concatenate(z_parts, axis=1)
     block = jnp.concatenate(
         [lax.dot_general(z_cat, part, contract_bins, preferred_element_type=jnp.float32) for part in lag_parts],
@@ -174,8 +174,8 @@
         q = half * (sigma % 2) + sigma // 2
         t2, t1 = divmod(q, side)
         coord = dict(zip(GENE_AXES, unravel(c, [sizes[a] for a in GENE_AXES])))
-        g = member(coord, ROW_AXES, t1)
-        s = member(coord, COL_AXES, t2)
+        g = member(coord, COL_AXES, t1)
+        s = member(coord, ROW_AXES, t2)
         return s * gene_n + g
 
     keep_perm, give_perm = [], []

time: 238 us -> 241 us (1.013)
  waiting for transfers between devices: 104 us -> 123 us
  starting transfers between devices: 72.9 us -> 55 us
    ppermute x2, waiting for transfers between devices: 27.8 us -> 47.7 us  [ring_gather(): prev = lax.ppermute(block, axes, fwd)]
    ppermute x1, starting transfers between devices: 10.2 us -> 0.01 us  [shards(): mine = mine + lax.ppermute(other, 'sc', [(0, 1), (1, 0)])]
    ppermute x1, waiting for transfers between devices: 5.75 us -> 13.8 us  [shards(): lax.ppermute(give, every, give_perm)]
    ppermute x2, waiting for transfers between devices: 16.2 us -> 10.6 us  [ring_gather(): far_lo = lax.ppermute(prev[:half], axes, fwd)]
    ppermute x2, starting transfers between devices: 5.27 us -> 0.09 us  [ring_gather(): far_hi = lax.ppermute(nxt[half:], axes, bwd)]
    ppermute x2, starting transfers between devices: 9.78 us -> 14.7 us  [ring_gather(): far_lo = lax.ppermute(prev[:half], axes, fwd)]
    ppermute x3, starting transfers between devices: 6.71 us -> 2.9 us  [shards(): lax.ppermute(sent, 'sx', [(k, (k + d) % ring_x) for k in range(ring_x)])]
    ppermute x2, starting transfers between devices: 6.41 us -> 3.12 us  [ring_gather(): nxt = lax.ppermute(block, axes, bwd)]
  transfers between devices with their start and end apart: 22 -> 22, of which waited for: 16 -> 15; matrix products, arithmetic and copies ran while one was open for 13% -> 13% of each run, Pallas kernels for 0% -> 0%
where the time goes in v5:
time: 241 us; the launch traced here: 238 us
  waiting for transfers between devices  123 us (51%)
  starting transfers between devices  55 us (23%)
  other arithmetic  28.6 us (12%)
  between operations  12.7 us (5%)
  local copies, waits for them, and re-layouts  9.48 us (4%)
  matrix products  8.83 us (4%)
    ppermute x2, waiting for transfers between devices, ring_gather(): prev = lax.ppermute(block, axes, fwd)  47.7 us
    ppermute x3, waiting for transfers between devices, shards(): lax.ppermute(sent, 'sx', [(k, (k + d) % ring_x) for k in range(ring_x)])  23.9 us
    ppermute x2, starting transfers between devices, ring_gather(): far_lo = lax.ppermute(prev[:half], axes, fwd)  14.7 us
    ppermute x1, waiting for transfers between devices, shards(): lax.ppermute(give, every, give_perm)  13.8 us
    convert_element_type x1, other arithmetic, shards(): lagged = lagged_sum.astype(jnp.bfloat16)  12.2 us
    ppermute x2, starting transfers between devices, padded(): lax.ppermute(head, axis, [((i + 1) % count, i) for i in range(ends)])  12.1 us
    ppermute x2, waiting for transfers between devices, ring_gather(): far_lo = lax.ppermute(prev[:half], axes, fwd)  10.6 us
    ppermute x4, waiting for transfers between devices, allreduce_moments(): packed = lax.ppermute(packed, axis, perm)  10.5 us
  transfers between devices with their start and end apart: 22, of which 15 were waited for; matrix products, arithmetic and copies ran while one was open for 13% of the time, Pallas kernels for 0%

profile of v5, /device:TPU:6, one launch (start us, length us, event | category | flops | bytes accessed | tf_op | source)
XLA Modules:
  0.0 237.9 jit_solution(16090544029518038558)
XLA Ops:
  0.0 0.9 multiply_add_fusion
  0.9 1.9 collective-permute-start
  2.8 6.0 %collective-permute-start.1 = (s32[2,512]{1,0:T(2,128)S(1)}, s32[2,512]{1,0:T(2,128)S(1)}, u32[]{:S(2)}, u32[]{:S(2)}) collective-permute-start(s32[2,512]{1,0:T(2,128)S(1)} %get-tuple-element.105), channel_id=1, source_target_pairs={{16,0},{32,16},{48,32},{64,48},{80,64},{96,80},{112,96},{128,112},... | collective-permute-start | bytes 12296 | tf_op jit(solution)/shard_map/ppermute | solution.py:33
  8.9 1.3 convert_reduce_fusion
  10.2 2.0 multiply_reduce_fusion.1
  12.7 0.4 multiply_reduce_fusion
  13.2 0.1 add_select_fusion.1
  13.3 0.2 broadcast_select_fusion.15
  13.4 0.1 fusion.46
  13.5 0.1 broadcast_select_fusion.4
  13.6 0.8 fusion.18
  14.4 1.3 pad_maximum_fusion.4
  15.7 1.2 collective-permute-done.2
  16.9 0.7 fusion.55
  21.9 2.3 collective-permute-start.3
  24.2 2.8 %collective-permute-done.3 = f32[514]{0:T(1024)S(1)} collective-permute-done((f32[514]{0:T(1024)S(1)}, f32[514]{0:T(1024)S(1)}, u32[]{:S(2)}, u32[]{:S(2)}) %collective-permute-start.3) | collective-permute-done | bytes 2088 | tf_op jit(solution)/shard_map/ppermute | solution.py:57
  27.0 0.7 fusion.54
  30.3 0.9 collective-permute-start.4
  31.1 2.8 %collective-permute-done.4 = f32[514]{0:T(1024)S(1)} collective-permute-done((f32[514]{0:T(1024)S(1)}, f32[514]{0:T(1024)S(1)}, u32[]{:S(2)}, u32[]{:S(2)}) %collective-permute-start.4) | collective-permute-done | bytes 2088 | tf_op jit(solution)/shard_map/ppermute | solution.py:57
  33.9 0.7 fusion.53
  37.2 1.4 collective-permute-start.5
  38.6 3.7 %collective-permute-done.5 = f32[514]{0:T(1024)S(1)} collective-permute-done((f32[514]{0:T(1024)S(1)}, f32[514]{0:T(1024)S(1)}, u32[]{:S(2)}, u32[]{:S(2)}) %collective-permute-start.5) | collective-permute-done | bytes 2088 | tf_op jit(solution)/shard_map/ppermute | solution.py:57
  42.3 0.7 fusion.52
  44.8 0.4 divide_convert_fusion
  45.2 1.9 collective-permute-start.10
  47.1 6.0 %collective-permute-start.11 = (bf16[2,512,256]{2,1,0:T(8,128)(2,1)S(1)}, bf16[2,512,256]{2,1,0:T(8,128)(2,1)S(1)}, u32[]{:S(2)}, u32[]{:S(2)}) collective-permute-start(bf16[2,512,256]{2,1,0:T(8,128)(2,1)S(1)} %get-tuple-element.57), channel_id=1, source_target_pairs={{16,0},{32,16},{48,32},{64,48},{80,64},{96,80},{112,96},{128,112},... | collective-permute-start | bytes 1572872 | tf_op jit(solution)/shard_map/ppermute | solution.py:33
  53.2 3.3 %collective-permute-start.6 = (bf16[2048,256]{1,0:T(8,128)(2,1)S(1)}, bf16[2048,256]{1,0:T(8,128)(2,1)S(1)}, u32[]{:S(2)}, u32[]{:S(2)}) collective-permute-start(bf16[2048,256]{1,0:T(8,128)(2,1)S(1)} %bitcast.25), channel_id=1, source_target_pairs={{0,2},{2,4},{4,6},{6,0},{1,3},{3,5},{5,7},{7,1},{8,10},{10,12},{12... | collective-permute-start | bytes 3145736 | tf_op jit(solution)/shard_map/ppermute | solution.py:68
  56.5 3.1 %collective-permute-start.8 = (bf16[2048,256]{1,0:T(8,128)(2,1)S(1)}, bf16[2048,256]{1,0:T(8,128)(2,1)S(1)}, u32[]{:S(2)}, u32[]{:S(2)}) collective-permute-start(bf16[2048,256]{1,0:T(8,128)(2,1)S(1)} %bitcast.26), channel_id=1, source_target_pairs={{2,0},{4,2},{6,4},{0,6},{3,1},{5,3},{7,5},{1,7},{10,8},{12,10},{14... | collective-permute-start | bytes 3145736 | tf_op jit(solution)/shard_map/ppermute | solution.py:69
  59.7 0.3 collective-permute-done.11
  59.9 0.7 fusion.5
  60.7 12.2 %add_convert_fusion = bf16[4,512,256]{2,1,0:T(8,128)(2,1)} fusion(bf16[4,512,256]{2,1,0:T(8,128)(2,1)S(1)} %divide_convert_fusion, bf16[2,512,256]{2,1,0:T(8,128)(2,1)S(1)} %collective-permute-done.11, bf16[2,512,256]{2,1,0:T(8,128)(2,1)S(1)} %collective-permute-done.10, bf16[8,516,256]{2,1,0:T(8,128)(2,1)S(1)} %fusion.5, ...), kind=kLoop, calls=%fused_computation.11 | loop fusion | flops 39845888 | bytes 24313856 | tf_op jit(solution)/shard_map/convert_element_type | solution.py:137
  72.9 1.9 collective-permute-start.12
  74.8 30.7 %collective-permute-done.6 = bf16[2048,256]{1,0:T(8,128)(2,1)S(1)} collective-permute-done((bf16[2048,256]{1,0:T(8,128)(2,1)S(1)}, bf16[2048,256]{1,0:T(8,128)(2,1)S(1)}, u32[]{:S(2)}, u32[]{:S(2)}) %collective-permute-start.6) | collective-permute-done | bytes 1048608 | tf_op jit(solution)/shard_map/ppermute | solution.py:68
  105.5 0.9 slice.442
  106.4 11.9 %collective-permute-start.7 = (bf16[1024,256]{1,0:T(8,128)(2,1)}, bf16[1024,256]{1,0:T(8,128)(2,1)}, u32[]{:S(2)}, u32[]{:S(2)}) collective-permute-start(bf16[1024,256]{1,0:T(8,128)(2,1)} %slice.442), channel_id=1, source_target_pairs={{0,2},{2,4},{4,6},{6,0},{1,3},{3,5},{5,7},{7,1},{8,10},{10,12},{12... | collective-permute-start | bytes 1572872 | tf_op jit(solution)/shard_map/ppermute | solution.py:71
  118.3 0.8 slice.443
  119.1 17.0 %collective-permute-done.12 = bf16[2048,256]{1,0:T(8,128)(2,1)} collective-permute-done((bf16[2048,256]{1,0:T(8,128)(2,1)}, bf16[2048,256]{1,0:T(8,128)(2,1)}, u32[]{:S(2)}, u32[]{:S(2)}) %collective-permute-start.12) | collective-permute-done | bytes 1048608 | tf_op jit(solution)/shard_map/ppermute | solution.py:68
  136.1 1.1 slice.470
  137.2 2.7 %collective-permute-start.13 = (bf16[1024,256]{1,0:T(8,128)(2,1)S(1)}, bf16[1024,256]{1,0:T(8,128)(2,1)S(1)}, u32[]{:S(2)}, u32[]{:S(2)}) collective-permute-start(bf16[1024,256]{1,0:T(8,128)(2,1)S(1)} %slice.470), channel_id=1, source_target_pairs={{0,1},{1,9},{9,8},{8,0},{2,3},{3,11},{11,10},{10,2},{4,5},{5,13},{... | collective-permute-start | bytes 1572872 | tf_op jit(solution)/shard_map/ppermute | solution.py:71
  139.9 10.6 %collective-permute-done.7 = bf16[1024,256]{1,0:T(8,128)(2,1)} collective-permute-done((bf16[1024,256]{1,0:T(8,128)(2,1)}, bf16[1024,256]{1,0:T(8,128)(2,1)}, u32[]{:S(2)}, u32[]{:S(2)}) %collective-permute-start.7) | collective-permute-done | bytes 524320 | tf_op jit(solution)/shard_map/ppermute | solution.py:71
  150.6 2.9 %pad_maximum_fusion = bf16[2048,1024]{1,0:T(8,128)(2,1)S(1)} fusion(bf16[2048,256]{1,0:T(8,128)(2,1)S(1)} %collective-permute-done.8, bf16[1024,256]{1,0:T(8,128)(2,1)} %collective-permute-done.9, bf16[1024,256]{1,0:T(8,128)(2,1)} %collective-permute-done.7, bf16[2048,256]{1,0:T(8,128)(2,1)S(1)} %collective-permute-done.6, bf16[2048,256]{1,0:T(8,128)(2,1)S(1)} %bitcast.27), kind=kLoop, calls=%fused_computation.3 | loop fusion | flops 20971520 | bytes 8388608 | tf_op jit(solution)/shard_map/concatenate | solution.py:143
  153.5 2.5 %fusion.56 = f32[1024,256]{1,0:T(8,128)S(1)} fusion(bf16[2048,1024]{1,0:T(8,128)(2,1)S(1)} %pad_maximum_fusion, bf16[2048,256]{1,0:T(8,128)(2,1)} %bitcast.16), kind=kOutput, calls=%fused_computation.174 | convolution fusion | flops 1073741824 | bytes 6291456 | tf_op jit(solution)/shard_map/dot_general | solution.py:145
  156.0 1.1 slice.471
  157.1 0.1 collective-permute-start.15
  157.2 2.5 %fusion.57 = f32[1024,256]{1,0:T(8,128)S(1)} fusion(bf16[2048,1024]{1,0:T(8,128)(2,1)S(1)} %pad_maximum_fusion, bf16[2048,256]{1,0:T(8,128)(2,1)} %collective-permute-done.12), kind=kOutput, calls=%fused_computation.175 | convolution fusion | flops 1073741824 | bytes 6291456 | tf_op jit(solution)/shard_map/dot_general | solution.py:145
  159.7 2.5 %fusion.58 = f32[1024,256]{1,0:T(8,128)S(1)} fusion(bf16[2048,1024]{1,0:T(8,128)(2,1)S(1)} %pad_maximum_fusion, bf16[2048,256]{1,0:T(8,128)(2,1)} %collective-permute-done.14), kind=kOutput, calls=%fused_computation.176 | convolution fusion | flops 1073741824 | bytes 6291456 | tf_op jit(solution)/shard_map/dot_general | solution.py:145
  162.2 5.6 %collective-permute-done.15 = bf16[1024,256]{1,0:T(8,128)(2,1)S(1)} collective-permute-done((bf16[1024,256]{1,0:T(8,128)(2,1)S(1)}, bf16[1024,256]{1,0:T(8,128)(2,1)S(1)}, u32[]{:S(2)}, u32[]{:S(2)}) %collective-permute-start.15) | collective-permute-done | bytes 524320 | tf_op jit(solution)/shard_map/ppermute | solution.py:72
  167.9 1.3 fusion.8
  169.1 0.3 pad_maximum_fusion.1
  169.4 0.1 constant_dynamic-slice_fusion.5
  169.6 1.8 copy-done.1
  171.4 4.3 %collective-permute-done.16 = f32[2048,256]{1,0:T(8,128)} collective-permute-done((f32[2048,256]{1,0:T(8,128)S(1)}, f32[2048,256]{1,0:T(8,128)}, u32[]{:S(2)}, u32[]{:S(2)}) %collective-permute-start.16) | collective-permute-done | bytes 2097184 | tf_op jit(solution)/shard_map/ppermute | solution.py:152
  175.7 2.5 %dynamic-slice_add_fusion = f32[2048,256]{1,0:T(8,128)S(1)} fusion(f32[2048,256]{1,0:T(8,128)} %collective-permute-done.16, f32[4096,256]{1,0:T(8,128)} %copy-done.1, s32[]{:T(128)S(6)} %select_n.52), kind=kLoop, calls=%fused_computation.10 | loop fusion | flops 524288 | bytes 6291460 | tf_op jit(solution)/shard_map/add | solution.py:152
  178.2 0.9 constant_dynamic-slice_fusion.4
  179.1 2.9 %collective-permute-start.18 = (f32[512,256]{1,0:T(8,128)S(1)}, f32[512,256]{1,0:T(8,128)}, u32[]{:S(2)}, u32[]{:S(2)}) collective-permute-start(f32[512,256]{1,0:T(8,128)S(1)} %get-tuple-element.55), channel_id=1, source_target_pairs={{0,128},{64,192},{128,0},{192,64},{1,129},{65,193},{129,1},{193,65... | collective-permute-start | bytes 1572872 | tf_op jit(solution)/shard_map/ppermute | solution.py:159
  182.0 12.2 %collective-permute-done.17 = f32[512,256]{1,0:T(8,128)} collective-permute-done((f32[512,256]{1,0:T(8,128)}, f32[512,256]{1,0:T(8,128)}, u32[]{:S(2)}, u32[]{:S(2)}) %collective-permute-start.17) | collective-permute-done | bytes 524320 | tf_op jit(solution)/shard_map/ppermute | solution.py:159
  194.2 1.3 collective-permute-done.18
  195.6 10.4 %collective-permute-done.19 = f32[512,256]{1,0:T(8,128)} collective-permute-done((f32[512,256]{1,0:T(8,128)S(1)}, f32[512,256]{1,0:T(8,128)}, u32[]{:S(2)}, u32[]{:S(2)}) %collective-permute-start.19) | collective-permute-done | bytes 524320 | tf_op jit(solution)/shard_map/ppermute | solution.py:159
  205.9 1.5 add_add_fusion
  207.5 6.5 %collective-permute-start.20 = (f32[256,256]{1,0:T(8,128)S(1)}, f32[256,256]{1,0:T(8,128)S(1)}, u32[]{:S(2)}, u32[]{:S(2)}) collective-permute-start(f32[256,256]{1,0:T(8,128)S(1)} %get-tuple-element.59), channel_id=1, source_target_pairs={{0,0},{1,17},{2,34},{3,51},{4,68},{5,85},{6,102},{7,119},{8,136},{... | collective-permute-start | bytes 786440 | tf_op jit(solution)/shard_map/ppermute | solution.py:187
  213.9 1.9 collective-permute-start.21
  216.6 6.8 %collective-permute-done.20 = f32[256,256]{1,0:T(8,128)S(1)} collective-permute-done((f32[256,256]{1,0:T(8,128)S(1)}, f32[256,256]{1,0:T(8,128)S(1)}, u32[]{:S(2)}, u32[]{:S(2)}) %collective-permute-start.20) | collective-permute-done | bytes 262176 | tf_op jit(solution)/shard_map/ppermute | solution.py:187
  223.3 13.8 %collective-permute-done.21 = f32[256,256]{1,0:T(8,128)S(1)} collective-permute-done((f32[256,256]{1,0:T(8,128)S(1)}, f32[256,256]{1,0:T(8,128)S(1)}, u32[]{:S(2)}, u32[]{:S(2)}) %collective-permute-start.21) | collective-permute-done | bytes 262176 | tf_op jit(solution)/shard_map/ppermute | solution.py:187
  237.1 0.7 add_divide_fusion
  (32 shorter events, 0.5 us)
Async XLA Ops:
  0.0 12.7 %copy-start = (s32[4,512,256]{2,1,0:T(8,128)S(1)}, s32[4,512,256]{2,1,0:T(8,128)}, u32[]{:S(2)}) copy-start(s32[4,512,256]{2,1,0:T(8,128)} %param.3) | copy-start | bytes 6291460
  0.9 12.2 %collective-permute-start = (s32[2,512]{1,0:T(2,128)S(1)}, s32[2,512]{1,0:T(2,128)S(1)}, u32[]{:S(2)}, u32[]{:S(2)}) collective-permute-start(s32[2,512]{1,0:T(2,128)S(1)} %get-tuple-element.104), channel_id=1, source_target_pairs={{0,16},{16,32},{32,48},{48,64},{64,80},{80,96},{96,112},{112,128},... | collective-permute-start | bytes 12296 | tf_op jit(solution)/shard_map/ppermute | solution.py:31
  2.8 10.3 %collective-permute-start.1 = (s32[2,512]{1,0:T(2,128)S(1)}, s32[2,512]{1,0:T(2,128)S(1)}, u32[]{:S(2)}, u32[]{:S(2)}) collective-permute-start(s32[2,512]{1,0:T(2,128)S(1)} %get-tuple-element.105), channel_id=1, source_target_pairs={{16,0},{32,16},{48,32},{64,48},{80,64},{96,80},{112,96},{128,112},... | collective-permute-start | bytes 12296 | tf_op jit(solution)/shard_map/ppermute | solution.py:33
  10.2 3.1 %copy-start.2 = (s32[4,512]{1,0:T(4,128)S(1)}, s32[4,512]{1,0:T(4,128)}, u32[]{:S(2)}) copy-start(s32[4,512]{1,0:T(4,128)} %param.5) | copy-start | bytes 24580
  10.2 3.4 %copy-start.3 = (s32[4,512]{1,0:T(4,128)S(1)}, s32[4,512]{1,0:T(4,128)}, u32[]{:S(2)}) copy-start(s32[4,512]{1,0:T(4,128)} %param.4) | copy-start | bytes 24580
  15.7 1.2 collective-permute-start.2
  21.9 5.1 %collective-permute-start.3 = (f32[514]{0:T(1024)S(1)}, f32[514]{0:T(1024)S(1)}, u32[]{:S(2)}, u32[]{:S(2)}) collective-permute-start(f32[514]{0:T(1024)S(1)} %pad_maximum_fusion.5), channel_id=1, source_target_pairs={{0,32},{16,48},{32,0},{48,16},{64,96},{80,112},{96,64},{112,80},{1... | collective-permute-start | bytes 6176 | tf_op jit(solution)/shard_map/ppermute | solution.py:57
  30.3 3.6 %collective-permute-start.4 = (f32[514]{0:T(1024)S(1)}, f32[514]{0:T(1024)S(1)}, u32[]{:S(2)}, u32[]{:S(2)}) collective-permute-start(f32[514]{0:T(1024)S(1)} %pad_maximum_fusion.6), channel_id=1, source_target_pairs={{0,64},{16,80},{32,96},{48,112},{64,0},{80,16},{96,32},{112,48},{1... | collective-permute-start | bytes 6176 | tf_op jit(solution)/shard_map/ppermute | solution.py:57
  37.2 5.1 %collective-permute-start.5 = (f32[514]{0:T(1024)S(1)}, f32[514]{0:T(1024)S(1)}, u32[]{:S(2)}, u32[]{:S(2)}) collective-permute-start(f32[514]{0:T(1024)S(1)} %pad_maximum_fusion.7), channel_id=1, source_target_pairs={{0,128},{16,144},{32,160},{48,176},{64,192},{80,208},{96,224},{112... | collective-permute-start | bytes 6176 | tf_op jit(solution)/shard_map/ppermute | solution.py:57
  45.2 14.5 %collective-permute-start.10 = (bf16[2,512,256]{2,1,0:T(8,128)(2,1)S(1)}, bf16[2,512,256]{2,1,0:T(8,128)(2,1)S(1)}, u32[]{:S(2)}, u32[]{:S(2)}) collective-permute-start(bf16[2,512,256]{2,1,0:T(8,128)(2,1)S(1)} %get-tuple-element.56), channel_id=1, source_target_pairs={{0,16},{16,32},{32,48},{48,64},{64,80},{80,96},{96,112},{112,128},... | collective-permute-start | bytes 1572872 | tf_op jit(solution)/shard_map/ppermute | solution.py:31
  47.1 12.8 %collective-permute-start.11 = (bf16[2,512,256]{2,1,0:T(8,128)(2,1)S(1)}, bf16[2,512,256]{2,1,0:T(8,128)(2,1)S(1)}, u32[]{:S(2)}, u32[]{:S(2)}) collective-permute-start(bf16[2,512,256]{2,1,0:T(8,128)(2,1)S(1)} %get-tuple-element.57), channel_id=1, source_target_pairs={{16,0},{32,16},{48,32},{64,48},{80,64},{96,80},{112,96},{128,112},... | collective-permute-start | bytes 1572872 | tf_op jit(solution)/shard_map/ppermute | solution.py:33
  53.2 52.3 %collective-permute-start.6 = (bf16[2048,256]{1,0:T(8,128)(2,1)S(1)}, bf16[2048,256]{1,0:T(8,128)(2,1)S(1)}, u32[]{:S(2)}, u32[]{:S(2)}) collective-permute-start(bf16[2048,256]{1,0:T(8,128)(2,1)S(1)} %bitcast.25), channel_id=1, source_target_pairs={{0,2},{2,4},{4,6},{6,0},{1,3},{3,5},{5,7},{7,1},{8,10},{10,12},{12... | collective-permute-start | bytes 3145736 | tf_op jit(solution)/shard_map/ppermute | solution.py:68
  56.5 61.7 %collective-permute-start.8 = (bf16[2048,256]{1,0:T(8,128)(2,1)S(1)}, bf16[2048,256]{1,0:T(8,128)(2,1)S(1)}, u32[]{:S(2)}, u32[]{:S(2)}) collective-permute-start(bf16[2048,256]{1,0:T(8,128)(2,1)S(1)} %bitcast.26), channel_id=1, source_target_pairs={{2,0},{4,2},{6,4},{0,6},{3,1},{5,3},{7,5},{1,7},{10,8},{12,10},{14... | collective-permute-start | bytes 3145736 | tf_op jit(solution)/shard_map/ppermute | solution.py:69
  72.9 63.2 %collective-permute-start.12 = (bf16[2048,256]{1,0:T(8,128)(2,1)}, bf16[2048,256]{1,0:T(8,128)(2,1)}, u32[]{:S(2)}, u32[]{:S(2)}) collective-permute-start(bf16[2048,256]{1,0:T(8,128)(2,1)} %bitcast.16), channel_id=1, source_target_pairs={{0,1},{1,9},{9,8},{8,0},{2,3},{3,11},{11,10},{10,2},{4,5},{5,13},{... | collective-permute-start | bytes 3145736 | tf_op jit(solution)/shard_map/ppermute | solution.py:68
  106.4 44.2 %collective-permute-start.7 = (bf16[1024,256]{1,0:T(8,128)(2,1)}, bf16[1024,256]{1,0:T(8,128)(2,1)}, u32[]{:S(2)}, u32[]{:S(2)}) collective-permute-start(bf16[1024,256]{1,0:T(8,128)(2,1)} %slice.442), channel_id=1, source_target_pairs={{0,2},{2,4},{4,6},{6,0},{1,3},{3,5},{5,7},{7,1},{8,10},{10,12},{12... | collective-permute-start | bytes 1572872 | tf_op jit(solution)/shard_map/ppermute | solution.py:71
  119.1 31.4 %collective-permute-start.9 = (bf16[1024,256]{1,0:T(8,128)(2,1)}, bf16[1024,256]{1,0:T(8,128)(2,1)}, u32[]{:S(2)}, u32[]{:S(2)}) collective-permute-start(bf16[1024,256]{1,0:T(8,128)(2,1)} %slice.443), channel_id=1, source_target_pairs={{2,0},{4,2},{6,4},{0,6},{3,1},{5,3},{7,5},{1,7},{10,8},{12,10},{14... | collective-permute-start | bytes 1572872 | tf_op jit(solution)/shard_map/ppermute | solution.py:72
  119.1 36.9 %collective-permute-start.14 = (bf16[2048,256]{1,0:T(8,128)(2,1)}, bf16[2048,256]{1,0:T(8,128)(2,1)}, u32[]{:S(2)}, u32[]{:S(2)}) collective-permute-start(bf16[2048,256]{1,0:T(8,128)(2,1)} %bitcast.16), channel_id=1, source_target_pairs={{1,0},{9,1},{8,9},{0,8},{3,2},{11,3},{10,11},{2,10},{5,4},{13,5},{... | collective-permute-start | bytes 3145736 | tf_op jit(solution)/shard_map/ppermute | solution.py:69
  137.2 25.0 %collective-permute-start.13 = (bf16[1024,256]{1,0:T(8,128)(2,1)S(1)}, bf16[1024,256]{1,0:T(8,128)(2,1)S(1)}, u32[]{:S(2)}, u32[]{:S(2)}) collective-permute-start(bf16[1024,256]{1,0:T(8,128)(2,1)S(1)} %slice.470), channel_id=1, source_target_pairs={{0,1},{1,9},{9,8},{8,0},{2,3},{3,11},{11,10},{10,2},{4,5},{5,13},{... | collective-permute-start | bytes 1572872 | tf_op jit(solution)/shard_map/ppermute | solution.py:71
  157.1 10.8 %collective-permute-start.15 = (bf16[1024,256]{1,0:T(8,128)(2,1)S(1)}, bf16[1024,256]{1,0:T(8,128)(2,1)S(1)}, u32[]{:S(2)}, u32[]{:S(2)}) collective-permute-start(bf16[1024,256]{1,0:T(8,128)(2,1)S(1)} %slice.471), channel_id=1, source_target_pairs={{1,0},{9,1},{8,9},{0,8},{3,2},{11,3},{10,11},{2,10},{5,4},{13,5},{... | collective-permute-start | bytes 1572872 | tf_op jit(solution)/shard_map/ppermute | solution.py:72
  169.4 2.0 copy-start.1
  171.4 4.3 %collective-permute-start.16 = (f32[2048,256]{1,0:T(8,128)S(1)}, f32[2048,256]{1,0:T(8,128)}, u32[]{:S(2)}, u32[]{:S(2)}) collective-permute-start(f32[2048,256]{1,0:T(8,128)S(1)} %constant_dynamic-slice_fusion.5), channel_id=1, source_target_pairs={{0,16},{16,0},{1,17},{17,1},{2,18},{18,2},{3,19},{19,3},{4,20},{20... | collective-permute-start | bytes 6291464 | tf_op jit(solution)/shard_map/ppermute | solution.py:152
  179.1 15.1 %collective-permute-start.17 = (f32[512,256]{1,0:T(8,128)}, f32[512,256]{1,0:T(8,128)}, u32[]{:S(2)}, u32[]{:S(2)}) collective-permute-start(f32[512,256]{1,0:T(8,128)} %get-tuple-element.53), channel_id=1, source_target_pairs={{0,64},{64,128},{128,192},{192,0},{1,65},{65,129},{129,193},{193,1... | collective-permute-start | bytes 1572872 | tf_op jit(solution)/shard_map/ppermute | solution.py:159
  179.1 16.4 %collective-permute-start.18 = (f32[512,256]{1,0:T(8,128)S(1)}, f32[512,256]{1,0:T(8,128)}, u32[]{:S(2)}, u32[]{:S(2)}) collective-permute-start(f32[512,256]{1,0:T(8,128)S(1)} %get-tuple-element.55), channel_id=1, source_target_pairs={{0,128},{64,192},{128,0},{192,64},{1,129},{65,193},{129,1},{193,65... | collective-permute-start | bytes 1572872 | tf_op jit(solution)/shard_map/ppermute | solution.py:159
  182.0 23.9 %collective-permute-start.19 = (f32[512,256]{1,0:T(8,128)S(1)}, f32[512,256]{1,0:T(8,128)}, u32[]{:S(2)}, u32[]{:S(2)}) collective-permute-start(f32[512,256]{1,0:T(8,128)S(1)} %get-tuple-element.54), channel_id=1, source_target_pairs={{0,192},{64,0},{128,64},{192,128},{1,193},{65,1},{129,65},{193,129... | collective-permute-start | bytes 1572872 | tf_op jit(solution)/shard_map/ppermute | solution.py:159
  207.5 15.9 %collective-permute-start.20 = (f32[256,256]{1,0:T(8,128)S(1)}, f32[256,256]{1,0:T(8,128)S(1)}, u32[]{:S(2)}, u32[]{:S(2)}) collective-permute-start(f32[256,256]{1,0:T(8,128)S(1)} %get-tuple-element.59), channel_id=1, source_target_pairs={{0,0},{1,17},{2,34},{3,51},{4,68},{5,85},{6,102},{7,119},{8,136},{... | collective-permute-start | bytes 786440 | tf_op jit(solution)/shard_map/ppermute | solution.py:187
  213.9 23.2 %collective-permute-start.21 = (f32[256,256]{1,0:T(8,128)S(1)}, f32[256,256]{1,0:T(8,128)S(1)}, u32[]{:S(2)}, u32[]{:S(2)}) collective-permute-start(f32[256,256]{1,0:T(8,128)S(1)} %get-tuple-element.58), channel_id=1, source_target_pairs={{0,6},{1,23},{2,32},{3,49},{4,66},{5,83},{6,100},{7,117},{8,142},{... | collective-permute-start | bytes 786440 | tf_op jit(solution)/shard_map/ppermute | solution.py:187

commit v6 on v4

--- a/solution.py
+++ b/solution.py
@@ -37,28 +37,24 @@
     return cells
 
 
-def merge_moments(left, right):
-    n_a, s_a, m_a, q_a = left
-    n_b, s_b, m_b, q_b = right
-    n = n_a + n_b
-    gap = s_a / jnp.maximum(n_a, 1.0) - s_b / jnp.maximum(n_b, 1.0)
-    m = m_a + m_b + gap * gap * (n_a * n_b / jnp.maximum(n, 1.0))
-    return n, s_a + s_b, m, q_a + q_b
-
-
-def allreduce_moments(moments, axis):
-    count = lax.axis_size(axis)
-    width = moments[1].shape[0]
+def allreduce_sum(vector, axes):
+    count = math.prod(lax.axis_size(a) for a in axes)
     step = 1
     while step < count:
-        perm = [(i, i ^ step) for i in range(count)]
-        n, s, m, q = moments
-        packed = jnp.concatenate([s, m, jnp.stack([n, q])])
-        packed = lax.ppermute(packed, axis, perm)
-        other = (packed[2 * width], packed[:width], packed[width : 2 * width], packed[2 * width + 1])
-        moments = merge_moments(moments, other)
+        vector = vector + lax.ppermute(vector, axes, [(i, i ^ step) for i in range(count)])
         step *= 2
-    return moments
+    return vector
+
+
+def centred_square_sum(n, s1, s2):
+    base = 1 << 14
+    s2_hi, s2_lo = s2 >> 14, s2 & (base - 1)
+    s1_hi, s1_lo = s1 >> 14, s1 & (base - 1)
+    c0 = n * s2_lo - s1_lo * s1_lo
+    c1 = n * s2_hi - 2 * s1_hi * s1_lo + (c0 >> 14)
+    c2 = -s1_hi * s1_hi + (c1 >> 14)
+    upper = (c2 * base + (c1 & (base - 1))).astype(jnp.float32)
+    return upper * base + (c0 & (base - 1)).astype(jnp.float32)
 
 
 def ring_gather(block, axes, ring):
@@ -96,10 +92,9 @@
     tile_code = tile_ids * 2 + tissue
     code_rims = padded(tile_code, ((SPOT_AXES, 0),), 2)
     code_wide = jnp.pad(code_rims, ((0, 0), (2, 2)))
-    tissue_wide = (code_wide % 2).astype(jnp.float32)
+    tissue_wide = code_wide % 2
     ids_wide = code_wide // 2
-    in_tissue = tissue.astype(jnp.float32)
-    weight_sq = jnp.zeros((row_count, col_count), jnp.float32)
+    weight_sq = jnp.zeros((row_count, col_count), jnp.int32)
     same_list = []
     for row_off, col_off, weight in stencil_taps:
         near_ids = ids_wide[
@@ -108,22 +103,31 @@
         near_tissue = tissue_wide[
             2 + row_off : 2 + row_off + row_count, 2 + col_off : 2 + col_off + col_count
         ]
-        same_tile = (near_ids == tile_ids).astype(jnp.float32)
-        weight_sq = weight_sq + weight * weight * same_tile * near_tissue
-        same_list.append(same_tile)
-    pair_local = jnp.sum(in_tissue * weight_sq)
-    count_local = jnp.sum(in_tissue)
+        same = near_ids == tile_ids
+        scaled = round(1600 * weight * weight)
+        weight_sq = weight_sq + jnp.where(same, near_tissue * scaled, 0)
+        same_list.append(same.astype(jnp.float32))
+    in_tissue = tissue.astype(jnp.float32)
+    mask = in_tissue[:, :, None]
+    inside = jnp.where(tissue[:, :, None] > 0, counts, 0)
+    local = jnp.concatenate(
+        [
+            jnp.sum(inside, axis=(0, 1)),
+            jnp.sum(inside * inside, axis=(0, 1)),
+            jnp.stack([jnp.sum(tissue), jnp.sum(tissue * weight_sq)]),
+        ]
+    )
+    total = allreduce_sum(local, SPOT_AXES)
+    count_int = total[2 * panel_width]
+    tissue_count = count_int.astype(jnp.float32)
+    pair_norm = total[2 * panel_width + 1].astype(jnp.float32) / 1600.0
+    gene_mean = total[:panel_width].astype(jnp.float32) / tissue_count
+    variance = (
+        centred_square_sum(count_int, total[:panel_width], total[panel_width : 2 * panel_width])
+        / tissue_count
+        / tissue_count
+    )
     values = counts.astype(jnp.float32)
-    mask = in_tissue[:, :, None]
-    sum_local = jnp.sum(values * mask, axis=(0, 1))
-    mean_local = sum_local / jnp.maximum(count_local, 1.0)
-    dev_local = (values - mean_local) * mask
-    sq_local = jnp.sum(dev_local * dev_local, axis=(0, 1))
-    tissue_count, total_first, sq_total, pair_norm = allreduce_moments(
-        (count_local, sum_local, sq_local, pair_local), SPOT_AXES
-    )
-    gene_mean = total_first / tissue_count
-    variance = sq_total / tissue_count
     centred = (values - gene_mean) * mask
     zscores = (centred / jnp.sqrt(variance + 1e-05)).astype(jnp.bfloat16)
     zscore_rims = padded(zscores, ((SPOT_AXES, 0),), 2)

time: 238 us -> 227 us (0.954)
  starting transfers between devices: 72.9 us -> 84.8 us
  waiting for transfers between devices: 104 us -> 92.3 us
  between operations: 12.6 us -> 1.55 us
    ppermute x2, waiting for transfers between devices: 27.8 us -> 17.8 us  [ring_gather(): prev = lax.ppermute(block, axes, fwd)]
    ppermute x2, starting transfers between devices: 9.78 us -> 18.1 us  [ring_gather(): far_lo = lax.ppermute(prev[:half], axes, fwd)]
    ppermute x1, starting transfers between devices: 10.2 us -> 14.8 us  [shards(): mine = mine + lax.ppermute(other, 'sc', [(0, 1), (1, 0)])]
    ppermute x1, starting transfers between devices: 1.92 us -> 4.91 us  [shards(): lax.ppermute(give, every, give_perm)]
    ppermute x1, waiting for transfers between devices: 4.73 us -> 1.8 us  [shards(): lax.ppermute(keep, every, keep_perm) + lax.ppermute(give, every, give_perm)]
where the time goes in v6:
time: 227 us; the launch traced here: 225 us
  waiting for transfers between devices  92.3 us (41%)
  starting transfers between devices  84.8 us (37%)
  other arithmetic  29.7 us (13%)
  matrix products  8.83 us (4%)
  local copies, waits for them, and re-layouts  7.41 us (3%)
    ppermute x3, waiting for transfers between devices, shards(): lax.ppermute(sent, 'sx', [(k, (k + d) % ring_x) for k in range(ring_x)])  23.5 us
    ppermute x2, starting transfers between devices, ring_gather(): far_lo = lax.ppermute(prev[:half], axes, fwd)  18.1 us
    ppermute x2, waiting for transfers between devices, ring_gather(): prev = lax.ppermute(block, axes, fwd)  17.8 us
    ppermute x2, waiting for transfers between devices, ring_gather(): far_lo = lax.ppermute(prev[:half], axes, fwd)  16.5 us
    ppermute x1, starting transfers between devices, shards(): mine = mine + lax.ppermute(other, 'sc', [(0, 1), (1, 0)])  14.8 us
    convert_element_type x1, other arithmetic, shards(): lagged = lagged_sum.astype(jnp.bfloat16)  12.2 us
    ppermute x2, starting transfers between devices, padded(): lax.ppermute(head, axis, [((i + 1) % count, i) for i in range(ends)])  12.1 us
    ppermute x4, waiting for transfers between devices, allreduce_sum(): lax.ppermute(vector, axes, [(i, i ^ step) for i in range(count)])  11 us
  transfers between devices with their start and end apart: 22, of which 16 were waited for; matrix products, arithmetic and copies ran while one was open for 13% of the time, Pallas kernels for 0%

profile of v6, /device:TPU:6, one launch (start us, length us, event | category | flops | bytes accessed | tf_op | source)
XLA Modules:
  0.0 224.6 jit_solution(15538213562699959574)
XLA Ops:
  0.0 1.5 fusion.74
  1.5 1.9 collective-permute-start
  3.5 6.0 %collective-permute-start.1 = (s32[2,512]{1,0:T(2,128)S(1)}, s32[2,512]{1,0:T(2,128)S(1)}, u32[]{:S(2)}, u32[]{:S(2)}) collective-permute-start(s32[2,512]{1,0:T(2,128)S(1)} %get-tuple-element.110), channel_id=1, source_target_pairs={{16,0},{32,16},{48,32},{64,48},{80,64},{96,80},{112,96},{128,112},... | collective-permute-start | bytes 12296 | tf_op jit(solution)/shard_map/ppermute | solution.py:33
  9.5 0.7 broadcast_compare_fusion
  10.2 1.8 select_reduce_fusion
  12.1 0.2 broadcast_select_fusion.19
  12.5 0.8 fusion.63
  13.3 1.3 pad_add_fusion.1
  14.6 1.2 collective-permute-start.2
  15.8 0.8 collective-permute-done.2
  16.6 1.3 fusion.68
  17.9 1.5 collective-permute-start.3
  19.4 3.6 %collective-permute-done.3 = s32[514]{0:T(1024)S(1)} collective-permute-done((s32[514]{0:T(1024)S(1)}, s32[514]{0:T(1024)S(1)}, u32[]{:S(2)}, u32[]{:S(2)}) %collective-permute-start.3) | collective-permute-done | bytes 2088 | tf_op jit(solution)/shard_map/ppermute | solution.py:44
  23.0 0.8 collective-permute-start.4
  23.8 2.8 %collective-permute-done.4 = s32[514]{0:T(1024)S(1)} collective-permute-done((s32[514]{0:T(1024)S(1)}, s32[514]{0:T(1024)S(1)}, u32[]{:S(2)}, u32[]{:S(2)}) %collective-permute-start.4) | collective-permute-done | bytes 2088 | tf_op jit(solution)/shard_map/ppermute | solution.py:44
  26.7 1.4 collective-permute-start.5
  28.0 3.7 %collective-permute-done.5 = s32[514]{0:T(1024)S(1)} collective-permute-done((s32[514]{0:T(1024)S(1)}, s32[514]{0:T(1024)S(1)}, u32[]{:S(2)}, u32[]{:S(2)}) %collective-permute-start.5) | collective-permute-done | bytes 2088 | tf_op jit(solution)/shard_map/ppermute | solution.py:44
  31.8 0.6 fusion.76
  33.0 0.6 convert_divide_fusion
  33.6 0.4 divide_convert_fusion
  34.0 1.9 collective-permute-start.10
  35.9 6.0 %collective-permute-start.11 = (bf16[2,512,256]{2,1,0:T(8,128)(2,1)S(1)}, bf16[2,512,256]{2,1,0:T(8,128)(2,1)S(1)}, u32[]{:S(2)}, u32[]{:S(2)}) collective-permute-start(bf16[2,512,256]{2,1,0:T(8,128)(2,1)S(1)} %get-tuple-element.59), channel_id=1, source_target_pairs={{16,0},{32,16},{48,32},{64,48},{80,64},{96,80},{112,96},{128,112},... | collective-permute-start | bytes 1572872 | tf_op jit(solution)/shard_map/ppermute | solution.py:33
  42.0 2.0 collective-permute-start.6
  44.0 0.1 collective-permute-start.8
  44.1 2.9 %collective-permute-done.10 = bf16[2,512,256]{2,1,0:T(8,128)(2,1)S(1)} collective-permute-done((bf16[2,512,256]{2,1,0:T(8,128)(2,1)S(1)}, bf16[2,512,256]{2,1,0:T(8,128)(2,1)S(1)}, u32[]{:S(2)}, u32[]{:S(2)}) %collective-permute-start.10) | collective-permute-done | bytes 524320 | tf_op jit(solution)/shard_map/ppermute | solution.py:31
  47.0 1.7 collective-permute-done.11
  48.7 0.7 fusion.5
  49.5 12.2 %add_convert_fusion = bf16[4,512,256]{2,1,0:T(8,128)(2,1)} fusion(bf16[4,512,256]{2,1,0:T(8,128)(2,1)S(1)} %divide_convert_fusion, bf16[2,512,256]{2,1,0:T(8,128)(2,1)S(1)} %collective-permute-done.11, bf16[2,512,256]{2,1,0:T(8,128)(2,1)S(1)} %collective-permute-done.10, bf16[8,516,256]{2,1,0:T(8,128)(2,1)S(1)} %fusion.5, ...), kind=kLoop, calls=%fused_computation.11 | loop fusion | flops 39845888 | bytes 24313856 | tf_op jit(solution)/shard_map/convert_element_type | solution.py:141
  61.7 3.3 %collective-permute-start.12 = (bf16[2048,256]{1,0:T(8,128)(2,1)}, bf16[2048,256]{1,0:T(8,128)(2,1)}, u32[]{:S(2)}, u32[]{:S(2)}) collective-permute-start(bf16[2048,256]{1,0:T(8,128)(2,1)} %bitcast.4), channel_id=1, source_target_pairs={{0,2},{2,4},{4,6},{6,0},{1,3},{3,5},{5,7},{7,1},{8,10},{10,12},{12... | collective-permute-start | bytes 3145736 | tf_op jit(solution)/shard_map/ppermute | solution.py:64
  65.0 2.2 collective-permute-done.6
  67.2 0.8 slice.395
  68.0 0.7 collective-permute-start.7
  68.7 0.8 slice.396
  69.5 1.3 collective-permute-start.9
  70.9 6.3 %collective-permute-start.14 = (bf16[2048,256]{1,0:T(8,128)(2,1)}, bf16[2048,256]{1,0:T(8,128)(2,1)}, u32[]{:S(2)}, u32[]{:S(2)}) collective-permute-start(bf16[2048,256]{1,0:T(8,128)(2,1)} %bitcast.4), channel_id=1, source_target_pairs={{2,0},{4,2},{6,4},{0,6},{3,1},{5,3},{7,5},{1,7},{10,8},{12,10},{14... | collective-permute-start | bytes 3145736 | tf_op jit(solution)/shard_map/ppermute | solution.py:65
  77.2 15.6 %collective-permute-done.12 = bf16[2048,256]{1,0:T(8,128)(2,1)} collective-permute-done((bf16[2048,256]{1,0:T(8,128)(2,1)}, bf16[2048,256]{1,0:T(8,128)(2,1)}, u32[]{:S(2)}, u32[]{:S(2)}) %collective-permute-start.12) | collective-permute-done | bytes 1048608 | tf_op jit(solution)/shard_map/ppermute | solution.py:64
  92.8 1.1 slice.423
  93.9 17.4 %collective-permute-start.13 = (bf16[1024,256]{1,0:T(8,128)(2,1)S(1)}, bf16[1024,256]{1,0:T(8,128)(2,1)S(1)}, u32[]{:S(2)}, u32[]{:S(2)}) collective-permute-start(bf16[1024,256]{1,0:T(8,128)(2,1)S(1)} %slice.423), channel_id=1, source_target_pairs={{0,2},{2,4},{4,6},{6,0},{1,3},{3,5},{5,7},{7,1},{8,10},{10,12},{12... | collective-permute-start | bytes 1572872 | tf_op jit(solution)/shard_map/ppermute | solution.py:67
  111.3 16.5 %collective-permute-done.7 = bf16[1024,256]{1,0:T(8,128)(2,1)} collective-permute-done((bf16[1024,256]{1,0:T(8,128)(2,1)}, bf16[1024,256]{1,0:T(8,128)(2,1)}, u32[]{:S(2)}, u32[]{:S(2)}) %collective-permute-start.7) | collective-permute-done | bytes 524320 | tf_op jit(solution)/shard_map/ppermute | solution.py:67
  127.8 2.9 %pad_maximum_fusion = bf16[2048,1024]{1,0:T(8,128)(2,1)S(1)} fusion(bf16[2048,256]{1,0:T(8,128)(2,1)S(1)} %collective-permute-done.8, bf16[1024,256]{1,0:T(8,128)(2,1)} %collective-permute-done.9, bf16[1024,256]{1,0:T(8,128)(2,1)} %collective-permute-done.7, bf16[2048,256]{1,0:T(8,128)(2,1)S(1)} %collective-permute-done.6, bf16[2048,256]{1,0:T(8,128)(2,1)S(1)} %bitcast.15), kind=kLoop, calls=%fused_computation.3 | loop fusion | flops 20971520 | bytes 8388608 | tf_op jit(solution)/shard_map/concatenate | solution.py:147
  130.8 2.5 %fusion.77 = f32[1024,256]{1,0:T(8,128)S(1)} fusion(bf16[2048,1024]{1,0:T(8,128)(2,1)S(1)} %pad_maximum_fusion, bf16[2048,256]{1,0:T(8,128)(2,1)} %bitcast.4), kind=kOutput, calls=%fused_computation.182 | convolution fusion | flops 1073741824 | bytes 6291456 | tf_op jit(solution)/shard_map/dot_general | solution.py:149
  133.3 1.1 slice.424
  134.4 2.8 %collective-permute-start.15 = (bf16[1024,256]{1,0:T(8,128)(2,1)S(1)}, bf16[1024,256]{1,0:T(8,128)(2,1)S(1)}, u32[]{:S(2)}, u32[]{:S(2)}) collective-permute-start(bf16[1024,256]{1,0:T(8,128)(2,1)S(1)} %slice.424), channel_id=1, source_target_pairs={{2,0},{4,2},{6,4},{0,6},{3,1},{5,3},{7,5},{1,7},{10,8},{12,10},{14... | collective-permute-start | bytes 1572872 | tf_op jit(solution)/shard_map/ppermute | solution.py:68
  137.1 2.5 %fusion.78 = f32[1024,256]{1,0:T(8,128)S(1)} fusion(bf16[2048,1024]{1,0:T(8,128)(2,1)S(1)} %pad_maximum_fusion, bf16[2048,256]{1,0:T(8,128)(2,1)} %collective-permute-done.12), kind=kOutput, calls=%fused_computation.183 | convolution fusion | flops 1073741824 | bytes 6291456 | tf_op jit(solution)/shard_map/dot_general | solution.py:149
  139.7 2.5 %fusion.79 = f32[1024,256]{1,0:T(8,128)S(1)} fusion(bf16[2048,1024]{1,0:T(8,128)(2,1)S(1)} %pad_maximum_fusion, bf16[2048,256]{1,0:T(8,128)(2,1)} %collective-permute-done.14), kind=kOutput, calls=%fused_computation.184 | convolution fusion | flops 1073741824 | bytes 6291456 | tf_op jit(solution)/shard_map/dot_general | solution.py:149
  142.2 7.6 %collective-permute-done.15 = bf16[1024,256]{1,0:T(8,128)(2,1)S(1)} collective-permute-done((bf16[1024,256]{1,0:T(8,128)(2,1)S(1)}, bf16[1024,256]{1,0:T(8,128)(2,1)S(1)}, u32[]{:S(2)}, u32[]{:S(2)}) %collective-permute-start.15) | collective-permute-done | bytes 524320 | tf_op jit(solution)/shard_map/ppermute | solution.py:68
  149.8 1.3 fusion.8
  151.1 0.3 pad_maximum_fusion.1
  151.4 0.1 constant_dynamic-slice_fusion.5
  151.5 1.8 copy-done
  153.3 14.8 %collective-permute-start.16 = (f32[2048,256]{1,0:T(8,128)S(1)}, f32[2048,256]{1,0:T(8,128)}, u32[]{:S(2)}, u32[]{:S(2)}) collective-permute-start(f32[2048,256]{1,0:T(8,128)S(1)} %constant_dynamic-slice_fusion.5), channel_id=1, source_target_pairs={{0,16},{16,0},{1,17},{17,1},{2,18},{18,2},{3,19},{19,3},{4,20},{20... | collective-permute-start | bytes 6291464 | tf_op jit(solution)/shard_map/ppermute | solution.py:156
  168.1 3.9 %collective-permute-done.16 = f32[2048,256]{1,0:T(8,128)} collective-permute-done((f32[2048,256]{1,0:T(8,128)S(1)}, f32[2048,256]{1,0:T(8,128)}, u32[]{:S(2)}, u32[]{:S(2)}) %collective-permute-start.16) | collective-permute-done | bytes 2097184 | tf_op jit(solution)/shard_map/ppermute | solution.py:156
  172.0 2.5 %dynamic-slice_add_fusion = f32[2048,256]{1,0:T(8,128)S(1)} fusion(f32[2048,256]{1,0:T(8,128)} %collective-permute-done.16, f32[4096,256]{1,0:T(8,128)} %copy-done, s32[]{:T(128)S(6)} %select_n.154), kind=kLoop, calls=%fused_computation.10 | loop fusion | flops 524288 | bytes 6291460 | tf_op jit(solution)/shard_map/add | solution.py:156
  174.5 0.9 constant_dynamic-slice_fusion.4
  175.4 5.0 %collective-permute-start.18 = (f32[512,256]{1,0:T(8,128)S(1)}, f32[512,256]{1,0:T(8,128)}, u32[]{:S(2)}, u32[]{:S(2)}) collective-permute-start(f32[512,256]{1,0:T(8,128)S(1)} %get-tuple-element.57), channel_id=1, source_target_pairs={{0,128},{64,192},{128,0},{192,64},{1,129},{65,193},{129,1},{193,65... | collective-permute-start | bytes 1572872 | tf_op jit(solution)/shard_map/ppermute | solution.py:163
  180.4 11.0 %collective-permute-done.17 = f32[512,256]{1,0:T(8,128)} collective-permute-done((f32[512,256]{1,0:T(8,128)}, f32[512,256]{1,0:T(8,128)}, u32[]{:S(2)}, u32[]{:S(2)}) %collective-permute-start.17) | collective-permute-done | bytes 524320 | tf_op jit(solution)/shard_map/ppermute | solution.py:163
  191.4 1.9 collective-permute-done.18
  193.3 10.6 %collective-permute-done.19 = f32[512,256]{1,0:T(8,128)} collective-permute-done((f32[512,256]{1,0:T(8,128)S(1)}, f32[512,256]{1,0:T(8,128)}, u32[]{:S(2)}, u32[]{:S(2)}) %collective-permute-start.19) | collective-permute-done | bytes 524320 | tf_op jit(solution)/shard_map/ppermute | solution.py:163
  203.9 1.5 add_add_fusion
  205.4 5.5 %collective-permute-start.20 = (f32[256,256]{1,0:T(8,128)S(1)}, f32[256,256]{1,0:T(8,128)S(1)}, u32[]{:S(2)}, u32[]{:S(2)}) collective-permute-start(f32[256,256]{1,0:T(8,128)S(1)} %get-tuple-element.61), channel_id=1, source_target_pairs={{0,0},{1,17},{2,34},{3,51},{4,68},{5,85},{6,102},{7,119},{8,136},{... | collective-permute-start | bytes 786440 | tf_op jit(solution)/shard_map/ppermute | solution.py:191
  211.0 4.9 %collective-permute-start.21 = (f32[256,256]{1,0:T(8,128)S(1)}, f32[256,256]{1,0:T(8,128)S(1)}, u32[]{:S(2)}, u32[]{:S(2)}) collective-permute-start(f32[256,256]{1,0:T(8,128)S(1)} %get-tuple-element.60), channel_id=1, source_target_pairs={{0,8},{1,16},{2,42},{3,50},{4,76},{5,84},{6,110},{7,118},{8,137},{... | collective-permute-start | bytes 786440 | tf_op jit(solution)/shard_map/ppermute | solution.py:191
  216.6 1.8 collective-permute-done.20
  218.4 5.5 %collective-permute-done.21 = f32[256,256]{1,0:T(8,128)S(1)} collective-permute-done((f32[256,256]{1,0:T(8,128)S(1)}, f32[256,256]{1,0:T(8,128)S(1)}, u32[]{:S(2)}, u32[]{:S(2)}) %collective-permute-start.21) | collective-permute-done | bytes 262176 | tf_op jit(solution)/shard_map/ppermute | solution.py:191
  223.8 0.7 add_divide_fusion
  (25 shorter events, 0.4 us)
Async XLA Ops:
  0.0 12.5 %copy-start.3 = (s32[4,512]{1,0:T(4,128)S(1)}, s32[4,512]{1,0:T(4,128)}, u32[]{:S(2)}) copy-start(s32[4,512]{1,0:T(4,128)} %param.4) | copy-start | bytes 24580
  0.0 12.1 %copy-start.2 = (s32[4,512]{1,0:T(4,128)S(1)}, s32[4,512]{1,0:T(4,128)}, u32[]{:S(2)}) copy-start(s32[4,512]{1,0:T(4,128)} %param.5) | copy-start | bytes 24580
  0.0 33.5 %copy-start.1 = (s32[4,512,256]{2,1,0:T(8,128)S(1)}, s32[4,512,256]{2,1,0:T(8,128)}, u32[]{:S(2)}) copy-start(s32[4,512,256]{2,1,0:T(8,128)} %param.3) | copy-start | bytes 6291460
  1.5 10.5 %collective-permute-start = (s32[2,512]{1,0:T(2,128)S(1)}, s32[2,512]{1,0:T(2,128)S(1)}, u32[]{:S(2)}, u32[]{:S(2)}) collective-permute-start(s32[2,512]{1,0:T(2,128)S(1)} %get-tuple-element.109), channel_id=1, source_target_pairs={{0,16},{16,32},{32,48},{48,64},{64,80},{80,96},{96,112},{112,128},... | collective-permute-start | bytes 12296 | tf_op jit(solution)/shard_map/ppermute | solution.py:31
  3.5 8.6 %collective-permute-start.1 = (s32[2,512]{1,0:T(2,128)S(1)}, s32[2,512]{1,0:T(2,128)S(1)}, u32[]{:S(2)}, u32[]{:S(2)}) collective-permute-start(s32[2,512]{1,0:T(2,128)S(1)} %get-tuple-element.110), channel_id=1, source_target_pairs={{16,0},{32,16},{48,32},{64,48},{80,64},{96,80},{112,96},{128,112},... | collective-permute-start | bytes 12296 | tf_op jit(solution)/shard_map/ppermute | solution.py:33
  14.6 2.0 collective-permute-start.2
  17.9 5.1 %collective-permute-start.3 = (s32[514]{0:T(1024)S(1)}, s32[514]{0:T(1024)S(1)}, u32[]{:S(2)}, u32[]{:S(2)}) collective-permute-start(s32[514]{0:T(1024)S(1)} %fusion.68), channel_id=1, source_target_pairs={{0,32},{16,48},{32,0},{48,16},{64,96},{80,112},{96,64},{112,80},{1... | collective-permute-start | bytes 6176 | tf_op jit(solution)/shard_map/ppermute | solution.py:44
  23.0 3.6 %collective-permute-start.4 = (s32[514]{0:T(1024)S(1)}, s32[514]{0:T(1024)S(1)}, u32[]{:S(2)}, u32[]{:S(2)}) collective-permute-start(s32[514]{0:T(1024)S(1)} %add.266), channel_id=1, source_target_pairs={{0,64},{16,80},{32,96},{48,112},{64,0},{80,16},{96,32},{112,48},{1... | collective-permute-start | bytes 6176 | tf_op jit(solution)/shard_map/ppermute | solution.py:44
  26.7 5.1 %collective-permute-start.5 = (s32[514]{0:T(1024)S(1)}, s32[514]{0:T(1024)S(1)}, u32[]{:S(2)}, u32[]{:S(2)}) collective-permute-start(s32[514]{0:T(1024)S(1)} %add.267), channel_id=1, source_target_pairs={{0,128},{16,144},{32,160},{48,176},{64,192},{80,208},{96,224},{112... | collective-permute-start | bytes 6176 | tf_op jit(solution)/shard_map/ppermute | solution.py:44
  34.0 13.0 %collective-permute-start.10 = (bf16[2,512,256]{2,1,0:T(8,128)(2,1)S(1)}, bf16[2,512,256]{2,1,0:T(8,128)(2,1)S(1)}, u32[]{:S(2)}, u32[]{:S(2)}) collective-permute-start(bf16[2,512,256]{2,1,0:T(8,128)(2,1)S(1)} %get-tuple-element.58), channel_id=1, source_target_pairs={{0,16},{16,32},{32,48},{48,64},{64,80},{80,96},{96,112},{112,128},... | collective-permute-start | bytes 1572872 | tf_op jit(solution)/shard_map/ppermute | solution.py:31
  35.9 12.8 %collective-permute-start.11 = (bf16[2,512,256]{2,1,0:T(8,128)(2,1)S(1)}, bf16[2,512,256]{2,1,0:T(8,128)(2,1)S(1)}, u32[]{:S(2)}, u32[]{:S(2)}) collective-permute-start(bf16[2,512,256]{2,1,0:T(8,128)(2,1)S(1)} %get-tuple-element.59), channel_id=1, source_target_pairs={{16,0},{32,16},{48,32},{64,48},{80,64},{96,80},{112,96},{128,112},... | collective-permute-start | bytes 1572872 | tf_op jit(solution)/shard_map/ppermute | solution.py:33
  42.0 25.2 %collective-permute-start.6 = (bf16[2048,256]{1,0:T(8,128)(2,1)S(1)}, bf16[2048,256]{1,0:T(8,128)(2,1)S(1)}, u32[]{:S(2)}, u32[]{:S(2)}) collective-permute-start(bf16[2048,256]{1,0:T(8,128)(2,1)S(1)} %bitcast.13), channel_id=1, source_target_pairs={{0,1},{1,9},{9,8},{8,0},{2,3},{3,11},{11,10},{10,2},{4,5},{5,13},{... | collective-permute-start | bytes 3145736 | tf_op jit(solution)/shard_map/ppermute | solution.py:64
  44.0 24.7 %collective-permute-start.8 = (bf16[2048,256]{1,0:T(8,128)(2,1)S(1)}, bf16[2048,256]{1,0:T(8,128)(2,1)S(1)}, u32[]{:S(2)}, u32[]{:S(2)}) collective-permute-start(bf16[2048,256]{1,0:T(8,128)(2,1)S(1)} %bitcast.14), channel_id=1, source_target_pairs={{1,0},{9,1},{8,9},{0,8},{3,2},{11,3},{10,11},{2,10},{5,4},{13,5},{... | collective-permute-start | bytes 3145736 | tf_op jit(solution)/shard_map/ppermute | solution.py:65
  61.7 31.1 %collective-permute-start.12 = (bf16[2048,256]{1,0:T(8,128)(2,1)}, bf16[2048,256]{1,0:T(8,128)(2,1)}, u32[]{:S(2)}, u32[]{:S(2)}) collective-permute-start(bf16[2048,256]{1,0:T(8,128)(2,1)} %bitcast.4), channel_id=1, source_target_pairs={{0,2},{2,4},{4,6},{6,0},{1,3},{3,5},{5,7},{7,1},{8,10},{10,12},{12... | collective-permute-start | bytes 3145736 | tf_op jit(solution)/shard_map/ppermute | solution.py:64
  68.0 59.8 %collective-permute-start.7 = (bf16[1024,256]{1,0:T(8,128)(2,1)}, bf16[1024,256]{1,0:T(8,128)(2,1)}, u32[]{:S(2)}, u32[]{:S(2)}) collective-permute-start(bf16[1024,256]{1,0:T(8,128)(2,1)} %slice.395), channel_id=1, source_target_pairs={{0,1},{1,9},{9,8},{8,0},{2,3},{3,11},{11,10},{10,2},{4,5},{5,13},{... | collective-permute-start | bytes 1572872 | tf_op jit(solution)/shard_map/ppermute | solution.py:67
  69.5 58.3 %collective-permute-start.9 = (bf16[1024,256]{1,0:T(8,128)(2,1)}, bf16[1024,256]{1,0:T(8,128)(2,1)}, u32[]{:S(2)}, u32[]{:S(2)}) collective-permute-start(bf16[1024,256]{1,0:T(8,128)(2,1)} %slice.396), channel_id=1, source_target_pairs={{1,0},{9,1},{8,9},{0,8},{3,2},{11,3},{10,11},{2,10},{5,4},{13,5},{... | collective-permute-start | bytes 1572872 | tf_op jit(solution)/shard_map/ppermute | solution.py:68
  70.9 62.4 %collective-permute-start.14 = (bf16[2048,256]{1,0:T(8,128)(2,1)}, bf16[2048,256]{1,0:T(8,128)(2,1)}, u32[]{:S(2)}, u32[]{:S(2)}) collective-permute-start(bf16[2048,256]{1,0:T(8,128)(2,1)} %bitcast.4), channel_id=1, source_target_pairs={{2,0},{4,2},{6,4},{0,6},{3,1},{5,3},{7,5},{1,7},{10,8},{12,10},{14... | collective-permute-start | bytes 3145736 | tf_op jit(solution)/shard_map/ppermute | solution.py:65
  93.9 48.3 %collective-permute-start.13 = (bf16[1024,256]{1,0:T(8,128)(2,1)S(1)}, bf16[1024,256]{1,0:T(8,128)(2,1)S(1)}, u32[]{:S(2)}, u32[]{:S(2)}) collective-permute-start(bf16[1024,256]{1,0:T(8,128)(2,1)S(1)} %slice.423), channel_id=1, source_target_pairs={{0,2},{2,4},{4,6},{6,0},{1,3},{3,5},{5,7},{7,1},{8,10},{10,12},{12... | collective-permute-start | bytes 1572872 | tf_op jit(solution)/shard_map/ppermute | solution.py:67
  134.4 15.4 %collective-permute-start.15 = (bf16[1024,256]{1,0:T(8,128)(2,1)S(1)}, bf16[1024,256]{1,0:T(8,128)(2,1)S(1)}, u32[]{:S(2)}, u32[]{:S(2)}) collective-permute-start(bf16[1024,256]{1,0:T(8,128)(2,1)S(1)} %slice.424), channel_id=1, source_target_pairs={{2,0},{4,2},{6,4},{0,6},{3,1},{5,3},{7,5},{1,7},{10,8},{12,10},{14... | collective-permute-start | bytes 1572872 | tf_op jit(solution)/shard_map/ppermute | solution.py:68
  151.4 1.9 copy-start
  153.3 18.7 %collective-permute-start.16 = (f32[2048,256]{1,0:T(8,128)S(1)}, f32[2048,256]{1,0:T(8,128)}, u32[]{:S(2)}, u32[]{:S(2)}) collective-permute-start(f32[2048,256]{1,0:T(8,128)S(1)} %constant_dynamic-slice_fusion.5), channel_id=1, source_target_pairs={{0,16},{16,0},{1,17},{17,1},{2,18},{18,2},{3,19},{19,3},{4,20},{20... | collective-permute-start | bytes 6291464 | tf_op jit(solution)/shard_map/ppermute | solution.py:156
  175.4 16.0 %collective-permute-start.17 = (f32[512,256]{1,0:T(8,128)}, f32[512,256]{1,0:T(8,128)}, u32[]{:S(2)}, u32[]{:S(2)}) collective-permute-start(f32[512,256]{1,0:T(8,128)} %get-tuple-element.55), channel_id=1, source_target_pairs={{0,64},{64,128},{128,192},{192,0},{1,65},{65,129},{129,193},{193,1... | collective-permute-start | bytes 1572872 | tf_op jit(solution)/shard_map/ppermute | solution.py:163
  175.4 17.9 %collective-permute-start.18 = (f32[512,256]{1,0:T(8,128)S(1)}, f32[512,256]{1,0:T(8,128)}, u32[]{:S(2)}, u32[]{:S(2)}) collective-permute-start(f32[512,256]{1,0:T(8,128)S(1)} %get-tuple-element.57), channel_id=1, source_target_pairs={{0,128},{64,192},{128,0},{192,64},{1,129},{65,193},{129,1},{193,65... | collective-permute-start | bytes 1572872 | tf_op jit(solution)/shard_map/ppermute | solution.py:163
  180.4 23.5 %collective-permute-start.19 = (f32[512,256]{1,0:T(8,128)S(1)}, f32[512,256]{1,0:T(8,128)}, u32[]{:S(2)}, u32[]{:S(2)}) collective-permute-start(f32[512,256]{1,0:T(8,128)S(1)} %get-tuple-element.56), channel_id=1, source_target_pairs={{0,192},{64,0},{128,64},{192,128},{1,193},{65,1},{129,65},{193,129... | collective-permute-start | bytes 1572872 | tf_op jit(solution)/shard_map/ppermute | solution.py:163
  205.4 12.9 %collective-permute-start.20 = (f32[256,256]{1,0:T(8,128)S(1)}, f32[256,256]{1,0:T(8,128)S(1)}, u32[]{:S(2)}, u32[]{:S(2)}) collective-permute-start(f32[256,256]{1,0:T(8,128)S(1)} %get-tuple-element.61), channel_id=1, source_target_pairs={{0,0},{1,17},{2,34},{3,51},{4,68},{5,85},{6,102},{7,119},{8,136},{... | collective-permute-start | bytes 786440 | tf_op jit(solution)/shard_map/ppermute | solution.py:191
  211.0 12.9 %collective-permute-start.21 = (f32[256,256]{1,0:T(8,128)S(1)}, f32[256,256]{1,0:T(8,128)S(1)}, u32[]{:S(2)}, u32[]{:S(2)}) collective-permute-start(f32[256,256]{1,0:T(8,128)S(1)} %get-tuple-element.60), channel_id=1, source_target_pairs={{0,8},{1,16},{2,42},{3,50},{4,76},{5,84},{6,110},{7,118},{8,137},{... | collective-permute-start | bytes 786440 | tf_op jit(solution)/shard_map/ppermute | solution.py:191

commit v7 on v6

--- a/solution.py
+++ b/solution.py
@@ -157,10 +157,22 @@
     ring_x = lax.axis_size("sx")
     pos_x = lax.axis_index("sx")
     pair = 2 * panel_width
-    total = lax.dynamic_slice_in_dim(mine, pos_x * pair, pair, 0)
-    for d in range(1, ring_x):
-        sent = lax.dynamic_slice_in_dim(mine, ((pos_x + d) % ring_x) * pair, pair, 0)
-        total = total + lax.ppermute(sent, "sx", [(k, (k + d) % ring_x) for k in range(ring_x)])
+    def part(d):
+        return lax.dynamic_slice_in_dim(mine, ((pos_x + d) % ring_x) * pair, pair, 0)
+
+    up = [(k, (k + 1) % ring_x) for k in range(ring_x)]
+    down = [((k + 1) % ring_x, k) for k in range(ring_x)]
+    if ring_x == 4:
+        far = part(2)
+        got_up = lax.ppermute(jnp.concatenate([part(1), far[:panel_width]]), "sx", up)
+        got_down = lax.ppermute(jnp.concatenate([part(3), far[panel_width:]]), "sx", down)
+        relay_lo = lax.ppermute(got_up[pair:], "sx", up)
+        relay_hi = lax.ppermute(got_down[pair:], "sx", down)
+        total = part(0) + got_up[:pair] + got_down[:pair] + jnp.concatenate([relay_lo, relay_hi])
+    else:
+        total = part(0)
+        for d in range(1, ring_x):
+            total = total + lax.ppermute(part(d), "sx", [(k, (k + d) % ring_x) for k in range(ring_x)])
     high = lax.axis_index("syh")
     keep = lax.dynamic_slice_in_dim(total, high * panel_width, panel_width, 0)
     give = lax.dynamic_slice_in_dim(total, (1 - high) * panel_width, panel_width, 0)

time: 227 us -> 230 us (1.013)
    ppermute x3 -> x4, waiting for transfers between devices: 23.5 us -> 25.3 us  [the longest x1 17.9 us: shards(): lax.ppermute(jnp.concatenate([part(1), far[:panel_width]]), 'sx', up)]
    ppermute x3 -> x4, starting transfers between devices: 4.97 us -> 5.27 us  [the longest x1 3.01 us: shards(): lax.ppermute(jnp.concatenate([part(3), far[panel_width:]]), 'sx', down)]
  transfers between devices with their start and end apart: 22 -> 23, of which waited for: 16 -> 16; matrix products, arithmetic and copies ran while one was open for 13% -> 13% of each run, Pallas kernels for 0% -> 0%
where the time goes in v7:
time: 230 us; the launch traced here: 226 us
  waiting for transfers between devices  93.7 us (41%)
  starting transfers between devices  84.1 us (37%)
  other arithmetic  29.8 us (13%)
  matrix products  8.83 us (4%)
  local copies, waits for them, and re-layouts  7.55 us (3%)
    ppermute x2, starting transfers between devices, ring_gather(): far_lo = lax.ppermute(prev[:half], axes, fwd)  18.1 us
    ppermute x1, waiting for transfers between devices, shards(): lax.ppermute(jnp.concatenate([part(1), far[:panel_width]]), 'sx', up)  17.9 us
    ppermute x2, waiting for transfers between devices, ring_gather(): prev = lax.ppermute(block, axes, fwd)  17.8 us
    ppermute x2, waiting for transfers between devices, ring_gather(): far_lo = lax.ppermute(prev[:half], axes, fwd)  16.5 us
    ppermute x1, starting transfers between devices, shards(): mine = mine + lax.ppermute(other, 'sc', [(0, 1), (1, 0)])  14.7 us
    convert_element_type x1, other arithmetic, shards(): lagged = lagged_sum.astype(jnp.bfloat16)  12.2 us
    ppermute x2, starting transfers between devices, padded(): lax.ppermute(head, axis, [((i + 1) % count, i) for i in range(ends)])  12.1 us
    ppermute x4, waiting for transfers between devices, allreduce_sum(): lax.ppermute(vector, axes, [(i, i ^ step) for i in range(count)])  11 us
  transfers between devices with their start and end apart: 23, of which 16 were waited for; matrix products, arithmetic and copies ran while one was open for 13% of the time, Pallas kernels for 0%

profile of v7, /device:TPU:6, one launch (start us, length us, event | category | flops | bytes accessed | tf_op | source)
XLA Modules:
  0.0 225.6 jit_solution(3963149389573806437)
XLA Ops:
  0.0 1.5 fusion.75
  1.5 1.9 collective-permute-start
  3.5 6.0 %collective-permute-start.1 = (s32[2,512]{1,0:T(2,128)S(1)}, s32[2,512]{1,0:T(2,128)S(1)}, u32[]{:S(2)}, u32[]{:S(2)}) collective-permute-start(s32[2,512]{1,0:T(2,128)S(1)} %get-tuple-element.111), channel_id=1, source_target_pairs={{16,0},{32,16},{48,32},{64,48},{80,64},{96,80},{112,96},{128,112},... | collective-permute-start | bytes 12296 | tf_op jit(solution)/shard_map/ppermute | solution.py:33
  9.5 0.7 broadcast_compare_fusion
  10.2 1.8 select_reduce_fusion
  12.1 0.2 broadcast_select_fusion.19
  12.5 0.8 fusion.64
  13.3 1.4 pad_add_fusion.1
  14.7 1.2 collective-permute-start.2
  15.8 0.8 collective-permute-done.2
  16.7 1.4 fusion.69
  18.0 1.5 collective-permute-start.3
  19.5 3.6 %collective-permute-done.3 = s32[514]{0:T(1024)S(1)} collective-permute-done((s32[514]{0:T(1024)S(1)}, s32[514]{0:T(1024)S(1)}, u32[]{:S(2)}, u32[]{:S(2)}) %collective-permute-start.3) | collective-permute-done | bytes 2088 | tf_op jit(solution)/shard_map/ppermute | solution.py:44
  23.2 0.8 collective-permute-start.4
  24.0 2.8 %collective-permute-done.4 = s32[514]{0:T(1024)S(1)} collective-permute-done((s32[514]{0:T(1024)S(1)}, s32[514]{0:T(1024)S(1)}, u32[]{:S(2)}, u32[]{:S(2)}) %collective-permute-start.4) | collective-permute-done | bytes 2088 | tf_op jit(solution)/shard_map/ppermute | solution.py:44
  26.8 1.4 collective-permute-start.5
  28.2 3.7 %collective-permute-done.5 = s32[514]{0:T(1024)S(1)} collective-permute-done((s32[514]{0:T(1024)S(1)}, s32[514]{0:T(1024)S(1)}, u32[]{:S(2)}, u32[]{:S(2)}) %collective-permute-start.5) | collective-permute-done | bytes 2088 | tf_op jit(solution)/shard_map/ppermute | solution.py:44
  31.9 0.6 fusion.77
  33.2 0.7 convert_divide_fusion
  33.8 0.4 divide_convert_fusion
  34.3 1.9 collective-permute-start.10
  36.2 6.0 %collective-permute-start.11 = (bf16[2,512,256]{2,1,0:T(8,128)(2,1)S(1)}, bf16[2,512,256]{2,1,0:T(8,128)(2,1)S(1)}, u32[]{:S(2)}, u32[]{:S(2)}) collective-permute-start(bf16[2,512,256]{2,1,0:T(8,128)(2,1)S(1)} %get-tuple-element.60), channel_id=1, source_target_pairs={{16,0},{32,16},{48,32},{64,48},{80,64},{96,80},{112,96},{128,112},... | collective-permute-start | bytes 1572872 | tf_op jit(solution)/shard_map/ppermute | solution.py:33
  42.3 2.0 collective-permute-start.6
  44.4 2.9 %collective-permute-done.10 = bf16[2,512,256]{2,1,0:T(8,128)(2,1)S(1)} collective-permute-done((bf16[2,512,256]{2,1,0:T(8,128)(2,1)S(1)}, bf16[2,512,256]{2,1,0:T(8,128)(2,1)S(1)}, u32[]{:S(2)}, u32[]{:S(2)}) %collective-permute-start.10) | collective-permute-done | bytes 524320 | tf_op jit(solution)/shard_map/ppermute | solution.py:31
  47.3 1.7 collective-permute-done.11
  49.0 0.7 fusion.5
  49.7 12.2 %add_convert_fusion = bf16[4,512,256]{2,1,0:T(8,128)(2,1)} fusion(bf16[4,512,256]{2,1,0:T(8,128)(2,1)S(1)} %divide_convert_fusion, bf16[2,512,256]{2,1,0:T(8,128)(2,1)S(1)} %collective-permute-done.11, bf16[2,512,256]{2,1,0:T(8,128)(2,1)S(1)} %collective-permute-done.10, bf16[8,516,256]{2,1,0:T(8,128)(2,1)S(1)} %fusion.5, ...), kind=kLoop, calls=%fused_computation.11 | loop fusion | flops 39845888 | bytes 24313856 | tf_op jit(solution)/shard_map/convert_element_type | solution.py:141
  62.0 3.3 %collective-permute-start.12 = (bf16[2048,256]{1,0:T(8,128)(2,1)}, bf16[2048,256]{1,0:T(8,128)(2,1)}, u32[]{:S(2)}, u32[]{:S(2)}) collective-permute-start(bf16[2048,256]{1,0:T(8,128)(2,1)} %bitcast.4), channel_id=1, source_target_pairs={{0,2},{2,4},{4,6},{6,0},{1,3},{3,5},{5,7},{7,1},{8,10},{10,12},{12... | collective-permute-start | bytes 3145736 | tf_op jit(solution)/shard_map/ppermute | solution.py:64
  65.2 2.2 collective-permute-done.6
  67.4 0.8 slice.419
  68.3 0.7 collective-permute-start.7
  69.0 0.8 slice.420
  69.8 1.3 collective-permute-start.9
  71.1 6.3 %collective-permute-start.14 = (bf16[2048,256]{1,0:T(8,128)(2,1)}, bf16[2048,256]{1,0:T(8,128)(2,1)}, u32[]{:S(2)}, u32[]{:S(2)}) collective-permute-start(bf16[2048,256]{1,0:T(8,128)(2,1)} %bitcast.4), channel_id=1, source_target_pairs={{2,0},{4,2},{6,4},{0,6},{3,1},{5,3},{7,5},{1,7},{10,8},{12,10},{14... | collective-permute-start | bytes 3145736 | tf_op jit(solution)/shard_map/ppermute | solution.py:65
  77.4 15.6 %collective-permute-done.12 = bf16[2048,256]{1,0:T(8,128)(2,1)} collective-permute-done((bf16[2048,256]{1,0:T(8,128)(2,1)}, bf16[2048,256]{1,0:T(8,128)(2,1)}, u32[]{:S(2)}, u32[]{:S(2)}) %collective-permute-start.12) | collective-permute-done | bytes 1048608 | tf_op jit(solution)/shard_map/ppermute | solution.py:64
  93.1 1.1 slice.447
  94.2 17.4 %collective-permute-start.13 = (bf16[1024,256]{1,0:T(8,128)(2,1)S(1)}, bf16[1024,256]{1,0:T(8,128)(2,1)S(1)}, u32[]{:S(2)}, u32[]{:S(2)}) collective-permute-start(bf16[1024,256]{1,0:T(8,128)(2,1)S(1)} %slice.447), channel_id=1, source_target_pairs={{0,2},{2,4},{4,6},{6,0},{1,3},{3,5},{5,7},{7,1},{8,10},{10,12},{12... | collective-permute-start | bytes 1572872 | tf_op jit(solution)/shard_map/ppermute | solution.py:67
  111.6 16.5 %collective-permute-done.7 = bf16[1024,256]{1,0:T(8,128)(2,1)} collective-permute-done((bf16[1024,256]{1,0:T(8,128)(2,1)}, bf16[1024,256]{1,0:T(8,128)(2,1)}, u32[]{:S(2)}, u32[]{:S(2)}) %collective-permute-start.7) | collective-permute-done | bytes 524320 | tf_op jit(solution)/shard_map/ppermute | solution.py:67
  128.1 2.9 %pad_maximum_fusion = bf16[2048,1024]{1,0:T(8,128)(2,1)S(1)} fusion(bf16[2048,256]{1,0:T(8,128)(2,1)S(1)} %collective-permute-done.8, bf16[1024,256]{1,0:T(8,128)(2,1)} %collective-permute-done.9, bf16[1024,256]{1,0:T(8,128)(2,1)} %collective-permute-done.7, bf16[2048,256]{1,0:T(8,128)(2,1)S(1)} %collective-permute-done.6, bf16[2048,256]{1,0:T(8,128)(2,1)S(1)} %bitcast.15), kind=kLoop, calls=%fused_computation.3 | loop fusion | flops 20971520 | bytes 8388608 | tf_op jit(solution)/shard_map/concatenate | solution.py:147
  131.0 2.5 %fusion.78 = f32[1024,256]{1,0:T(8,128)S(1)} fusion(bf16[2048,1024]{1,0:T(8,128)(2,1)S(1)} %pad_maximum_fusion, bf16[2048,256]{1,0:T(8,128)(2,1)} %bitcast.4), kind=kOutput, calls=%fused_computation.187 | convolution fusion | flops 1073741824 | bytes 6291456 | tf_op jit(solution)/shard_map/dot_general | solution.py:149
  133.6 1.1 slice.448
  134.6 2.8 %collective-permute-start.15 = (bf16[1024,256]{1,0:T(8,128)(2,1)S(1)}, bf16[1024,256]{1,0:T(8,128)(2,1)S(1)}, u32[]{:S(2)}, u32[]{:S(2)}) collective-permute-start(bf16[1024,256]{1,0:T(8,128)(2,1)S(1)} %slice.448), channel_id=1, source_target_pairs={{2,0},{4,2},{6,4},{0,6},{3,1},{5,3},{7,5},{1,7},{10,8},{12,10},{14... | collective-permute-start | bytes 1572872 | tf_op jit(solution)/shard_map/ppermute | solution.py:68
  137.4 2.5 %fusion.79 = f32[1024,256]{1,0:T(8,128)S(1)} fusion(bf16[2048,1024]{1,0:T(8,128)(2,1)S(1)} %pad_maximum_fusion, bf16[2048,256]{1,0:T(8,128)(2,1)} %collective-permute-done.12), kind=kOutput, calls=%fused_computation.188 | convolution fusion | flops 1073741824 | bytes 6291456 | tf_op jit(solution)/shard_map/dot_general | solution.py:149
  139.9 2.5 %fusion.80 = f32[1024,256]{1,0:T(8,128)S(1)} fusion(bf16[2048,1024]{1,0:T(8,128)(2,1)S(1)} %pad_maximum_fusion, bf16[2048,256]{1,0:T(8,128)(2,1)} %collective-permute-done.14), kind=kOutput, calls=%fused_computation.189 | convolution fusion | flops 1073741824 | bytes 6291456 | tf_op jit(solution)/shard_map/dot_general | solution.py:149
  142.5 7.6 %collective-permute-done.15 = bf16[1024,256]{1,0:T(8,128)(2,1)S(1)} collective-permute-done((bf16[1024,256]{1,0:T(8,128)(2,1)S(1)}, bf16[1024,256]{1,0:T(8,128)(2,1)S(1)}, u32[]{:S(2)}, u32[]{:S(2)}) %collective-permute-start.15) | collective-permute-done | bytes 524320 | tf_op jit(solution)/shard_map/ppermute | solution.py:68
  150.1 1.3 fusion.8
  151.4 0.3 pad_maximum_fusion.1
  151.8 1.8 copy-done
  153.6 14.7 %collective-permute-start.16 = (f32[2048,256]{1,0:T(8,128)S(1)}, f32[2048,256]{1,0:T(8,128)}, u32[]{:S(2)}, u32[]{:S(2)}) collective-permute-start(f32[2048,256]{1,0:T(8,128)S(1)} %constant_dynamic-slice_fusion.5), channel_id=1, source_target_pairs={{0,16},{16,0},{1,17},{17,1},{2,18},{18,2},{3,19},{19,3},{4,20},{20... | collective-permute-start | bytes 6291464 | tf_op jit(solution)/shard_map/ppermute | solution.py:156
  168.3 3.9 %collective-permute-done.16 = f32[2048,256]{1,0:T(8,128)} collective-permute-done((f32[2048,256]{1,0:T(8,128)S(1)}, f32[2048,256]{1,0:T(8,128)}, u32[]{:S(2)}, u32[]{:S(2)}) %collective-permute-start.16) | collective-permute-done | bytes 2097184 | tf_op jit(solution)/shard_map/ppermute | solution.py:156
  172.3 2.5 %dynamic-slice_add_fusion = f32[2048,256]{1,0:T(8,128)S(1)} fusion(f32[2048,256]{1,0:T(8,128)} %collective-permute-done.16, f32[4096,256]{1,0:T(8,128)} %copy-done, s32[]{:T(128)S(6)} %select_n.158), kind=kLoop, calls=%fused_computation.10 | loop fusion | flops 524288 | bytes 6291460 | tf_op jit(solution)/shard_map/add | solution.py:156
  175.1 3.0 %collective-permute-start.18 = (f32[768,256]{1,0:T(8,128)S(1)}, f32[768,256]{1,0:T(8,128)S(1)}, u32[]{:S(2)}, u32[]{:S(2)}) collective-permute-start(f32[768,256]{1,0:T(8,128)S(1)} %pad_maximum_fusion.5), channel_id=1, source_target_pairs={{64,0},{128,64},{192,128},{0,192},{65,1},{129,65},{193,129},{1,193... | collective-permute-start | bytes 2359304 | tf_op jit(solution)/shard_map/ppermute | solution.py:168
  178.1 17.9 %collective-permute-done.17 = f32[768,256]{1,0:T(8,128)S(1)} collective-permute-done((f32[768,256]{1,0:T(8,128)S(1)}, f32[768,256]{1,0:T(8,128)S(1)}, u32[]{:S(2)}, u32[]{:S(2)}) %collective-permute-start.17) | collective-permute-done | bytes 786464 | tf_op jit(solution)/shard_map/ppermute | solution.py:167
  196.1 0.4 collective-permute-start.19
  196.4 0.9 copy-done.2
  197.4 1.8 collective-permute-start.20
  199.2 5.1 %collective-permute-done.19 = f32[256,256]{1,0:T(8,128)} collective-permute-done((f32[256,256]{1,0:T(8,128)S(1)}, f32[256,256]{1,0:T(8,128)}, u32[]{:S(2)}, u32[]{:S(2)}) %collective-permute-start.19) | collective-permute-done | bytes 262176 | tf_op jit(solution)/shard_map/ppermute | solution.py:169
  204.2 2.2 collective-permute-done.20
  206.5 1.3 fusion.12
  207.9 4.0 %collective-permute-start.21 = (f32[256,256]{1,0:T(8,128)S(1)}, f32[256,256]{1,0:T(8,128)S(1)}, u32[]{:S(2)}, u32[]{:S(2)}) collective-permute-start(f32[256,256]{1,0:T(8,128)S(1)} %get-tuple-element.62), channel_id=1, source_target_pairs={{0,0},{1,17},{2,34},{3,51},{4,68},{5,85},{6,102},{7,119},{8,136},{... | collective-permute-start | bytes 786440 | tf_op jit(solution)/shard_map/ppermute | solution.py:203
  211.9 5.4 %collective-permute-start.22 = (f32[256,256]{1,0:T(8,128)S(1)}, f32[256,256]{1,0:T(8,128)S(1)}, u32[]{:S(2)}, u32[]{:S(2)}) collective-permute-start(f32[256,256]{1,0:T(8,128)S(1)} %get-tuple-element.61), channel_id=1, source_target_pairs={{0,8},{1,16},{2,42},{3,50},{4,76},{5,84},{6,110},{7,118},{8,137},{... | collective-permute-start | bytes 786440 | tf_op jit(solution)/shard_map/ppermute | solution.py:203
  218.0 2.8 %collective-permute-done.21 = f32[256,256]{1,0:T(8,128)S(1)} collective-permute-done((f32[256,256]{1,0:T(8,128)S(1)}, f32[256,256]{1,0:T(8,128)S(1)}, u32[]{:S(2)}, u32[]{:S(2)}) %collective-permute-start.21) | collective-permute-done | bytes 262176 | tf_op jit(solution)/shard_map/ppermute | solution.py:203
  220.8 4.1 %collective-permute-done.22 = f32[256,256]{1,0:T(8,128)S(1)} collective-permute-done((f32[256,256]{1,0:T(8,128)S(1)}, f32[256,256]{1,0:T(8,128)S(1)}, u32[]{:S(2)}, u32[]{:S(2)}) %collective-permute-start.22) | collective-permute-done | bytes 262176 | tf_op jit(solution)/shard_map/ppermute | solution.py:203
  224.9 0.7 add_divide_fusion
  (34 shorter events, 1.0 us)
Async XLA Ops:
  0.0 12.5 %copy-start.4 = (s32[4,512]{1,0:T(4,128)S(1)}, s32[4,512]{1,0:T(4,128)}, u32[]{:S(2)}) copy-start(s32[4,512]{1,0:T(4,128)} %param.4) | copy-start | bytes 24580
  0.0 12.1 %copy-start.3 = (s32[4,512]{1,0:T(4,128)S(1)}, s32[4,512]{1,0:T(4,128)}, u32[]{:S(2)}) copy-start(s32[4,512]{1,0:T(4,128)} %param.5) | copy-start | bytes 24580
  0.0 33.8 %copy-start.1 = (s32[4,512,256]{2,1,0:T(8,128)S(1)}, s32[4,512,256]{2,1,0:T(8,128)}, u32[]{:S(2)}) copy-start(s32[4,512,256]{2,1,0:T(8,128)} %param.3) | copy-start | bytes 6291460
  1.5 10.5 %collective-permute-start = (s32[2,512]{1,0:T(2,128)S(1)}, s32[2,512]{1,0:T(2,128)S(1)}, u32[]{:S(2)}, u32[]{:S(2)}) collective-permute-start(s32[2,512]{1,0:T(2,128)S(1)} %get-tuple-element.110), channel_id=1, source_target_pairs={{0,16},{16,32},{32,48},{48,64},{64,80},{80,96},{96,112},{112,128},... | collective-permute-start | bytes 12296 | tf_op jit(solution)/shard_map/ppermute | solution.py:31
  3.5 8.6 %collective-permute-start.1 = (s32[2,512]{1,0:T(2,128)S(1)}, s32[2,512]{1,0:T(2,128)S(1)}, u32[]{:S(2)}, u32[]{:S(2)}) collective-permute-start(s32[2,512]{1,0:T(2,128)S(1)} %get-tuple-element.111), channel_id=1, source_target_pairs={{16,0},{32,16},{48,32},{64,48},{80,64},{96,80},{112,96},{128,112},... | collective-permute-start | bytes 12296 | tf_op jit(solution)/shard_map/ppermute | solution.py:33
  14.7 2.0 collective-permute-start.2
  18.0 5.1 %collective-permute-start.3 = (s32[514]{0:T(1024)S(1)}, s32[514]{0:T(1024)S(1)}, u32[]{:S(2)}, u32[]{:S(2)}) collective-permute-start(s32[514]{0:T(1024)S(1)} %fusion.69), channel_id=1, source_target_pairs={{0,32},{16,48},{32,0},{48,16},{64,96},{80,112},{96,64},{112,80},{1... | collective-permute-start | bytes 6176 | tf_op jit(solution)/shard_map/ppermute | solution.py:44
  23.2 3.6 %collective-permute-start.4 = (s32[514]{0:T(1024)S(1)}, s32[514]{0:T(1024)S(1)}, u32[]{:S(2)}, u32[]{:S(2)}) collective-permute-start(s32[514]{0:T(1024)S(1)} %add.269), channel_id=1, source_target_pairs={{0,64},{16,80},{32,96},{48,112},{64,0},{80,16},{96,32},{112,48},{1... | collective-permute-start | bytes 6176 | tf_op jit(solution)/shard_map/ppermute | solution.py:44
  26.8 5.1 %collective-permute-start.5 = (s32[514]{0:T(1024)S(1)}, s32[514]{0:T(1024)S(1)}, u32[]{:S(2)}, u32[]{:S(2)}) collective-permute-start(s32[514]{0:T(1024)S(1)} %add.270), channel_id=1, source_target_pairs={{0,128},{16,144},{32,160},{48,176},{64,192},{80,208},{96,224},{112... | collective-permute-start | bytes 6176 | tf_op jit(solution)/shard_map/ppermute | solution.py:44
  34.3 13.0 %collective-permute-start.10 = (bf16[2,512,256]{2,1,0:T(8,128)(2,1)S(1)}, bf16[2,512,256]{2,1,0:T(8,128)(2,1)S(1)}, u32[]{:S(2)}, u32[]{:S(2)}) collective-permute-start(bf16[2,512,256]{2,1,0:T(8,128)(2,1)S(1)} %get-tuple-element.59), channel_id=1, source_target_pairs={{0,16},{16,32},{32,48},{48,64},{64,80},{80,96},{96,112},{112,128},... | collective-permute-start | bytes 1572872 | tf_op jit(solution)/shard_map/ppermute | solution.py:31
  36.2 12.8 %collective-permute-start.11 = (bf16[2,512,256]{2,1,0:T(8,128)(2,1)S(1)}, bf16[2,512,256]{2,1,0:T(8,128)(2,1)S(1)}, u32[]{:S(2)}, u32[]{:S(2)}) collective-permute-start(bf16[2,512,256]{2,1,0:T(8,128)(2,1)S(1)} %get-tuple-element.60), channel_id=1, source_target_pairs={{16,0},{32,16},{48,32},{64,48},{80,64},{96,80},{112,96},{128,112},... | collective-permute-start | bytes 1572872 | tf_op jit(solution)/shard_map/ppermute | solution.py:33
  42.3 25.2 %collective-permute-start.6 = (bf16[2048,256]{1,0:T(8,128)(2,1)S(1)}, bf16[2048,256]{1,0:T(8,128)(2,1)S(1)}, u32[]{:S(2)}, u32[]{:S(2)}) collective-permute-start(bf16[2048,256]{1,0:T(8,128)(2,1)S(1)} %bitcast.13), channel_id=1, source_target_pairs={{0,1},{1,9},{9,8},{8,0},{2,3},{3,11},{11,10},{10,2},{4,5},{5,13},{... | collective-permute-start | bytes 3145736 | tf_op jit(solution)/shard_map/ppermute | solution.py:64
  44.3 24.7 %collective-permute-start.8 = (bf16[2048,256]{1,0:T(8,128)(2,1)S(1)}, bf16[2048,256]{1,0:T(8,128)(2,1)S(1)}, u32[]{:S(2)}, u32[]{:S(2)}) collective-permute-start(bf16[2048,256]{1,0:T(8,128)(2,1)S(1)} %bitcast.14), channel_id=1, source_target_pairs={{1,0},{9,1},{8,9},{0,8},{3,2},{11,3},{10,11},{2,10},{5,4},{13,5},{... | collective-permute-start | bytes 3145736 | tf_op jit(solution)/shard_map/ppermute | solution.py:65
  62.0 31.1 %collective-permute-start.12 = (bf16[2048,256]{1,0:T(8,128)(2,1)}, bf16[2048,256]{1,0:T(8,128)(2,1)}, u32[]{:S(2)}, u32[]{:S(2)}) collective-permute-start(bf16[2048,256]{1,0:T(8,128)(2,1)} %bitcast.4), channel_id=1, source_target_pairs={{0,2},{2,4},{4,6},{6,0},{1,3},{3,5},{5,7},{7,1},{8,10},{10,12},{12... | collective-permute-start | bytes 3145736 | tf_op jit(solution)/shard_map/ppermute | solution.py:64
  68.3 59.8 %collective-permute-start.7 = (bf16[1024,256]{1,0:T(8,128)(2,1)}, bf16[1024,256]{1,0:T(8,128)(2,1)}, u32[]{:S(2)}, u32[]{:S(2)}) collective-permute-start(bf16[1024,256]{1,0:T(8,128)(2,1)} %slice.419), channel_id=1, source_target_pairs={{0,1},{1,9},{9,8},{8,0},{2,3},{3,11},{11,10},{10,2},{4,5},{5,13},{... | collective-permute-start | bytes 1572872 | tf_op jit(solution)/shard_map/ppermute | solution.py:67
  69.8 58.3 %collective-permute-start.9 = (bf16[1024,256]{1,0:T(8,128)(2,1)}, bf16[1024,256]{1,0:T(8,128)(2,1)}, u32[]{:S(2)}, u32[]{:S(2)}) collective-permute-start(bf16[1024,256]{1,0:T(8,128)(2,1)} %slice.420), channel_id=1, source_target_pairs={{1,0},{9,1},{8,9},{0,8},{3,2},{11,3},{10,11},{2,10},{5,4},{13,5},{... | collective-permute-start | bytes 1572872 | tf_op jit(solution)/shard_map/ppermute | solution.py:68
  71.1 62.4 %collective-permute-start.14 = (bf16[2048,256]{1,0:T(8,128)(2,1)}, bf16[2048,256]{1,0:T(8,128)(2,1)}, u32[]{:S(2)}, u32[]{:S(2)}) collective-permute-start(bf16[2048,256]{1,0:T(8,128)(2,1)} %bitcast.4), channel_id=1, source_target_pairs={{2,0},{4,2},{6,4},{0,6},{3,1},{5,3},{7,5},{1,7},{10,8},{12,10},{14... | collective-permute-start | bytes 3145736 | tf_op jit(solution)/shard_map/ppermute | solution.py:65
  94.2 48.3 %collective-permute-start.13 = (bf16[1024,256]{1,0:T(8,128)(2,1)S(1)}, bf16[1024,256]{1,0:T(8,128)(2,1)S(1)}, u32[]{:S(2)}, u32[]{:S(2)}) collective-permute-start(bf16[1024,256]{1,0:T(8,128)(2,1)S(1)} %slice.447), channel_id=1, source_target_pairs={{0,2},{2,4},{4,6},{6,0},{1,3},{3,5},{5,7},{7,1},{8,10},{10,12},{12... | collective-permute-start | bytes 1572872 | tf_op jit(solution)/shard_map/ppermute | solution.py:67
  134.6 15.4 %collective-permute-start.15 = (bf16[1024,256]{1,0:T(8,128)(2,1)S(1)}, bf16[1024,256]{1,0:T(8,128)(2,1)S(1)}, u32[]{:S(2)}, u32[]{:S(2)}) collective-permute-start(bf16[1024,256]{1,0:T(8,128)(2,1)S(1)} %slice.448), channel_id=1, source_target_pairs={{2,0},{4,2},{6,4},{0,6},{3,1},{5,3},{7,5},{1,7},{10,8},{12,10},{14... | collective-permute-start | bytes 1572872 | tf_op jit(solution)/shard_map/ppermute | solution.py:68
  151.6 2.0 copy-start
  153.6 18.7 %collective-permute-start.16 = (f32[2048,256]{1,0:T(8,128)S(1)}, f32[2048,256]{1,0:T(8,128)}, u32[]{:S(2)}, u32[]{:S(2)}) collective-permute-start(f32[2048,256]{1,0:T(8,128)S(1)} %constant_dynamic-slice_fusion.5), channel_id=1, source_target_pairs={{0,16},{16,0},{1,17},{17,1},{2,18},{18,2},{3,19},{19,3},{4,20},{20... | collective-permute-start | bytes 6291464 | tf_op jit(solution)/shard_map/ppermute | solution.py:156
  174.9 21.1 %collective-permute-start.17 = (f32[768,256]{1,0:T(8,128)S(1)}, f32[768,256]{1,0:T(8,128)S(1)}, u32[]{:S(2)}, u32[]{:S(2)}) collective-permute-start(f32[768,256]{1,0:T(8,128)S(1)} %pad_maximum_fusion.4), channel_id=1, source_target_pairs={{0,64},{64,128},{128,192},{192,0},{1,65},{65,129},{129,193},{193,1... | collective-permute-start | bytes 2359304 | tf_op jit(solution)/shard_map/ppermute | solution.py:167
  175.1 21.3 %collective-permute-start.18 = (f32[768,256]{1,0:T(8,128)S(1)}, f32[768,256]{1,0:T(8,128)S(1)}, u32[]{:S(2)}, u32[]{:S(2)}) collective-permute-start(f32[768,256]{1,0:T(8,128)S(1)} %pad_maximum_fusion.5), channel_id=1, source_target_pairs={{64,0},{128,64},{192,128},{0,192},{65,1},{129,65},{193,129},{1,193... | collective-permute-start | bytes 2359304 | tf_op jit(solution)/shard_map/ppermute | solution.py:168
  196.1 8.2 %collective-permute-start.19 = (f32[256,256]{1,0:T(8,128)S(1)}, f32[256,256]{1,0:T(8,128)}, u32[]{:S(2)}, u32[]{:S(2)}) collective-permute-start(f32[256,256]{1,0:T(8,128)S(1)} %slice.451), channel_id=1, source_target_pairs={{0,64},{64,128},{128,192},{192,0},{1,65},{65,129},{129,193},{193,1... | collective-permute-start | bytes 786440 | tf_op jit(solution)/shard_map/ppermute | solution.py:169
  196.4 0.9 copy-start.2
  197.4 9.1 %collective-permute-start.20 = (f32[256,256]{1,0:T(8,128)S(1)}, f32[256,256]{1,0:T(8,128)}, u32[]{:S(2)}, u32[]{:S(2)}) collective-permute-start(f32[256,256]{1,0:T(8,128)S(1)} %slice.452), channel_id=1, source_target_pairs={{64,0},{128,64},{192,128},{0,192},{65,1},{129,65},{193,129},{1,193... | collective-permute-start | bytes 786440 | tf_op jit(solution)/shard_map/ppermute | solution.py:170
  207.9 12.9 %collective-permute-start.21 = (f32[256,256]{1,0:T(8,128)S(1)}, f32[256,256]{1,0:T(8,128)S(1)}, u32[]{:S(2)}, u32[]{:S(2)}) collective-permute-start(f32[256,256]{1,0:T(8,128)S(1)} %get-tuple-element.62), channel_id=1, source_target_pairs={{0,0},{1,17},{2,34},{3,51},{4,68},{5,85},{6,102},{7,119},{8,136},{... | collective-permute-start | bytes 786440 | tf_op jit(solution)/shard_map/ppermute | solution.py:203
  211.9 13.0 %collective-permute-start.22 = (f32[256,256]{1,0:T(8,128)S(1)}, f32[256,256]{1,0:T(8,128)S(1)}, u32[]{:S(2)}, u32[]{:S(2)}) collective-permute-start(f32[256,256]{1,0:T(8,128)S(1)} %get-tuple-element.61), channel_id=1, source_target_pairs={{0,8},{1,16},{2,42},{3,50},{4,76},{5,84},{6,110},{7,118},{8,137},{... | collective-permute-start | bytes 786440 | tf_op jit(solution)/shard_map/ppermute | solution.py:203

commit v8 on v6

--- a/solution.py
+++ b/solution.py
@@ -145,25 +145,6 @@
     z_parts = ring_gather(flat_z, ROW_AXES, ROW_RING)
     lag_parts = ring_gather(flat_lag, COL_AXES, COL_RING)
     z_cat = jnp.concatenate(z_parts, axis=1)
-    block = jnp.concatenate(
-        [lax.dot_general(z_cat, part, contract_bins, preferred_element_type=jnp.float32) for part in lag_parts],
-        axis=0,
-    )
-    half = side * side // 2
-    core = lax.axis_index("sc")
-    mine = lax.dynamic_slice_in_dim(block, core * half * panel_width, half * panel_width, 0)
-    other = lax.dynamic_slice_in_dim(block, (1 - core) * half * panel_width, half * panel_width, 0)
-    mine = mine + lax.ppermute(other, "sc", [(0, 1), (1, 0)])
-    ring_x = lax.axis_size("sx")
-    pos_x = lax.axis_index("sx")
-    pair = 2 * panel_width
-    total = lax.dynamic_slice_in_dim(mine, pos_x * pair, pair, 0)
-    for d in range(1, ring_x):
-        sent = lax.dynamic_slice_in_dim(mine, ((pos_x + d) % ring_x) * pair, pair, 0)
-        total = total + lax.ppermute(sent, "sx", [(k, (k + d) % ring_x) for k in range(ring_x)])
-    high = lax.axis_index("syh")
-    keep = lax.dynamic_slice_in_dim(total, high * panel_width, panel_width, 0)
-    give = lax.dynamic_slice_in_dim(total, (1 - high) * panel_width, panel_width, 0)
     sizes = {a: lax.axis_size(a) for a in GENE_AXES}
     rings = {ROW_AXES: ROW_RING, COL_AXES: COL_RING}
 
@@ -174,21 +155,34 @@
         out.update(zip(axes, unravel(ring[(pos - back) % len(ring)], [sizes[a] for a in axes])))
         return ravel([out[a] for a in GENE_AXES], [sizes[a] for a in GENE_AXES])
 
-    def home(sigma, c):
-        q = half * (sigma % 2) + sigma // 2
-        t2, t1 = divmod(q, side)
+    def home(t1, t2, c):
         coord = dict(zip(GENE_AXES, unravel(c, [sizes[a] for a in GENE_AXES])))
-        g = member(coord, ROW_AXES, t1)
-        s = member(coord, COL_AXES, t2)
-        return s * gene_n + g
-
-    keep_perm, give_perm = [], []
-    for sigma in range(spot_n):
-        for c in range(gene_n):
-            keep_perm.append((sigma * gene_n + c, home(sigma, c)))
-            give_perm.append((sigma * gene_n + c, home(sigma ^ 2, c)))
+        return member(coord, COL_AXES, t2) * gene_n + member(coord, ROW_AXES, t1)
+
+    core = lax.axis_index("sc")
+    ring_x = lax.axis_size("sx")
+    pos_x = lax.axis_index("sx")
     every = SPOT_AXES + GENE_AXES
-    share = lax.ppermute(keep, every, keep_perm) + lax.ppermute(give, every, give_perm)
+    received = []
+    for phase in range(2):
+        keep_lag = jnp.where(core == 0, lag_parts[2 * phase], lag_parts[2 * phase + 1])
+        give_lag = jnp.where(core == 0, lag_parts[2 * phase + 1], lag_parts[2 * phase])
+        keep = lax.dot_general(z_cat, keep_lag, contract_bins, preferred_element_type=jnp.float32)
+        give = lax.dot_general(z_cat, give_lag, contract_bins, preferred_element_type=jnp.float32)
+        mine = keep + lax.ppermute(give, "sc", [(0, 1), (1, 0)])
+        total = lax.dynamic_slice_in_dim(mine, pos_x * panel_width, panel_width, 0)
+        for d in range(1, ring_x):
+            sent = lax.dynamic_slice_in_dim(mine, ((pos_x + d) % ring_x) * panel_width, panel_width, 0)
+            total = total + lax.ppermute(sent, "sx", [(k, (k + d) % ring_x) for k in range(ring_x)])
+        for high in range(2):
+            perm = []
+            for sx in range(ring_x):
+                for sc in range(2):
+                    sigma = (sx * 2 + high) * 2 + sc
+                    for c in range(gene_n):
+                        perm.append((sigma * gene_n + c, home(sx, sc + 2 * phase, c)))
+            received.append(lax.ppermute(total, every, perm))
+    share = received[0] + received[1] + received[2] + received[3]
     return share / jnp.sqrt(pair_norm)
 
 

time: 227 us -> 214 us (0.943)
  waiting for transfers between devices: 92.3 us -> 81.6 us
  matrix products: 8.83 us -> 18.9 us
  other arithmetic: 29.7 us -> 23.7 us
  local copies, waits for them, and re-layouts: 7.41 us -> 4.59 us
  starting transfers between devices: 84.8 us -> 82.4 us
    ppermute x2, waiting for transfers between devices: 17.8 us -> 40.1 us  [ring_gather(): prev = lax.ppermute(block, axes, fwd)]
    ppermute x3 -> x6, waiting for transfers between devices: 23.5 us -> 10.9 us  [shards(): lax.ppermute(sent, 'sx', [(k, (k + d) % ring_x) for k in range(ring_x)])]
    dot_general x4, matrix products: 8.83 us -> 18.9 us  [the longest x2 10.7 us: shards(): lax.dot_general(z_cat, give_lag, contract_bins, preferred_element_type=jn...]
    ppermute x2, waiting for transfers between devices: 16.5 us -> 7.35 us  [ring_gather(): far_lo = lax.ppermute(prev[:half], axes, fwd)]
    ppermute x2, waiting for transfers between devices: 7.62 us -> 0.01 us  [ring_gather(): far_hi = lax.ppermute(nxt[half:], axes, bwd)]
    ppermute x2, starting transfers between devices: 18.1 us -> 13.5 us  [ring_gather(): far_lo = lax.ppermute(prev[:half], axes, fwd)]
    ppermute x3 -> x6, starting transfers between devices: 4.97 us -> 9.18 us  [shards(): lax.ppermute(sent, 'sx', [(k, (k + d) % ring_x) for k in range(ring_x)])]
    ppermute x3 -> x6, starting transfers between devices: 25.2 us -> 28.9 us  [the longest x4 18.6 us: shards(): received.append(lax.ppermute(total, every, perm))]
  transfers between devices with their start and end apart: 22 -> 28, of which waited for: 16 -> 15; matrix products, arithmetic and copies ran while one was open for 13% -> 18% of each run, Pallas kernels for 0% -> 0%
where the time goes in v8:
time: 214 us; the launch traced here: 213 us
  starting transfers between devices  82.4 us (39%)
  waiting for transfers between devices  81.6 us (38%)
  other arithmetic  23.7 us (11%)
  matrix products  18.9 us (9%)
  local copies, waits for them, and re-layouts  4.59 us (2%)
    ppermute x2, waiting for transfers between devices, ring_gather(): prev = lax.ppermute(block, axes, fwd)  40.1 us
    ppermute x4, starting transfers between devices, shards(): received.append(lax.ppermute(total, every, perm))  18.6 us
    ppermute x2, starting transfers between devices, ring_gather(): far_lo = lax.ppermute(prev[:half], axes, fwd)  13.5 us
    ppermute x2, starting transfers between devices, padded(): lax.ppermute(head, axis, [((i + 1) % count, i) for i in range(ends)])  12.1 us
    convert_element_type x1, other arithmetic, shards(): lagged = lagged_sum.astype(jnp.bfloat16)  11.1 us
    ppermute x4, waiting for transfers between devices, allreduce_sum(): lax.ppermute(vector, axes, [(i, i ^ step) for i in range(count)])  11 us
    ppermute x6, waiting for transfers between devices, shards(): lax.ppermute(sent, 'sx', [(k, (k + d) % ring_x) for k in range(ring_x)])  10.9 us
    dot_general x2, matrix products, shards(): lax.dot_general(z_cat, give_lag, contract_bins, preferred_element_type=jn...  10.7 us
  transfers between devices with their start and end apart: 28, of which 15 were waited for; matrix products, arithmetic and copies ran while one was open for 18% of the time, Pallas kernels for 0%

profile of v8, /device:TPU:6, one launch (start us, length us, event | category | flops | bytes accessed | tf_op | source)
XLA Modules:
  0.0 212.8 jit_solution(10894270418427902450)
XLA Ops:
  0.0 1.5 fusion.79
  1.5 1.9 collective-permute-start
  3.5 6.0 %collective-permute-start.1 = (s32[2,512]{1,0:T(2,128)S(1)}, s32[2,512]{1,0:T(2,128)S(1)}, u32[]{:S(2)}, u32[]{:S(2)}) collective-permute-start(s32[2,512]{1,0:T(2,128)S(1)} %get-tuple-element.111), channel_id=1, source_target_pairs={{16,0},{32,16},{48,32},{64,48},{80,64},{96,80},{112,96},{128,112},... | collective-permute-start | bytes 12296 | tf_op jit(solution)/shard_map/ppermute | solution.py:33
  9.5 0.7 broadcast_compare_fusion
  10.2 1.8 select_reduce_fusion
  12.0 0.1 add_select_fusion
  12.1 0.2 broadcast_select_fusion.19
  12.5 0.8 fusion.69
  13.3 1.3 pad_add_fusion.1
  14.6 1.2 collective-permute-start.2
  15.8 0.8 collective-permute-done.2
  16.6 1.3 fusion.73
  18.0 1.5 collective-permute-start.3
  19.5 3.6 %collective-permute-done.3 = s32[514]{0:T(1024)S(1)} collective-permute-done((s32[514]{0:T(1024)S(1)}, s32[514]{0:T(1024)S(1)}, u32[]{:S(2)}, u32[]{:S(2)}) %collective-permute-start.3) | collective-permute-done | bytes 2088 | tf_op jit(solution)/shard_map/ppermute | solution.py:44
  23.1 0.8 collective-permute-start.4
  24.0 2.8 %collective-permute-done.4 = s32[514]{0:T(1024)S(1)} collective-permute-done((s32[514]{0:T(1024)S(1)}, s32[514]{0:T(1024)S(1)}, u32[]{:S(2)}, u32[]{:S(2)}) %collective-permute-start.4) | collective-permute-done | bytes 2088 | tf_op jit(solution)/shard_map/ppermute | solution.py:44
  26.8 1.4 collective-permute-start.5
  28.1 3.7 %collective-permute-done.5 = s32[514]{0:T(1024)S(1)} collective-permute-done((s32[514]{0:T(1024)S(1)}, s32[514]{0:T(1024)S(1)}, u32[]{:S(2)}, u32[]{:S(2)}) %collective-permute-start.5) | collective-permute-done | bytes 2088 | tf_op jit(solution)/shard_map/ppermute | solution.py:44
  31.9 0.6 fusion.81
  33.1 0.7 convert_divide_fusion
  33.8 0.4 divide_convert_fusion
  34.2 1.9 collective-permute-start.10
  36.2 6.0 %collective-permute-start.11 = (bf16[2,512,256]{2,1,0:T(8,128)(2,1)S(1)}, bf16[2,512,256]{2,1,0:T(8,128)(2,1)S(1)}, u32[]{:S(2)}, u32[]{:S(2)}) collective-permute-start(bf16[2,512,256]{2,1,0:T(8,128)(2,1)S(1)} %get-tuple-element.62), channel_id=1, source_target_pairs={{16,0},{32,16},{48,32},{64,48},{80,64},{96,80},{112,96},{128,112},... | collective-permute-start | bytes 1572872 | tf_op jit(solution)/shard_map/ppermute | solution.py:33
  42.2 2.0 collective-permute-start.6
  44.2 0.1 collective-permute-start.8
  44.3 2.9 %collective-permute-done.10 = bf16[2,512,256]{2,1,0:T(8,128)(2,1)S(1)} collective-permute-done((bf16[2,512,256]{2,1,0:T(8,128)(2,1)S(1)}, bf16[2,512,256]{2,1,0:T(8,128)(2,1)S(1)}, u32[]{:S(2)}, u32[]{:S(2)}) %collective-permute-start.10) | collective-permute-done | bytes 524320 | tf_op jit(solution)/shard_map/ppermute | solution.py:31
  47.2 1.7 collective-permute-done.11
  48.9 0.7 fusion.5
  49.7 11.1 %add_convert_fusion = bf16[4,512,256]{2,1,0:T(8,128)(2,1)S(1)} fusion(bf16[4,512,256]{2,1,0:T(8,128)(2,1)S(1)} %divide_convert_fusion, bf16[2,512,256]{2,1,0:T(8,128)(2,1)S(1)} %collective-permute-done.11, bf16[2,512,256]{2,1,0:T(8,128)(2,1)S(1)} %collective-permute-done.10, bf16[8,516,256]{2,1,0:T(8,128)(2,1)S(1)} %fusion.5, ...), kind=kLoop, calls=%fused_computation.9 | loop fusion | flops 39845888 | bytes 24313856 | tf_op jit(solution)/shard_map/convert_element_type | solution.py:141
  60.8 3.3 %collective-permute-start.12 = (bf16[2048,256]{1,0:T(8,128)(2,1)S(1)}, bf16[2048,256]{1,0:T(8,128)(2,1)}, u32[]{:S(2)}, u32[]{:S(2)}) collective-permute-start(bf16[2048,256]{1,0:T(8,128)(2,1)S(1)} %bitcast.12), channel_id=1, source_target_pairs={{0,2},{2,4},{4,6},{6,0},{1,3},{3,5},{5,7},{7,1},{8,10},{10,12},{12... | collective-permute-start | bytes 3145736 | tf_op jit(solution)/shard_map/ppermute | solution.py:64
  64.2 3.1 %collective-permute-start.20 = (bf16[2048,256]{1,0:T(8,128)(2,1)S(1)}, bf16[2048,256]{1,0:T(8,128)(2,1)}, u32[]{:S(2)}, u32[]{:S(2)}) collective-permute-start(bf16[2048,256]{1,0:T(8,128)(2,1)S(1)} %bitcast.13), channel_id=1, source_target_pairs={{2,0},{4,2},{6,4},{0,6},{3,1},{5,3},{7,5},{1,7},{10,8},{12,10},{14... | collective-permute-start | bytes 3145736 | tf_op jit(solution)/shard_map/ppermute | solution.py:65
  67.3 0.1 collective-permute-done.6
  67.4 1.0 collective-permute-start.7
  68.5 1.2 collective-permute-start.9
  69.7 40.0 %collective-permute-done.12 = bf16[2048,256]{1,0:T(8,128)(2,1)} collective-permute-done((bf16[2048,256]{1,0:T(8,128)(2,1)S(1)}, bf16[2048,256]{1,0:T(8,128)(2,1)}, u32[]{:S(2)}, u32[]{:S(2)}) %collective-permute-start.12) | collective-permute-done | bytes 1048608 | tf_op jit(solution)/shard_map/ppermute | solution.py:64
  109.7 1.1 slice.423
  110.7 12.5 %collective-permute-start.19 = (bf16[1024,256]{1,0:T(8,128)(2,1)S(1)}, bf16[1024,256]{1,0:T(8,128)(2,1)S(1)}, u32[]{:S(2)}, u32[]{:S(2)}) collective-permute-start(bf16[1024,256]{1,0:T(8,128)(2,1)S(1)} %slice.423), channel_id=1, source_target_pairs={{0,2},{2,4},{4,6},{6,0},{1,3},{3,5},{5,7},{7,1},{8,10},{10,12},{12... | collective-permute-start | bytes 1572872 | tf_op jit(solution)/shard_map/ppermute | solution.py:67
  123.3 1.1 slice.424
  124.3 0.3 collective-permute-start.21
  124.6 3.7 %collective-permute-done.7 = bf16[1024,256]{1,0:T(8,128)(2,1)} collective-permute-done((bf16[1024,256]{1,0:T(8,128)(2,1)S(1)}, bf16[1024,256]{1,0:T(8,128)(2,1)}, u32[]{:S(2)}, u32[]{:S(2)}) %collective-permute-start.7) | collective-permute-done | bytes 524320 | tf_op jit(solution)/shard_map/ppermute | solution.py:67
  128.3 4.8 %fusion.11 = f32[1024,256]{1,0:T(8,128)S(1)} fusion(bf16[2048,256]{1,0:T(8,128)(2,1)} %collective-permute-done.12, bf16[2048,256]{1,0:T(8,128)(2,1)S(1)} %bitcast.14, pred[]{:T(512)S(6)} %eq.111, bf16[2048,256]{1,0:T(8,128)(2,1)S(1)} %copy-done.5, bf16[1024,256]{1,0:T(8,128)(2,1)} %collective-permute-done.9, bf16[1024,256]{1,0:T(8,128)(2,1)} %collective-permute-done.7, ...), kind=kOutput, calls=%fused_computation.26 | convolution fusion | flops 1095237632 | bytes 7340033 | tf_op jit(solution)/shard_map/dot_general | solution.py:171
  133.1 7.8 %collective-permute-start.13 = (f32[1024,256]{1,0:T(8,128)S(1)}, f32[1024,256]{1,0:T(8,128)}, u32[]{:S(2)}, u32[]{:S(2)}) collective-permute-start(f32[1024,256]{1,0:T(8,128)S(1)} %fusion.11), channel_id=1, source_target_pairs={{0,16},{16,0},{1,17},{17,1},{2,18},{18,2},{3,19},{19,3},{4,20},{20... | collective-permute-start | bytes 3145736 | tf_op jit(solution)/shard_map/ppermute | solution.py:172
  140.9 3.7 %collective-permute-done.19 = bf16[1024,256]{1,0:T(8,128)(2,1)S(1)} collective-permute-done((bf16[1024,256]{1,0:T(8,128)(2,1)S(1)}, bf16[1024,256]{1,0:T(8,128)(2,1)S(1)}, u32[]{:S(2)}, u32[]{:S(2)}) %collective-permute-start.19) | collective-permute-done | bytes 524320 | tf_op jit(solution)/shard_map/ppermute | solution.py:67
  144.7 5.9 %fusion.8 = f32[1024,256]{1,0:T(8,128)} fusion(bf16[2048,256]{1,0:T(8,128)(2,1)} %collective-permute-done.20, bf16[2048,256]{1,0:T(8,128)(2,1)S(1)} %constant_dynamic-update-slice_fusion, pred[]{:T(512)S(6)} %eq.111, bf16[2048,256]{1,0:T(8,128)(2,1)S(1)} %copy-done.5, bf16[1024,256]{1,0:T(8,128)(2,1)} %collective-permute-done.9, ...), kind=kOutput, calls=%fused_computation.23 | convolution fusion | flops 1095237632 | bytes 7340033 | tf_op jit(solution)/shard_map/dot_general | solution.py:171
  150.5 2.5 %collective-permute-start.22 = (f32[1024,256]{1,0:T(8,128)}, f32[1024,256]{1,0:T(8,128)}, u32[]{:S(2)}, u32[]{:S(2)}) collective-permute-start(f32[1024,256]{1,0:T(8,128)} %fusion.8), channel_id=1, source_target_pairs={{0,16},{16,0},{1,17},{17,1},{2,18},{18,2},{3,19},{19,3},{4,20},{20... | collective-permute-start | bytes 3145736 | tf_op jit(solution)/shard_map/ppermute | solution.py:172
  153.0 3.6 %convolution_add_fusion.1 = f32[1024,256]{1,0:T(8,128)S(1)} fusion(f32[1024,256]{1,0:T(8,128)} %collective-permute-done.13, bf16[2048,256]{1,0:T(8,128)(2,1)S(1)} %bitcast.15, bf16[2048,256]{1,0:T(8,128)(2,1)} %collective-permute-done.12, pred[]{:T(512)S(6)} %eq.111, bf16[2048,256]{1,0:T(8,128)(2,1)} %copy-done.4, ...), kind=kOutput, calls=%fused_computation.18 | convolution fusion | flops 1095499776 | bytes 8388609 | tf_op jit(solution)/shard_map/dot_general | solution.py:170
  156.6 0.9 constant_dynamic-slice_fusion.5
  157.5 5.1 %collective-permute-start.15 = (f32[256,256]{1,0:T(8,128)}, f32[256,256]{1,0:T(8,128)}, u32[]{:S(2)}, u32[]{:S(2)}) collective-permute-start(f32[256,256]{1,0:T(8,128)} %get-tuple-element.57), channel_id=1, source_target_pairs={{0,128},{64,192},{128,0},{192,64},{1,129},{65,193},{129,1},{193,65... | collective-permute-start | bytes 786440 | tf_op jit(solution)/shard_map/ppermute | solution.py:176
  162.6 4.6 %convolution_add_fusion = f32[1024,256]{1,0:T(8,128)S(1)} fusion(f32[1024,256]{1,0:T(8,128)} %collective-permute-done.22, bf16[2048,256]{1,0:T(8,128)(2,1)S(1)} %copy-done.8, bf16[2048,256]{1,0:T(8,128)(2,1)} %collective-permute-done.20, pred[]{:T(512)S(6)} %eq.111, bf16[2048,256]{1,0:T(8,128)(2,1)S(1)} %copy-done.6, ...), kind=kOutput, calls=%fused_computation.17 | convolution fusion | flops 1095499776 | bytes 8388609 | tf_op jit(solution)/shard_map/dot_general | solution.py:170
  167.2 0.8 constant_dynamic-slice_fusion.2
  168.0 3.2 %collective-permute-start.23 = (f32[256,256]{1,0:T(8,128)}, f32[256,256]{1,0:T(8,128)S(1)}, u32[]{:S(2)}, u32[]{:S(2)}) collective-permute-start(f32[256,256]{1,0:T(8,128)} %get-tuple-element.58), channel_id=1, source_target_pairs={{0,64},{64,128},{128,192},{192,0},{1,65},{65,129},{129,193},{193,1... | collective-permute-start | bytes 786440 | tf_op jit(solution)/shard_map/ppermute | solution.py:176
  171.2 0.9 collective-permute-start.25
  172.1 3.6 %collective-permute-done.16 = f32[256,256]{1,0:T(8,128)} collective-permute-done((f32[256,256]{1,0:T(8,128)}, f32[256,256]{1,0:T(8,128)}, u32[]{:S(2)}, u32[]{:S(2)}) %collective-permute-start.16) | collective-permute-done | bytes 262176 | tf_op jit(solution)/shard_map/ppermute | solution.py:176
  175.6 1.1 add_add_fusion.1
  176.7 1.9 collective-permute-start.17
  178.6 0.7 collective-permute-start.18
  179.3 2.6 %collective-permute-done.24 = f32[256,256]{1,0:T(8,128)S(1)} collective-permute-done((f32[256,256]{1,0:T(8,128)S(1)}, f32[256,256]{1,0:T(8,128)S(1)}, u32[]{:S(2)}, u32[]{:S(2)}) %collective-permute-start.24) | collective-permute-done | bytes 262176 | tf_op jit(solution)/shard_map/ppermute | solution.py:176
  182.0 4.8 %collective-permute-done.25 = f32[256,256]{1,0:T(8,128)} collective-permute-done((f32[256,256]{1,0:T(8,128)S(1)}, f32[256,256]{1,0:T(8,128)}, u32[]{:S(2)}, u32[]{:S(2)}) %collective-permute-start.25) | collective-permute-done | bytes 262176 | tf_op jit(solution)/shard_map/ppermute | solution.py:176
  186.7 1.0 add_add_fusion
  187.7 14.8 %collective-permute-start.26 = (f32[256,256]{1,0:T(8,128)S(1)}, f32[256,256]{1,0:T(8,128)S(1)}, u32[]{:S(2)}, u32[]{:S(2)}) collective-permute-start(f32[256,256]{1,0:T(8,128)S(1)} %add_add_fusion), channel_id=1, source_target_pairs={{0,64},{1,81},{2,98},{3,115},{4,4},{5,21},{6,38},{7,55},{8,200},{9... | collective-permute-start | bytes 786440 | tf_op jit(solution)/shard_map/ppermute | solution.py:184
  202.5 1.3 collective-permute-start.27
  204.4 2.0 collective-permute-done.26
  206.4 5.6 %collective-permute-done.27 = f32[256,256]{1,0:T(8,128)S(1)} collective-permute-done((f32[256,256]{1,0:T(8,128)S(1)}, f32[256,256]{1,0:T(8,128)S(1)}, u32[]{:S(2)}, u32[]{:S(2)}) %collective-permute-start.27) | collective-permute-done | bytes 262176 | tf_op jit(solution)/shard_map/ppermute | solution.py:184
  212.0 0.8 add_divide_fusion
  (50 shorter events, 0.5 us)
Async XLA Ops:
  0.0 12.5 %copy-start.10 = (s32[4,512]{1,0:T(4,128)S(1)}, s32[4,512]{1,0:T(4,128)}, u32[]{:S(2)}) copy-start(s32[4,512]{1,0:T(4,128)} %param.4) | copy-start | bytes 24580
  0.0 12.1 %copy-start.9 = (s32[4,512]{1,0:T(4,128)S(1)}, s32[4,512]{1,0:T(4,128)}, u32[]{:S(2)}) copy-start(s32[4,512]{1,0:T(4,128)} %param.5) | copy-start | bytes 24580
  0.0 33.8 %copy-start = (s32[4,512,256]{2,1,0:T(8,128)S(1)}, s32[4,512,256]{2,1,0:T(8,128)}, u32[]{:S(2)}) copy-start(s32[4,512,256]{2,1,0:T(8,128)} %param.3) | copy-start | bytes 6291460
  1.5 10.5 %collective-permute-start = (s32[2,512]{1,0:T(2,128)S(1)}, s32[2,512]{1,0:T(2,128)S(1)}, u32[]{:S(2)}, u32[]{:S(2)}) collective-permute-start(s32[2,512]{1,0:T(2,128)S(1)} %get-tuple-element.110), channel_id=1, source_target_pairs={{0,16},{16,32},{32,48},{48,64},{64,80},{80,96},{96,112},{112,128},... | collective-permute-start | bytes 12296 | tf_op jit(solution)/shard_map/ppermute | solution.py:31
  3.5 8.6 %collective-permute-start.1 = (s32[2,512]{1,0:T(2,128)S(1)}, s32[2,512]{1,0:T(2,128)S(1)}, u32[]{:S(2)}, u32[]{:S(2)}) collective-permute-start(s32[2,512]{1,0:T(2,128)S(1)} %get-tuple-element.111), channel_id=1, source_target_pairs={{16,0},{32,16},{48,32},{64,48},{80,64},{96,80},{112,96},{128,112},... | collective-permute-start | bytes 12296 | tf_op jit(solution)/shard_map/ppermute | solution.py:33
  14.6 2.0 collective-permute-start.2
  18.0 5.1 %collective-permute-start.3 = (s32[514]{0:T(1024)S(1)}, s32[514]{0:T(1024)S(1)}, u32[]{:S(2)}, u32[]{:S(2)}) collective-permute-start(s32[514]{0:T(1024)S(1)} %fusion.73), channel_id=1, source_target_pairs={{0,32},{16,48},{32,0},{48,16},{64,96},{80,112},{96,64},{112,80},{1... | collective-permute-start | bytes 6176 | tf_op jit(solution)/shard_map/ppermute | solution.py:44
  23.1 3.6 %collective-permute-start.4 = (s32[514]{0:T(1024)S(1)}, s32[514]{0:T(1024)S(1)}, u32[]{:S(2)}, u32[]{:S(2)}) collective-permute-start(s32[514]{0:T(1024)S(1)} %add.282), channel_id=1, source_target_pairs={{0,64},{16,80},{32,96},{48,112},{64,0},{80,16},{96,32},{112,48},{1... | collective-permute-start | bytes 6176 | tf_op jit(solution)/shard_map/ppermute | solution.py:44
  26.8 5.1 %collective-permute-start.5 = (s32[514]{0:T(1024)S(1)}, s32[514]{0:T(1024)S(1)}, u32[]{:S(2)}, u32[]{:S(2)}) collective-permute-start(s32[514]{0:T(1024)S(1)} %add.283), channel_id=1, source_target_pairs={{0,128},{16,144},{32,160},{48,176},{64,192},{80,208},{96,224},{112... | collective-permute-start | bytes 6176 | tf_op jit(solution)/shard_map/ppermute | solution.py:44
  34.2 13.0 %collective-permute-start.10 = (bf16[2,512,256]{2,1,0:T(8,128)(2,1)S(1)}, bf16[2,512,256]{2,1,0:T(8,128)(2,1)S(1)}, u32[]{:S(2)}, u32[]{:S(2)}) collective-permute-start(bf16[2,512,256]{2,1,0:T(8,128)(2,1)S(1)} %get-tuple-element.61), channel_id=1, source_target_pairs={{0,16},{16,32},{32,48},{48,64},{64,80},{80,96},{96,112},{112,128},... | collective-permute-start | bytes 1572872 | tf_op jit(solution)/shard_map/ppermute | solution.py:31
  36.2 12.8 %collective-permute-start.11 = (bf16[2,512,256]{2,1,0:T(8,128)(2,1)S(1)}, bf16[2,512,256]{2,1,0:T(8,128)(2,1)S(1)}, u32[]{:S(2)}, u32[]{:S(2)}) collective-permute-start(bf16[2,512,256]{2,1,0:T(8,128)(2,1)S(1)} %get-tuple-element.62), channel_id=1, source_target_pairs={{16,0},{32,16},{48,32},{64,48},{80,64},{96,80},{112,96},{128,112},... | collective-permute-start | bytes 1572872 | tf_op jit(solution)/shard_map/ppermute | solution.py:33
  42.2 25.2 %collective-permute-start.6 = (bf16[2048,256]{1,0:T(8,128)(2,1)S(1)}, bf16[2048,256]{1,0:T(8,128)(2,1)S(1)}, u32[]{:S(2)}, u32[]{:S(2)}) collective-permute-start(bf16[2048,256]{1,0:T(8,128)(2,1)S(1)} %bitcast.6), channel_id=1, source_target_pairs={{0,1},{1,9},{9,8},{8,0},{2,3},{3,11},{11,10},{10,2},{4,5},{5,13},{... | collective-permute-start | bytes 3145736 | tf_op jit(solution)/shard_map/ppermute | solution.py:64
  44.2 24.2 %collective-permute-start.8 = (bf16[2048,256]{1,0:T(8,128)(2,1)S(1)}, bf16[2048,256]{1,0:T(8,128)(2,1)S(1)}, u32[]{:S(2)}, u32[]{:S(2)}) collective-permute-start(bf16[2048,256]{1,0:T(8,128)(2,1)S(1)} %bitcast.7), channel_id=1, source_target_pairs={{1,0},{9,1},{8,9},{0,8},{3,2},{11,3},{10,11},{2,10},{5,4},{13,5},{... | collective-permute-start | bytes 3145736 | tf_op jit(solution)/shard_map/ppermute | solution.py:65
  60.8 48.8 %collective-permute-start.12 = (bf16[2048,256]{1,0:T(8,128)(2,1)S(1)}, bf16[2048,256]{1,0:T(8,128)(2,1)}, u32[]{:S(2)}, u32[]{:S(2)}) collective-permute-start(bf16[2048,256]{1,0:T(8,128)(2,1)S(1)} %bitcast.12), channel_id=1, source_target_pairs={{0,2},{2,4},{4,6},{6,0},{1,3},{3,5},{5,7},{7,1},{8,10},{10,12},{12... | collective-permute-start | bytes 3145736 | tf_op jit(solution)/shard_map/ppermute | solution.py:64
  64.2 59.1 %collective-permute-start.20 = (bf16[2048,256]{1,0:T(8,128)(2,1)S(1)}, bf16[2048,256]{1,0:T(8,128)(2,1)}, u32[]{:S(2)}, u32[]{:S(2)}) collective-permute-start(bf16[2048,256]{1,0:T(8,128)(2,1)S(1)} %bitcast.13), channel_id=1, source_target_pairs={{2,0},{4,2},{6,4},{0,6},{3,1},{5,3},{7,5},{1,7},{10,8},{12,10},{14... | collective-permute-start | bytes 3145736 | tf_op jit(solution)/shard_map/ppermute | solution.py:65
  67.4 2.3 %copy-start.1 = (bf16[2048,256]{1,0:T(8,128)(2,1)}, bf16[2048,256]{1,0:T(8,128)(2,1)S(1)}, u32[]{:S(2)}) copy-start(bf16[2048,256]{1,0:T(8,128)(2,1)S(1)} %collective-permute-done.6) | copy-start | bytes 3145732
  67.4 60.8 %collective-permute-start.7 = (bf16[1024,256]{1,0:T(8,128)(2,1)S(1)}, bf16[1024,256]{1,0:T(8,128)(2,1)}, u32[]{:S(2)}, u32[]{:S(2)}) collective-permute-start(bf16[1024,256]{1,0:T(8,128)(2,1)S(1)} %slice.395), channel_id=1, source_target_pairs={{0,1},{1,9},{9,8},{8,0},{2,3},{3,11},{11,10},{10,2},{4,5},{5,13},{... | collective-permute-start | bytes 1572872 | tf_op jit(solution)/shard_map/ppermute | solution.py:67
  68.4 1.2 copy-start.4
  68.5 59.8 %collective-permute-start.9 = (bf16[1024,256]{1,0:T(8,128)(2,1)S(1)}, bf16[1024,256]{1,0:T(8,128)(2,1)}, u32[]{:S(2)}, u32[]{:S(2)}) collective-permute-start(bf16[1024,256]{1,0:T(8,128)(2,1)S(1)} %slice.396), channel_id=1, source_target_pairs={{1,0},{9,1},{8,9},{0,8},{3,2},{11,3},{10,11},{2,10},{5,4},{13,5},{... | collective-permute-start | bytes 1572872 | tf_op jit(solution)/shard_map/ppermute | solution.py:68
  69.7 58.6 %copy-start.2 = (bf16[2048,256]{1,0:T(8,128)(2,1)S(1)}, bf16[2048,256]{1,0:T(8,128)(2,1)}, u32[]{:S(2)}) copy-start(bf16[2048,256]{1,0:T(8,128)(2,1)} %copy-done.1) | copy-start | bytes 3145732
  69.7 58.6 %copy-start.5 = (bf16[2048,256]{1,0:T(8,128)(2,1)S(1)}, bf16[2048,256]{1,0:T(8,128)(2,1)}, u32[]{:S(2)}) copy-start(bf16[2048,256]{1,0:T(8,128)(2,1)} %copy-done.4) | copy-start | bytes 3145732
  110.7 33.8 %collective-permute-start.19 = (bf16[1024,256]{1,0:T(8,128)(2,1)S(1)}, bf16[1024,256]{1,0:T(8,128)(2,1)S(1)}, u32[]{:S(2)}, u32[]{:S(2)}) collective-permute-start(bf16[1024,256]{1,0:T(8,128)(2,1)S(1)} %slice.423), channel_id=1, source_target_pairs={{0,2},{2,4},{4,6},{6,0},{1,3},{3,5},{5,7},{7,1},{8,10},{10,12},{12... | collective-permute-start | bytes 1572872 | tf_op jit(solution)/shard_map/ppermute | solution.py:67
  124.3 20.3 %collective-permute-start.21 = (bf16[1024,256]{1,0:T(8,128)(2,1)S(1)}, bf16[1024,256]{1,0:T(8,128)(2,1)S(1)}, u32[]{:S(2)}, u32[]{:S(2)}) collective-permute-start(bf16[1024,256]{1,0:T(8,128)(2,1)S(1)} %slice.424), channel_id=1, source_target_pairs={{2,0},{4,2},{6,4},{0,6},{3,1},{5,3},{7,5},{1,7},{10,8},{12,10},{14... | collective-permute-start | bytes 1572872 | tf_op jit(solution)/shard_map/ppermute | solution.py:68
  133.1 19.9 %collective-permute-start.13 = (f32[1024,256]{1,0:T(8,128)S(1)}, f32[1024,256]{1,0:T(8,128)}, u32[]{:S(2)}, u32[]{:S(2)}) collective-permute-start(f32[1024,256]{1,0:T(8,128)S(1)} %fusion.11), channel_id=1, source_target_pairs={{0,16},{16,0},{1,17},{17,1},{2,18},{18,2},{3,19},{19,3},{4,20},{20... | collective-permute-start | bytes 3145736 | tf_op jit(solution)/shard_map/ppermute | solution.py:172
  144.7 5.9 %copy-start.7 = (bf16[2048,256]{1,0:T(8,128)(2,1)}, bf16[2048,256]{1,0:T(8,128)(2,1)S(1)}, u32[]{:S(2)}) copy-start(bf16[2048,256]{1,0:T(8,128)(2,1)S(1)} %constant_dynamic-update-slice_fusion) | copy-start | bytes 3145732
  150.5 12.1 %collective-permute-start.22 = (f32[1024,256]{1,0:T(8,128)}, f32[1024,256]{1,0:T(8,128)}, u32[]{:S(2)}, u32[]{:S(2)}) collective-permute-start(f32[1024,256]{1,0:T(8,128)} %fusion.8), channel_id=1, source_target_pairs={{0,16},{16,0},{1,17},{17,1},{2,18},{18,2},{3,19},{19,3},{4,20},{20... | collective-permute-start | bytes 3145736 | tf_op jit(solution)/shard_map/ppermute | solution.py:172
  153.0 9.6 %copy-start.3 = (bf16[2048,256]{1,0:T(8,128)(2,1)S(1)}, bf16[2048,256]{1,0:T(8,128)(2,1)}, u32[]{:S(2)}) copy-start(bf16[2048,256]{1,0:T(8,128)(2,1)} %copy-done.1) | copy-start | bytes 3145732
  153.0 9.6 %copy-start.6 = (bf16[2048,256]{1,0:T(8,128)(2,1)S(1)}, bf16[2048,256]{1,0:T(8,128)(2,1)}, u32[]{:S(2)}) copy-start(bf16[2048,256]{1,0:T(8,128)(2,1)} %copy-done.4) | copy-start | bytes 3145732
  153.0 9.6 %copy-start.8 = (bf16[2048,256]{1,0:T(8,128)(2,1)S(1)}, bf16[2048,256]{1,0:T(8,128)(2,1)}, u32[]{:S(2)}) copy-start(bf16[2048,256]{1,0:T(8,128)(2,1)} %copy-done.7) | copy-start | bytes 3145732
  157.5 13.7 %collective-permute-start.14 = (f32[256,256]{1,0:T(8,128)S(1)}, f32[256,256]{1,0:T(8,128)S(1)}, u32[]{:S(2)}, u32[]{:S(2)}) collective-permute-start(f32[256,256]{1,0:T(8,128)S(1)} %get-tuple-element.55), channel_id=1, source_target_pairs={{0,64},{64,128},{128,192},{192,0},{1,65},{65,129},{129,193},{193,1... | collective-permute-start | bytes 786440 | tf_op jit(solution)/shard_map/ppermute | solution.py:176
  157.5 14.6 %collective-permute-start.15 = (f32[256,256]{1,0:T(8,128)}, f32[256,256]{1,0:T(8,128)}, u32[]{:S(2)}, u32[]{:S(2)}) collective-permute-start(f32[256,256]{1,0:T(8,128)} %get-tuple-element.57), channel_id=1, source_target_pairs={{0,128},{64,192},{128,0},{192,64},{1,129},{65,193},{129,1},{193,65... | collective-permute-start | bytes 786440 | tf_op jit(solution)/shard_map/ppermute | solution.py:176
  162.6 13.0 %collective-permute-start.16 = (f32[256,256]{1,0:T(8,128)}, f32[256,256]{1,0:T(8,128)}, u32[]{:S(2)}, u32[]{:S(2)}) collective-permute-start(f32[256,256]{1,0:T(8,128)} %get-tuple-element.56), channel_id=1, source_target_pairs={{0,192},{64,0},{128,64},{192,128},{1,193},{65,1},{129,65},{193,129... | collective-permute-start | bytes 786440 | tf_op jit(solution)/shard_map/ppermute | solution.py:176
  168.0 11.3 %collective-permute-start.23 = (f32[256,256]{1,0:T(8,128)}, f32[256,256]{1,0:T(8,128)S(1)}, u32[]{:S(2)}, u32[]{:S(2)}) collective-permute-start(f32[256,256]{1,0:T(8,128)} %get-tuple-element.58), channel_id=1, source_target_pairs={{0,64},{64,128},{128,192},{192,0},{1,65},{65,129},{129,193},{193,1... | collective-permute-start | bytes 786440 | tf_op jit(solution)/shard_map/ppermute | solution.py:176
  171.2 10.7 %collective-permute-start.24 = (f32[256,256]{1,0:T(8,128)S(1)}, f32[256,256]{1,0:T(8,128)S(1)}, u32[]{:S(2)}, u32[]{:S(2)}) collective-permute-start(f32[256,256]{1,0:T(8,128)S(1)} %get-tuple-element.60), channel_id=1, source_target_pairs={{0,128},{64,192},{128,0},{192,64},{1,129},{65,193},{129,1},{193,65... | collective-permute-start | bytes 786440 | tf_op jit(solution)/shard_map/ppermute | solution.py:176
  171.2 15.5 %collective-permute-start.25 = (f32[256,256]{1,0:T(8,128)S(1)}, f32[256,256]{1,0:T(8,128)}, u32[]{:S(2)}, u32[]{:S(2)}) collective-permute-start(f32[256,256]{1,0:T(8,128)S(1)} %get-tuple-element.59), channel_id=1, source_target_pairs={{0,192},{64,0},{128,64},{192,128},{1,193},{65,1},{129,65},{193,129... | collective-permute-start | bytes 786440 | tf_op jit(solution)/shard_map/ppermute | solution.py:176
  176.7 27.7 %collective-permute-start.17 = (f32[256,256]{1,0:T(8,128)S(1)}, f32[256,256]{1,0:T(8,128)S(1)}, u32[]{:S(2)}, u32[]{:S(2)}) collective-permute-start(f32[256,256]{1,0:T(8,128)S(1)} %add_add_fusion.1), channel_id=1, source_target_pairs={{0,0},{1,17},{2,34},{3,51},{4,68},{5,85},{6,102},{7,119},{8,136},{... | collective-permute-start | bytes 786440 | tf_op jit(solution)/shard_map/ppermute | solution.py:184
  178.6 25.8 %collective-permute-start.18 = (f32[256,256]{1,0:T(8,128)S(1)}, f32[256,256]{1,0:T(8,128)S(1)}, u32[]{:S(2)}, u32[]{:S(2)}) collective-permute-start(f32[256,256]{1,0:T(8,128)S(1)} %add_add_fusion.1), channel_id=1, source_target_pairs={{32,0},{33,17},{34,34},{35,51},{36,68},{37,85},{38,102},{39,119},{... | collective-permute-start | bytes 786440 | tf_op jit(solution)/shard_map/ppermute | solution.py:184
  187.7 18.7 %collective-permute-start.26 = (f32[256,256]{1,0:T(8,128)S(1)}, f32[256,256]{1,0:T(8,128)S(1)}, u32[]{:S(2)}, u32[]{:S(2)}) collective-permute-start(f32[256,256]{1,0:T(8,128)S(1)} %add_add_fusion), channel_id=1, source_target_pairs={{0,64},{1,81},{2,98},{3,115},{4,4},{5,21},{6,38},{7,55},{8,200},{9... | collective-permute-start | bytes 786440 | tf_op jit(solution)/shard_map/ppermute | solution.py:184
  202.5 9.5 %collective-permute-start.27 = (f32[256,256]{1,0:T(8,128)S(1)}, f32[256,256]{1,0:T(8,128)S(1)}, u32[]{:S(2)}, u32[]{:S(2)}) collective-permute-start(f32[256,256]{1,0:T(8,128)S(1)} %add_add_fusion), channel_id=1, source_target_pairs={{32,64},{33,81},{34,98},{35,115},{36,4},{37,21},{38,38},{39,55},{4... | collective-permute-start | bytes 786440 | tf_op jit(solution)/shard_map/ppermute | solution.py:184

commit v9 on v8

--- a/solution.py
+++ b/solution.py
@@ -142,9 +142,9 @@
     bin_count = row_count * col_count
     flat_z = zscores.reshape(bin_count, panel_width)
     flat_lag = lagged.reshape(bin_count, panel_width)
-    z_parts = ring_gather(flat_z, ROW_AXES, ROW_RING)
-    lag_parts = ring_gather(flat_lag, COL_AXES, COL_RING)
-    z_cat = jnp.concatenate(z_parts, axis=1)
+    z_parts = ring_gather(flat_z, COL_AXES, COL_RING)
+    lag_parts = ring_gather(flat_lag, ROW_AXES, ROW_RING)
+    lag_cat = jnp.concatenate(lag_parts, axis=1)
     sizes = {a: lax.axis_size(a) for a in GENE_AXES}
     rings = {ROW_AXES: ROW_RING, COL_AXES: COL_RING}
 
@@ -157,7 +157,7 @@
 
     def home(t1, t2, c):
         coord = dict(zip(GENE_AXES, unravel(c, [sizes[a] for a in GENE_AXES])))
-        return member(coord, COL_AXES, t2) * gene_n + member(coord, ROW_AXES, t1)
+        return member(coord, ROW_AXES, t2) * gene_n + member(coord, COL_AXES, t1)
 
     core = lax.axis_index("sc")
     ring_x = lax.axis_size("sx")
@@ -165,14 +165,14 @@
     every = SPOT_AXES + GENE_AXES
     received = []
     for phase in range(2):
-        keep_lag = jnp.where(core == 0, lag_parts[2 * phase], lag_parts[2 * phase + 1])
-        give_lag = jnp.where(core == 0, lag_parts[2 * phase + 1], lag_parts[2 * phase])
-        keep = lax.dot_general(z_cat, keep_lag, contract_bins, preferred_element_type=jnp.float32)
-        give = lax.dot_general(z_cat, give_lag, contract_bins, preferred_element_type=jnp.float32)
+        keep_z = jnp.where(core == 0, z_parts[2 * phase], z_parts[2 * phase + 1])
+        give_z = jnp.where(core == 0, z_parts[2 * phase + 1], z_parts[2 * phase])
+        keep = lax.dot_general(keep_z, lag_cat, contract_bins, preferred_element_type=jnp.float32)
+        give = lax.dot_general(give_z, lag_cat, contract_bins, preferred_element_type=jnp.float32)
         mine = keep + lax.ppermute(give, "sc", [(0, 1), (1, 0)])
-        total = lax.dynamic_slice_in_dim(mine, pos_x * panel_width, panel_width, 0)
+        total = lax.dynamic_slice_in_dim(mine, pos_x * panel_width, panel_width, 1)
         for d in range(1, ring_x):
-            sent = lax.dynamic_slice_in_dim(mine, ((pos_x + d) % ring_x) * panel_width, panel_width, 0)
+            sent = lax.dynamic_slice_in_dim(mine, ((pos_x + d) % ring_x) * panel_width, panel_width, 1)
             total = total + lax.ppermute(sent, "sx", [(k, (k + d) % ring_x) for k in range(ring_x)])
         for high in range(2):
             perm = []
@@ -180,7 +180,7 @@
                 for sc in range(2):
                     sigma = (sx * 2 + high) * 2 + sc
                     for c in range(gene_n):
-                        perm.append((sigma * gene_n + c, home(sx, sc + 2 * phase, c)))
+                        perm.append((sigma * gene_n + c, home(sc + 2 * phase, sx, c)))
             received.append(lax.ppermute(total, every, perm))
     share = received[0] + received[1] + received[2] + received[3]
     return share / jnp.sqrt(pair_norm)

time: 214 us -> 239 us (1.12)
  the two profiles are of different devices: /device:TPU:6 before, /device:TPU:10 now
where the time goes in v9:
time: 239 us
  waiting for transfers between devices  125 us (52%)
  starting transfers between devices  63.8 us (27%)
  other arithmetic  23.7 us (10%)
  matrix products  19.7 us (8%)
  local copies, waits for them, and re-layouts  4.62 us (2%)
    ppermute x2, waiting for transfers between devices, ring_gather(): prev = lax.ppermute(block, axes, fwd)  67.7 us
    ppermute x4, waiting for transfers between devices, shards(): received.append(lax.ppermute(total, every, perm))  22.8 us
    ppermute x2, starting transfers between devices, padded(): lax.ppermute(head, axis, [((i + 1) % count, i) for i in range(ends)])  12.1 us
    dot_general x2, matrix products, shards(): lax.dot_general(give_z, lag_cat, contract_bins, preferred_element_type=jn...  11.2 us
    convert_element_type x1, other arithmetic, shards(): lagged = lagged_sum.astype(jnp.bfloat16)  11.1 us
    ppermute x2, starting transfers between devices, ring_gather(): far_hi = lax.ppermute(nxt[half:], axes, bwd)  10.9 us
    ppermute x6, waiting for transfers between devices, shards(): lax.ppermute(sent, 'sx', [(k, (k + d) % ring_x) for k in range(ring_x)])  10.2 us
    ppermute x4, waiting for transfers between devices, allreduce_sum(): lax.ppermute(vector, axes, [(i, i ^ step) for i in range(count)])  9.18 us
  transfers between devices with their start and end apart: 28, of which 16 were waited for; matrix products, arithmetic and copies ran while one was open for 12% of the time, Pallas kernels for 0%

profile of v9, /device:TPU:10, one launch (start us, length us, event | category | flops | bytes accessed | tf_op | source)
XLA Modules:
  0.0 238.6 jit_solution(5772145792801599754)
XLA Ops:
  0.0 1.5 fusion.79
  1.5 1.9 collective-permute-start
  3.5 6.0 %collective-permute-start.1 = (s32[2,512]{1,0:T(2,128)S(1)}, s32[2,512]{1,0:T(2,128)S(1)}, u32[]{:S(2)}, u32[]{:S(2)}) collective-permute-start(s32[2,512]{1,0:T(2,128)S(1)} %get-tuple-element.111), channel_id=1, source_target_pairs={{16,0},{32,16},{48,32},{64,48},{80,64},{96,80},{112,96},{128,112},... | collective-permute-start | bytes 12296 | tf_op jit(solution)/shard_map/ppermute | solution.py:33
  9.5 0.7 broadcast_compare_fusion
  10.2 1.8 select_reduce_fusion
  12.1 0.2 broadcast_select_fusion.19
  12.5 0.8 fusion.69
  13.3 1.3 pad_add_fusion.1
  14.6 0.3 collective-permute-start.2
  14.9 0.9 collective-permute-done.2
  15.8 1.3 fusion.73
  17.2 3.0 %collective-permute-start.3 = (s32[514]{0:T(1024)S(1)}, s32[514]{0:T(1024)S(1)}, u32[]{:S(2)}, u32[]{:S(2)}) collective-permute-start(s32[514]{0:T(1024)S(1)} %fusion.73), channel_id=1, source_target_pairs={{0,32},{16,48},{32,0},{48,16},{64,96},{80,112},{96,64},{112,80},{1... | collective-permute-start | bytes 6176 | tf_op jit(solution)/shard_map/ppermute | solution.py:44
  20.2 2.1 collective-permute-done.3
  22.3 0.5 collective-permute-start.4
  22.8 3.2 %collective-permute-done.4 = s32[514]{0:T(1024)S(1)} collective-permute-done((s32[514]{0:T(1024)S(1)}, s32[514]{0:T(1024)S(1)}, u32[]{:S(2)}, u32[]{:S(2)}) %collective-permute-start.4) | collective-permute-done | bytes 2088 | tf_op jit(solution)/shard_map/ppermute | solution.py:44
  25.9 2.1 collective-permute-start.5
  28.1 3.0 %collective-permute-done.5 = s32[514]{0:T(1024)S(1)} collective-permute-done((s32[514]{0:T(1024)S(1)}, s32[514]{0:T(1024)S(1)}, u32[]{:S(2)}, u32[]{:S(2)}) %collective-permute-start.5) | collective-permute-done | bytes 2088 | tf_op jit(solution)/shard_map/ppermute | solution.py:44
  31.0 0.6 fusion.81
  32.3 0.7 convert_divide_fusion
  32.9 0.4 divide_convert_fusion
  33.4 1.9 collective-permute-start.7
  35.3 6.0 %collective-permute-start.8 = (bf16[2,512,256]{2,1,0:T(8,128)(2,1)S(1)}, bf16[2,512,256]{2,1,0:T(8,128)(2,1)S(1)}, u32[]{:S(2)}, u32[]{:S(2)}) collective-permute-start(bf16[2,512,256]{2,1,0:T(8,128)(2,1)S(1)} %get-tuple-element.62), channel_id=1, source_target_pairs={{16,0},{32,16},{48,32},{64,48},{80,64},{96,80},{112,96},{128,112},... | collective-permute-start | bytes 1572872 | tf_op jit(solution)/shard_map/ppermute | solution.py:33
  41.4 5.0 %collective-permute-done.7 = bf16[2,512,256]{2,1,0:T(8,128)(2,1)S(1)} collective-permute-done((bf16[2,512,256]{2,1,0:T(8,128)(2,1)S(1)}, bf16[2,512,256]{2,1,0:T(8,128)(2,1)S(1)}, u32[]{:S(2)}, u32[]{:S(2)}) %collective-permute-start.7) | collective-permute-done | bytes 524320 | tf_op jit(solution)/shard_map/ppermute | solution.py:31
  46.4 1.7 collective-permute-done.8
  48.1 0.7 fusion.5
  48.8 11.1 %add_convert_fusion = bf16[4,512,256]{2,1,0:T(8,128)(2,1)S(1)} fusion(bf16[4,512,256]{2,1,0:T(8,128)(2,1)S(1)} %divide_convert_fusion, bf16[2,512,256]{2,1,0:T(8,128)(2,1)S(1)} %collective-permute-done.8, bf16[2,512,256]{2,1,0:T(8,128)(2,1)S(1)} %collective-permute-done.7, bf16[8,516,256]{2,1,0:T(8,128)(2,1)S(1)} %fusion.5, ...), kind=kLoop, calls=%fused_computation.9 | loop fusion | flops 39845888 | bytes 24313856 | tf_op jit(solution)/shard_map/convert_element_type | solution.py:141
  60.0 1.3 collective-permute-start.9
  61.3 0.8 collective-permute-start.11
  62.1 3.3 %collective-permute-start.6 = (bf16[2048,256]{1,0:T(8,128)(2,1)S(1)}, bf16[2048,256]{1,0:T(8,128)(2,1)}, u32[]{:S(2)}, u32[]{:S(2)}) collective-permute-start(bf16[2048,256]{1,0:T(8,128)(2,1)S(1)} %bitcast.6), channel_id=1, source_target_pairs={{0,2},{2,4},{4,6},{6,0},{1,3},{3,5},{5,7},{7,1},{8,10},{10,12},{12... | collective-permute-start | bytes 3145736 | tf_op jit(solution)/shard_map/ppermute | solution.py:64
  65.3 3.0 %collective-permute-start.20 = (bf16[2048,256]{1,0:T(8,128)(2,1)S(1)}, bf16[2048,256]{1,0:T(8,128)(2,1)}, u32[]{:S(2)}, u32[]{:S(2)}) collective-permute-start(bf16[2048,256]{1,0:T(8,128)(2,1)S(1)} %bitcast.7), channel_id=1, source_target_pairs={{2,0},{4,2},{6,4},{0,6},{3,1},{5,3},{7,5},{1,7},{10,8},{12,10},{14... | collective-permute-start | bytes 3145736 | tf_op jit(solution)/shard_map/ppermute | solution.py:65
  68.4 37.3 %collective-permute-done.9 = bf16[2048,256]{1,0:T(8,128)(2,1)S(1)} collective-permute-done((bf16[2048,256]{1,0:T(8,128)(2,1)S(1)}, bf16[2048,256]{1,0:T(8,128)(2,1)S(1)}, u32[]{:S(2)}, u32[]{:S(2)}) %collective-permute-start.9) | collective-permute-done | bytes 1048608 | tf_op jit(solution)/shard_map/ppermute | solution.py:64
  105.7 1.0 collective-permute-start.10
  106.7 1.3 collective-permute-start.12
  108.0 30.3 %collective-permute-done.6 = bf16[2048,256]{1,0:T(8,128)(2,1)} collective-permute-done((bf16[2048,256]{1,0:T(8,128)(2,1)S(1)}, bf16[2048,256]{1,0:T(8,128)(2,1)}, u32[]{:S(2)}, u32[]{:S(2)}) %collective-permute-start.6) | collective-permute-done | bytes 1048608 | tf_op jit(solution)/shard_map/ppermute | solution.py:64
  138.4 1.1 slice.423
  139.6 1.1 slice.424
  140.6 9.6 %collective-permute-start.21 = (bf16[1024,256]{1,0:T(8,128)(2,1)S(1)}, bf16[1024,256]{1,0:T(8,128)(2,1)S(1)}, u32[]{:S(2)}, u32[]{:S(2)}) collective-permute-start(bf16[1024,256]{1,0:T(8,128)(2,1)S(1)} %slice.424), channel_id=1, source_target_pairs={{2,0},{4,2},{6,4},{0,6},{3,1},{5,3},{7,5},{1,7},{10,8},{12,10},{14... | collective-permute-start | bytes 1572872 | tf_op jit(solution)/shard_map/ppermute | solution.py:68
  150.3 0.2 collective-permute-done.12
  150.4 5.1 %fusion.11 = f32[256,1024]{1,0:T(8,128)S(1)} fusion(bf16[2048,256]{1,0:T(8,128)(2,1)} %collective-permute-done.6, bf16[2048,256]{1,0:T(8,128)(2,1)S(1)} %bitcast.8, pred[]{:T(512)S(6)} %eq.87, bf16[2048,256]{1,0:T(8,128)(2,1)S(1)} %copy-done.5, bf16[1024,256]{1,0:T(8,128)(2,1)} %collective-permute-done.12, bf16[1024,256]{1,0:T(8,128)(2,1)} %collective-permute-done.10, ...), kind=kOutput, calls=%fused_computation.26 | convolution fusion | flops 1095237632 | bytes 7340033 | tf_op jit(solution)/shard_map/dot_general | solution.py:171
  155.5 5.1 %collective-permute-start.13 = (f32[256,1024]{1,0:T(8,128)S(1)}, f32[256,1024]{1,0:T(8,128)}, u32[]{:S(2)}, u32[]{:S(2)}) collective-permute-start(f32[256,1024]{1,0:T(8,128)S(1)} %fusion.11), channel_id=1, source_target_pairs={{0,16},{16,0},{1,17},{17,1},{2,18},{18,2},{3,19},{19,3},{4,20},{20... | collective-permute-start | bytes 3145736 | tf_op jit(solution)/shard_map/ppermute | solution.py:172
  160.6 8.4 %collective-permute-done.19 = bf16[1024,256]{1,0:T(8,128)(2,1)S(1)} collective-permute-done((bf16[1024,256]{1,0:T(8,128)(2,1)S(1)}, bf16[1024,256]{1,0:T(8,128)(2,1)S(1)}, u32[]{:S(2)}, u32[]{:S(2)}) %collective-permute-start.19) | collective-permute-done | bytes 524320 | tf_op jit(solution)/shard_map/ppermute | solution.py:67
  169.1 6.2 %fusion.8 = f32[256,1024]{1,0:T(8,128)} fusion(bf16[2048,256]{1,0:T(8,128)(2,1)} %collective-permute-done.20, bf16[2048,256]{1,0:T(8,128)(2,1)S(1)} %constant_dynamic-update-slice_fusion, pred[]{:T(512)S(6)} %eq.87, bf16[2048,256]{1,0:T(8,128)(2,1)S(1)} %copy-done.5, bf16[1024,256]{1,0:T(8,128)(2,1)} %collective-permute-done.12, ...), kind=kOutput, calls=%fused_computation.23 | convolution fusion | flops 1095237632 | bytes 7340033 | tf_op jit(solution)/shard_map/dot_general | solution.py:171
  175.3 0.3 collective-permute-start.22
  175.7 3.6 %convolution_add_fusion.1 = f32[256,1024]{1,0:T(8,128)S(1)} fusion(f32[256,1024]{1,0:T(8,128)} %collective-permute-done.13, bf16[2048,256]{1,0:T(8,128)(2,1)S(1)} %bitcast.9, bf16[2048,256]{1,0:T(8,128)(2,1)} %collective-permute-done.6, pred[]{:T(512)S(6)} %eq.87, bf16[2048,256]{1,0:T(8,128)(2,1)} %copy-done.4, ...), kind=kOutput, calls=%fused_computation.18 | convolution fusion | flops 1095499776 | bytes 8388609 | tf_op jit(solution)/shard_map/dot_general | solution.py:170
  179.3 0.9 constant_dynamic-slice_fusion.5
  180.1 1.5 collective-permute-start.14
  181.6 0.6 collective-permute-start.15
  182.3 2.6 %collective-permute-start.16 = (f32[256,256]{1,0:T(8,128)}, f32[256,256]{1,0:T(8,128)}, u32[]{:S(2)}, u32[]{:S(2)}) collective-permute-start(f32[256,256]{1,0:T(8,128)} %get-tuple-element.56), channel_id=1, source_target_pairs={{0,192},{64,0},{128,64},{192,128},{1,193},{65,1},{129,65},{193,129... | collective-permute-start | bytes 786440 | tf_op jit(solution)/shard_map/ppermute | solution.py:176
  184.9 4.9 %convolution_add_fusion = f32[256,1024]{1,0:T(8,128)S(1)} fusion(f32[256,1024]{1,0:T(8,128)} %collective-permute-done.22, bf16[2048,256]{1,0:T(8,128)(2,1)S(1)} %copy-done.8, bf16[2048,256]{1,0:T(8,128)(2,1)} %collective-permute-done.20, pred[]{:T(512)S(6)} %eq.87, bf16[2048,256]{1,0:T(8,128)(2,1)S(1)} %copy-done.6, ...), kind=kOutput, calls=%fused_computation.17 | convolution fusion | flops 1095499776 | bytes 8388609 | tf_op jit(solution)/shard_map/dot_general | solution.py:170
  189.8 0.8 constant_dynamic-slice_fusion.2
  190.6 3.5 %collective-permute-start.24 = (f32[256,256]{1,0:T(8,128)S(1)}, f32[256,256]{1,0:T(8,128)S(1)}, u32[]{:S(2)}, u32[]{:S(2)}) collective-permute-start(f32[256,256]{1,0:T(8,128)S(1)} %get-tuple-element.60), channel_id=1, source_target_pairs={{0,128},{64,192},{128,0},{192,64},{1,129},{65,193},{129,1},{193,65... | collective-permute-start | bytes 786440 | tf_op jit(solution)/shard_map/ppermute | solution.py:176
  194.1 3.1 %collective-permute-done.16 = f32[256,256]{1,0:T(8,128)} collective-permute-done((f32[256,256]{1,0:T(8,128)}, f32[256,256]{1,0:T(8,128)}, u32[]{:S(2)}, u32[]{:S(2)}) %collective-permute-start.16) | collective-permute-done | bytes 262176 | tf_op jit(solution)/shard_map/ppermute | solution.py:176
  197.2 1.1 add_add_fusion.1
  198.4 1.7 collective-permute-start.17
  200.1 0.7 collective-permute-start.18
  200.8 3.1 %collective-permute-done.24 = f32[256,256]{1,0:T(8,128)S(1)} collective-permute-done((f32[256,256]{1,0:T(8,128)S(1)}, f32[256,256]{1,0:T(8,128)S(1)}, u32[]{:S(2)}, u32[]{:S(2)}) %collective-permute-start.24) | collective-permute-done | bytes 262176 | tf_op jit(solution)/shard_map/ppermute | solution.py:176
  203.9 4.0 %collective-permute-done.25 = f32[256,256]{1,0:T(8,128)} collective-permute-done((f32[256,256]{1,0:T(8,128)S(1)}, f32[256,256]{1,0:T(8,128)}, u32[]{:S(2)}, u32[]{:S(2)}) %collective-permute-start.25) | collective-permute-done | bytes 262176 | tf_op jit(solution)/shard_map/ppermute | solution.py:176
  207.8 1.0 add_add_fusion
  208.9 4.3 %collective-permute-start.26 = (f32[256,256]{1,0:T(8,128)S(1)}, f32[256,256]{1,0:T(8,128)S(1)}, u32[]{:S(2)}, u32[]{:S(2)}) collective-permute-start(f32[256,256]{1,0:T(8,128)S(1)} %add_add_fusion), channel_id=1, source_target_pairs={{0,4},{1,21},{2,38},{3,55},{4,64},{5,81},{6,98},{7,115},{8,140},{9... | collective-permute-start | bytes 786440 | tf_op jit(solution)/shard_map/ppermute | solution.py:184
  213.2 1.3 collective-permute-start.27
  215.1 0.8 collective-permute-done.17
  215.9 10.9 %collective-permute-done.26 = f32[256,256]{1,0:T(8,128)S(1)} collective-permute-done((f32[256,256]{1,0:T(8,128)S(1)}, f32[256,256]{1,0:T(8,128)S(1)}, u32[]{:S(2)}, u32[]{:S(2)}) %collective-permute-start.26) | collective-permute-done | bytes 262176 | tf_op jit(solution)/shard_map/ppermute | solution.py:184
  226.9 11.0 %collective-permute-done.27 = f32[256,256]{1,0:T(8,128)S(1)} collective-permute-done((f32[256,256]{1,0:T(8,128)S(1)}, f32[256,256]{1,0:T(8,128)S(1)}, u32[]{:S(2)}, u32[]{:S(2)}) %collective-permute-start.27) | collective-permute-done | bytes 262176 | tf_op jit(solution)/shard_map/ppermute | solution.py:184
  237.9 0.8 add_divide_fusion
  (50 shorter events, 0.7 us)
Async XLA Ops:
  0.0 12.5 %copy-start.10 = (s32[4,512]{1,0:T(4,128)S(1)}, s32[4,512]{1,0:T(4,128)}, u32[]{:S(2)}) copy-start(s32[4,512]{1,0:T(4,128)} %param.4) | copy-start | bytes 24580
  0.0 12.1 %copy-start.9 = (s32[4,512]{1,0:T(4,128)S(1)}, s32[4,512]{1,0:T(4,128)}, u32[]{:S(2)}) copy-start(s32[4,512]{1,0:T(4,128)} %param.5) | copy-start | bytes 24580
  0.0 32.9 %copy-start = (s32[4,512,256]{2,1,0:T(8,128)S(1)}, s32[4,512,256]{2,1,0:T(8,128)}, u32[]{:S(2)}) copy-start(s32[4,512,256]{2,1,0:T(8,128)} %param.3) | copy-start | bytes 6291460
  1.5 10.5 %collective-permute-start = (s32[2,512]{1,0:T(2,128)S(1)}, s32[2,512]{1,0:T(2,128)S(1)}, u32[]{:S(2)}, u32[]{:S(2)}) collective-permute-start(s32[2,512]{1,0:T(2,128)S(1)} %get-tuple-element.110), channel_id=1, source_target_pairs={{0,16},{16,32},{32,48},{48,64},{64,80},{80,96},{96,112},{112,128},... | collective-permute-start | bytes 12296 | tf_op jit(solution)/shard_map/ppermute | solution.py:31
  3.5 8.6 %collective-permute-start.1 = (s32[2,512]{1,0:T(2,128)S(1)}, s32[2,512]{1,0:T(2,128)S(1)}, u32[]{:S(2)}, u32[]{:S(2)}) collective-permute-start(s32[2,512]{1,0:T(2,128)S(1)} %get-tuple-element.111), channel_id=1, source_target_pairs={{16,0},{32,16},{48,32},{64,48},{80,64},{96,80},{112,96},{128,112},... | collective-permute-start | bytes 12296 | tf_op jit(solution)/shard_map/ppermute | solution.py:33
  14.6 1.2 collective-permute-start.2
  17.2 5.1 %collective-permute-start.3 = (s32[514]{0:T(1024)S(1)}, s32[514]{0:T(1024)S(1)}, u32[]{:S(2)}, u32[]{:S(2)}) collective-permute-start(s32[514]{0:T(1024)S(1)} %fusion.73), channel_id=1, source_target_pairs={{0,32},{16,48},{32,0},{48,16},{64,96},{80,112},{96,64},{112,80},{1... | collective-permute-start | bytes 6176 | tf_op jit(solution)/shard_map/ppermute | solution.py:44
  22.3 3.6 %collective-permute-start.4 = (s32[514]{0:T(1024)S(1)}, s32[514]{0:T(1024)S(1)}, u32[]{:S(2)}, u32[]{:S(2)}) collective-permute-start(s32[514]{0:T(1024)S(1)} %add.282), channel_id=1, source_target_pairs={{0,64},{16,80},{32,96},{48,112},{64,0},{80,16},{96,32},{112,48},{1... | collective-permute-start | bytes 6176 | tf_op jit(solution)/shard_map/ppermute | solution.py:44
  25.9 5.1 %collective-permute-start.5 = (s32[514]{0:T(1024)S(1)}, s32[514]{0:T(1024)S(1)}, u32[]{:S(2)}, u32[]{:S(2)}) collective-permute-start(s32[514]{0:T(1024)S(1)} %add.283), channel_id=1, source_target_pairs={{0,128},{16,144},{32,160},{48,176},{64,192},{80,208},{96,224},{112... | collective-permute-start | bytes 6176 | tf_op jit(solution)/shard_map/ppermute | solution.py:44
  33.4 13.0 %collective-permute-start.7 = (bf16[2,512,256]{2,1,0:T(8,128)(2,1)S(1)}, bf16[2,512,256]{2,1,0:T(8,128)(2,1)S(1)}, u32[]{:S(2)}, u32[]{:S(2)}) collective-permute-start(bf16[2,512,256]{2,1,0:T(8,128)(2,1)S(1)} %get-tuple-element.61), channel_id=1, source_target_pairs={{0,16},{16,32},{32,48},{48,64},{64,80},{80,96},{96,112},{112,128},... | collective-permute-start | bytes 1572872 | tf_op jit(solution)/shard_map/ppermute | solution.py:31
  35.3 12.8 %collective-permute-start.8 = (bf16[2,512,256]{2,1,0:T(8,128)(2,1)S(1)}, bf16[2,512,256]{2,1,0:T(8,128)(2,1)S(1)}, u32[]{:S(2)}, u32[]{:S(2)}) collective-permute-start(bf16[2,512,256]{2,1,0:T(8,128)(2,1)S(1)} %get-tuple-element.62), channel_id=1, source_target_pairs={{16,0},{32,16},{48,32},{64,48},{80,64},{96,80},{112,96},{128,112},... | collective-permute-start | bytes 1572872 | tf_op jit(solution)/shard_map/ppermute | solution.py:33
  60.0 45.7 %collective-permute-start.9 = (bf16[2048,256]{1,0:T(8,128)(2,1)S(1)}, bf16[2048,256]{1,0:T(8,128)(2,1)S(1)}, u32[]{:S(2)}, u32[]{:S(2)}) collective-permute-start(bf16[2048,256]{1,0:T(8,128)(2,1)S(1)} %bitcast.10), channel_id=1, source_target_pairs={{0,1},{1,9},{9,8},{8,0},{2,3},{3,11},{11,10},{10,2},{4,5},{5,13},{... | collective-permute-start | bytes 3145736 | tf_op jit(solution)/shard_map/ppermute | solution.py:64
  61.3 45.4 %collective-permute-start.11 = (bf16[2048,256]{1,0:T(8,128)(2,1)S(1)}, bf16[2048,256]{1,0:T(8,128)(2,1)S(1)}, u32[]{:S(2)}, u32[]{:S(2)}) collective-permute-start(bf16[2048,256]{1,0:T(8,128)(2,1)S(1)} %bitcast.11), channel_id=1, source_target_pairs={{1,0},{9,1},{8,9},{0,8},{3,2},{11,3},{10,11},{2,10},{5,4},{13,5},{... | collective-permute-start | bytes 3145736 | tf_op jit(solution)/shard_map/ppermute | solution.py:65
  62.1 76.3 %collective-permute-start.6 = (bf16[2048,256]{1,0:T(8,128)(2,1)S(1)}, bf16[2048,256]{1,0:T(8,128)(2,1)}, u32[]{:S(2)}, u32[]{:S(2)}) collective-permute-start(bf16[2048,256]{1,0:T(8,128)(2,1)S(1)} %bitcast.6), channel_id=1, source_target_pairs={{0,2},{2,4},{4,6},{6,0},{1,3},{3,5},{5,7},{7,1},{8,10},{10,12},{12... | collective-permute-start | bytes 3145736 | tf_op jit(solution)/shard_map/ppermute | solution.py:64
  65.3 74.2 %collective-permute-start.20 = (bf16[2048,256]{1,0:T(8,128)(2,1)S(1)}, bf16[2048,256]{1,0:T(8,128)(2,1)}, u32[]{:S(2)}, u32[]{:S(2)}) collective-permute-start(bf16[2048,256]{1,0:T(8,128)(2,1)S(1)} %bitcast.7), channel_id=1, source_target_pairs={{2,0},{4,2},{6,4},{0,6},{3,1},{5,3},{7,5},{1,7},{10,8},{12,10},{14... | collective-permute-start | bytes 3145736 | tf_op jit(solution)/shard_map/ppermute | solution.py:65
  105.7 2.3 copy-start.1
  105.7 44.5 %collective-permute-start.10 = (bf16[1024,256]{1,0:T(8,128)(2,1)S(1)}, bf16[1024,256]{1,0:T(8,128)(2,1)}, u32[]{:S(2)}, u32[]{:S(2)}) collective-permute-start(bf16[1024,256]{1,0:T(8,128)(2,1)S(1)} %slice.421), channel_id=1, source_target_pairs={{0,1},{1,9},{9,8},{8,0},{2,3},{3,11},{11,10},{10,2},{4,5},{5,13},{... | collective-permute-start | bytes 1572872 | tf_op jit(solution)/shard_map/ppermute | solution.py:67
  106.7 1.3 copy-start.4
  106.7 43.7 %collective-permute-start.12 = (bf16[1024,256]{1,0:T(8,128)(2,1)S(1)}, bf16[1024,256]{1,0:T(8,128)(2,1)}, u32[]{:S(2)}, u32[]{:S(2)}) collective-permute-start(bf16[1024,256]{1,0:T(8,128)(2,1)S(1)} %slice.422), channel_id=1, source_target_pairs={{1,0},{9,1},{8,9},{0,8},{3,2},{11,3},{10,11},{2,10},{5,4},{13,5},{... | collective-permute-start | bytes 1572872 | tf_op jit(solution)/shard_map/ppermute | solution.py:68
  108.0 42.4 %copy-start.2 = (bf16[2048,256]{1,0:T(8,128)(2,1)S(1)}, bf16[2048,256]{1,0:T(8,128)(2,1)}, u32[]{:S(2)}) copy-start(bf16[2048,256]{1,0:T(8,128)(2,1)} %copy-done.1) | copy-start | bytes 3145732
  108.0 42.4 %copy-start.5 = (bf16[2048,256]{1,0:T(8,128)(2,1)S(1)}, bf16[2048,256]{1,0:T(8,128)(2,1)}, u32[]{:S(2)}) copy-start(bf16[2048,256]{1,0:T(8,128)(2,1)} %copy-done.4) | copy-start | bytes 3145732
  139.5 29.6 %collective-permute-start.19 = (bf16[1024,256]{1,0:T(8,128)(2,1)S(1)}, bf16[1024,256]{1,0:T(8,128)(2,1)S(1)}, u32[]{:S(2)}, u32[]{:S(2)}) collective-permute-start(bf16[1024,256]{1,0:T(8,128)(2,1)S(1)} %slice.423), channel_id=1, source_target_pairs={{0,2},{2,4},{4,6},{6,0},{1,3},{3,5},{5,7},{7,1},{8,10},{10,12},{12... | collective-permute-start | bytes 1572872 | tf_op jit(solution)/shard_map/ppermute | solution.py:67
  140.6 28.4 %collective-permute-start.21 = (bf16[1024,256]{1,0:T(8,128)(2,1)S(1)}, bf16[1024,256]{1,0:T(8,128)(2,1)S(1)}, u32[]{:S(2)}, u32[]{:S(2)}) collective-permute-start(bf16[1024,256]{1,0:T(8,128)(2,1)S(1)} %slice.424), channel_id=1, source_target_pairs={{2,0},{4,2},{6,4},{0,6},{3,1},{5,3},{7,5},{1,7},{10,8},{12,10},{14... | collective-permute-start | bytes 1572872 | tf_op jit(solution)/shard_map/ppermute | solution.py:68
  155.5 20.2 %collective-permute-start.13 = (f32[256,1024]{1,0:T(8,128)S(1)}, f32[256,1024]{1,0:T(8,128)}, u32[]{:S(2)}, u32[]{:S(2)}) collective-permute-start(f32[256,1024]{1,0:T(8,128)S(1)} %fusion.11), channel_id=1, source_target_pairs={{0,16},{16,0},{1,17},{17,1},{2,18},{18,2},{3,19},{19,3},{4,20},{20... | collective-permute-start | bytes 3145736 | tf_op jit(solution)/shard_map/ppermute | solution.py:172
  169.1 6.2 %copy-start.7 = (bf16[2048,256]{1,0:T(8,128)(2,1)}, bf16[2048,256]{1,0:T(8,128)(2,1)S(1)}, u32[]{:S(2)}) copy-start(bf16[2048,256]{1,0:T(8,128)(2,1)S(1)} %constant_dynamic-update-slice_fusion) | copy-start | bytes 3145732
  175.3 9.6 %collective-permute-start.22 = (f32[256,1024]{1,0:T(8,128)}, f32[256,1024]{1,0:T(8,128)}, u32[]{:S(2)}, u32[]{:S(2)}) collective-permute-start(f32[256,1024]{1,0:T(8,128)} %fusion.8), channel_id=1, source_target_pairs={{0,16},{16,0},{1,17},{17,1},{2,18},{18,2},{3,19},{19,3},{4,20},{20... | collective-permute-start | bytes 3145736 | tf_op jit(solution)/shard_map/ppermute | solution.py:172
  175.6 9.3 %copy-start.3 = (bf16[2048,256]{1,0:T(8,128)(2,1)S(1)}, bf16[2048,256]{1,0:T(8,128)(2,1)}, u32[]{:S(2)}) copy-start(bf16[2048,256]{1,0:T(8,128)(2,1)} %copy-done.1) | copy-start | bytes 3145732
  175.7 9.3 %copy-start.6 = (bf16[2048,256]{1,0:T(8,128)(2,1)S(1)}, bf16[2048,256]{1,0:T(8,128)(2,1)}, u32[]{:S(2)}) copy-start(bf16[2048,256]{1,0:T(8,128)(2,1)} %copy-done.4) | copy-start | bytes 3145732
  175.7 9.3 %copy-start.8 = (bf16[2048,256]{1,0:T(8,128)(2,1)S(1)}, bf16[2048,256]{1,0:T(8,128)(2,1)}, u32[]{:S(2)}) copy-start(bf16[2048,256]{1,0:T(8,128)(2,1)} %copy-done.7) | copy-start | bytes 3145732
  180.1 14.0 %collective-permute-start.14 = (f32[256,256]{1,0:T(8,128)S(1)}, f32[256,256]{1,0:T(8,128)S(1)}, u32[]{:S(2)}, u32[]{:S(2)}) collective-permute-start(f32[256,256]{1,0:T(8,128)S(1)} %get-tuple-element.55), channel_id=1, source_target_pairs={{0,64},{64,128},{128,192},{192,0},{1,65},{65,129},{129,193},{193,1... | collective-permute-start | bytes 786440 | tf_op jit(solution)/shard_map/ppermute | solution.py:176
  181.6 12.5 %collective-permute-start.15 = (f32[256,256]{1,0:T(8,128)}, f32[256,256]{1,0:T(8,128)}, u32[]{:S(2)}, u32[]{:S(2)}) collective-permute-start(f32[256,256]{1,0:T(8,128)} %get-tuple-element.57), channel_id=1, source_target_pairs={{0,128},{64,192},{128,0},{192,64},{1,129},{65,193},{129,1},{193,65... | collective-permute-start | bytes 786440 | tf_op jit(solution)/shard_map/ppermute | solution.py:176
  182.3 15.0 %collective-permute-start.16 = (f32[256,256]{1,0:T(8,128)}, f32[256,256]{1,0:T(8,128)}, u32[]{:S(2)}, u32[]{:S(2)}) collective-permute-start(f32[256,256]{1,0:T(8,128)} %get-tuple-element.56), channel_id=1, source_target_pairs={{0,192},{64,0},{128,64},{192,128},{1,193},{65,1},{129,65},{193,129... | collective-permute-start | bytes 786440 | tf_op jit(solution)/shard_map/ppermute | solution.py:176
  190.6 10.2 %collective-permute-start.23 = (f32[256,256]{1,0:T(8,128)}, f32[256,256]{1,0:T(8,128)S(1)}, u32[]{:S(2)}, u32[]{:S(2)}) collective-permute-start(f32[256,256]{1,0:T(8,128)} %get-tuple-element.58), channel_id=1, source_target_pairs={{0,64},{64,128},{128,192},{192,0},{1,65},{65,129},{129,193},{193,1... | collective-permute-start | bytes 786440 | tf_op jit(solution)/shard_map/ppermute | solution.py:176
  190.6 13.3 %collective-permute-start.24 = (f32[256,256]{1,0:T(8,128)S(1)}, f32[256,256]{1,0:T(8,128)S(1)}, u32[]{:S(2)}, u32[]{:S(2)}) collective-permute-start(f32[256,256]{1,0:T(8,128)S(1)} %get-tuple-element.60), channel_id=1, source_target_pairs={{0,128},{64,192},{128,0},{192,64},{1,129},{65,193},{129,1},{193,65... | collective-permute-start | bytes 786440 | tf_op jit(solution)/shard_map/ppermute | solution.py:176
  194.1 13.8 %collective-permute-start.25 = (f32[256,256]{1,0:T(8,128)S(1)}, f32[256,256]{1,0:T(8,128)}, u32[]{:S(2)}, u32[]{:S(2)}) collective-permute-start(f32[256,256]{1,0:T(8,128)S(1)} %get-tuple-element.59), channel_id=1, source_target_pairs={{0,192},{64,0},{128,64},{192,128},{1,193},{65,1},{129,65},{193,129... | collective-permute-start | bytes 786440 | tf_op jit(solution)/shard_map/ppermute | solution.py:176
  198.4 17.6 %collective-permute-start.17 = (f32[256,256]{1,0:T(8,128)S(1)}, f32[256,256]{1,0:T(8,128)S(1)}, u32[]{:S(2)}, u32[]{:S(2)}) collective-permute-start(f32[256,256]{1,0:T(8,128)S(1)} %add_add_fusion.1), channel_id=1, source_target_pairs={{0,0},{1,17},{2,34},{3,51},{4,68},{5,85},{6,102},{7,119},{8,136},{... | collective-permute-start | bytes 786440 | tf_op jit(solution)/shard_map/ppermute | solution.py:184
  200.1 15.9 %collective-permute-start.18 = (f32[256,256]{1,0:T(8,128)S(1)}, f32[256,256]{1,0:T(8,128)S(1)}, u32[]{:S(2)}, u32[]{:S(2)}) collective-permute-start(f32[256,256]{1,0:T(8,128)S(1)} %add_add_fusion.1), channel_id=1, source_target_pairs={{32,0},{33,17},{34,34},{35,51},{36,68},{37,85},{38,102},{39,119},{... | collective-permute-start | bytes 786440 | tf_op jit(solution)/shard_map/ppermute | solution.py:184
  208.9 18.0 %collective-permute-start.26 = (f32[256,256]{1,0:T(8,128)S(1)}, f32[256,256]{1,0:T(8,128)S(1)}, u32[]{:S(2)}, u32[]{:S(2)}) collective-permute-start(f32[256,256]{1,0:T(8,128)S(1)} %add_add_fusion), channel_id=1, source_target_pairs={{0,4},{1,21},{2,38},{3,55},{4,64},{5,81},{6,98},{7,115},{8,140},{9... | collective-permute-start | bytes 786440 | tf_op jit(solution)/shard_map/ppermute | solution.py:184
  213.2 24.7 %collective-permute-start.27 = (f32[256,256]{1,0:T(8,128)S(1)}, f32[256,256]{1,0:T(8,128)S(1)}, u32[]{:S(2)}, u32[]{:S(2)}) collective-permute-start(f32[256,256]{1,0:T(8,128)S(1)} %add_add_fusion), channel_id=1, source_target_pairs={{32,4},{33,21},{34,38},{35,55},{36,64},{37,81},{38,98},{39,115},{4... | collective-permute-start | bytes 786440 | tf_op jit(solution)/shard_map/ppermute | solution.py:184

commit v10 on v8

--- a/solution.py
+++ b/solution.py
@@ -57,6 +57,14 @@
     return upper * base + (c0 & (base - 1)).astype(jnp.float32)
 
 
+def ring_shift(block, axes, ring):
+    size = len(ring)
+    out = [block]
+    for t in range(1, size):
+        out.append(lax.ppermute(block, axes, [(ring[k], ring[(k + t) % size]) for k in range(size)]))
+    return out
+
+
 def ring_gather(block, axes, ring):
     size = len(ring)
     fwd = [(ring[k], ring[(k + 1) % size]) for k in range(size)]
@@ -142,7 +150,7 @@
     bin_count = row_count * col_count
     flat_z = zscores.reshape(bin_count, panel_width)
     flat_lag = lagged.reshape(bin_count, panel_width)
-    z_parts = ring_gather(flat_z, ROW_AXES, ROW_RING)
+    z_parts = ring_shift(flat_z, ROW_AXES, ROW_RING)
     lag_parts = ring_gather(flat_lag, COL_AXES, COL_RING)
     z_cat = jnp.concatenate(z_parts, axis=1)
     sizes = {a: lax.axis_size(a) for a in GENE_AXES}

time: 214 us -> 250 us (1.17)
  waiting for transfers between devices: 81.6 us -> 126 us
  starting transfers between devices: 82.4 us -> 78.4 us
  matrix products: 18.9 us -> 15.8 us
    ppermute x0 -> x3, waiting for transfers between devices: none -> 53.1 us  [ring_shift(): lax.ppermute(block, axes, [(ring[k], ring[(k + t) % size]) for k in range...]
    ppermute x2 -> x1, waiting for transfers between devices: 40.1 us -> 29.3 us  [ring_gather(): prev = lax.ppermute(block, axes, fwd)]
    ppermute x2, starting transfers between devices: 10.3 us -> 0.15 us  [shards(): mine = keep + lax.ppermute(give, 'sc', [(0, 1), (1, 0)])]
    ppermute x4, starting transfers between devices: 18.6 us -> 26.7 us  [shards(): received.append(lax.ppermute(total, every, perm))]
    ppermute x2, starting transfers between devices: 12.1 us -> 7.97 us  [padded(): lax.ppermute(head, axis, [((i + 1) % count, i) for i in range(ends)])]
    ppermute x2, waiting for transfers between devices: 2.92 us -> 6.29 us  [padded(): lax.ppermute(tail, axis, [(i, (i + 1) % count) for i in range(ends)])]
    ppermute x0 -> x3, starting transfers between devices: none -> 3.2 us  [ring_shift(): lax.ppermute(block, axes, [(ring[k], ring[(k + t) % size]) for k in range...]
    ppermute x2, waiting for transfers between devices: 1.71 us -> 4.31 us  [padded(): lax.ppermute(head, axis, [((i + 1) % count, i) for i in range(ends)])]
  transfers between devices with their start and end apart: 28 -> 27, of which waited for: 15 -> 14; matrix products, arithmetic and copies ran while one was open for 18% -> 9% of each run, Pallas kernels for 0% -> 0%
where the time goes in v10:
time: 250 us; the launch traced here: 249 us
  waiting for transfers between devices  126 us (50%)
  starting transfers between devices  78.4 us (31%)
  other arithmetic  23.7 us (9%)
  matrix products  15.8 us (6%)
  local copies, waits for them, and re-layouts  3.54 us (1%)
    ppermute x3, waiting for transfers between devices, ring_shift(): lax.ppermute(block, axes, [(ring[k], ring[(k + t) % size]) for k in range...  53.1 us
    ppermute x1, waiting for transfers between devices, ring_gather(): prev = lax.ppermute(block, axes, fwd)  29.3 us
    ppermute x4, starting transfers between devices, shards(): received.append(lax.ppermute(total, every, perm))  26.7 us
    ppermute x1, starting transfers between devices, ring_gather(): far_lo = lax.ppermute(prev[:half], axes, fwd)  14.8 us
    convert_element_type x1, other arithmetic, shards(): lagged = lagged_sum.astype(jnp.bfloat16)  11.1 us
    ppermute x4, waiting for transfers between devices, allreduce_sum(): lax.ppermute(vector, axes, [(i, i ^ step) for i in range(count)])  11 us
    ppermute x6, waiting for transfers between devices, shards(): lax.ppermute(sent, 'sx', [(k, (k + d) % ring_x) for k in range(ring_x)])  9.07 us
    dot_general x2, matrix products, shards(): lax.dot_general(z_cat, give_lag, contract_bins, preferred_element_type=jn...  8.82 us
  transfers between devices with their start and end apart: 27, of which 14 were waited for; matrix products, arithmetic and copies ran while one was open for 9% of the time, Pallas kernels for 0%

profile of v10, /device:TPU:6, one launch (start us, length us, event | category | flops | bytes accessed | tf_op | source)
XLA Modules:
  0.0 248.9 jit_solution(8544389791388143013)
XLA Ops:
  0.0 1.5 fusion.79
  1.5 1.9 collective-permute-start
  3.5 6.0 %collective-permute-start.1 = (s32[2,512]{1,0:T(2,128)S(1)}, s32[2,512]{1,0:T(2,128)S(1)}, u32[]{:S(2)}, u32[]{:S(2)}) collective-permute-start(s32[2,512]{1,0:T(2,128)S(1)} %get-tuple-element.111), channel_id=1, source_target_pairs={{16,0},{32,16},{48,32},{64,48},{80,64},{96,80},{112,96},{128,112},... | collective-permute-start | bytes 12296 | tf_op jit(solution)/shard_map/ppermute | solution.py:33
  9.5 0.7 broadcast_compare_fusion
  10.2 1.8 select_reduce_fusion
  12.0 0.1 add_select_fusion
  12.1 0.2 broadcast_select_fusion.19
  12.3 0.1 fusion.74
  12.4 0.1 broadcast_select_fusion.8
  12.5 0.8 fusion.69
  13.3 1.3 pad_add_fusion.1
  14.6 1.2 collective-permute-start.2
  15.8 0.8 collective-permute-done.2
  16.7 1.3 fusion.73
  18.0 1.5 collective-permute-start.3
  19.5 3.6 %collective-permute-done.3 = s32[514]{0:T(1024)S(1)} collective-permute-done((s32[514]{0:T(1024)S(1)}, s32[514]{0:T(1024)S(1)}, u32[]{:S(2)}, u32[]{:S(2)}) %collective-permute-start.3) | collective-permute-done | bytes 2088 | tf_op jit(solution)/shard_map/ppermute | solution.py:44
  23.1 0.8 collective-permute-start.4
  24.0 2.8 %collective-permute-done.4 = s32[514]{0:T(1024)S(1)} collective-permute-done((s32[514]{0:T(1024)S(1)}, s32[514]{0:T(1024)S(1)}, u32[]{:S(2)}, u32[]{:S(2)}) %collective-permute-start.4) | collective-permute-done | bytes 2088 | tf_op jit(solution)/shard_map/ppermute | solution.py:44
  26.8 1.4 collective-permute-start.5
  28.1 3.7 %collective-permute-done.5 = s32[514]{0:T(1024)S(1)} collective-permute-done((s32[514]{0:T(1024)S(1)}, s32[514]{0:T(1024)S(1)}, u32[]{:S(2)}, u32[]{:S(2)}) %collective-permute-start.5) | collective-permute-done | bytes 2088 | tf_op jit(solution)/shard_map/ppermute | solution.py:44
  31.9 0.6 fusion.81
  33.2 0.7 convert_divide_fusion
  33.8 0.4 divide_convert_fusion
  34.2 0.1 fusion.78
  34.3 1.9 collective-permute-start.10
  36.2 2.4 collective-permute-start.9
  38.6 4.3 %collective-permute-done.10 = bf16[2,512,256]{2,1,0:T(8,128)(2,1)S(1)} collective-permute-done((bf16[2,512,256]{2,1,0:T(8,128)(2,1)S(1)}, bf16[2,512,256]{2,1,0:T(8,128)(2,1)S(1)}, u32[]{:S(2)}, u32[]{:S(2)}) %collective-permute-start.10) | collective-permute-done | bytes 524320 | tf_op jit(solution)/shard_map/ppermute | solution.py:33
  42.9 6.3 %collective-permute-done.9 = bf16[2,512,256]{2,1,0:T(8,128)(2,1)S(1)} collective-permute-done((bf16[2,512,256]{2,1,0:T(8,128)(2,1)S(1)}, bf16[2,512,256]{2,1,0:T(8,128)(2,1)S(1)}, u32[]{:S(2)}, u32[]{:S(2)}) %collective-permute-start.9) | collective-permute-done | bytes 524320 | tf_op jit(solution)/shard_map/ppermute | solution.py:31
  49.2 0.7 fusion.5
  50.0 11.1 %add_convert_fusion = bf16[4,512,256]{2,1,0:T(8,128)(2,1)S(1)} fusion(bf16[4,512,256]{2,1,0:T(8,128)(2,1)S(1)} %divide_convert_fusion, bf16[2,512,256]{2,1,0:T(8,128)(2,1)S(1)} %collective-permute-done.10, bf16[2,512,256]{2,1,0:T(8,128)(2,1)S(1)} %collective-permute-done.9, bf16[8,516,256]{2,1,0:T(8,128)(2,1)S(1)} %fusion.5, ...), kind=kLoop, calls=%fused_computation.9 | loop fusion | flops 39845888 | bytes 24313856 | tf_op jit(solution)/shard_map/convert_element_type | solution.py:149
  61.1 3.3 %collective-permute-start.11 = (bf16[2048,256]{1,0:T(8,128)(2,1)S(1)}, bf16[2048,256]{1,0:T(8,128)(2,1)}, u32[]{:S(2)}, u32[]{:S(2)}) collective-permute-start(bf16[2048,256]{1,0:T(8,128)(2,1)S(1)} %bitcast.13), channel_id=1, source_target_pairs={{0,2},{2,4},{4,6},{6,0},{1,3},{3,5},{5,7},{7,1},{8,10},{10,12},{12... | collective-permute-start | bytes 3145736 | tf_op jit(solution)/shard_map/ppermute | solution.py:72
  64.4 3.1 %collective-permute-start.19 = (bf16[2048,256]{1,0:T(8,128)(2,1)S(1)}, bf16[2048,256]{1,0:T(8,128)(2,1)S(1)}, u32[]{:S(2)}, u32[]{:S(2)}) collective-permute-start(bf16[2048,256]{1,0:T(8,128)(2,1)S(1)} %bitcast.14), channel_id=1, source_target_pairs={{2,0},{4,2},{6,4},{0,6},{3,1},{5,3},{7,5},{1,7},{10,8},{12,10},{14... | collective-permute-start | bytes 3145736 | tf_op jit(solution)/shard_map/ppermute | solution.py:73
  67.6 1.0 collective-permute-start.6
  68.6 1.2 collective-permute-start.7
  69.7 1.0 collective-permute-start.8
  70.8 29.3 %collective-permute-done.11 = bf16[2048,256]{1,0:T(8,128)(2,1)} collective-permute-done((bf16[2048,256]{1,0:T(8,128)(2,1)S(1)}, bf16[2048,256]{1,0:T(8,128)(2,1)}, u32[]{:S(2)}, u32[]{:S(2)}) %collective-permute-start.11) | collective-permute-done | bytes 1048608 | tf_op jit(solution)/shard_map/ppermute | solution.py:72
  100.1 1.1 slice.413
  101.1 14.8 %collective-permute-start.18 = (bf16[1024,256]{1,0:T(8,128)(2,1)S(1)}, bf16[1024,256]{1,0:T(8,128)(2,1)S(1)}, u32[]{:S(2)}, u32[]{:S(2)}) collective-permute-start(bf16[1024,256]{1,0:T(8,128)(2,1)S(1)} %slice.413), channel_id=1, source_target_pairs={{0,2},{2,4},{4,6},{6,0},{1,3},{3,5},{5,7},{7,1},{8,10},{10,12},{12... | collective-permute-start | bytes 1572872 | tf_op jit(solution)/shard_map/ppermute | solution.py:75
  116.0 2.3 collective-permute-start.20
  118.3 25.9 %collective-permute-done.6 = bf16[2048,256]{1,0:T(8,128)(2,1)} collective-permute-done((bf16[2048,256]{1,0:T(8,128)(2,1)S(1)}, bf16[2048,256]{1,0:T(8,128)(2,1)}, u32[]{:S(2)}, u32[]{:S(2)}) %collective-permute-start.6) | collective-permute-done | bytes 1048608 | tf_op jit(solution)/shard_map/ppermute | solution.py:64
  144.2 27.2 %collective-permute-done.7 = bf16[2048,256]{1,0:T(8,128)(2,1)} collective-permute-done((bf16[2048,256]{1,0:T(8,128)(2,1)S(1)}, bf16[2048,256]{1,0:T(8,128)(2,1)}, u32[]{:S(2)}, u32[]{:S(2)}) %collective-permute-start.7) | collective-permute-done | bytes 1048608 | tf_op jit(solution)/shard_map/ppermute | solution.py:64
  171.4 4.5 %fusion.11 = f32[1024,256]{1,0:T(8,128)} fusion(bf16[2048,256]{1,0:T(8,128)(2,1)} %collective-permute-done.11, bf16[2048,256]{1,0:T(8,128)(2,1)S(1)} %bitcast.15, pred[]{:T(512)S(6)} %eq.111, bf16[2048,256]{1,0:T(8,128)(2,1)} %collective-permute-done.8, bf16[2048,256]{1,0:T(8,128)(2,1)} %collective-permute-done.7, ...), kind=kOutput, calls=%fused_computation.26 | convolution fusion | flops 1091043328 | bytes 7340033 | tf_op jit(solution)/shard_map/dot_general | solution.py:179
  175.9 5.2 %collective-permute-done.18 = bf16[1024,256]{1,0:T(8,128)(2,1)S(1)} collective-permute-done((bf16[1024,256]{1,0:T(8,128)(2,1)S(1)}, bf16[1024,256]{1,0:T(8,128)(2,1)S(1)}, u32[]{:S(2)}, u32[]{:S(2)}) %collective-permute-start.18) | collective-permute-done | bytes 524320 | tf_op jit(solution)/shard_map/ppermute | solution.py:75
  181.2 4.4 %fusion.8 = f32[1024,256]{1,0:T(8,128)} fusion(bf16[2048,256]{1,0:T(8,128)(2,1)S(1)} %collective-permute-done.19, bf16[2048,256]{1,0:T(8,128)(2,1)S(1)} %constant_dynamic-update-slice_fusion, pred[]{:T(512)S(6)} %eq.111, bf16[2048,256]{1,0:T(8,128)(2,1)} %collective-permute-done.8, bf16[2048,256]{1,0:T(8,128)(2,1)} %collective-permute-done.7, ...), kind=kOutput, calls=%fused_computation.23 | convolution fusion | flops 1091043328 | bytes 7340033 | tf_op jit(solution)/shard_map/dot_general | solution.py:179
  185.6 0.1 collective-permute-start.21
  185.7 3.6 %convolution_add_fusion.1 = f32[1024,256]{1,0:T(8,128)S(1)} fusion(f32[1024,256]{1,0:T(8,128)} %collective-permute-done.12, bf16[2048,256]{1,0:T(8,128)(2,1)S(1)} %bitcast.16, bf16[2048,256]{1,0:T(8,128)(2,1)} %collective-permute-done.11, pred[]{:T(512)S(6)} %eq.111, bf16[2048,256]{1,0:T(8,128)(2,1)} %collective-permute-done.8, ...), kind=kOutput, calls=%fused_computation.18 | convolution fusion | flops 1091305472 | bytes 8388609 | tf_op jit(solution)/shard_map/dot_general | solution.py:178
  189.3 0.9 constant_dynamic-slice_fusion.5
  190.2 2.8 %collective-permute-start.14 = (f32[256,256]{1,0:T(8,128)}, f32[256,256]{1,0:T(8,128)}, u32[]{:S(2)}, u32[]{:S(2)}) collective-permute-start(f32[256,256]{1,0:T(8,128)} %get-tuple-element.57), channel_id=1, source_target_pairs={{0,128},{64,192},{128,0},{192,64},{1,129},{65,193},{129,1},{193,65... | collective-permute-start | bytes 786440 | tf_op jit(solution)/shard_map/ppermute | solution.py:184
  193.1 3.4 %convolution_add_fusion = f32[1024,256]{1,0:T(8,128)S(1)} fusion(f32[1024,256]{1,0:T(8,128)} %collective-permute-done.21, bf16[2048,256]{1,0:T(8,128)(2,1)S(1)} %copy-done.4, bf16[2048,256]{1,0:T(8,128)(2,1)S(1)} %copy-done.2, pred[]{:T(512)S(6)} %eq.111, bf16[2048,256]{1,0:T(8,128)(2,1)} %collective-permute-done.8, ...), kind=kOutput, calls=%fused_computation.17 | convolution fusion | flops 1091305472 | bytes 8388609 | tf_op jit(solution)/shard_map/dot_general | solution.py:178
  196.5 0.8 constant_dynamic-slice_fusion.2
  197.3 3.2 %collective-permute-start.22 = (f32[256,256]{1,0:T(8,128)}, f32[256,256]{1,0:T(8,128)S(1)}, u32[]{:S(2)}, u32[]{:S(2)}) collective-permute-start(f32[256,256]{1,0:T(8,128)} %get-tuple-element.58), channel_id=1, source_target_pairs={{0,64},{64,128},{128,192},{192,0},{1,65},{65,129},{129,193},{193,1... | collective-permute-start | bytes 786440 | tf_op jit(solution)/shard_map/ppermute | solution.py:184
  200.5 0.1 collective-permute-start.23
  200.6 1.4 collective-permute-start.24
  202.0 4.9 %collective-permute-done.15 = f32[256,256]{1,0:T(8,128)} collective-permute-done((f32[256,256]{1,0:T(8,128)}, f32[256,256]{1,0:T(8,128)}, u32[]{:S(2)}, u32[]{:S(2)}) %collective-permute-start.15) | collective-permute-done | bytes 262176 | tf_op jit(solution)/shard_map/ppermute | solution.py:184
  206.9 1.1 add_add_fusion.1
  208.0 4.9 %collective-permute-start.16 = (f32[256,256]{1,0:T(8,128)S(1)}, f32[256,256]{1,0:T(8,128)S(1)}, u32[]{:S(2)}, u32[]{:S(2)}) collective-permute-start(f32[256,256]{1,0:T(8,128)S(1)} %add_add_fusion.1), channel_id=1, source_target_pairs={{0,0},{1,17},{2,34},{3,51},{4,68},{5,85},{6,102},{7,119},{8,136},{... | collective-permute-start | bytes 786440 | tf_op jit(solution)/shard_map/ppermute | solution.py:192
  213.0 0.7 collective-permute-start.17
  213.7 4.1 %collective-permute-done.24 = f32[256,256]{1,0:T(8,128)} collective-permute-done((f32[256,256]{1,0:T(8,128)S(1)}, f32[256,256]{1,0:T(8,128)}, u32[]{:S(2)}, u32[]{:S(2)}) %collective-permute-start.24) | collective-permute-done | bytes 262176 | tf_op jit(solution)/shard_map/ppermute | solution.py:184
  217.8 1.0 add_add_fusion
  218.8 19.8 %collective-permute-start.25 = (f32[256,256]{1,0:T(8,128)S(1)}, f32[256,256]{1,0:T(8,128)S(1)}, u32[]{:S(2)}, u32[]{:S(2)}) collective-permute-start(f32[256,256]{1,0:T(8,128)S(1)} %add_add_fusion), channel_id=1, source_target_pairs={{0,64},{1,81},{2,98},{3,115},{4,4},{5,21},{6,38},{7,55},{8,200},{9... | collective-permute-start | bytes 786440 | tf_op jit(solution)/shard_map/ppermute | solution.py:192
  238.6 1.3 collective-permute-start.26
  240.6 1.9 collective-permute-done.25
  242.5 5.6 %collective-permute-done.26 = f32[256,256]{1,0:T(8,128)S(1)} collective-permute-done((f32[256,256]{1,0:T(8,128)S(1)}, f32[256,256]{1,0:T(8,128)S(1)}, u32[]{:S(2)}, u32[]{:S(2)}) %collective-permute-start.26) | collective-permute-done | bytes 262176 | tf_op jit(solution)/shard_map/ppermute | solution.py:192
  248.1 0.8 add_divide_fusion
  (38 shorter events, 0.2 us)
Async XLA Ops:
  0.0 12.5 %copy-start.6 = (s32[4,512]{1,0:T(4,128)S(1)}, s32[4,512]{1,0:T(4,128)}, u32[]{:S(2)}) copy-start(s32[4,512]{1,0:T(4,128)} %param.4) | copy-start | bytes 24580
  0.0 12.1 %copy-start.5 = (s32[4,512]{1,0:T(4,128)S(1)}, s32[4,512]{1,0:T(4,128)}, u32[]{:S(2)}) copy-start(s32[4,512]{1,0:T(4,128)} %param.5) | copy-start | bytes 24580
  0.0 33.8 %copy-start = (s32[4,512,256]{2,1,0:T(8,128)S(1)}, s32[4,512,256]{2,1,0:T(8,128)}, u32[]{:S(2)}) copy-start(s32[4,512,256]{2,1,0:T(8,128)} %param.3) | copy-start | bytes 6291460
  1.5 10.5 %collective-permute-start = (s32[2,512]{1,0:T(2,128)S(1)}, s32[2,512]{1,0:T(2,128)S(1)}, u32[]{:S(2)}, u32[]{:S(2)}) collective-permute-start(s32[2,512]{1,0:T(2,128)S(1)} %get-tuple-element.110), channel_id=1, source_target_pairs={{0,16},{16,32},{32,48},{48,64},{64,80},{80,96},{96,112},{112,128},... | collective-permute-start | bytes 12296 | tf_op jit(solution)/shard_map/ppermute | solution.py:31
  3.5 8.6 %collective-permute-start.1 = (s32[2,512]{1,0:T(2,128)S(1)}, s32[2,512]{1,0:T(2,128)S(1)}, u32[]{:S(2)}, u32[]{:S(2)}) collective-permute-start(s32[2,512]{1,0:T(2,128)S(1)} %get-tuple-element.111), channel_id=1, source_target_pairs={{16,0},{32,16},{48,32},{64,48},{80,64},{96,80},{112,96},{128,112},... | collective-permute-start | bytes 12296 | tf_op jit(solution)/shard_map/ppermute | solution.py:33
  14.6 2.0 collective-permute-start.2
  18.0 5.1 %collective-permute-start.3 = (s32[514]{0:T(1024)S(1)}, s32[514]{0:T(1024)S(1)}, u32[]{:S(2)}, u32[]{:S(2)}) collective-permute-start(s32[514]{0:T(1024)S(1)} %fusion.73), channel_id=1, source_target_pairs={{0,32},{16,48},{32,0},{48,16},{64,96},{80,112},{96,64},{112,80},{1... | collective-permute-start | bytes 6176 | tf_op jit(solution)/shard_map/ppermute | solution.py:44
  23.1 3.6 %collective-permute-start.4 = (s32[514]{0:T(1024)S(1)}, s32[514]{0:T(1024)S(1)}, u32[]{:S(2)}, u32[]{:S(2)}) collective-permute-start(s32[514]{0:T(1024)S(1)} %add.282), channel_id=1, source_target_pairs={{0,64},{16,80},{32,96},{48,112},{64,0},{80,16},{96,32},{112,48},{1... | collective-permute-start | bytes 6176 | tf_op jit(solution)/shard_map/ppermute | solution.py:44
  26.8 5.1 %collective-permute-start.5 = (s32[514]{0:T(1024)S(1)}, s32[514]{0:T(1024)S(1)}, u32[]{:S(2)}, u32[]{:S(2)}) collective-permute-start(s32[514]{0:T(1024)S(1)} %add.283), channel_id=1, source_target_pairs={{0,128},{16,144},{32,160},{48,176},{64,192},{80,208},{96,224},{112... | collective-permute-start | bytes 6176 | tf_op jit(solution)/shard_map/ppermute | solution.py:44
  34.3 8.6 %collective-permute-start.10 = (bf16[2,512,256]{2,1,0:T(8,128)(2,1)S(1)}, bf16[2,512,256]{2,1,0:T(8,128)(2,1)S(1)}, u32[]{:S(2)}, u32[]{:S(2)}) collective-permute-start(bf16[2,512,256]{2,1,0:T(8,128)(2,1)S(1)} %get-tuple-element.62), channel_id=1, source_target_pairs={{16,0},{32,16},{48,32},{64,48},{80,64},{96,80},{112,96},{128,112},... | collective-permute-start | bytes 1572872 | tf_op jit(solution)/shard_map/ppermute | solution.py:33
  36.2 13.0 %collective-permute-start.9 = (bf16[2,512,256]{2,1,0:T(8,128)(2,1)S(1)}, bf16[2,512,256]{2,1,0:T(8,128)(2,1)S(1)}, u32[]{:S(2)}, u32[]{:S(2)}) collective-permute-start(bf16[2,512,256]{2,1,0:T(8,128)(2,1)S(1)} %get-tuple-element.61), channel_id=1, source_target_pairs={{0,16},{16,32},{32,48},{48,64},{64,80},{80,96},{96,112},{112,128},... | collective-permute-start | bytes 1572872 | tf_op jit(solution)/shard_map/ppermute | solution.py:31
  61.1 39.0 %collective-permute-start.11 = (bf16[2048,256]{1,0:T(8,128)(2,1)S(1)}, bf16[2048,256]{1,0:T(8,128)(2,1)}, u32[]{:S(2)}, u32[]{:S(2)}) collective-permute-start(bf16[2048,256]{1,0:T(8,128)(2,1)S(1)} %bitcast.13), channel_id=1, source_target_pairs={{0,2},{2,4},{4,6},{6,0},{1,3},{3,5},{5,7},{7,1},{8,10},{10,12},{12... | collective-permute-start | bytes 3145736 | tf_op jit(solution)/shard_map/ppermute | solution.py:72
  64.4 51.5 %collective-permute-start.19 = (bf16[2048,256]{1,0:T(8,128)(2,1)S(1)}, bf16[2048,256]{1,0:T(8,128)(2,1)S(1)}, u32[]{:S(2)}, u32[]{:S(2)}) collective-permute-start(bf16[2048,256]{1,0:T(8,128)(2,1)S(1)} %bitcast.14), channel_id=1, source_target_pairs={{2,0},{4,2},{6,4},{0,6},{3,1},{5,3},{7,5},{1,7},{10,8},{12,10},{14... | collective-permute-start | bytes 3145736 | tf_op jit(solution)/shard_map/ppermute | solution.py:73
  67.6 76.7 %collective-permute-start.6 = (bf16[2048,256]{1,0:T(8,128)(2,1)S(1)}, bf16[2048,256]{1,0:T(8,128)(2,1)}, u32[]{:S(2)}, u32[]{:S(2)}) collective-permute-start(bf16[2048,256]{1,0:T(8,128)(2,1)S(1)} %bitcast.6), channel_id=1, source_target_pairs={{0,1},{1,9},{9,8},{8,0},{2,3},{3,11},{11,10},{10,2},{4,5},{5,13},{... | collective-permute-start | bytes 3145736 | tf_op jit(solution)/shard_map/ppermute | solution.py:64
  68.6 102.8 %collective-permute-start.7 = (bf16[2048,256]{1,0:T(8,128)(2,1)S(1)}, bf16[2048,256]{1,0:T(8,128)(2,1)}, u32[]{:S(2)}, u32[]{:S(2)}) collective-permute-start(bf16[2048,256]{1,0:T(8,128)(2,1)S(1)} %bitcast.7), channel_id=1, source_target_pairs={{0,9},{1,8},{9,0},{8,1},{2,11},{3,10},{11,2},{10,3},{4,13},{5,12},... | collective-permute-start | bytes 3145736 | tf_op jit(solution)/shard_map/ppermute | solution.py:64
  69.7 101.7 %collective-permute-start.8 = (bf16[2048,256]{1,0:T(8,128)(2,1)S(1)}, bf16[2048,256]{1,0:T(8,128)(2,1)}, u32[]{:S(2)}, u32[]{:S(2)}) collective-permute-start(bf16[2048,256]{1,0:T(8,128)(2,1)S(1)} %bitcast.8), channel_id=1, source_target_pairs={{0,8},{1,0},{9,1},{8,9},{2,10},{3,2},{11,3},{10,11},{4,12},{5,4},{... | collective-permute-start | bytes 3145736 | tf_op jit(solution)/shard_map/ppermute | solution.py:64
  101.1 80.0 %collective-permute-start.18 = (bf16[1024,256]{1,0:T(8,128)(2,1)S(1)}, bf16[1024,256]{1,0:T(8,128)(2,1)S(1)}, u32[]{:S(2)}, u32[]{:S(2)}) collective-permute-start(bf16[1024,256]{1,0:T(8,128)(2,1)S(1)} %slice.413), channel_id=1, source_target_pairs={{0,2},{2,4},{4,6},{6,0},{1,3},{3,5},{5,7},{7,1},{8,10},{10,12},{12... | collective-permute-start | bytes 1572872 | tf_op jit(solution)/shard_map/ppermute | solution.py:75
  116.0 65.2 %copy-start.1 = (bf16[2048,256]{1,0:T(8,128)(2,1)}, bf16[2048,256]{1,0:T(8,128)(2,1)S(1)}, u32[]{:S(2)}) copy-start(bf16[2048,256]{1,0:T(8,128)(2,1)S(1)} %collective-permute-done.19) | copy-start | bytes 3145732
  116.0 65.1 %collective-permute-start.20 = (bf16[1024,256]{1,0:T(8,128)(2,1)S(1)}, bf16[1024,256]{1,0:T(8,128)(2,1)S(1)}, u32[]{:S(2)}, u32[]{:S(2)}) collective-permute-start(bf16[1024,256]{1,0:T(8,128)(2,1)S(1)} %slice.414), channel_id=1, source_target_pairs={{2,0},{4,2},{6,4},{0,6},{3,1},{5,3},{7,5},{1,7},{10,8},{12,10},{14... | collective-permute-start | bytes 1572872 | tf_op jit(solution)/shard_map/ppermute | solution.py:76
  175.9 9.8 %collective-permute-start.12 = (f32[1024,256]{1,0:T(8,128)}, f32[1024,256]{1,0:T(8,128)}, u32[]{:S(2)}, u32[]{:S(2)}) collective-permute-start(f32[1024,256]{1,0:T(8,128)} %fusion.11), channel_id=1, source_target_pairs={{0,16},{16,0},{1,17},{17,1},{2,18},{18,2},{3,19},{19,3},{4,20},{20... | collective-permute-start | bytes 3145736 | tf_op jit(solution)/shard_map/ppermute | solution.py:180
  181.2 4.4 %copy-start.3 = (bf16[2048,256]{1,0:T(8,128)(2,1)}, bf16[2048,256]{1,0:T(8,128)(2,1)S(1)}, u32[]{:S(2)}) copy-start(bf16[2048,256]{1,0:T(8,128)(2,1)S(1)} %constant_dynamic-update-slice_fusion) | copy-start | bytes 3145732
  185.6 7.5 %collective-permute-start.21 = (f32[1024,256]{1,0:T(8,128)}, f32[1024,256]{1,0:T(8,128)}, u32[]{:S(2)}, u32[]{:S(2)}) collective-permute-start(f32[1024,256]{1,0:T(8,128)} %fusion.8), channel_id=1, source_target_pairs={{0,16},{16,0},{1,17},{17,1},{2,18},{18,2},{3,19},{19,3},{4,20},{20... | collective-permute-start | bytes 3145736 | tf_op jit(solution)/shard_map/ppermute | solution.py:180
  185.7 7.4 %copy-start.2 = (bf16[2048,256]{1,0:T(8,128)(2,1)S(1)}, bf16[2048,256]{1,0:T(8,128)(2,1)}, u32[]{:S(2)}) copy-start(bf16[2048,256]{1,0:T(8,128)(2,1)} %copy-done.1) | copy-start | bytes 3145732
  185.7 7.4 %copy-start.4 = (bf16[2048,256]{1,0:T(8,128)(2,1)S(1)}, bf16[2048,256]{1,0:T(8,128)(2,1)}, u32[]{:S(2)}) copy-start(bf16[2048,256]{1,0:T(8,128)(2,1)} %copy-done.3) | copy-start | bytes 3145732
  190.2 10.4 %collective-permute-start.13 = (f32[256,256]{1,0:T(8,128)S(1)}, f32[256,256]{1,0:T(8,128)S(1)}, u32[]{:S(2)}, u32[]{:S(2)}) collective-permute-start(f32[256,256]{1,0:T(8,128)S(1)} %get-tuple-element.55), channel_id=1, source_target_pairs={{0,64},{64,128},{128,192},{192,0},{1,65},{65,129},{129,193},{193,1... | collective-permute-start | bytes 786440 | tf_op jit(solution)/shard_map/ppermute | solution.py:184
  190.2 11.8 %collective-permute-start.14 = (f32[256,256]{1,0:T(8,128)}, f32[256,256]{1,0:T(8,128)}, u32[]{:S(2)}, u32[]{:S(2)}) collective-permute-start(f32[256,256]{1,0:T(8,128)} %get-tuple-element.57), channel_id=1, source_target_pairs={{0,128},{64,192},{128,0},{192,64},{1,129},{65,193},{129,1},{193,65... | collective-permute-start | bytes 786440 | tf_op jit(solution)/shard_map/ppermute | solution.py:184
  193.1 13.9 %collective-permute-start.15 = (f32[256,256]{1,0:T(8,128)}, f32[256,256]{1,0:T(8,128)}, u32[]{:S(2)}, u32[]{:S(2)}) collective-permute-start(f32[256,256]{1,0:T(8,128)} %get-tuple-element.56), channel_id=1, source_target_pairs={{0,192},{64,0},{128,64},{192,128},{1,193},{65,1},{129,65},{193,129... | collective-permute-start | bytes 786440 | tf_op jit(solution)/shard_map/ppermute | solution.py:184
  197.3 16.4 %collective-permute-start.22 = (f32[256,256]{1,0:T(8,128)}, f32[256,256]{1,0:T(8,128)S(1)}, u32[]{:S(2)}, u32[]{:S(2)}) collective-permute-start(f32[256,256]{1,0:T(8,128)} %get-tuple-element.58), channel_id=1, source_target_pairs={{0,64},{64,128},{128,192},{192,0},{1,65},{65,129},{129,193},{193,1... | collective-permute-start | bytes 786440 | tf_op jit(solution)/shard_map/ppermute | solution.py:184
  200.5 13.2 %collective-permute-start.23 = (f32[256,256]{1,0:T(8,128)S(1)}, f32[256,256]{1,0:T(8,128)S(1)}, u32[]{:S(2)}, u32[]{:S(2)}) collective-permute-start(f32[256,256]{1,0:T(8,128)S(1)} %get-tuple-element.60), channel_id=1, source_target_pairs={{0,128},{64,192},{128,0},{192,64},{1,129},{65,193},{129,1},{193,65... | collective-permute-start | bytes 786440 | tf_op jit(solution)/shard_map/ppermute | solution.py:184
  200.6 17.2 %collective-permute-start.24 = (f32[256,256]{1,0:T(8,128)S(1)}, f32[256,256]{1,0:T(8,128)}, u32[]{:S(2)}, u32[]{:S(2)}) collective-permute-start(f32[256,256]{1,0:T(8,128)S(1)} %get-tuple-element.59), channel_id=1, source_target_pairs={{0,192},{64,0},{128,64},{192,128},{1,193},{65,1},{129,65},{193,129... | collective-permute-start | bytes 786440 | tf_op jit(solution)/shard_map/ppermute | solution.py:184
  208.0 32.5 %collective-permute-start.16 = (f32[256,256]{1,0:T(8,128)S(1)}, f32[256,256]{1,0:T(8,128)S(1)}, u32[]{:S(2)}, u32[]{:S(2)}) collective-permute-start(f32[256,256]{1,0:T(8,128)S(1)} %add_add_fusion.1), channel_id=1, source_target_pairs={{0,0},{1,17},{2,34},{3,51},{4,68},{5,85},{6,102},{7,119},{8,136},{... | collective-permute-start | bytes 786440 | tf_op jit(solution)/shard_map/ppermute | solution.py:192
  213.0 27.6 %collective-permute-start.17 = (f32[256,256]{1,0:T(8,128)S(1)}, f32[256,256]{1,0:T(8,128)S(1)}, u32[]{:S(2)}, u32[]{:S(2)}) collective-permute-start(f32[256,256]{1,0:T(8,128)S(1)} %add_add_fusion.1), channel_id=1, source_target_pairs={{32,0},{33,17},{34,34},{35,51},{36,68},{37,85},{38,102},{39,119},{... | collective-permute-start | bytes 786440 | tf_op jit(solution)/shard_map/ppermute | solution.py:192
  218.8 23.7 %collective-permute-start.25 = (f32[256,256]{1,0:T(8,128)S(1)}, f32[256,256]{1,0:T(8,128)S(1)}, u32[]{:S(2)}, u32[]{:S(2)}) collective-permute-start(f32[256,256]{1,0:T(8,128)S(1)} %add_add_fusion), channel_id=1, source_target_pairs={{0,64},{1,81},{2,98},{3,115},{4,4},{5,21},{6,38},{7,55},{8,200},{9... | collective-permute-start | bytes 786440 | tf_op jit(solution)/shard_map/ppermute | solution.py:192
  238.6 9.5 %collective-permute-start.26 = (f32[256,256]{1,0:T(8,128)S(1)}, f32[256,256]{1,0:T(8,128)S(1)}, u32[]{:S(2)}, u32[]{:S(2)}) collective-permute-start(f32[256,256]{1,0:T(8,128)S(1)} %add_add_fusion), channel_id=1, source_target_pairs={{32,64},{33,81},{34,98},{35,115},{36,4},{37,21},{38,38},{39,55},{4... | collective-permute-start | bytes 786440 | tf_op jit(solution)/shard_map/ppermute | solution.py:192

commit v11 on v8

--- a/solution.py
+++ b/solution.py
@@ -66,7 +66,7 @@
     half = block.shape[0] // 2
     far_lo = lax.ppermute(prev[:half], axes, fwd)
     far_hi = lax.ppermute(nxt[half:], axes, bwd)
-    return [block, prev, jnp.concatenate([far_lo, far_hi], axis=0), nxt]
+    return [block, prev, (far_lo, far_hi), nxt]
 
 
 def unravel(index, sizes):
@@ -143,8 +143,20 @@
     flat_z = zscores.reshape(bin_count, panel_width)
     flat_lag = lagged.reshape(bin_count, panel_width)
     z_parts = ring_gather(flat_z, ROW_AXES, ROW_RING)
+    z_parts[2] = jnp.concatenate(z_parts[2], axis=0)
     lag_parts = ring_gather(flat_lag, COL_AXES, COL_RING)
     z_cat = jnp.concatenate(z_parts, axis=1)
+    half_bins = bin_count // 2
+    lag_halves = [
+        part if isinstance(part, tuple) else (part[:half_bins], part[half_bins:]) for part in lag_parts
+    ]
+    z_halves = (z_cat[:half_bins], z_cat[half_bins:])
+
+    def product(pick):
+        return sum(
+            lax.dot_general(z_halves[h], pick(h), contract_bins, preferred_element_type=jnp.float32)
+            for h in range(2)
+        )
     sizes = {a: lax.axis_size(a) for a in GENE_AXES}
     rings = {ROW_AXES: ROW_RING, COL_AXES: COL_RING}
 
@@ -165,10 +177,9 @@
     every = SPOT_AXES + GENE_AXES
     received = []
     for phase in range(2):
-        keep_lag = jnp.where(core == 0, lag_parts[2 * phase], lag_parts[2 * phase + 1])
-        give_lag = jnp.where(core == 0, lag_parts[2 * phase + 1], lag_parts[2 * phase])
-        keep = lax.dot_general(z_cat, keep_lag, contract_bins, preferred_element_type=jnp.float32)
-        give = lax.dot_general(z_cat, give_lag, contract_bins, preferred_element_type=jnp.float32)
+        first, second = lag_halves[2 * phase], lag_halves[2 * phase + 1]
+        keep = product(lambda h: jnp.where(core == 0, first[h], second[h]))
+        give = product(lambda h: jnp.where(core == 0, second[h], first[h]))
         mine = keep + lax.ppermute(give, "sc", [(0, 1), (1, 0)])
         total = lax.dynamic_slice_in_dim(mine, pos_x * panel_width, panel_width, 0)
         for d in range(1, ring_x):

time: 214 us -> 214 us (level)
  the two profiles are of different devices: /device:TPU:6 before, /device:TPU:123 now
where the time goes in v11:
time: 214 us
  waiting for transfers between devices  88.3 us (41%)
  starting transfers between devices  73 us (34%)
  other arithmetic  36.4 us (17%)
  matrix products  10.3 us (5%)
  local copies, waits for them, and re-layouts  3.9 us (2%)
    ppermute x2, waiting for transfers between devices, ring_gather(): nxt = lax.ppermute(block, axes, bwd)  41 us
    ppermute x4, starting transfers between devices, shards(): received.append(lax.ppermute(total, every, perm))  30.6 us
    ppermute x2, waiting for transfers between devices, ring_gather(): prev = lax.ppermute(block, axes, fwd)  16 us
    ppermute x4, waiting for transfers between devices, shards(): received.append(lax.ppermute(total, every, perm))  11.4 us
    concatenate x1, other arithmetic, shards(): z_cat = jnp.concatenate(z_parts, axis=1)  11.2 us
    convert_element_type x1, other arithmetic, shards(): lagged = lagged_sum.astype(jnp.bfloat16)  11.1 us
    dot_general x8, matrix products, product(): lax.dot_general(z_halves[h], pick(h), contract_bins, preferred_element_ty...  10.3 us
    ppermute x2, starting transfers between devices, padded(): lax.ppermute(tail, axis, [(i, (i + 1) % count) for i in range(ends)])  10 us
  transfers between devices with their start and end apart: 28, of which 15 were waited for; matrix products, arithmetic and copies ran while one was open for 20% of the time, Pallas kernels for 0%

profile of v11, /device:TPU:123, one launch (start us, length us, event | category | flops | bytes accessed | tf_op | source)
XLA Modules:
  0.0 213.7 jit_solution(3207444273778678943)
XLA Ops:
  0.0 1.5 fusion.96
  1.5 2.6 %collective-permute-start.1 = (s32[2,512]{1,0:T(2,128)S(1)}, s32[2,512]{1,0:T(2,128)S(1)}, u32[]{:S(2)}, u32[]{:S(2)}) collective-permute-start(s32[2,512]{1,0:T(2,128)S(1)} %get-tuple-element.120), channel_id=1, source_target_pairs={{16,0},{32,16},{48,32},{64,48},{80,64},{96,80},{112,96},{128,112},... | collective-permute-start | bytes 12296 | tf_op jit(solution)/shard_map/ppermute | solution.py:33
  4.1 5.4 %collective-permute-start = (s32[2,512]{1,0:T(2,128)S(1)}, s32[2,512]{1,0:T(2,128)S(1)}, u32[]{:S(2)}, u32[]{:S(2)}) collective-permute-start(s32[2,512]{1,0:T(2,128)S(1)} %get-tuple-element.119), channel_id=1, source_target_pairs={{0,16},{16,32},{32,48},{48,64},{64,80},{80,96},{96,112},{112,128},... | collective-permute-start | bytes 12296 | tf_op jit(solution)/shard_map/ppermute | solution.py:31
  9.5 0.7 broadcast_compare_fusion
  10.2 1.8 select_reduce_fusion
  12.5 0.9 fusion.83
  13.4 1.4 pad_add_fusion.1
  14.7 1.2 collective-permute-done.2
  15.9 1.4 fusion.87
  17.3 1.8 collective-permute-start.3
  19.0 2.2 %collective-permute-done.3 = s32[514]{0:T(1024)S(1)} collective-permute-done((s32[514]{0:T(1024)S(1)}, s32[514]{0:T(1024)S(1)}, u32[]{:S(2)}, u32[]{:S(2)}) %collective-permute-start.3) | collective-permute-done | bytes 2088 | tf_op jit(solution)/shard_map/ppermute | solution.py:44
  21.3 0.3 collective-permute-start.4
  21.5 2.2 %collective-permute-done.4 = s32[514]{0:T(1024)S(1)} collective-permute-done((s32[514]{0:T(1024)S(1)}, s32[514]{0:T(1024)S(1)}, u32[]{:S(2)}, u32[]{:S(2)}) %collective-permute-start.4) | collective-permute-done | bytes 2088 | tf_op jit(solution)/shard_map/ppermute | solution.py:44
  23.7 0.9 collective-permute-start.5
  24.6 3.0 %collective-permute-done.5 = s32[514]{0:T(1024)S(1)} collective-permute-done((s32[514]{0:T(1024)S(1)}, s32[514]{0:T(1024)S(1)}, u32[]{:S(2)}, u32[]{:S(2)}) %collective-permute-start.5) | collective-permute-done | bytes 2088 | tf_op jit(solution)/shard_map/ppermute | solution.py:44
  27.7 0.7 fusion.98
  29.0 0.7 convert_divide_fusion
  29.7 0.4 divide_convert_fusion
  30.1 5.5 %collective-permute-start.11 = (bf16[2,512,256]{2,1,0:T(8,128)(2,1)S(1)}, bf16[2,512,256]{2,1,0:T(8,128)(2,1)S(1)}, u32[]{:S(2)}, u32[]{:S(2)}) collective-permute-start(bf16[2,512,256]{2,1,0:T(8,128)(2,1)S(1)} %get-tuple-element.71), channel_id=1, source_target_pairs={{16,0},{32,16},{48,32},{64,48},{80,64},{96,80},{112,96},{128,112},... | collective-permute-start | bytes 1572872 | tf_op jit(solution)/shard_map/ppermute | solution.py:33
  35.7 4.7 %collective-permute-start.10 = (bf16[2,512,256]{2,1,0:T(8,128)(2,1)S(1)}, bf16[2,512,256]{2,1,0:T(8,128)(2,1)S(1)}, u32[]{:S(2)}, u32[]{:S(2)}) collective-permute-start(bf16[2,512,256]{2,1,0:T(8,128)(2,1)S(1)} %get-tuple-element.70), channel_id=1, source_target_pairs={{0,16},{16,32},{32,48},{48,64},{64,80},{80,96},{96,112},{112,128},... | collective-permute-start | bytes 1572872 | tf_op jit(solution)/shard_map/ppermute | solution.py:31
  40.3 0.5 collective-permute-start.8
  40.9 1.0 collective-permute-start.6
  41.9 3.5 %collective-permute-done.11 = bf16[2,512,256]{2,1,0:T(8,128)(2,1)S(1)} collective-permute-done((bf16[2,512,256]{2,1,0:T(8,128)(2,1)S(1)}, bf16[2,512,256]{2,1,0:T(8,128)(2,1)S(1)}, u32[]{:S(2)}, u32[]{:S(2)}) %collective-permute-start.11) | collective-permute-done | bytes 524320 | tf_op jit(solution)/shard_map/ppermute | solution.py:33
  45.3 1.1 collective-permute-done.10
  46.5 0.7 fusion.5
  47.2 11.1 %add_convert_fusion = bf16[4,512,256]{2,1,0:T(8,128)(2,1)S(1)} fusion(bf16[4,512,256]{2,1,0:T(8,128)(2,1)S(1)} %divide_convert_fusion, bf16[2,512,256]{2,1,0:T(8,128)(2,1)S(1)} %collective-permute-done.11, bf16[2,512,256]{2,1,0:T(8,128)(2,1)S(1)} %collective-permute-done.10, bf16[8,516,256]{2,1,0:T(8,128)(2,1)S(1)} %fusion.5, ...), kind=kLoop, calls=%fused_computation.9 | loop fusion | flops 39845888 | bytes 24313856 | tf_op jit(solution)/shard_map/convert_element_type | solution.py:141
  58.4 3.6 %collective-permute-start.12 = (bf16[2048,256]{1,0:T(8,128)(2,1)S(1)}, bf16[2048,256]{1,0:T(8,128)(2,1)}, u32[]{:S(2)}, u32[]{:S(2)}) collective-permute-start(bf16[2048,256]{1,0:T(8,128)(2,1)S(1)} %bitcast.20), channel_id=1, source_target_pairs={{0,2},{2,4},{4,6},{6,0},{1,3},{3,5},{5,7},{7,1},{8,10},{10,12},{12... | collective-permute-start | bytes 3145736 | tf_op jit(solution)/shard_map/ppermute | solution.py:64
  62.0 7.0 %collective-permute-done.8 = bf16[2048,256]{1,0:T(8,128)(2,1)S(1)} collective-permute-done((bf16[2048,256]{1,0:T(8,128)(2,1)S(1)}, bf16[2048,256]{1,0:T(8,128)(2,1)S(1)}, u32[]{:S(2)}, u32[]{:S(2)}) %collective-permute-start.8) | collective-permute-done | bytes 1048608 | tf_op jit(solution)/shard_map/ppermute | solution.py:65
  69.0 2.3 %collective-permute-start.9 = (bf16[1024,256]{1,0:T(8,128)(2,1)S(1)}, bf16[1024,256]{1,0:T(8,128)(2,1)S(1)}, u32[]{:S(2)}, u32[]{:S(2)}) collective-permute-start(bf16[1024,256]{1,0:T(8,128)(2,1)S(1)} %slice.430), channel_id=1, source_target_pairs={{1,0},{9,1},{8,9},{0,8},{3,2},{11,3},{10,11},{2,10},{5,4},{13,5},{... | collective-permute-start | bytes 1572872 | tf_op jit(solution)/shard_map/ppermute | solution.py:68
  71.3 16.0 %collective-permute-done.6 = bf16[2048,256]{1,0:T(8,128)(2,1)} collective-permute-done((bf16[2048,256]{1,0:T(8,128)(2,1)S(1)}, bf16[2048,256]{1,0:T(8,128)(2,1)}, u32[]{:S(2)}, u32[]{:S(2)}) %collective-permute-start.6) | collective-permute-done | bytes 1048608 | tf_op jit(solution)/shard_map/ppermute | solution.py:64
  87.3 1.1 slice.429
  88.4 2.4 %collective-permute-start.7 = (bf16[1024,256]{1,0:T(8,128)(2,1)S(1)}, bf16[1024,256]{1,0:T(8,128)(2,1)S(1)}, u32[]{:S(2)}, u32[]{:S(2)}) collective-permute-start(bf16[1024,256]{1,0:T(8,128)(2,1)S(1)} %slice.429), channel_id=1, source_target_pairs={{0,1},{1,9},{9,8},{8,0},{2,3},{3,11},{11,10},{10,2},{4,5},{5,13},{... | collective-permute-start | bytes 1572872 | tf_op jit(solution)/shard_map/ppermute | solution.py:67
  90.8 34.1 %collective-permute-done.20 = bf16[2048,256]{1,0:T(8,128)(2,1)} collective-permute-done((bf16[2048,256]{1,0:T(8,128)(2,1)S(1)}, bf16[2048,256]{1,0:T(8,128)(2,1)}, u32[]{:S(2)}, u32[]{:S(2)}) %collective-permute-start.20) | collective-permute-done | bytes 1048608 | tf_op jit(solution)/shard_map/ppermute | solution.py:65
  124.9 1.1 slice.464
  126.1 1.4 bitcast_select_fusion.3
  127.5 3.8 %collective-permute-start.19 = (bf16[1024,256]{1,0:T(8,128)(2,1)S(1)}, bf16[1024,256]{1,0:T(8,128)(2,1)S(1)}, u32[]{:S(2)}, u32[]{:S(2)}) collective-permute-start(bf16[1024,256]{1,0:T(8,128)(2,1)S(1)} %get-tuple-element.62), channel_id=1, source_target_pairs={{0,2},{2,4},{4,6},{6,0},{1,3},{3,5},{5,7},{7,1},{8,10},{10,12},{12... | collective-permute-start | bytes 1572872 | tf_op jit(solution)/shard_map/ppermute | solution.py:67
  131.3 0.9 collective-permute-done.7
  132.2 11.2 %pad_maximum_fusion = bf16[2048,1024]{1,0:T(8,128)(2,1)S(1)} fusion(bf16[2048,256]{1,0:T(8,128)(2,1)S(1)} %collective-permute-done.8, bf16[1024,256]{1,0:T(8,128)(2,1)S(1)} %collective-permute-done.9, bf16[1024,256]{1,0:T(8,128)(2,1)S(1)} %collective-permute-done.7, bf16[2048,256]{1,0:T(8,128)(2,1)} %collective-permute-done.6, bf16[2048,256]{1,0:T(8,128)(2,1)S(1)} %bitcast.18), kind=kLoop, calls=%fused_computation.3 | loop fusion | flops 20971520 | bytes 8388608 | tf_op jit(solution)/shard_map/concatenate | solution.py:148
  143.4 0.7 fusion.12
  144.2 0.7 convolution_add_fusion.2
  145.0 0.8 collective-permute-done.21
  145.8 1.8 fusion.8
  147.6 1.8 convolution_add_fusion
  149.5 0.8 fusion.14
  150.3 1.8 fusion.10
  152.1 0.8 fusion.7
  153.0 0.6 collective-permute-start.16
  153.5 2.1 %collective-permute-start.15 = (f32[256,256]{1,0:T(8,128)S(1)}, f32[256,256]{1,0:T(8,128)S(1)}, u32[]{:S(2)}, u32[]{:S(2)}) collective-permute-start(f32[256,256]{1,0:T(8,128)S(1)} %get-tuple-element.61), channel_id=1, source_target_pairs={{0,128},{64,192},{128,0},{192,64},{1,129},{65,193},{129,1},{193,65... | collective-permute-start | bytes 786440 | tf_op jit(solution)/shard_map/ppermute | solution.py:187
  155.7 1.8 fusion.6
  157.5 0.8 constant_dynamic-slice_fusion.2
  158.3 1.5 collective-permute-start.25
  159.8 1.2 collective-permute-start.24
  161.0 2.1 collective-permute-start.23
  163.1 4.2 %collective-permute-done.15 = f32[256,256]{1,0:T(8,128)S(1)} collective-permute-done((f32[256,256]{1,0:T(8,128)S(1)}, f32[256,256]{1,0:T(8,128)S(1)}, u32[]{:S(2)}, u32[]{:S(2)}) %collective-permute-start.15) | collective-permute-done | bytes 262176 | tf_op jit(solution)/shard_map/ppermute | solution.py:187
  167.2 0.7 collective-permute-done.14
  168.0 1.0 add_add_fusion.1
  169.0 0.7 collective-permute-start.17
  169.7 10.6 %collective-permute-start.18 = (f32[256,256]{1,0:T(8,128)S(1)}, f32[256,256]{1,0:T(8,128)S(1)}, u32[]{:S(2)}, u32[]{:S(2)}) collective-permute-start(f32[256,256]{1,0:T(8,128)S(1)} %add_add_fusion.1), channel_id=1, source_target_pairs={{32,0},{33,17},{34,34},{35,51},{36,68},{37,85},{38,102},{39,119},{... | collective-permute-start | bytes 786440 | tf_op jit(solution)/shard_map/ppermute | solution.py:195
  180.3 1.2 add_add_fusion
  181.5 18.0 %collective-permute-start.27 = (f32[256,256]{1,0:T(8,128)S(1)}, f32[256,256]{1,0:T(8,128)S(1)}, u32[]{:S(2)}, u32[]{:S(2)}) collective-permute-start(f32[256,256]{1,0:T(8,128)S(1)} %add_add_fusion), channel_id=1, source_target_pairs={{32,64},{33,81},{34,98},{35,115},{36,4},{37,21},{38,38},{39,55},{4... | collective-permute-start | bytes 786440 | tf_op jit(solution)/shard_map/ppermute | solution.py:195
  199.5 1.3 collective-permute-start.26
  201.5 1.3 collective-permute-done.27
  202.9 10.0 %collective-permute-done.26 = f32[256,256]{1,0:T(8,128)S(1)} collective-permute-done((f32[256,256]{1,0:T(8,128)S(1)}, f32[256,256]{1,0:T(8,128)S(1)}, u32[]{:S(2)}, u32[]{:S(2)}) %collective-permute-start.26) | collective-permute-done | bytes 262176 | tf_op jit(solution)/shard_map/ppermute | solution.py:195
  212.9 0.8 add_divide_fusion
  (38 shorter events, 1.1 us)
Async XLA Ops:
  0.0 12.5 %copy-start.2 = (s32[4,512]{1,0:T(4,128)S(1)}, s32[4,512]{1,0:T(4,128)}, u32[]{:S(2)}) copy-start(s32[4,512]{1,0:T(4,128)} %param.4) | copy-start | bytes 24580
  0.0 12.1 %copy-start.1 = (s32[4,512]{1,0:T(4,128)S(1)}, s32[4,512]{1,0:T(4,128)}, u32[]{:S(2)}) copy-start(s32[4,512]{1,0:T(4,128)} %param.5) | copy-start | bytes 24580
  0.0 29.7 %copy-start = (s32[4,512,256]{2,1,0:T(8,128)S(1)}, s32[4,512,256]{2,1,0:T(8,128)}, u32[]{:S(2)}) copy-start(s32[4,512,256]{2,1,0:T(8,128)} %param.3) | copy-start | bytes 6291460
  1.5 10.5 %collective-permute-start.1 = (s32[2,512]{1,0:T(2,128)S(1)}, s32[2,512]{1,0:T(2,128)S(1)}, u32[]{:S(2)}, u32[]{:S(2)}) collective-permute-start(s32[2,512]{1,0:T(2,128)S(1)} %get-tuple-element.120), channel_id=1, source_target_pairs={{16,0},{32,16},{48,32},{64,48},{80,64},{96,80},{112,96},{128,112},... | collective-permute-start | bytes 12296 | tf_op jit(solution)/shard_map/ppermute | solution.py:33
  4.1 7.9 %collective-permute-start = (s32[2,512]{1,0:T(2,128)S(1)}, s32[2,512]{1,0:T(2,128)S(1)}, u32[]{:S(2)}, u32[]{:S(2)}) collective-permute-start(s32[2,512]{1,0:T(2,128)S(1)} %get-tuple-element.119), channel_id=1, source_target_pairs={{0,16},{16,32},{32,48},{48,64},{64,80},{80,96},{96,112},{112,128},... | collective-permute-start | bytes 12296 | tf_op jit(solution)/shard_map/ppermute | solution.py:31
  14.7 1.2 collective-permute-start.2
  17.3 4.0 %collective-permute-start.3 = (s32[514]{0:T(1024)S(1)}, s32[514]{0:T(1024)S(1)}, u32[]{:S(2)}, u32[]{:S(2)}) collective-permute-start(s32[514]{0:T(1024)S(1)} %fusion.87), channel_id=1, source_target_pairs={{0,32},{16,48},{32,0},{48,16},{64,96},{80,112},{96,64},{112,80},{1... | collective-permute-start | bytes 6176 | tf_op jit(solution)/shard_map/ppermute | solution.py:44
  21.3 2.5 %collective-permute-start.4 = (s32[514]{0:T(1024)S(1)}, s32[514]{0:T(1024)S(1)}, u32[]{:S(2)}, u32[]{:S(2)}) collective-permute-start(s32[514]{0:T(1024)S(1)} %add.294), channel_id=1, source_target_pairs={{0,64},{16,80},{32,96},{48,112},{64,0},{80,16},{96,32},{112,48},{1... | collective-permute-start | bytes 6176 | tf_op jit(solution)/shard_map/ppermute | solution.py:44
  23.7 4.0 %collective-permute-start.5 = (s32[514]{0:T(1024)S(1)}, s32[514]{0:T(1024)S(1)}, u32[]{:S(2)}, u32[]{:S(2)}) collective-permute-start(s32[514]{0:T(1024)S(1)} %add.295), channel_id=1, source_target_pairs={{0,128},{16,144},{32,160},{48,176},{64,192},{80,208},{96,224},{112... | collective-permute-start | bytes 6176 | tf_op jit(solution)/shard_map/ppermute | solution.py:44
  30.1 15.2 %collective-permute-start.11 = (bf16[2,512,256]{2,1,0:T(8,128)(2,1)S(1)}, bf16[2,512,256]{2,1,0:T(8,128)(2,1)S(1)}, u32[]{:S(2)}, u32[]{:S(2)}) collective-permute-start(bf16[2,512,256]{2,1,0:T(8,128)(2,1)S(1)} %get-tuple-element.71), channel_id=1, source_target_pairs={{16,0},{32,16},{48,32},{64,48},{80,64},{96,80},{112,96},{128,112},... | collective-permute-start | bytes 1572872 | tf_op jit(solution)/shard_map/ppermute | solution.py:33
  35.7 10.8 %collective-permute-start.10 = (bf16[2,512,256]{2,1,0:T(8,128)(2,1)S(1)}, bf16[2,512,256]{2,1,0:T(8,128)(2,1)S(1)}, u32[]{:S(2)}, u32[]{:S(2)}) collective-permute-start(bf16[2,512,256]{2,1,0:T(8,128)(2,1)S(1)} %get-tuple-element.70), channel_id=1, source_target_pairs={{0,16},{16,32},{32,48},{48,64},{64,80},{80,96},{96,112},{112,128},... | collective-permute-start | bytes 1572872 | tf_op jit(solution)/shard_map/ppermute | solution.py:31
  40.3 28.6 %collective-permute-start.8 = (bf16[2048,256]{1,0:T(8,128)(2,1)S(1)}, bf16[2048,256]{1,0:T(8,128)(2,1)S(1)}, u32[]{:S(2)}, u32[]{:S(2)}) collective-permute-start(bf16[2048,256]{1,0:T(8,128)(2,1)S(1)} %bitcast.16), channel_id=1, source_target_pairs={{1,0},{9,1},{8,9},{0,8},{3,2},{11,3},{10,11},{2,10},{5,4},{13,5},{... | collective-permute-start | bytes 3145736 | tf_op jit(solution)/shard_map/ppermute | solution.py:65
  40.9 46.5 %collective-permute-start.6 = (bf16[2048,256]{1,0:T(8,128)(2,1)S(1)}, bf16[2048,256]{1,0:T(8,128)(2,1)}, u32[]{:S(2)}, u32[]{:S(2)}) collective-permute-start(bf16[2048,256]{1,0:T(8,128)(2,1)S(1)} %bitcast.17), channel_id=1, source_target_pairs={{0,1},{1,9},{9,8},{8,0},{2,3},{3,11},{11,10},{10,2},{4,5},{5,13},{... | collective-permute-start | bytes 3145736 | tf_op jit(solution)/shard_map/ppermute | solution.py:64
  58.3 66.6 %collective-permute-start.20 = (bf16[2048,256]{1,0:T(8,128)(2,1)S(1)}, bf16[2048,256]{1,0:T(8,128)(2,1)}, u32[]{:S(2)}, u32[]{:S(2)}) collective-permute-start(bf16[2048,256]{1,0:T(8,128)(2,1)S(1)} %bitcast.19), channel_id=1, source_target_pairs={{2,0},{4,2},{6,4},{0,6},{3,1},{5,3},{7,5},{1,7},{10,8},{12,10},{14... | collective-permute-start | bytes 3145736 | tf_op jit(solution)/shard_map/ppermute | solution.py:65
  58.4 67.7 %collective-permute-start.12 = (bf16[2048,256]{1,0:T(8,128)(2,1)S(1)}, bf16[2048,256]{1,0:T(8,128)(2,1)}, u32[]{:S(2)}, u32[]{:S(2)}) collective-permute-start(bf16[2048,256]{1,0:T(8,128)(2,1)S(1)} %bitcast.20), channel_id=1, source_target_pairs={{0,2},{2,4},{4,6},{6,0},{1,3},{3,5},{5,7},{7,1},{8,10},{10,12},{12... | collective-permute-start | bytes 3145736 | tf_op jit(solution)/shard_map/ppermute | solution.py:64
  69.0 62.3 %collective-permute-start.9 = (bf16[1024,256]{1,0:T(8,128)(2,1)S(1)}, bf16[1024,256]{1,0:T(8,128)(2,1)S(1)}, u32[]{:S(2)}, u32[]{:S(2)}) collective-permute-start(bf16[1024,256]{1,0:T(8,128)(2,1)S(1)} %slice.430), channel_id=1, source_target_pairs={{1,0},{9,1},{8,9},{0,8},{3,2},{11,3},{10,11},{2,10},{5,4},{13,5},{... | collective-permute-start | bytes 1572872 | tf_op jit(solution)/shard_map/ppermute | solution.py:68
  88.4 43.9 %collective-permute-start.7 = (bf16[1024,256]{1,0:T(8,128)(2,1)S(1)}, bf16[1024,256]{1,0:T(8,128)(2,1)S(1)}, u32[]{:S(2)}, u32[]{:S(2)}) collective-permute-start(bf16[1024,256]{1,0:T(8,128)(2,1)S(1)} %slice.429), channel_id=1, source_target_pairs={{0,1},{1,9},{9,8},{8,0},{2,3},{3,11},{11,10},{10,2},{4,5},{5,13},{... | collective-permute-start | bytes 1572872 | tf_op jit(solution)/shard_map/ppermute | solution.py:67
  126.0 19.8 %collective-permute-start.21 = (bf16[1024,256]{1,0:T(8,128)(2,1)S(1)}, bf16[1024,256]{1,0:T(8,128)(2,1)S(1)}, u32[]{:S(2)}, u32[]{:S(2)}) collective-permute-start(bf16[1024,256]{1,0:T(8,128)(2,1)S(1)} %slice.464), channel_id=1, source_target_pairs={{2,0},{4,2},{6,4},{0,6},{3,1},{5,3},{7,5},{1,7},{10,8},{12,10},{14... | collective-permute-start | bytes 1572872 | tf_op jit(solution)/shard_map/ppermute | solution.py:68
  127.5 20.1 %collective-permute-start.19 = (bf16[1024,256]{1,0:T(8,128)(2,1)S(1)}, bf16[1024,256]{1,0:T(8,128)(2,1)S(1)}, u32[]{:S(2)}, u32[]{:S(2)}) collective-permute-start(bf16[1024,256]{1,0:T(8,128)(2,1)S(1)} %get-tuple-element.62), channel_id=1, source_target_pairs={{0,2},{2,4},{4,6},{6,0},{1,3},{3,5},{5,7},{7,1},{8,10},{10,12},{12... | collective-permute-start | bytes 1572872 | tf_op jit(solution)/shard_map/ppermute | solution.py:67
  144.9 7.2 %collective-permute-start.13 = (f32[1024,256]{1,0:T(8,128)S(1)}, f32[1024,256]{1,0:T(8,128)S(1)}, u32[]{:S(2)}, u32[]{:S(2)}) collective-permute-start(f32[1024,256]{1,0:T(8,128)S(1)} %convolution_add_fusion.2), channel_id=1, source_target_pairs={{0,16},{16,0},{1,17},{17,1},{2,18},{18,2},{3,19},{19,3},{4,20},{20... | collective-permute-start | bytes 3145736 | tf_op jit(solution)/shard_map/ppermute | solution.py:183
  149.4 6.2 %collective-permute-start.22 = (f32[1024,256]{1,0:T(8,128)S(1)}, f32[1024,256]{1,0:T(8,128)S(1)}, u32[]{:S(2)}, u32[]{:S(2)}) collective-permute-start(f32[1024,256]{1,0:T(8,128)S(1)} %convolution_add_fusion), channel_id=1, source_target_pairs={{0,16},{16,0},{1,17},{17,1},{2,18},{18,2},{3,19},{19,3},{4,20},{20... | collective-permute-start | bytes 3145736 | tf_op jit(solution)/shard_map/ppermute | solution.py:183
  153.0 8.0 %collective-permute-start.16 = (f32[256,256]{1,0:T(8,128)S(1)}, f32[256,256]{1,0:T(8,128)S(1)}, u32[]{:S(2)}, u32[]{:S(2)}) collective-permute-start(f32[256,256]{1,0:T(8,128)S(1)} %get-tuple-element.60), channel_id=1, source_target_pairs={{0,192},{64,0},{128,64},{192,128},{1,193},{65,1},{129,65},{193,129... | collective-permute-start | bytes 786440 | tf_op jit(solution)/shard_map/ppermute | solution.py:187
  153.5 13.7 %collective-permute-start.15 = (f32[256,256]{1,0:T(8,128)S(1)}, f32[256,256]{1,0:T(8,128)S(1)}, u32[]{:S(2)}, u32[]{:S(2)}) collective-permute-start(f32[256,256]{1,0:T(8,128)S(1)} %get-tuple-element.61), channel_id=1, source_target_pairs={{0,128},{64,192},{128,0},{192,64},{1,129},{65,193},{129,1},{193,65... | collective-permute-start | bytes 786440 | tf_op jit(solution)/shard_map/ppermute | solution.py:187
  155.7 12.3 %collective-permute-start.14 = (f32[256,256]{1,0:T(8,128)S(1)}, f32[256,256]{1,0:T(8,128)}, u32[]{:S(2)}, u32[]{:S(2)}) collective-permute-start(f32[256,256]{1,0:T(8,128)S(1)} %get-tuple-element.59), channel_id=1, source_target_pairs={{0,64},{64,128},{128,192},{192,0},{1,65},{65,129},{129,193},{193,1... | collective-permute-start | bytes 786440 | tf_op jit(solution)/shard_map/ppermute | solution.py:187
  158.3 21.9 %collective-permute-start.25 = (f32[256,256]{1,0:T(8,128)}, f32[256,256]{1,0:T(8,128)}, u32[]{:S(2)}, u32[]{:S(2)}) collective-permute-start(f32[256,256]{1,0:T(8,128)} %get-tuple-element.68), channel_id=1, source_target_pairs={{0,192},{64,0},{128,64},{192,128},{1,193},{65,1},{129,65},{193,129... | collective-permute-start | bytes 786440 | tf_op jit(solution)/shard_map/ppermute | solution.py:187
  159.8 20.4 %collective-permute-start.24 = (f32[256,256]{1,0:T(8,128)}, f32[256,256]{1,0:T(8,128)}, u32[]{:S(2)}, u32[]{:S(2)}) collective-permute-start(f32[256,256]{1,0:T(8,128)} %get-tuple-element.69), channel_id=1, source_target_pairs={{0,128},{64,192},{128,0},{192,64},{1,129},{65,193},{129,1},{193,65... | collective-permute-start | bytes 786440 | tf_op jit(solution)/shard_map/ppermute | solution.py:187
  161.0 19.3 %collective-permute-start.23 = (f32[256,256]{1,0:T(8,128)S(1)}, f32[256,256]{1,0:T(8,128)}, u32[]{:S(2)}, u32[]{:S(2)}) collective-permute-start(f32[256,256]{1,0:T(8,128)S(1)} %get-tuple-element.67), channel_id=1, source_target_pairs={{0,64},{64,128},{128,192},{192,0},{1,65},{65,129},{129,193},{193,1... | collective-permute-start | bytes 786440 | tf_op jit(solution)/shard_map/ppermute | solution.py:187
  169.0 32.5 %collective-permute-start.17 = (f32[256,256]{1,0:T(8,128)S(1)}, f32[256,256]{1,0:T(8,128)S(1)}, u32[]{:S(2)}, u32[]{:S(2)}) collective-permute-start(f32[256,256]{1,0:T(8,128)S(1)} %add_add_fusion.1), channel_id=1, source_target_pairs={{0,0},{1,17},{2,34},{3,51},{4,68},{5,85},{6,102},{7,119},{8,136},{... | collective-permute-start | bytes 786440 | tf_op jit(solution)/shard_map/ppermute | solution.py:195
  169.7 31.8 %collective-permute-start.18 = (f32[256,256]{1,0:T(8,128)S(1)}, f32[256,256]{1,0:T(8,128)S(1)}, u32[]{:S(2)}, u32[]{:S(2)}) collective-permute-start(f32[256,256]{1,0:T(8,128)S(1)} %add_add_fusion.1), channel_id=1, source_target_pairs={{32,0},{33,17},{34,34},{35,51},{36,68},{37,85},{38,102},{39,119},{... | collective-permute-start | bytes 786440 | tf_op jit(solution)/shard_map/ppermute | solution.py:195
  181.5 21.4 %collective-permute-start.27 = (f32[256,256]{1,0:T(8,128)S(1)}, f32[256,256]{1,0:T(8,128)S(1)}, u32[]{:S(2)}, u32[]{:S(2)}) collective-permute-start(f32[256,256]{1,0:T(8,128)S(1)} %add_add_fusion), channel_id=1, source_target_pairs={{32,64},{33,81},{34,98},{35,115},{36,4},{37,21},{38,38},{39,55},{4... | collective-permute-start | bytes 786440 | tf_op jit(solution)/shard_map/ppermute | solution.py:195
  199.5 13.4 %collective-permute-start.26 = (f32[256,256]{1,0:T(8,128)S(1)}, f32[256,256]{1,0:T(8,128)S(1)}, u32[]{:S(2)}, u32[]{:S(2)}) collective-permute-start(f32[256,256]{1,0:T(8,128)S(1)} %add_add_fusion), channel_id=1, source_target_pairs={{0,64},{1,81},{2,98},{3,115},{4,4},{5,21},{6,38},{7,55},{8,200},{9... | collective-permute-start | bytes 786440 | tf_op jit(solution)/shard_map/ppermute | solution.py:195

commit v12 on v8

--- a/solution.py
+++ b/solution.py
@@ -114,13 +114,14 @@
         [
             jnp.sum(inside, axis=(0, 1)),
             jnp.sum(inside * inside, axis=(0, 1)),
-            jnp.stack([jnp.sum(tissue), jnp.sum(tissue * weight_sq)]),
+            jnp.sum(tissue)[None],
         ]
     )
     total = allreduce_sum(local, SPOT_AXES)
     count_int = total[2 * panel_width]
     tissue_count = count_int.astype(jnp.float32)
-    pair_norm = total[2 * panel_width + 1].astype(jnp.float32) / 1600.0
+    pair_int = allreduce_sum(jnp.sum(tissue * weight_sq)[None], SPOT_AXES)
+    pair_norm = pair_int[0].astype(jnp.float32) / 1600.0
     gene_mean = total[:panel_width].astype(jnp.float32) / tissue_count
     variance = (
         centred_square_sum(count_int, total[:panel_width], total[panel_width : 2 * panel_width])

time: 214 us -> 220 us (1.028)
  the two profiles are of different devices: /device:TPU:6 before, /device:TPU:66 now
where the time goes in v12:
time: 220 us; the launch traced here: 219 us
  waiting for transfers between devices  107 us (49%)
  starting transfers between devices  62.4 us (28%)
  other arithmetic  22.3 us (10%)
  matrix products  18.9 us (9%)
  local copies, waits for them, and re-layouts  4.57 us (2%)
  between operations  4.41 us (2%)
    ppermute x2, waiting for transfers between devices, ring_gather(): prev = lax.ppermute(block, axes, fwd)  54 us
    ppermute x8, waiting for transfers between devices, allreduce_sum(): lax.ppermute(vector, axes, [(i, i ^ step) for i in range(count)])  23.4 us
    ppermute x8, starting transfers between devices, allreduce_sum(): lax.ppermute(vector, axes, [(i, i ^ step) for i in range(count)])  12 us
    ppermute x2, starting transfers between devices, padded(): lax.ppermute(head, axis, [((i + 1) % count, i) for i in range(ends)])  11.6 us
    ppermute x4, starting transfers between devices, shards(): received.append(lax.ppermute(total, every, perm))  11.3 us
    convert_element_type x1, other arithmetic, shards(): lagged = lagged_sum.astype(jnp.bfloat16)  11.1 us
    dot_general x2, matrix products, shards(): lax.dot_general(z_cat, give_lag, contract_bins, preferred_element_type=jn...  10.7 us
    ppermute x6, waiting for transfers between devices, shards(): lax.ppermute(sent, 'sx', [(k, (k + d) % ring_x) for k in range(ring_x)])  9.85 us
  transfers between devices with their start and end apart: 32, of which 16 were waited for; matrix products, arithmetic and copies ran while one was open for 18% of the time, Pallas kernels for 0%

profile of v12, /device:TPU:66, one launch (start us, length us, event | category | flops | bytes accessed | tf_op | source)
XLA Modules:
  0.0 219.1 jit_solution(1417488349828341553)
XLA Ops:
  0.0 0.9 broadcast_compare_fusion
  0.9 1.4 multiply_add_fusion
  2.3 1.8 select_reduce_fusion
  4.1 0.7 pad_add_fusion.1
  4.8 2.4 %collective-permute-start.8 = (s32[2,512]{1,0:T(2,128)S(1)}, s32[2,512]{1,0:T(2,128)S(1)}, u32[]{:S(2)}, u32[]{:S(2)}) collective-permute-start(s32[2,512]{1,0:T(2,128)S(1)} %get-tuple-element.42), channel_id=1, source_target_pairs={{0,16},{16,32},{32,48},{48,64},{64,80},{80,96},{96,112},{112,128},... | collective-permute-start | bytes 12296 | tf_op jit(solution)/shard_map/ppermute | solution.py:31
  7.2 5.6 %collective-permute-start.9 = (s32[2,512]{1,0:T(2,128)S(1)}, s32[2,512]{1,0:T(2,128)S(1)}, u32[]{:S(2)}, u32[]{:S(2)}) collective-permute-start(s32[2,512]{1,0:T(2,128)S(1)} %get-tuple-element.43), channel_id=1, source_target_pairs={{16,0},{32,16},{48,32},{64,48},{80,64},{96,80},{112,96},{128,112},... | collective-permute-start | bytes 12296 | tf_op jit(solution)/shard_map/ppermute | solution.py:33
  12.8 0.7 fusion.73
  13.5 2.4 %collective-permute-start.1 = (s32[513]{0:T(1024)S(1)}, s32[513]{0:T(1024)S(1)}, u32[]{:S(2)}, u32[]{:S(2)}) collective-permute-start(s32[513]{0:T(1024)S(1)} %fusion.73), channel_id=1, source_target_pairs={{0,32},{16,48},{32,0},{48,16},{64,96},{80,112},{96,64},{112,80},{1... | collective-permute-start | bytes 6164 | tf_op jit(solution)/shard_map/ppermute | solution.py:44
  16.0 0.9 fusion.69
  17.0 1.7 collective-permute-done.1
  18.7 3.6 %collective-permute-done.2 = s32[513]{0:T(1024)S(1)} collective-permute-done((s32[513]{0:T(1024)S(1)}, s32[513]{0:T(1024)S(1)}, u32[]{:S(2)}, u32[]{:S(2)}) %collective-permute-start.2) | collective-permute-done | bytes 2084 | tf_op jit(solution)/shard_map/ppermute | solution.py:44
  22.3 2.1 collective-permute-start.3
  24.4 3.0 %collective-permute-done.3 = s32[513]{0:T(1024)S(1)} collective-permute-done((s32[513]{0:T(1024)S(1)}, s32[513]{0:T(1024)S(1)}, u32[]{:S(2)}, u32[]{:S(2)}) %collective-permute-start.3) | collective-permute-done | bytes 2084 | tf_op jit(solution)/shard_map/ppermute | solution.py:44
  27.4 0.5 slice.259
  28.6 0.7 convert_divide_fusion
  29.3 0.4 divide_convert_fusion
  29.7 1.9 collective-permute-start.10
  31.7 6.0 %collective-permute-start.11 = (bf16[2,512,256]{2,1,0:T(8,128)(2,1)S(1)}, bf16[2,512,256]{2,1,0:T(8,128)(2,1)S(1)}, u32[]{:S(2)}, u32[]{:S(2)}) collective-permute-start(bf16[2,512,256]{2,1,0:T(8,128)(2,1)S(1)} %get-tuple-element.39), channel_id=1, source_target_pairs={{16,0},{32,16},{48,32},{64,48},{80,64},{96,80},{112,96},{128,112},... | collective-permute-start | bytes 1572872 | tf_op jit(solution)/shard_map/ppermute | solution.py:33
  37.8 2.0 collective-permute-start.4
  39.8 0.1 collective-permute-start.6
  39.9 2.8 %collective-permute-done.10 = bf16[2,512,256]{2,1,0:T(8,128)(2,1)S(1)} collective-permute-done((bf16[2,512,256]{2,1,0:T(8,128)(2,1)S(1)}, bf16[2,512,256]{2,1,0:T(8,128)(2,1)S(1)}, u32[]{:S(2)}, u32[]{:S(2)}) %collective-permute-start.10) | collective-permute-done | bytes 524320 | tf_op jit(solution)/shard_map/ppermute | solution.py:31
  42.7 1.7 collective-permute-done.11
  44.4 0.7 fusion.5
  45.2 11.1 %add_convert_fusion = bf16[4,512,256]{2,1,0:T(8,128)(2,1)S(1)} fusion(bf16[4,512,256]{2,1,0:T(8,128)(2,1)S(1)} %divide_convert_fusion, bf16[2,512,256]{2,1,0:T(8,128)(2,1)S(1)} %collective-permute-done.11, bf16[2,512,256]{2,1,0:T(8,128)(2,1)S(1)} %collective-permute-done.10, bf16[8,516,256]{2,1,0:T(8,128)(2,1)S(1)} %fusion.5, ...), kind=kLoop, calls=%fused_computation.9 | loop fusion | flops 39845888 | bytes 24313856 | tf_op jit(solution)/shard_map/convert_element_type | solution.py:142
  56.3 4.6 %collective-permute-start.12 = (bf16[2048,256]{1,0:T(8,128)(2,1)S(1)}, bf16[2048,256]{1,0:T(8,128)(2,1)}, u32[]{:S(2)}, u32[]{:S(2)}) collective-permute-start(bf16[2048,256]{1,0:T(8,128)(2,1)S(1)} %bitcast.12), channel_id=1, source_target_pairs={{0,2},{2,4},{4,6},{6,0},{1,3},{3,5},{5,7},{7,1},{8,10},{10,12},{12... | collective-permute-start | bytes 3145736 | tf_op jit(solution)/shard_map/ppermute | solution.py:64
  60.9 8.4 %collective-permute-done.4 = bf16[2048,256]{1,0:T(8,128)(2,1)S(1)} collective-permute-done((bf16[2048,256]{1,0:T(8,128)(2,1)S(1)}, bf16[2048,256]{1,0:T(8,128)(2,1)S(1)}, u32[]{:S(2)}, u32[]{:S(2)}) %collective-permute-start.4) | collective-permute-done | bytes 1048608 | tf_op jit(solution)/shard_map/ppermute | solution.py:64
  69.3 0.6 collective-permute-start.5
  70.0 1.6 collective-permute-start.7
  71.5 45.6 %collective-permute-done.12 = bf16[2048,256]{1,0:T(8,128)(2,1)} collective-permute-done((bf16[2048,256]{1,0:T(8,128)(2,1)S(1)}, bf16[2048,256]{1,0:T(8,128)(2,1)}, u32[]{:S(2)}, u32[]{:S(2)}) %collective-permute-start.12) | collective-permute-done | bytes 1048608 | tf_op jit(solution)/shard_map/ppermute | solution.py:64
  117.1 1.1 slice.395
  118.2 4.8 %collective-permute-start.19 = (bf16[1024,256]{1,0:T(8,128)(2,1)S(1)}, bf16[1024,256]{1,0:T(8,128)(2,1)S(1)}, u32[]{:S(2)}, u32[]{:S(2)}) collective-permute-start(bf16[1024,256]{1,0:T(8,128)(2,1)S(1)} %slice.395), channel_id=1, source_target_pairs={{0,2},{2,4},{4,6},{6,0},{1,3},{3,5},{5,7},{7,1},{8,10},{10,12},{12... | collective-permute-start | bytes 1572872 | tf_op jit(solution)/shard_map/ppermute | solution.py:67
  123.0 1.1 slice.396
  124.0 0.4 collective-permute-start.21
  124.4 3.9 %collective-permute-done.5 = bf16[1024,256]{1,0:T(8,128)(2,1)} collective-permute-done((bf16[1024,256]{1,0:T(8,128)(2,1)S(1)}, bf16[1024,256]{1,0:T(8,128)(2,1)}, u32[]{:S(2)}, u32[]{:S(2)}) %collective-permute-start.5) | collective-permute-done | bytes 524320 | tf_op jit(solution)/shard_map/ppermute | solution.py:67
  128.4 4.8 %fusion.11 = f32[1024,256]{1,0:T(8,128)S(1)} fusion(bf16[2048,256]{1,0:T(8,128)(2,1)} %collective-permute-done.12, bf16[2048,256]{1,0:T(8,128)(2,1)S(1)} %bitcast.14, pred[]{:T(512)S(6)} %eq.87, bf16[2048,256]{1,0:T(8,128)(2,1)S(1)} %copy-done.5, bf16[1024,256]{1,0:T(8,128)(2,1)} %collective-permute-done.7, bf16[1024,256]{1,0:T(8,128)(2,1)} %collective-permute-done.5, ...), kind=kOutput, calls=%fused_computation.26 | convolution fusion | flops 1095237632 | bytes 7340033 | tf_op jit(solution)/shard_map/dot_general | solution.py:172
  133.2 0.9 collective-permute-start.13
  134.0 5.5 %collective-permute-done.19 = bf16[1024,256]{1,0:T(8,128)(2,1)S(1)} collective-permute-done((bf16[1024,256]{1,0:T(8,128)(2,1)S(1)}, bf16[1024,256]{1,0:T(8,128)(2,1)S(1)}, u32[]{:S(2)}, u32[]{:S(2)}) %collective-permute-start.19) | collective-permute-done | bytes 524320 | tf_op jit(solution)/shard_map/ppermute | solution.py:67
  139.6 5.3 %collective-permute-done.21 = bf16[1024,256]{1,0:T(8,128)(2,1)S(1)} collective-permute-done((bf16[1024,256]{1,0:T(8,128)(2,1)S(1)}, bf16[1024,256]{1,0:T(8,128)(2,1)S(1)}, u32[]{:S(2)}, u32[]{:S(2)}) %collective-permute-start.21) | collective-permute-done | bytes 524320 | tf_op jit(solution)/shard_map/ppermute | solution.py:68
  144.9 5.9 %fusion.8 = f32[1024,256]{1,0:T(8,128)} fusion(bf16[2048,256]{1,0:T(8,128)(2,1)} %collective-permute-done.20, bf16[2048,256]{1,0:T(8,128)(2,1)S(1)} %constant_dynamic-update-slice_fusion, pred[]{:T(512)S(6)} %eq.87, bf16[2048,256]{1,0:T(8,128)(2,1)S(1)} %copy-done.5, bf16[1024,256]{1,0:T(8,128)(2,1)} %collective-permute-done.7, ...), kind=kOutput, calls=%fused_computation.23 | convolution fusion | flops 1095237632 | bytes 7340033 | tf_op jit(solution)/shard_map/dot_general | solution.py:172
  150.9 3.6 %convolution_add_fusion.1 = f32[1024,256]{1,0:T(8,128)S(1)} fusion(f32[1024,256]{1,0:T(8,128)} %collective-permute-done.13, bf16[2048,256]{1,0:T(8,128)(2,1)S(1)} %bitcast.15, bf16[2048,256]{1,0:T(8,128)(2,1)} %collective-permute-done.12, pred[]{:T(512)S(6)} %eq.87, bf16[2048,256]{1,0:T(8,128)(2,1)} %copy-done.4, ...), kind=kOutput, calls=%fused_computation.18 | convolution fusion | flops 1095499776 | bytes 8388609 | tf_op jit(solution)/shard_map/dot_general | solution.py:171
  154.6 0.9 constant_dynamic-slice_fusion.5
  155.4 1.5 collective-permute-start.14
  156.9 0.6 collective-permute-start.15
  157.6 2.6 %collective-permute-start.16 = (f32[256,256]{1,0:T(8,128)}, f32[256,256]{1,0:T(8,128)}, u32[]{:S(2)}, u32[]{:S(2)}) collective-permute-start(f32[256,256]{1,0:T(8,128)} %get-tuple-element.33), channel_id=1, source_target_pairs={{0,192},{64,0},{128,64},{192,128},{1,193},{65,1},{129,65},{193,129... | collective-permute-start | bytes 786440 | tf_op jit(solution)/shard_map/ppermute | solution.py:177
  160.2 4.6 %convolution_add_fusion = f32[1024,256]{1,0:T(8,128)S(1)} fusion(f32[1024,256]{1,0:T(8,128)} %collective-permute-done.22, bf16[2048,256]{1,0:T(8,128)(2,1)S(1)} %copy-done.8, bf16[2048,256]{1,0:T(8,128)(2,1)} %collective-permute-done.20, pred[]{:T(512)S(6)} %eq.87, bf16[2048,256]{1,0:T(8,128)(2,1)S(1)} %copy-done.6, ...), kind=kOutput, calls=%fused_computation.17 | convolution fusion | flops 1095499776 | bytes 8388609 | tf_op jit(solution)/shard_map/dot_general | solution.py:171
  164.8 0.8 constant_dynamic-slice_fusion.2
  165.6 3.5 %collective-permute-start.24 = (f32[256,256]{1,0:T(8,128)S(1)}, f32[256,256]{1,0:T(8,128)S(1)}, u32[]{:S(2)}, u32[]{:S(2)}) collective-permute-start(f32[256,256]{1,0:T(8,128)S(1)} %get-tuple-element.37), channel_id=1, source_target_pairs={{0,128},{64,192},{128,0},{192,64},{1,129},{65,193},{129,1},{193,65... | collective-permute-start | bytes 786440 | tf_op jit(solution)/shard_map/ppermute | solution.py:177
  169.1 3.7 %collective-permute-done.16 = f32[256,256]{1,0:T(8,128)} collective-permute-done((f32[256,256]{1,0:T(8,128)}, f32[256,256]{1,0:T(8,128)}, u32[]{:S(2)}, u32[]{:S(2)}) %collective-permute-start.16) | collective-permute-done | bytes 262176 | tf_op jit(solution)/shard_map/ppermute | solution.py:177
  172.8 1.1 add_add_fusion.1
  173.9 6.3 %collective-permute-start.17 = (f32[256,256]{1,0:T(8,128)S(1)}, f32[256,256]{1,0:T(8,128)S(1)}, u32[]{:S(2)}, u32[]{:S(2)}) collective-permute-start(f32[256,256]{1,0:T(8,128)S(1)} %add_add_fusion.1), channel_id=1, source_target_pairs={{0,0},{1,17},{2,34},{3,51},{4,68},{5,85},{6,102},{7,119},{8,136},{... | collective-permute-start | bytes 786440 | tf_op jit(solution)/shard_map/ppermute | solution.py:185
  180.2 0.7 collective-permute-start.18
  180.9 6.2 %collective-permute-done.25 = f32[256,256]{1,0:T(8,128)} collective-permute-done((f32[256,256]{1,0:T(8,128)S(1)}, f32[256,256]{1,0:T(8,128)}, u32[]{:S(2)}, u32[]{:S(2)}) %collective-permute-start.25) | collective-permute-done | bytes 262176 | tf_op jit(solution)/shard_map/ppermute | solution.py:177
  187.1 1.0 add_add_fusion
  188.1 3.0 %collective-permute-start.26 = (f32[256,256]{1,0:T(8,128)S(1)}, f32[256,256]{1,0:T(8,128)S(1)}, u32[]{:S(2)}, u32[]{:S(2)}) collective-permute-start(f32[256,256]{1,0:T(8,128)S(1)} %add_add_fusion), channel_id=1, source_target_pairs={{0,64},{1,81},{2,98},{3,115},{4,4},{5,21},{6,38},{7,55},{8,200},{9... | collective-permute-start | bytes 786440 | tf_op jit(solution)/shard_map/ppermute | solution.py:185
  191.1 1.3 collective-permute-start.27
  192.4 0.1 collective-permute-start.28
  192.5 1.2 collective-permute-done.28
  195.0 4.6 %collective-permute-start.29 = (s32[1]{0:T(128)}, s32[1]{0:T(128)}, u32[]{:S(2)}, u32[]{:S(2)}) collective-permute-start(s32[1]{0:T(128)} %add.347), channel_id=1, source_target_pairs={{0,32},{16,48},{32,0},{48,16},{64,96},{80,112},{96,64},{112,80},{1... | collective-permute-start | bytes 20 | tf_op jit(solution)/shard_map/ppermute | solution.py:44
  199.5 8.1 %collective-permute-done.29 = s32[1]{0:T(128)} collective-permute-done((s32[1]{0:T(128)}, s32[1]{0:T(128)}, u32[]{:S(2)}, u32[]{:S(2)}) %collective-permute-start.29) | collective-permute-done | bytes 36 | tf_op jit(solution)/shard_map/ppermute | solution.py:44
  208.2 1.4 collective-permute-start.30
  209.6 2.2 %collective-permute-done.30 = s32[1]{0:T(128)} collective-permute-done((s32[1]{0:T(128)}, s32[1]{0:T(128)}, u32[]{:S(2)}, u32[]{:S(2)}) %collective-permute-start.30) | collective-permute-done | bytes 36 | tf_op jit(solution)/shard_map/ppermute | solution.py:44
  212.5 1.4 collective-permute-start.31
  213.9 3.7 %collective-permute-done.31 = s32[1]{0:T(128)} collective-permute-done((s32[1]{0:T(128)}, s32[1]{0:T(128)}, u32[]{:S(2)}, u32[]{:S(2)}) %collective-permute-start.31) | collective-permute-done | bytes 36 | tf_op jit(solution)/shard_map/ppermute | solution.py:44
  218.3 0.8 add_divide_fusion
  (69 shorter events, 0.6 us)
Async XLA Ops:
  0.0 16.0 %copy-start.9 = (s32[4,512]{1,0:T(4,128)S(1)}, s32[4,512]{1,0:T(4,128)}, u32[]{:S(2)}) copy-start(s32[4,512]{1,0:T(4,128)} %param.4) | copy-start | bytes 24580
  0.0 16.0 %copy-start.10 = (s32[4,512]{1,0:T(4,128)S(1)}, s32[4,512]{1,0:T(4,128)}, u32[]{:S(2)}) copy-start(s32[4,512]{1,0:T(4,128)} %param.5) | copy-start | bytes 24580
  0.0 29.3 %copy-start = (s32[4,512,256]{2,1,0:T(8,128)S(1)}, s32[4,512,256]{2,1,0:T(8,128)}, u32[]{:S(2)}) copy-start(s32[4,512,256]{2,1,0:T(8,128)} %param.3) | copy-start | bytes 6291460
  4.7 8.1 %collective-permute-start = (s32[513]{0:T(1024)S(1)}, s32[513]{0:T(1024)S(1)}, u32[]{:S(2)}, u32[]{:S(2)}) collective-permute-start(s32[513]{0:T(1024)S(1)} %pad_add_fusion.1), channel_id=1, source_target_pairs={{0,16},{16,0},{32,48},{48,32},{64,80},{80,64},{96,112},{112,96},{1... | collective-permute-start | bytes 6164 | tf_op jit(solution)/shard_map/ppermute | solution.py:44
  4.8 11.0 %collective-permute-start.8 = (s32[2,512]{1,0:T(2,128)S(1)}, s32[2,512]{1,0:T(2,128)S(1)}, u32[]{:S(2)}, u32[]{:S(2)}) collective-permute-start(s32[2,512]{1,0:T(2,128)S(1)} %get-tuple-element.42), channel_id=1, source_target_pairs={{0,16},{16,32},{32,48},{48,64},{64,80},{80,96},{96,112},{112,128},... | collective-permute-start | bytes 12296 | tf_op jit(solution)/shard_map/ppermute | solution.py:31
  7.2 8.6 %collective-permute-start.9 = (s32[2,512]{1,0:T(2,128)S(1)}, s32[2,512]{1,0:T(2,128)S(1)}, u32[]{:S(2)}, u32[]{:S(2)}) collective-permute-start(s32[2,512]{1,0:T(2,128)S(1)} %get-tuple-element.43), channel_id=1, source_target_pairs={{16,0},{32,16},{48,32},{64,48},{80,64},{96,80},{112,96},{128,112},... | collective-permute-start | bytes 12296 | tf_op jit(solution)/shard_map/ppermute | solution.py:33
  13.5 5.2 %collective-permute-start.1 = (s32[513]{0:T(1024)S(1)}, s32[513]{0:T(1024)S(1)}, u32[]{:S(2)}, u32[]{:S(2)}) collective-permute-start(s32[513]{0:T(1024)S(1)} %fusion.73), channel_id=1, source_target_pairs={{0,32},{16,48},{32,0},{48,16},{64,96},{80,112},{96,64},{112,80},{1... | collective-permute-start | bytes 6164 | tf_op jit(solution)/shard_map/ppermute | solution.py:44
  18.7 3.6 %collective-permute-start.2 = (s32[513]{0:T(1024)S(1)}, s32[513]{0:T(1024)S(1)}, u32[]{:S(2)}, u32[]{:S(2)}) collective-permute-start(s32[513]{0:T(1024)S(1)} %add.269), channel_id=1, source_target_pairs={{0,64},{16,80},{32,96},{48,112},{64,0},{80,16},{96,32},{112,48},{1... | collective-permute-start | bytes 6164 | tf_op jit(solution)/shard_map/ppermute | solution.py:44
  22.3 5.1 %collective-permute-start.3 = (s32[513]{0:T(1024)S(1)}, s32[513]{0:T(1024)S(1)}, u32[]{:S(2)}, u32[]{:S(2)}) collective-permute-start(s32[513]{0:T(1024)S(1)} %add.270), channel_id=1, source_target_pairs={{0,128},{16,144},{32,160},{48,176},{64,192},{80,208},{96,224},{112... | collective-permute-start | bytes 6164 | tf_op jit(solution)/shard_map/ppermute | solution.py:44
  29.7 13.0 %collective-permute-start.10 = (bf16[2,512,256]{2,1,0:T(8,128)(2,1)S(1)}, bf16[2,512,256]{2,1,0:T(8,128)(2,1)S(1)}, u32[]{:S(2)}, u32[]{:S(2)}) collective-permute-start(bf16[2,512,256]{2,1,0:T(8,128)(2,1)S(1)} %get-tuple-element.38), channel_id=1, source_target_pairs={{0,16},{16,32},{32,48},{48,64},{64,80},{80,96},{96,112},{112,128},... | collective-permute-start | bytes 1572872 | tf_op jit(solution)/shard_map/ppermute | solution.py:31
  31.7 12.8 %collective-permute-start.11 = (bf16[2,512,256]{2,1,0:T(8,128)(2,1)S(1)}, bf16[2,512,256]{2,1,0:T(8,128)(2,1)S(1)}, u32[]{:S(2)}, u32[]{:S(2)}) collective-permute-start(bf16[2,512,256]{2,1,0:T(8,128)(2,1)S(1)} %get-tuple-element.39), channel_id=1, source_target_pairs={{16,0},{32,16},{48,32},{64,48},{80,64},{96,80},{112,96},{128,112},... | collective-permute-start | bytes 1572872 | tf_op jit(solution)/shard_map/ppermute | solution.py:33
  37.8 31.5 %collective-permute-start.4 = (bf16[2048,256]{1,0:T(8,128)(2,1)S(1)}, bf16[2048,256]{1,0:T(8,128)(2,1)S(1)}, u32[]{:S(2)}, u32[]{:S(2)}) collective-permute-start(bf16[2048,256]{1,0:T(8,128)(2,1)S(1)} %bitcast.6), channel_id=1, source_target_pairs={{0,1},{1,9},{9,8},{8,0},{2,3},{3,11},{11,10},{10,2},{4,5},{5,13},{... | collective-permute-start | bytes 3145736 | tf_op jit(solution)/shard_map/ppermute | solution.py:64
  39.8 30.1 %collective-permute-start.6 = (bf16[2048,256]{1,0:T(8,128)(2,1)S(1)}, bf16[2048,256]{1,0:T(8,128)(2,1)S(1)}, u32[]{:S(2)}, u32[]{:S(2)}) collective-permute-start(bf16[2048,256]{1,0:T(8,128)(2,1)S(1)} %bitcast.7), channel_id=1, source_target_pairs={{1,0},{9,1},{8,9},{0,8},{3,2},{11,3},{10,11},{2,10},{5,4},{13,5},{... | collective-permute-start | bytes 3145736 | tf_op jit(solution)/shard_map/ppermute | solution.py:65
  56.3 60.8 %collective-permute-start.12 = (bf16[2048,256]{1,0:T(8,128)(2,1)S(1)}, bf16[2048,256]{1,0:T(8,128)(2,1)}, u32[]{:S(2)}, u32[]{:S(2)}) collective-permute-start(bf16[2048,256]{1,0:T(8,128)(2,1)S(1)} %bitcast.12), channel_id=1, source_target_pairs={{0,2},{2,4},{4,6},{6,0},{1,3},{3,5},{5,7},{7,1},{8,10},{10,12},{12... | collective-permute-start | bytes 3145736 | tf_op jit(solution)/shard_map/ppermute | solution.py:64
  60.8 62.1 %collective-permute-start.20 = (bf16[2048,256]{1,0:T(8,128)(2,1)S(1)}, bf16[2048,256]{1,0:T(8,128)(2,1)}, u32[]{:S(2)}, u32[]{:S(2)}) collective-permute-start(bf16[2048,256]{1,0:T(8,128)(2,1)S(1)} %bitcast.13), channel_id=1, source_target_pairs={{2,0},{4,2},{6,4},{0,6},{3,1},{5,3},{7,5},{1,7},{10,8},{12,10},{14... | collective-permute-start | bytes 3145736 | tf_op jit(solution)/shard_map/ppermute | solution.py:65
  69.3 2.3 %copy-start.1 = (bf16[2048,256]{1,0:T(8,128)(2,1)}, bf16[2048,256]{1,0:T(8,128)(2,1)S(1)}, u32[]{:S(2)}) copy-start(bf16[2048,256]{1,0:T(8,128)(2,1)S(1)} %collective-permute-done.4) | copy-start | bytes 3145732
  69.3 59.0 %collective-permute-start.5 = (bf16[1024,256]{1,0:T(8,128)(2,1)S(1)}, bf16[1024,256]{1,0:T(8,128)(2,1)}, u32[]{:S(2)}, u32[]{:S(2)}) collective-permute-start(bf16[1024,256]{1,0:T(8,128)(2,1)S(1)} %slice.341), channel_id=1, source_target_pairs={{0,1},{1,9},{9,8},{8,0},{2,3},{3,11},{11,10},{10,2},{4,5},{5,13},{... | collective-permute-start | bytes 1572872 | tf_op jit(solution)/shard_map/ppermute | solution.py:67
  69.9 1.6 copy-start.4
  70.0 58.4 %collective-permute-start.7 = (bf16[1024,256]{1,0:T(8,128)(2,1)S(1)}, bf16[1024,256]{1,0:T(8,128)(2,1)}, u32[]{:S(2)}, u32[]{:S(2)}) collective-permute-start(bf16[1024,256]{1,0:T(8,128)(2,1)S(1)} %slice.342), channel_id=1, source_target_pairs={{1,0},{9,1},{8,9},{0,8},{3,2},{11,3},{10,11},{2,10},{5,4},{13,5},{... | collective-permute-start | bytes 1572872 | tf_op jit(solution)/shard_map/ppermute | solution.py:68
  71.5 56.8 %copy-start.2 = (bf16[2048,256]{1,0:T(8,128)(2,1)S(1)}, bf16[2048,256]{1,0:T(8,128)(2,1)}, u32[]{:S(2)}) copy-start(bf16[2048,256]{1,0:T(8,128)(2,1)} %copy-done.1) | copy-start | bytes 3145732
  71.5 56.8 %copy-start.5 = (bf16[2048,256]{1,0:T(8,128)(2,1)S(1)}, bf16[2048,256]{1,0:T(8,128)(2,1)}, u32[]{:S(2)}) copy-start(bf16[2048,256]{1,0:T(8,128)(2,1)} %copy-done.4) | copy-start | bytes 3145732
  118.2 21.4 %collective-permute-start.19 = (bf16[1024,256]{1,0:T(8,128)(2,1)S(1)}, bf16[1024,256]{1,0:T(8,128)(2,1)S(1)}, u32[]{:S(2)}, u32[]{:S(2)}) collective-permute-start(bf16[1024,256]{1,0:T(8,128)(2,1)S(1)} %slice.395), channel_id=1, source_target_pairs={{0,2},{2,4},{4,6},{6,0},{1,3},{3,5},{5,7},{7,1},{8,10},{10,12},{12... | collective-permute-start | bytes 1572872 | tf_op jit(solution)/shard_map/ppermute | solution.py:67
  124.0 20.8 %collective-permute-start.21 = (bf16[1024,256]{1,0:T(8,128)(2,1)S(1)}, bf16[1024,256]{1,0:T(8,128)(2,1)S(1)}, u32[]{:S(2)}, u32[]{:S(2)}) collective-permute-start(bf16[1024,256]{1,0:T(8,128)(2,1)S(1)} %slice.396), channel_id=1, source_target_pairs={{2,0},{4,2},{6,4},{0,6},{3,1},{5,3},{7,5},{1,7},{10,8},{12,10},{14... | collective-permute-start | bytes 1572872 | tf_op jit(solution)/shard_map/ppermute | solution.py:68
  133.2 17.8 %collective-permute-start.13 = (f32[1024,256]{1,0:T(8,128)S(1)}, f32[1024,256]{1,0:T(8,128)}, u32[]{:S(2)}, u32[]{:S(2)}) collective-permute-start(f32[1024,256]{1,0:T(8,128)S(1)} %fusion.11), channel_id=1, source_target_pairs={{0,16},{16,0},{1,17},{17,1},{2,18},{18,2},{3,19},{19,3},{4,20},{20... | collective-permute-start | bytes 3145736 | tf_op jit(solution)/shard_map/ppermute | solution.py:173
  144.9 5.9 %copy-start.7 = (bf16[2048,256]{1,0:T(8,128)(2,1)}, bf16[2048,256]{1,0:T(8,128)(2,1)S(1)}, u32[]{:S(2)}) copy-start(bf16[2048,256]{1,0:T(8,128)(2,1)S(1)} %constant_dynamic-update-slice_fusion) | copy-start | bytes 3145732
  150.8 9.3 %collective-permute-start.22 = (f32[1024,256]{1,0:T(8,128)}, f32[1024,256]{1,0:T(8,128)}, u32[]{:S(2)}, u32[]{:S(2)}) collective-permute-start(f32[1024,256]{1,0:T(8,128)} %fusion.8), channel_id=1, source_target_pairs={{0,16},{16,0},{1,17},{17,1},{2,18},{18,2},{3,19},{19,3},{4,20},{20... | collective-permute-start | bytes 3145736 | tf_op jit(solution)/shard_map/ppermute | solution.py:173
  150.9 9.3 %copy-start.3 = (bf16[2048,256]{1,0:T(8,128)(2,1)S(1)}, bf16[2048,256]{1,0:T(8,128)(2,1)}, u32[]{:S(2)}) copy-start(bf16[2048,256]{1,0:T(8,128)(2,1)} %copy-done.1) | copy-start | bytes 3145732
  150.9 9.3 %copy-start.6 = (bf16[2048,256]{1,0:T(8,128)(2,1)S(1)}, bf16[2048,256]{1,0:T(8,128)(2,1)}, u32[]{:S(2)}) copy-start(bf16[2048,256]{1,0:T(8,128)(2,1)} %copy-done.4) | copy-start | bytes 3145732
  150.9 9.3 %copy-start.8 = (bf16[2048,256]{1,0:T(8,128)(2,1)S(1)}, bf16[2048,256]{1,0:T(8,128)(2,1)}, u32[]{:S(2)}) copy-start(bf16[2048,256]{1,0:T(8,128)(2,1)} %copy-done.7) | copy-start | bytes 3145732
  155.4 13.6 %collective-permute-start.14 = (f32[256,256]{1,0:T(8,128)S(1)}, f32[256,256]{1,0:T(8,128)S(1)}, u32[]{:S(2)}, u32[]{:S(2)}) collective-permute-start(f32[256,256]{1,0:T(8,128)S(1)} %get-tuple-element.32), channel_id=1, source_target_pairs={{0,64},{64,128},{128,192},{192,0},{1,65},{65,129},{129,193},{193,1... | collective-permute-start | bytes 786440 | tf_op jit(solution)/shard_map/ppermute | solution.py:177
  156.9 12.2 %collective-permute-start.15 = (f32[256,256]{1,0:T(8,128)}, f32[256,256]{1,0:T(8,128)}, u32[]{:S(2)}, u32[]{:S(2)}) collective-permute-start(f32[256,256]{1,0:T(8,128)} %get-tuple-element.34), channel_id=1, source_target_pairs={{0,128},{64,192},{128,0},{192,64},{1,129},{65,193},{129,1},{193,65... | collective-permute-start | bytes 786440 | tf_op jit(solution)/shard_map/ppermute | solution.py:177
  157.6 15.2 %collective-permute-start.16 = (f32[256,256]{1,0:T(8,128)}, f32[256,256]{1,0:T(8,128)}, u32[]{:S(2)}, u32[]{:S(2)}) collective-permute-start(f32[256,256]{1,0:T(8,128)} %get-tuple-element.33), channel_id=1, source_target_pairs={{0,192},{64,0},{128,64},{192,128},{1,193},{65,1},{129,65},{193,129... | collective-permute-start | bytes 786440 | tf_op jit(solution)/shard_map/ppermute | solution.py:177
  165.6 15.3 %collective-permute-start.23 = (f32[256,256]{1,0:T(8,128)}, f32[256,256]{1,0:T(8,128)S(1)}, u32[]{:S(2)}, u32[]{:S(2)}) collective-permute-start(f32[256,256]{1,0:T(8,128)} %get-tuple-element.35), channel_id=1, source_target_pairs={{0,64},{64,128},{128,192},{192,0},{1,65},{65,129},{129,193},{193,1... | collective-permute-start | bytes 786440 | tf_op jit(solution)/shard_map/ppermute | solution.py:177
  165.6 15.3 %collective-permute-start.24 = (f32[256,256]{1,0:T(8,128)S(1)}, f32[256,256]{1,0:T(8,128)S(1)}, u32[]{:S(2)}, u32[]{:S(2)}) collective-permute-start(f32[256,256]{1,0:T(8,128)S(1)} %get-tuple-element.37), channel_id=1, source_target_pairs={{0,128},{64,192},{128,0},{192,64},{1,129},{65,193},{129,1},{193,65... | collective-permute-start | bytes 786440 | tf_op jit(solution)/shard_map/ppermute | solution.py:177
  169.1 18.0 %collective-permute-start.25 = (f32[256,256]{1,0:T(8,128)S(1)}, f32[256,256]{1,0:T(8,128)}, u32[]{:S(2)}, u32[]{:S(2)}) collective-permute-start(f32[256,256]{1,0:T(8,128)S(1)} %get-tuple-element.36), channel_id=1, source_target_pairs={{0,192},{64,0},{128,64},{192,128},{1,193},{65,1},{129,65},{193,129... | collective-permute-start | bytes 786440 | tf_op jit(solution)/shard_map/ppermute | solution.py:177
  173.9 44.4 %collective-permute-start.17 = (f32[256,256]{1,0:T(8,128)S(1)}, f32[256,256]{1,0:T(8,128)S(1)}, u32[]{:S(2)}, u32[]{:S(2)}) collective-permute-start(f32[256,256]{1,0:T(8,128)S(1)} %add_add_fusion.1), channel_id=1, source_target_pairs={{0,0},{1,17},{2,34},{3,51},{4,68},{5,85},{6,102},{7,119},{8,136},{... | collective-permute-start | bytes 786440 | tf_op jit(solution)/shard_map/ppermute | solution.py:185
  180.2 38.1 %collective-permute-start.18 = (f32[256,256]{1,0:T(8,128)S(1)}, f32[256,256]{1,0:T(8,128)S(1)}, u32[]{:S(2)}, u32[]{:S(2)}) collective-permute-start(f32[256,256]{1,0:T(8,128)S(1)} %add_add_fusion.1), channel_id=1, source_target_pairs={{32,0},{33,17},{34,34},{35,51},{36,68},{37,85},{38,102},{39,119},{... | collective-permute-start | bytes 786440 | tf_op jit(solution)/shard_map/ppermute | solution.py:185
  188.1 30.2 %collective-permute-start.26 = (f32[256,256]{1,0:T(8,128)S(1)}, f32[256,256]{1,0:T(8,128)S(1)}, u32[]{:S(2)}, u32[]{:S(2)}) collective-permute-start(f32[256,256]{1,0:T(8,128)S(1)} %add_add_fusion), channel_id=1, source_target_pairs={{0,64},{1,81},{2,98},{3,115},{4,4},{5,21},{6,38},{7,55},{8,200},{9... | collective-permute-start | bytes 786440 | tf_op jit(solution)/shard_map/ppermute | solution.py:185
  191.1 27.2 %collective-permute-start.27 = (f32[256,256]{1,0:T(8,128)S(1)}, f32[256,256]{1,0:T(8,128)S(1)}, u32[]{:S(2)}, u32[]{:S(2)}) collective-permute-start(f32[256,256]{1,0:T(8,128)S(1)} %add_add_fusion), channel_id=1, source_target_pairs={{32,64},{33,81},{34,98},{35,115},{36,4},{37,21},{38,38},{39,55},{4... | collective-permute-start | bytes 786440 | tf_op jit(solution)/shard_map/ppermute | solution.py:185
  192.4 1.3 collective-permute-start.28
  195.0 12.7 %collective-permute-start.29 = (s32[1]{0:T(128)}, s32[1]{0:T(128)}, u32[]{:S(2)}, u32[]{:S(2)}) collective-permute-start(s32[1]{0:T(128)} %add.347), channel_id=1, source_target_pairs={{0,32},{16,48},{32,0},{48,16},{64,96},{80,112},{96,64},{112,80},{1... | collective-permute-start | bytes 20 | tf_op jit(solution)/shard_map/ppermute | solution.py:44
  208.2 3.6 %collective-permute-start.30 = (s32[1]{0:T(128)}, s32[1]{0:T(128)}, u32[]{:S(2)}, u32[]{:S(2)}) collective-permute-start(s32[1]{0:T(128)} %add.348), channel_id=1, source_target_pairs={{0,64},{16,80},{32,96},{48,112},{64,0},{80,16},{96,32},{112,48},{1... | collective-permute-start | bytes 20 | tf_op jit(solution)/shard_map/ppermute | solution.py:44
  212.5 5.1 %collective-permute-start.31 = (s32[1]{0:T(128)}, s32[1]{0:T(128)}, u32[]{:S(2)}, u32[]{:S(2)}) collective-permute-start(s32[1]{0:T(128)} %add.349), channel_id=1, source_target_pairs={{0,128},{16,144},{32,160},{48,176},{64,192},{80,208},{96,224},{112... | collective-permute-start | bytes 20 | tf_op jit(solution)/shard_map/ppermute | solution.py:44
